TPU v7x, 32 devices: a whole 2x2x4 slice. The times are simulated.
32 devices in a mesh: row: 4 (over y, x), col: 4 (over z), pts: 2 (over core).
Axes of the slice: x: 2, y: 2, z: 4, core: 2. Of those that a mesh axis runs over, the one named last changes fastest.
Arguments:
- green_panel: bfloat16 [4, 2, 512, 6144], P(None, None, 'col', 'pts'), may hold values from -6 to 6
- log_psd: float32 [2, 4, 3072], P('pts', None, ('row', 'col')), may hold values from -1.1 to 1.1
- observed: float32 [4, 2, 512, 512], P(None, None, 'row', 'col'), may hold values from -1 to 1
- pair_weights: int32 [512, 512], P('row', 'col'), may hold values from 0 to 4, as said below
Outputs:
- updated_log_psd: float32 [2, 4, 3072], P('pts', None, ('row', 'col'))
Inputs may be any that keep to these rules, and one draw needn't show every extreme that they name: pair_weights is 0 for pairs that are not listed and for every station paired with itself; the share of listed pairs differs from one block of 128 x 128 pairs (one index of row by one of col) to another, and some such blocks list no pair.
All inputs are finite; a program needn't handle non-finite values.
Results may differ from a plain program's by a relative error of at most 0.0014.
Values may be sent and summed in bfloat16 or wider, within the bound.
No kernel may reach another device: no remote copies, remote signals or barrier semaphores. Data moves between devices by JAX's collectives and lax.ppermute only.
A program may use at most 64 MiB of HBM per device.

v0:
```python
import jax
import jax.numpy as jnp
from jax import lax
from jax.sharding import PartitionSpec as P

ITERS = 2


epsilon = 1e-06
descent = 0.1


def from_root(block, axis, source):
    block = jnp.where(lax.axis_index(axis) == source, block, jnp.zeros_like(block))
    return lax.psum(block, axis)


def pair_total(partial_value):
    return lax.psum(partial_value.astype(jnp.bfloat16), "pts").astype(jnp.float32)


def descend(log_field, gradient, entry_count):
    squares = lax.psum(jnp.sum(gradient * gradient), ("row", "col", "pts"))
    return log_field - descent * gradient / jnp.sqrt(squares / entry_count + epsilon)


def correlate(left_rows, weighted):
    half_a = left_rows.shape[1] // 2
    half_b = weighted.shape[1] // 2
    products = jnp.einsum("fan,fbn->fab", left_rows, weighted, preferred_element_type=jnp.float32)
    corr_real = products[:, :half_a, :half_b] + products[:, half_a:, half_b:]
    corr_imag = products[:, half_a:, :half_b] - products[:, :half_a, half_b:]
    return jnp.stack([corr_real, corr_imag], axis=1)


def adjoint_block(adjoint):
    adj_real = adjoint[:, 0]
    adj_imag = adjoint[:, 1]
    top_half = jnp.concatenate([adj_real, -adj_imag], axis=2)
    low_half = jnp.concatenate([adj_imag, adj_real], axis=2)
    return jnp.concatenate([top_half, low_half], axis=1)


def point_terms(adjoint, right_rows, left_rows, psd_field, quad_weight):
    accumulated = jnp.einsum(
        "fab,fbn->fan", adjoint_block(adjoint), right_rows, preferred_element_type=jnp.float32
    )
    return quad_weight * psd_field * jnp.sum(left_rows * accumulated, axis=1)


def body(green_panel, log_psd, observed, pair_weights):
    freq_count, comp_count, span_j, local_pts = green_panel.shape
    span_i = observed.shape[2]
    row_count = lax.axis_size("row")
    col_count = lax.axis_size("col")
    pts_count = lax.axis_size("pts")
    quad_weight = 1.0 / (pts_count * local_pts)
    entry_count = freq_count * pts_count * local_pts
    pair_scale = pair_weights.astype(jnp.float32)
    log_start = log_psd[0]
    group_ratio = col_count // row_count
    pieces = []
    for member in range(group_ratio):
        pieces.append(from_root(green_panel, "col", lax.axis_index("row") * group_ratio + member))
    rows_block = jnp.concatenate(pieces, axis=2).reshape(freq_count, 2 * span_i, local_pts)
    cols_block = green_panel.reshape(freq_count, 2 * span_j, local_pts)

    def run_sweep(sweep_idx, log_field):
        whole_log = lax.all_gather(log_field, ("row", "col"), axis=1, tiled=True)
        psd_field = jnp.exp(whole_log)
        weighted = (green_panel * psd_field[:, None, None, :]).astype(jnp.bfloat16)
        weighted = weighted.reshape(freq_count, 2 * span_j, local_pts)
        partial_value = correlate(rows_block, weighted)
        pair_sum = pair_total(partial_value)
        adjoint = (pair_scale * (quad_weight * pair_sum - observed)).astype(jnp.bfloat16)
        point_part = point_terms(adjoint, cols_block, rows_block, psd_field, quad_weight)
        gradient = lax.psum_scatter(point_part, ("row", "col"), scatter_dimension=1, tiled=True)
        return descend(log_field, gradient, entry_count)

    log_final = lax.fori_loop(0, ITERS, run_sweep, log_start)
    return log_final[None]


def solution(mesh):
    return jax.shard_map(
        body,
        mesh=mesh,
        in_specs=(
            P(None, None, "col", "pts"),
            P("pts", None, ("row", "col")),
            P(None, None, "row", "col"),
            P("row", "col"),
        ),
        out_specs=P("pts", None, ("row", "col")),
        check_vma=False,
    )
```

profile of v0, /device:TPU:0, one launch (start us, length us, event | category | flops | bytes accessed | tf_op | source)
XLA Modules:
  0.0 727.3 jit_solution(13803645193533125202)
XLA Ops:
  6.5 5.8 broadcast_select_fusion
  12.4 1.0 copy-done
  13.4 0.2 copy.19
  13.6 0.1 copy.18
  13.8 224.4 %all-reduce.3.cloned.1.call-done = bf16[4,256,3072]{2,1,0:T(8,128)(2,1)} async-done(((bf16[4,256,3072]{2,1,0:T(8,128)(2,1)}), bf16[4,256,3072]{2,1,0:T(8,128)(2,1)}) %all-reduce.3.cloned.1.call-update) | async-done | bytes 6291472 | tf_op jit(solution)/shard_map/psum | solution.py:15
  238.1 482.1 %while.10 = (s32[]{:T(128)}, f32[4,192]{1,0:T(4,128)S(1)}, bf16[4,256,3072]{2,1,0:T(8,128)(2,1)}, f32[128,128]{0,1:T(8,128)S(1)}, bf16[4,2,128,3072]{3,2,1,0:T(8...) while((s32[]{:T(128)}, f32[4,192]{1,0:T(4,128)S(1)}, ...), condition=%wide.region_7.8_spmd, body=%wide.region_1.7_spmd.sunk | while | flops 3243458304 | bytes 34303204 | solution.py:80
  238.2 39.0 %all-gather.2 = f32[16,192,4]{1,2,0:T(4,128)S(1)} all-gather(f32[1,192,4]{1,2,0:T(4,128)S(1)} %bitcast.59), channel_id=1, replica_groups=mesh['row'=4,'col'=4,'pts'=2] {'row','col'}, dimensions={0}, use_global_device_ids=true | all-gather | bytes 52224 | tf_op jit(solution)/shard_map/while/body/eval_jaxpr/all_gather | solution.py:69
  277.1 0.1 reshape.21
  277.2 6.4 fusion.33
  283.7 0.1 fusion.34
  283.7 0.7 pad_maximum_fusion.2
  284.6 14.6 %all-reduce.5.cloned.1.call-done = bf16[4,2,128,128]{2,3,0,1:T(8,128)(2,1)} async-done(((bf16[4,2,128,128]{2,3,0,1:T(8,128)(2,1)}), bf16[4,2,128,128]{2,3,0,1:T(8,128)(2,1)}) %all-reduce.5.cloned.1.call-update) | async-done | bytes 262160 | tf_op jit(solution)/shard_map/while/body/eval_jaxpr/psum | solution.py:19
  299.2 1.0 multiply_convert_fusion.2
  300.3 6.8 multiply_reduce_fusion.4
  307.1 1.7 copy.28
  308.8 127.5 %reduce-scatter.6.cloned.1.call-done = f32[192,4]{1,0:T(8,128)} async-done(((f32[3072,4]{1,0:T(8,128)}), f32[192,4]{1,0:T(8,128)}) %reduce-scatter.6.cloned.1.call-update) | async-done | bytes 3088 | tf_op jit(solution)/shard_map/while
  436.3 1.0 copy.29
  437.3 0.6 multiply_reduce_fusion.5
  437.9 40.0 %psum.25 = f32[]{:T(128)} all-reduce(f32[]{:T(128)} %multiply_reduce_fusion.5), channel_id=1, replica_groups=mesh['row'=4,'col'=4,'pts'=2] {'row','col','pts'}, use_global_device_ids=true, to_apply=%region_6.6 | all-reduce | flops 1 | bytes 8 | tf_op jit(solution)/shard_map/while/body/eval_jaxpr/psum | solution.py:23
  478.6 39.4 %all-gather.2 = f32[16,192,4]{1,2,0:T(4,128)S(1)} all-gather(f32[1,192,4]{1,2,0:T(4,128)S(1)} %bitcast.59), channel_id=1, replica_groups=mesh['row'=4,'col'=4,'pts'=2] {'row','col'}, dimensions={0}, use_global_device_ids=true | all-gather | bytes 52224 | tf_op jit(solution)/shard_map/while/body/eval_jaxpr/all_gather | solution.py:69
  518.1 0.1 reshape.21
  518.2 6.4 fusion.33
  524.7 0.7 pad_maximum_fusion.2
  525.5 15.4 %all-reduce.5.cloned.1.call-done = bf16[4,2,128,128]{2,3,0,1:T(8,128)(2,1)} async-done(((bf16[4,2,128,128]{2,3,0,1:T(8,128)(2,1)}), bf16[4,2,128,128]{2,3,0,1:T(8,128)(2,1)}) %all-reduce.5.cloned.1.call-update) | async-done | bytes 262160 | tf_op jit(solution)/shard_map/while/body/eval_jaxpr/psum | solution.py:19
  540.9 1.0 multiply_convert_fusion.2
  542.0 6.8 multiply_reduce_fusion.4
  548.8 1.7 copy.28
  550.4 127.5 %reduce-scatter.6.cloned.1.call-done = f32[192,4]{1,0:T(8,128)} async-done(((f32[3072,4]{1,0:T(8,128)}), f32[192,4]{1,0:T(8,128)}) %reduce-scatter.6.cloned.1.call-update) | async-done | bytes 3088 | tf_op jit(solution)/shard_map/while
  677.9 1.0 copy.29
  678.9 0.6 multiply_reduce_fusion.5
  679.5 40.0 %psum.25 = f32[]{:T(128)} all-reduce(f32[]{:T(128)} %multiply_reduce_fusion.5), channel_id=1, replica_groups=mesh['row'=4,'col'=4,'pts'=2] {'row','col','pts'}, use_global_device_ids=true, to_apply=%region_6.6 | all-reduce | flops 1 | bytes 8 | tf_op jit(solution)/shard_map/while/body/eval_jaxpr/psum | solution.py:23
  720.2 0.6 copy-done.1
  (28 shorter events, 0.5 us)
Async XLA Ops:
  6.5 231.6 %all-reduce.3.cloned.1.call-start = ((), (), s32[]{:S(2)}) async-start(), calls=%async_computation.1 | async-start | bytes 12582912 | tf_op jit(solution)/shard_map/psum | solution.py:15
  12.4 1.0 copy-start
  12.4 1.2 copy-start.3
  12.4 225.8 %copy-start.2 = (f32[1,4,192]{2,1,0:T(4,128)S(1)}, f32[1,4,192]{2,1,0:T(4,128)}, u32[]{:S(2)}) copy-start(f32[1,4,192]{2,1,0:T(4,128)} %param.7) | copy-start | bytes 9220
  238.1 61.0 %all-reduce.5.cloned.1.call-start = ((), (), s32[]{:S(2)}) async-start(), calls=%async_computation.2 | async-start | bytes 524288 | tf_op jit(solution)/shard_map/while/body/eval_jaxpr/psum | solution.py:19
  284.5 151.8 %reduce-scatter.6.cloned.1.call-start = ((), (), s32[]{:S(2)}) async-start(), calls=%async_computation.3 | async-start | bytes 1671168 | tf_op jit(solution)/shard_map/while
  478.6 62.3 %all-reduce.5.cloned.1.call-start = ((), (), s32[]{:S(2)}) async-start(), calls=%async_computation.2 | async-start | bytes 524288 | tf_op jit(solution)/shard_map/while/body/eval_jaxpr/psum | solution.py:19
  525.4 152.5 %reduce-scatter.6.cloned.1.call-start = ((), (), s32[]{:S(2)}) async-start(), calls=%async_computation.3 | async-start | bytes 1671168 | tf_op jit(solution)/shard_map/while
  720.2 0.6 copy-start.1
Sparse Core Ops, SparseCore 0:
  12.5 225.5 all-reduce.2
  284.6 14.5 all-reduce.4
  308.9 127.3 reduce-scatter.5
  525.5 15.2 all-reduce.4
  550.6 127.3 reduce-scatter.5
where the time goes:
time: 728 us; the launch traced here: 727 us
  waiting for transfers between devices  510 us (70%)
  blocking collectives  158 us (22%)
  matrix products  26.4 us (4%)
  between operations  13.1 us (2%)
  other arithmetic  10.9 us (1%)
  local copies, waits for them, and re-layouts  7.41 us (1%)
    while x6, waiting for transfers between devices  255 us
    psum x1, waiting for transfers between devices, from_root(): return lax.psum(block, axis)  224 us
    psum x2, blocking collectives, descend(): squares = lax.psum(jnp.sum(gradient * gradient), ('row', 'col', 'pts'))  80.1 us
    all_gather x2, blocking collectives, run_sweep(): whole_log = lax.all_gather(log_field, ('row', 'col'), axis=1, tiled=True)  78.4 us
    psum x2, waiting for transfers between devices, pair_total(): lax.psum(partial_value.astype(jnp.bfloat16), 'pts').astype(jnp.float32)  30 us
  transfers between devices with their start and end apart: 5, of which 5 were waited for; matrix products, arithmetic and copies ran while one was open for 0% of the time, Pallas kernels for 0%

commit v1 on v0

--- a/solution.py
+++ b/solution.py
@@ -15,13 +15,25 @@
     return lax.psum(block, axis)
 
 
-def pair_total(partial_value):
-    return lax.psum(partial_value.astype(jnp.bfloat16), "pts").astype(jnp.float32)
+def butterfly_sum(value, axes):
+    for axis in axes:
+        size = lax.axis_size(axis)
+        if size & (size - 1):
+            value = lax.psum(value, axis)
+            continue
+        bit = 1
+        while bit < size:
+            pairs = [(i, i ^ bit) for i in range(size)]
+            value = value + lax.ppermute(value, axis, pairs)
+            bit *= 2
+    return value
 
 
-def descend(log_field, gradient, entry_count):
-    squares = lax.psum(jnp.sum(gradient * gradient), ("row", "col", "pts"))
-    return log_field - descent * gradient / jnp.sqrt(squares / entry_count + epsilon)
+def swap_add(value, axis):
+    size = lax.axis_size(axis)
+    if size != 2:
+        return lax.psum(value, axis)
+    return value + lax.ppermute(value, axis, [(0, 1), (1, 0)])
 
 
 def correlate(left_rows, weighted):
@@ -51,13 +63,13 @@
 def body(green_panel, log_psd, observed, pair_weights):
     freq_count, comp_count, span_j, local_pts = green_panel.shape
     span_i = observed.shape[2]
+    piece = log_psd.shape[2]
     row_count = lax.axis_size("row")
     col_count = lax.axis_size("col")
     pts_count = lax.axis_size("pts")
     quad_weight = 1.0 / (pts_count * local_pts)
     entry_count = freq_count * pts_count * local_pts
     pair_scale = pair_weights.astype(jnp.float32)
-    log_start = log_psd[0]
     group_ratio = col_count // row_count
     pieces = []
     for member in range(group_ratio):
@@ -65,20 +77,26 @@
     rows_block = jnp.concatenate(pieces, axis=2).reshape(freq_count, 2 * span_i, local_pts)
     cols_block = green_panel.reshape(freq_count, 2 * span_j, local_pts)
 
-    def run_sweep(sweep_idx, log_field):
-        whole_log = lax.all_gather(log_field, ("row", "col"), axis=1, tiled=True)
-        psd_field = jnp.exp(whole_log)
+    slot = lax.axis_index("row") * col_count + lax.axis_index("col")
+    offset = slot * piece
+    placed = lax.dynamic_update_slice_in_dim(
+        jnp.zeros((freq_count, local_pts), jnp.float32), log_psd[0], offset, axis=1
+    )
+    log_field = butterfly_sum(placed, ("row", "col"))
+
+    for _ in range(ITERS):
+        psd_field = jnp.exp(log_field)
         weighted = (green_panel * psd_field[:, None, None, :]).astype(jnp.bfloat16)
         weighted = weighted.reshape(freq_count, 2 * span_j, local_pts)
-        partial_value = correlate(rows_block, weighted)
-        pair_sum = pair_total(partial_value)
+        pair_sum = swap_add(correlate(rows_block, weighted), "pts")
         adjoint = (pair_scale * (quad_weight * pair_sum - observed)).astype(jnp.bfloat16)
         point_part = point_terms(adjoint, cols_block, rows_block, psd_field, quad_weight)
-        gradient = lax.psum_scatter(point_part, ("row", "col"), scatter_dimension=1, tiled=True)
-        return descend(log_field, gradient, entry_count)
+        gradient = butterfly_sum(point_part, ("row", "col"))
+        squares = swap_add(jnp.sum(gradient * gradient), "pts")
+        log_field = log_field - descent * gradient / jnp.sqrt(squares / entry_count + epsilon)
 
-    log_final = lax.fori_loop(0, ITERS, run_sweep, log_start)
-    return log_final[None]
+    own = lax.dynamic_slice_in_dim(log_field, offset, piece, axis=1)
+    return own[None]
 
 
 def solution(mesh):

time: 728 us -> 322 us (0.44)
  waiting for transfers between devices: 510 us -> 241 us
  blocking collectives: 158 us -> 0 us
  starting transfers between devices: 0.13 us -> 19.3 us
  other arithmetic: 10.9 us -> 20.3 us
    while x6 -> x0, waiting for transfers between devices: 255 us -> none
    psum x2 -> x0, blocking collectives: 80.1 us -> none  [descend(): squares = lax.psum(jnp.sum(gradient * gradient), ('row', 'col', 'pts'))]
    all_gather x2 -> x0, blocking collectives: 78.4 us -> none  [run_sweep(): whole_log = lax.all_gather(log_field, ('row', 'col'), axis=1, tiled=True)]
    ppermute x0 -> x16, waiting for transfers between devices: none -> 49.6 us  [the longest x12 43.6 us: butterfly_sum(): value = value + lax.ppermute(value, axis, pairs)]
    psum x1, waiting for transfers between devices: 224 us -> 192 us  [from_root(): return lax.psum(block, axis)]
    psum x2 -> x0, waiting for transfers between devices: 30 us -> none  [pair_total(): lax.psum(partial_value.astype(jnp.bfloat16), 'pts').astype(jnp.float32)]
    ppermute x0 -> x16, starting transfers between devices: none -> 19.3 us  [the longest x12 19 us: butterfly_sum(): value = value + lax.ppermute(value, axis, pairs)]
    convert_element_type x2 -> x4, other arithmetic: 2.08 us -> 12 us  [the longest x2 11.8 us: body(): weighted = (green_panel * psd_field[:, None, None, :]).astype(jnp.bfloat16)]
  transfers between devices with their start and end apart: 5 -> 17, of which waited for: 5 -> 17; matrix products, arithmetic and copies ran while one was open for 0% -> 2% of each run, Pallas kernels for 0% -> 0%
where the time goes in v1:
time: 322 us
  waiting for transfers between devices  241 us (75%)
  matrix products  23.4 us (7%)
  other arithmetic  20.3 us (6%)
  starting transfers between devices  19.3 us (6%)
  between operations  16.4 us (5%)
    psum x1, waiting for transfers between devices, from_root(): return lax.psum(block, axis)  192 us
    ppermute x12, waiting for transfers between devices, butterfly_sum(): value = value + lax.ppermute(value, axis, pairs)  43.6 us
    ppermute x12, starting transfers between devices, butterfly_sum(): value = value + lax.ppermute(value, axis, pairs)  19 us
    dot_general x2, matrix products, point_terms(): jnp.einsum('fab,fbn->fan', adjoint_block(adjoint), right_rows, preferred_...  12.2 us
    convert_element_type x2, other arithmetic, body(): weighted = (green_panel * psd_field[:, None, None, :]).astype(jnp.bfloat16)  11.8 us
    dot_general x2, matrix products, correlate(): jnp.einsum('fan,fbn->fab', left_rows, weighted, preferred_element_type=jn...  11.2 us
  transfers between devices with their start and end apart: 17, of which 17 were waited for; matrix products, arithmetic and copies ran while one was open for 2% of the time, Pallas kernels for 0%

profile of v1, /device:TPU:0, one launch (start us, length us, event | category | flops | bytes accessed | tf_op | source)
XLA Modules:
  0.0 322.2 jit_solution(18257072242729465649)
XLA Ops:
  6.5 5.8 %broadcast_select_fusion = bf16[4,2,128,3072]{3,2,1,0:T(8,128)(2,1)} fusion(bf16[4,2,128,3072]{3,2,1,0:T(8,128)(2,1)} %param.4, pred[]{:T(512)S(6)} %eq.3), kind=kLoop, calls=%fused_computation.8 | loop fusion | flops 3145728 | bytes 12582913 | tf_op jit(solution)/shard_map/jit(_where)/select_n | solution.py:14
  13.4 4.0 %collective-permute-done = f32[4,3072]{1,0:T(4,128)S(1)} collective-permute-done((f32[4,3072]{1,0:T(4,128)S(1)}, f32[4,3072]{1,0:T(4,128)S(1)}, u32[]{:S(2)}, u32[]{:S(2)}) %collective-permute-start) | collective-permute-done | bytes 49184 | tf_op jit(solution)/shard_map/ppermute | solution.py:27
  17.9 3.9 %collective-permute-done.1 = f32[4,3072]{1,0:T(4,128)S(1)} collective-permute-done((f32[4,3072]{1,0:T(4,128)S(1)}, f32[4,3072]{1,0:T(4,128)S(1)}, u32[]{:S(2)}, u32[]{:S(2)}) %collective-permute-start.1) | collective-permute-done | bytes 49184 | tf_op jit(solution)/shard_map/ppermute | solution.py:27
  21.8 2.7 collective-permute-start.2
  24.5 3.4 %collective-permute-done.2 = f32[4,3072]{1,0:T(4,128)S(1)} collective-permute-done((f32[4,3072]{1,0:T(4,128)S(1)}, f32[4,3072]{1,0:T(4,128)S(1)}, u32[]{:S(2)}, u32[]{:S(2)}) %collective-permute-start.2) | collective-permute-done | bytes 49184 | tf_op jit(solution)/shard_map/ppermute | solution.py:27
  28.0 6.2 %collective-permute-start.3 = (f32[4,3072]{1,0:T(4,128)S(1)}, f32[4,3072]{1,0:T(4,128)S(1)}, u32[]{:S(2)}, u32[]{:S(2)}) collective-permute-start(f32[4,3072]{1,0:T(4,128)S(1)} %add.74), channel_id=1, source_target_pairs={{0,4},{2,6},{4,0},{6,2},{1,5},{3,7},{5,1},{7,3},{8,12},{10,14},{12... | collective-permute-start | bytes 147464 | tf_op jit(solution)/shard_map/ppermute | solution.py:27
  34.1 7.0 %collective-permute-done.3 = f32[4,3072]{1,0:T(4,128)S(1)} collective-permute-done((f32[4,3072]{1,0:T(4,128)S(1)}, f32[4,3072]{1,0:T(4,128)S(1)}, u32[]{:S(2)}, u32[]{:S(2)}) %collective-permute-start.3) | collective-permute-done | bytes 49184 | tf_op jit(solution)/shard_map/ppermute | solution.py:27
  41.1 7.2 %fusion.2 = bf16[4,2,128,3072]{3,2,1,0:T(8,128)(2,1)} fusion(bf16[4,2,128,3072]{3,2,1,0:T(8,128)(2,1)} %param.4, f32[4,3072]{1,0:T(4,128)S(1)} %get-tuple-element.9), kind=kLoop, calls=%fused_computation.6 | loop fusion | flops 9437184 | bytes 12632064 | tf_op jit(solution)/shard_map/convert_element_type | solution.py:89
  48.4 191.8 %all-reduce.2.cloned.1.call-done = bf16[4,256,3072]{2,1,0:T(8,128)(2,1)} async-done(((bf16[4,256,3072]{2,1,0:T(8,128)(2,1)}), bf16[4,256,3072]{2,1,0:T(8,128)(2,1)}) %all-reduce.2.cloned.1.call-update) | async-done | bytes 6291472 | tf_op jit(solution)/shard_map/psum | solution.py:15
  240.2 6.5 %fusion.29 = f32[4,256,256]{1,2,0:T(8,128)S(1)} fusion(bf16[4,256,3072]{2,1,0:T(8,128)(2,1)} %all-reduce.2.cloned.1.call-done, bf16[4,256,3072]{2,1,0:T(8,128)(2,1)} %bitcast.39), kind=kOutput, calls=%fused_computation.54 | convolution fusion | flops 1610612736 | bytes 13631488 | tf_op jit(solution)/shard_map/fan,fbn->fab/dot_general | solution.py:42
  247.2 1.6 collective-permute-done.4
  248.9 6.8 %fusion = f32[4,3072]{1,0:T(4,128)S(1)} fusion(bf16[4,256,3072]{2,1,0:T(8,128)(2,1)} %all-reduce.2.cloned.1.call-done, bf16[4,256,3072]{2,1,0:T(8,128)(2,1)} %bitcast.34, bf16[4,128,128]{1,2,0:T(8,128)(2,1)S(1)} %get-tuple-element.18, bf16[4,128,128]{1,2,0:T(8,128)(2,1)S(1)} %get-tuple-element.17, bf16[4,128,128]{1,2,0:T(8,128)(2,1)S(1)} %fusion.25), kind=kOutput, calls=%fused_computation.4 | convolution fusion | flops 1622134784 | bytes 13025280 | tf_op jit(solution)/shard_map/fab,fbn->fan/dot_general | solution.py:57
  255.7 1.5 collective-permute-start.5
  257.3 2.6 collective-permute-done.5
  259.9 1.5 collective-permute-start.6
  261.4 2.6 collective-permute-done.6
  264.1 4.1 %collective-permute-done.7 = f32[4,3072]{1,0:T(4,128)S(1)} collective-permute-done((f32[4,3072]{1,0:T(4,128)S(1)}, f32[4,3072]{1,0:T(4,128)S(1)}, u32[]{:S(2)}, u32[]{:S(2)}) %collective-permute-start.7) | collective-permute-done | bytes 49184 | tf_op jit(solution)/shard_map/ppermute | solution.py:27
  268.2 1.7 collective-permute-start.8
  269.9 3.4 %collective-permute-done.8 = f32[4,3072]{1,0:T(4,128)S(1)} collective-permute-done((f32[4,3072]{1,0:T(4,128)S(1)}, f32[4,3072]{1,0:T(4,128)S(1)}, u32[]{:S(2)}, u32[]{:S(2)}) %collective-permute-start.8) | collective-permute-done | bytes 49184 | tf_op jit(solution)/shard_map/ppermute | solution.py:27
  273.9 1.4 collective-permute-done.9
  276.7 4.5 %fusion.3 = bf16[4,2,128,3072]{3,2,1,0:T(8,128)(2,1)S(1)} fusion(bf16[4,2,128,3072]{3,2,1,0:T(8,128)(2,1)} %param.4, f32[4,3072]{1,0:T(4,128)S(1)} %get-tuple-element.7), kind=kLoop, calls=%fused_computation.7 | loop fusion | flops 9437184 | bytes 12632064 | tf_op jit(solution)/shard_map/convert_element_type | solution.py:89
  281.3 4.8 %fusion.30 = f32[4,256,256]{1,2,0:T(8,128)S(1)} fusion(bf16[4,256,3072]{2,1,0:T(8,128)(2,1)} %all-reduce.2.cloned.1.call-done, bf16[4,256,3072]{2,1,0:T(8,128)(2,1)S(1)} %bitcast.40), kind=kOutput, calls=%fused_computation.55 | convolution fusion | flops 1610612736 | bytes 13631488 | tf_op jit(solution)/shard_map/fan,fbn->fab/dot_general | solution.py:42
  286.4 1.7 collective-permute-done.10
  288.4 5.4 %fusion.1 = f32[4,3072]{1,0:T(4,128)S(1)} fusion(bf16[4,256,3072]{2,1,0:T(8,128)(2,1)} %all-reduce.2.cloned.1.call-done, bf16[4,256,3072]{2,1,0:T(8,128)(2,1)S(1)} %bitcast.37, bf16[4,128,128]{1,2,0:T(8,128)(2,1)S(1)} %get-tuple-element.16, bf16[4,128,128]{1,2,0:T(8,128)(2,1)S(1)} %get-tuple-element.15, bf16[4,128,128]{1,2,0:T(8,128)(2,1)S(1)} %fusion.26), kind=kOutput, calls=%fused_computation.5 | convolution fusion | flops 1622134784 | bytes 13025280 | tf_op jit(solution)/shard_map/fab,fbn->fan/dot_general | solution.py:57
  293.8 1.5 collective-permute-start.11
  295.4 2.6 collective-permute-done.11
  298.0 1.5 collective-permute-start.12
  299.5 2.6 collective-permute-done.12
  302.2 4.1 %collective-permute-done.13 = f32[4,3072]{1,0:T(4,128)S(1)} collective-permute-done((f32[4,3072]{1,0:T(4,128)S(1)}, f32[4,3072]{1,0:T(4,128)S(1)}, u32[]{:S(2)}, u32[]{:S(2)}) %collective-permute-start.13) | collective-permute-done | bytes 49184 | tf_op jit(solution)/shard_map/ppermute | solution.py:27
  306.3 1.7 collective-permute-start.14
  308.0 3.4 %collective-permute-done.14 = f32[4,3072]{1,0:T(4,128)S(1)} collective-permute-done((f32[4,3072]{1,0:T(4,128)S(1)}, f32[4,3072]{1,0:T(4,128)S(1)}, u32[]{:S(2)}, u32[]{:S(2)}) %collective-permute-start.14) | collective-permute-done | bytes 49184 | tf_op jit(solution)/shard_map/ppermute | solution.py:27
  312.0 1.3 collective-permute-done.15
  (53 shorter events, 4.9 us)
Async XLA Ops:
  6.5 233.6 %all-reduce.2.cloned.1.call-start = ((), (), s32[]{:S(2)}) async-start(), calls=%async_computation | async-start | bytes 12582912 | tf_op jit(solution)/shard_map/psum | solution.py:15
  12.4 0.7 copy-start.2
  13.2 4.2 %collective-permute-start = (f32[4,3072]{1,0:T(4,128)S(1)}, f32[4,3072]{1,0:T(4,128)S(1)}, u32[]{:S(2)}, u32[]{:S(2)}) collective-permute-start(f32[4,3072]{1,0:T(4,128)S(1)} %dynamic_update_slice.5), channel_id=1, source_target_pairs={{0,8},{8,0},{16,24},{24,16},{1,9},{9,1},{17,25},{25,17},{2,10},{10... | collective-permute-start | bytes 147464 | tf_op jit(solution)/shard_map/ppermute | solution.py:27
  17.6 4.2 %collective-permute-start.1 = (f32[4,3072]{1,0:T(4,128)S(1)}, f32[4,3072]{1,0:T(4,128)S(1)}, u32[]{:S(2)}, u32[]{:S(2)}) collective-permute-start(f32[4,3072]{1,0:T(4,128)S(1)} %add.72), channel_id=1, source_target_pairs={{0,16},{8,24},{16,0},{24,8},{1,17},{9,25},{17,1},{25,9},{2,18},{10... | collective-permute-start | bytes 147464 | tf_op jit(solution)/shard_map/ppermute | solution.py:27
  21.8 6.1 %collective-permute-start.2 = (f32[4,3072]{1,0:T(4,128)S(1)}, f32[4,3072]{1,0:T(4,128)S(1)}, u32[]{:S(2)}, u32[]{:S(2)}) collective-permute-start(f32[4,3072]{1,0:T(4,128)S(1)} %add.73), channel_id=1, source_target_pairs={{0,2},{2,0},{4,6},{6,4},{1,3},{3,1},{5,7},{7,5},{8,10},{10,8},{12,... | collective-permute-start | bytes 147464 | tf_op jit(solution)/shard_map/ppermute | solution.py:27
  28.0 13.1 %collective-permute-start.3 = (f32[4,3072]{1,0:T(4,128)S(1)}, f32[4,3072]{1,0:T(4,128)S(1)}, u32[]{:S(2)}, u32[]{:S(2)}) collective-permute-start(f32[4,3072]{1,0:T(4,128)S(1)} %add.74), channel_id=1, source_target_pairs={{0,4},{2,6},{4,0},{6,2},{1,5},{3,7},{5,1},{7,3},{8,12},{10,14},{12... | collective-permute-start | bytes 147464 | tf_op jit(solution)/shard_map/ppermute | solution.py:27
  240.2 6.7 %copy-start = (f32[4,2,128,128]{3,2,1,0:T(8,128)S(1)}, f32[4,2,128,128]{3,2,1,0:T(8,128)}, u32[]{:S(2)}) copy-start(f32[4,2,128,128]{3,2,1,0:T(8,128)} %param.6) | copy-start | bytes 1572868
  240.2 6.9 %copy-start.1 = (s32[128,128]{1,0:T(8,128)S(1)}, s32[128,128]{1,0:T(8,128)}, u32[]{:S(2)}) copy-start(s32[128,128]{1,0:T(8,128)} %param.7) | copy-start | bytes 196612
  246.8 2.0 collective-permute-start.4
  255.7 4.2 %collective-permute-start.5 = (f32[4,3072]{1,0:T(4,128)S(1)}, f32[4,3072]{1,0:T(4,128)S(1)}, u32[]{:S(2)}, u32[]{:S(2)}) collective-permute-start(f32[4,3072]{1,0:T(4,128)S(1)} %multiply_multiply_fusion.1), channel_id=1, source_target_pairs={{0,8},{8,0},{16,24},{24,16},{1,9},{9,1},{17,25},{25,17},{2,10},{10... | collective-permute-start | bytes 147464 | tf_op jit(solution)/shard_map/ppermute | solution.py:27
  259.9 4.2 %collective-permute-start.6 = (f32[4,3072]{1,0:T(4,128)S(1)}, f32[4,3072]{1,0:T(4,128)S(1)}, u32[]{:S(2)}, u32[]{:S(2)}) collective-permute-start(f32[4,3072]{1,0:T(4,128)S(1)} %add.78), channel_id=1, source_target_pairs={{0,16},{8,24},{16,0},{24,8},{1,17},{9,25},{17,1},{25,9},{2,18},{10... | collective-permute-start | bytes 147464 | tf_op jit(solution)/shard_map/ppermute | solution.py:27
  264.1 4.2 %collective-permute-start.7 = (f32[4,3072]{1,0:T(4,128)S(1)}, f32[4,3072]{1,0:T(4,128)S(1)}, u32[]{:S(2)}, u32[]{:S(2)}) collective-permute-start(f32[4,3072]{1,0:T(4,128)S(1)} %add.79), channel_id=1, source_target_pairs={{0,2},{2,0},{4,6},{6,4},{1,3},{3,1},{5,7},{7,5},{8,10},{10,8},{12,... | collective-permute-start | bytes 147464 | tf_op jit(solution)/shard_map/ppermute | solution.py:27
  268.2 5.1 %collective-permute-start.8 = (f32[4,3072]{1,0:T(4,128)S(1)}, f32[4,3072]{1,0:T(4,128)S(1)}, u32[]{:S(2)}, u32[]{:S(2)}) collective-permute-start(f32[4,3072]{1,0:T(4,128)S(1)} %add.80), channel_id=1, source_target_pairs={{0,4},{2,6},{4,0},{6,2},{1,5},{3,7},{5,1},{7,3},{8,12},{10,14},{12... | collective-permute-start | bytes 147464 | tf_op jit(solution)/shard_map/ppermute | solution.py:27
  273.9 1.4 collective-permute-start.9
  276.7 11.6 %slice-start = ((s8[6291456]{0:T(1024)(128)(4,1)}), s8[2097152]{0:T(1024)(128)(4,1)S(1)}, s32[]{:S(2)}) async-start(s8[6291456]{0:T(1024)(128)(4,1)} %bitcast.35), calls=%async_computation.1 | async-start | bytes 4194304
  281.3 7.0 %slice-start.1 = ((s8[6291456]{0:T(1024)(128)(4,1)}), s8[4194304]{0:T(1024)(128)(4,1)S(1)}, s32[]{:S(2)}) async-start(s8[6291456]{0:T(1024)(128)(4,1)} %bitcast.35), calls=%async_computation.2 | async-start | bytes 8388608
  286.2 2.0 collective-permute-start.10
  293.8 4.2 %collective-permute-start.11 = (f32[4,3072]{1,0:T(4,128)S(1)}, f32[4,3072]{1,0:T(4,128)S(1)}, u32[]{:S(2)}, u32[]{:S(2)}) collective-permute-start(f32[4,3072]{1,0:T(4,128)S(1)} %multiply_multiply_fusion), channel_id=1, source_target_pairs={{0,8},{8,0},{16,24},{24,16},{1,9},{9,1},{17,25},{25,17},{2,10},{10... | collective-permute-start | bytes 147464 | tf_op jit(solution)/shard_map/ppermute | solution.py:27
  298.0 4.2 %collective-permute-start.12 = (f32[4,3072]{1,0:T(4,128)S(1)}, f32[4,3072]{1,0:T(4,128)S(1)}, u32[]{:S(2)}, u32[]{:S(2)}) collective-permute-start(f32[4,3072]{1,0:T(4,128)S(1)} %add.86), channel_id=1, source_target_pairs={{0,16},{8,24},{16,0},{24,8},{1,17},{9,25},{17,1},{25,9},{2,18},{10... | collective-permute-start | bytes 147464 | tf_op jit(solution)/shard_map/ppermute | solution.py:27
  302.2 4.2 %collective-permute-start.13 = (f32[4,3072]{1,0:T(4,128)S(1)}, f32[4,3072]{1,0:T(4,128)S(1)}, u32[]{:S(2)}, u32[]{:S(2)}) collective-permute-start(f32[4,3072]{1,0:T(4,128)S(1)} %add.87), channel_id=1, source_target_pairs={{0,2},{2,0},{4,6},{6,4},{1,3},{3,1},{5,7},{7,5},{8,10},{10,8},{12,... | collective-permute-start | bytes 147464 | tf_op jit(solution)/shard_map/ppermute | solution.py:27
  306.3 5.1 %collective-permute-start.14 = (f32[4,3072]{1,0:T(4,128)S(1)}, f32[4,3072]{1,0:T(4,128)S(1)}, u32[]{:S(2)}, u32[]{:S(2)}) collective-permute-start(f32[4,3072]{1,0:T(4,128)S(1)} %add.88), channel_id=1, source_target_pairs={{0,4},{2,6},{4,0},{6,2},{1,5},{3,7},{5,1},{7,3},{8,12},{10,14},{12... | collective-permute-start | bytes 147464 | tf_op jit(solution)/shard_map/ppermute | solution.py:27
  312.0 1.3 collective-permute-start.15
Sparse Core Ops, SparseCore 0:
  12.5 227.6 all-reduce.1

commit v2 on v1

--- a/solution.py
+++ b/solution.py
@@ -21,11 +21,22 @@
         if size & (size - 1):
             value = lax.psum(value, axis)
             continue
+        me = lax.axis_index(axis)
         bit = 1
         while bit < size:
-            pairs = [(i, i ^ bit) for i in range(size)]
-            value = value + lax.ppermute(value, axis, pairs)
-            bit *= 2
+            radix = 4 if bit * 4 <= size else 2
+            got = [value]
+            for m in range(1, radix):
+                mask = m * bit
+                got.append(lax.ppermute(value, axis, [(i, i ^ mask) for i in range(size)]))
+            stacked = jnp.stack(got)
+            local = (me // bit) % radix
+            ordered = [stacked[local ^ j] for j in range(radix)]
+            if radix == 4:
+                value = (ordered[0] + ordered[1]) + (ordered[2] + ordered[3])
+            else:
+                value = ordered[0] + ordered[1]
+            bit *= radix
     return value
 
 

time: 322 us -> 318 us (0.988)
  waiting for transfers between devices: 241 us -> 229 us
  starting transfers between devices: 19.3 us -> 26.5 us
    ppermute x12 -> x18, waiting for transfers between devices: 43.6 us -> 23.1 us  [butterfly_sum(): got.append(lax.ppermute(value, axis, [(i, i ^ mask) for i in range(size)]))]
    psum x1, waiting for transfers between devices: 192 us -> 200 us  [from_root(): return lax.psum(block, axis)]
    ppermute x12 -> x18, starting transfers between devices: 19 us -> 26.2 us  [butterfly_sum(): got.append(lax.ppermute(value, axis, [(i, i ^ mask) for i in range(size)]))]
  transfers between devices with their start and end apart: 17 -> 23, of which waited for: 17 -> 21; matrix products, arithmetic and copies ran while one was open for 2% -> 2% of each run, Pallas kernels for 0% -> 0%
where the time goes in v2:
time: 318 us; the launch traced here: 317 us
  waiting for transfers between devices  229 us (72%)
  starting transfers between devices  26.5 us (8%)
  matrix products  23.4 us (7%)
  other arithmetic  20.6 us (6%)
  between operations  16.4 us (5%)
    psum x1, waiting for transfers between devices, from_root(): return lax.psum(block, axis)  200 us
    ppermute x18, starting transfers between devices, butterfly_sum(): got.append(lax.ppermute(value, axis, [(i, i ^ mask) for i in range(size)]))  26.2 us
    ppermute x18, waiting for transfers between devices, butterfly_sum(): got.append(lax.ppermute(value, axis, [(i, i ^ mask) for i in range(size)]))  23.1 us
    dot_general x2, matrix products, point_terms(): jnp.einsum('fab,fbn->fan', adjoint_block(adjoint), right_rows, preferred_...  12.2 us
    convert_element_type x2, other arithmetic, body(): weighted = (green_panel * psd_field[:, None, None, :]).astype(jnp.bfloat16)  11.8 us
    dot_general x2, matrix products, correlate(): jnp.einsum('fan,fbn->fab', left_rows, weighted, preferred_element_type=jn...  11.2 us
  transfers between devices with their start and end apart: 23, of which 21 were waited for; matrix products, arithmetic and copies ran while one was open for 2% of the time, Pallas kernels for 0%

profile of v2, /device:TPU:0, one launch (start us, length us, event | category | flops | bytes accessed | tf_op | source)
XLA Modules:
  0.0 317.2 jit_solution(8995731297583439119)
XLA Ops:
  6.5 5.8 %broadcast_select_fusion = bf16[4,2,128,3072]{3,2,1,0:T(8,128)(2,1)} fusion(bf16[4,2,128,3072]{3,2,1,0:T(8,128)(2,1)} %param.4, pred[]{:T(512)S(6)} %eq.10), kind=kLoop, calls=%fused_computation.8 | loop fusion | flops 3145728 | bytes 12582913 | tf_op jit(solution)/shard_map/jit(_where)/select_n | solution.py:14
  13.1 1.2 collective-permute-start.2
  14.9 1.8 collective-permute-start
  16.7 2.0 collective-permute-done.2
  19.0 6.0 %collective-permute-start.5 = (f32[4,3072]{1,0:T(4,128)S(1)}, f32[4,3072]{1,0:T(4,128)S(1)}, u32[]{:S(2)}, u32[]{:S(2)}) collective-permute-start(f32[4,3072]{1,0:T(4,128)S(1)} %fusion.37), channel_id=1, source_target_pairs={{0,6},{2,4},{4,2},{6,0},{1,7},{3,5},{5,3},{7,1},{8,14},{10,12},{12... | collective-permute-start | bytes 147464 | tf_op jit(solution)/shard_map/ppermute | solution.py:31
  25.7 2.8 collective-permute-done.5
  28.5 6.1 %collective-permute-done.4 = f32[4,3072]{1,0:T(4,128)S(1)} collective-permute-done((f32[4,3072]{1,0:T(4,128)S(1)}, f32[4,3072]{1,0:T(4,128)S(1)}, u32[]{:S(2)}, u32[]{:S(2)}) %collective-permute-start.4) | collective-permute-done | bytes 49184 | tf_op jit(solution)/shard_map/ppermute | solution.py:31
  34.7 7.2 %fusion.2 = bf16[4,2,128,3072]{3,2,1,0:T(8,128)(2,1)} fusion(bf16[4,2,128,3072]{3,2,1,0:T(8,128)(2,1)} %param.4, f32[4,3072]{1,0:T(4,128)S(1)} %get-tuple-element.11), kind=kLoop, calls=%fused_computation.6 | loop fusion | flops 9437184 | bytes 12632064 | tf_op jit(solution)/shard_map/convert_element_type | solution.py:100
  41.9 200.2 %all-reduce.2.cloned.1.call-done = bf16[4,256,3072]{2,1,0:T(8,128)(2,1)} async-done(((bf16[4,256,3072]{2,1,0:T(8,128)(2,1)}), bf16[4,256,3072]{2,1,0:T(8,128)(2,1)}) %all-reduce.2.cloned.1.call-update) | async-done | bytes 6291472 | tf_op jit(solution)/shard_map/psum | solution.py:15
  242.1 6.5 %fusion.27 = f32[4,256,256]{1,2,0:T(8,128)S(1)} fusion(bf16[4,256,3072]{2,1,0:T(8,128)(2,1)} %all-reduce.2.cloned.1.call-done, bf16[4,256,3072]{2,1,0:T(8,128)(2,1)} %bitcast.73), kind=kOutput, calls=%fused_computation.68 | convolution fusion | flops 1610612736 | bytes 13631488 | tf_op jit(solution)/shard_map/fan,fbn->fab/dot_general | solution.py:53
  249.2 1.6 collective-permute-done.6
  250.9 6.8 %fusion = f32[4,3072]{1,0:T(4,128)S(1)} fusion(bf16[4,256,3072]{2,1,0:T(8,128)(2,1)} %all-reduce.2.cloned.1.call-done, bf16[4,256,3072]{2,1,0:T(8,128)(2,1)} %bitcast.68, bf16[4,128,128]{1,2,0:T(8,128)(2,1)S(1)} %get-tuple-element.20, bf16[4,128,128]{1,2,0:T(8,128)(2,1)S(1)} %get-tuple-element.19, bf16[4,128,128]{1,2,0:T(8,128)(2,1)S(1)} %fusion.25), kind=kOutput, calls=%fused_computation.4 | convolution fusion | flops 1622134784 | bytes 13025280 | tf_op jit(solution)/shard_map/fab,fbn->fan/dot_general | solution.py:68
  257.7 2.4 collective-permute-start.9
  261.3 1.5 collective-permute-done.9
  262.8 1.5 collective-permute-done.8
  264.9 1.3 collective-permute-start.12
  266.3 3.0 collective-permute-start.10
  269.3 1.5 collective-permute-done.12
  270.8 1.0 collective-permute-done.11
  272.6 1.3 collective-permute-done.13
  275.2 4.5 %fusion.3 = bf16[4,2,128,3072]{3,2,1,0:T(8,128)(2,1)S(1)} fusion(bf16[4,2,128,3072]{3,2,1,0:T(8,128)(2,1)} %param.4, f32[4,3072]{1,0:T(4,128)S(1)} %get-tuple-element.7), kind=kLoop, calls=%fused_computation.7 | loop fusion | flops 9437184 | bytes 12632064 | tf_op jit(solution)/shard_map/convert_element_type | solution.py:100
  279.8 4.8 %fusion.28 = f32[4,256,256]{1,2,0:T(8,128)S(1)} fusion(bf16[4,256,3072]{2,1,0:T(8,128)(2,1)} %all-reduce.2.cloned.1.call-done, bf16[4,256,3072]{2,1,0:T(8,128)(2,1)S(1)} %bitcast.74), kind=kOutput, calls=%fused_computation.69 | convolution fusion | flops 1610612736 | bytes 13631488 | tf_op jit(solution)/shard_map/fan,fbn->fab/dot_general | solution.py:53
  284.9 1.7 collective-permute-done.14
  286.8 5.4 %fusion.1 = f32[4,3072]{1,0:T(4,128)S(1)} fusion(bf16[4,256,3072]{2,1,0:T(8,128)(2,1)} %all-reduce.2.cloned.1.call-done, bf16[4,256,3072]{2,1,0:T(8,128)(2,1)S(1)} %bitcast.71, bf16[4,128,128]{1,2,0:T(8,128)(2,1)S(1)} %get-tuple-element.18, bf16[4,128,128]{1,2,0:T(8,128)(2,1)S(1)} %get-tuple-element.17, bf16[4,128,128]{1,2,0:T(8,128)(2,1)S(1)} %fusion.26), kind=kOutput, calls=%fused_computation.5 | convolution fusion | flops 1622134784 | bytes 13025280 | tf_op jit(solution)/shard_map/fab,fbn->fan/dot_general | solution.py:68
  292.3 1.5 collective-permute-start.17
  294.4 1.4 collective-permute-start.15
  295.9 1.5 collective-permute-done.17
  298.6 2.3 collective-permute-start.20
  301.6 1.4 collective-permute-start.18
  303.1 1.6 collective-permute-done.20
  304.6 1.7 collective-permute-done.19
  307.1 1.3 collective-permute-done.21
  (69 shorter events, 10.3 us)
Async XLA Ops:
  6.5 235.6 %all-reduce.2.cloned.1.call-start = ((), (), s32[]{:S(2)}) async-start(), calls=%async_computation | async-start | bytes 12582912 | tf_op jit(solution)/shard_map/psum | solution.py:15
  12.3 0.7 copy-start.2
  13.1 5.6 %collective-permute-start.2 = (f32[4,3072]{1,0:T(4,128)S(1)}, f32[4,3072]{1,0:T(4,128)S(1)}, u32[]{:S(2)}, u32[]{:S(2)}) collective-permute-start(f32[4,3072]{1,0:T(4,128)S(1)} %dynamic_update_slice.3), channel_id=1, source_target_pairs={{0,24},{8,16},{16,8},{24,0},{1,25},{9,17},{17,9},{25,1},{2,26},{10... | collective-permute-start | bytes 147464 | tf_op jit(solution)/shard_map/ppermute | solution.py:31
  14.4 4.5 %collective-permute-start.1 = (f32[4,3072]{1,0:T(4,128)S(1)}, f32[4,3072]{1,0:T(4,128)S(1)}, u32[]{:S(2)}, u32[]{:S(2)}) collective-permute-start(f32[4,3072]{1,0:T(4,128)S(1)} %dynamic_update_slice.3), channel_id=1, source_target_pairs={{0,16},{8,24},{16,0},{24,8},{1,17},{9,25},{17,1},{25,9},{2,18},{10... | collective-permute-start | bytes 147464 | tf_op jit(solution)/shard_map/ppermute | solution.py:31
  14.9 4.1 %collective-permute-start = (f32[4,3072]{1,0:T(4,128)S(1)}, f32[4,3072]{1,0:T(4,128)S(1)}, u32[]{:S(2)}, u32[]{:S(2)}) collective-permute-start(f32[4,3072]{1,0:T(4,128)S(1)} %dynamic_update_slice.3), channel_id=1, source_target_pairs={{0,8},{8,0},{16,24},{24,16},{1,9},{9,1},{17,25},{25,17},{2,10},{10... | collective-permute-start | bytes 147464 | tf_op jit(solution)/shard_map/ppermute | solution.py:31
  19.0 9.4 %collective-permute-start.5 = (f32[4,3072]{1,0:T(4,128)S(1)}, f32[4,3072]{1,0:T(4,128)S(1)}, u32[]{:S(2)}, u32[]{:S(2)}) collective-permute-start(f32[4,3072]{1,0:T(4,128)S(1)} %fusion.37), channel_id=1, source_target_pairs={{0,6},{2,4},{4,2},{6,0},{1,7},{3,5},{5,3},{7,1},{8,14},{10,12},{12... | collective-permute-start | bytes 147464 | tf_op jit(solution)/shard_map/ppermute | solution.py:31
  25.0 9.6 %collective-permute-start.4 = (f32[4,3072]{1,0:T(4,128)S(1)}, f32[4,3072]{1,0:T(4,128)S(1)}, u32[]{:S(2)}, u32[]{:S(2)}) collective-permute-start(f32[4,3072]{1,0:T(4,128)S(1)} %fusion.37), channel_id=1, source_target_pairs={{0,4},{2,6},{4,0},{6,2},{1,5},{3,7},{5,1},{7,3},{8,12},{10,14},{12... | collective-permute-start | bytes 147464 | tf_op jit(solution)/shard_map/ppermute | solution.py:31
  25.0 9.6 %collective-permute-start.3 = (f32[4,3072]{1,0:T(4,128)S(1)}, f32[4,3072]{1,0:T(4,128)S(1)}, u32[]{:S(2)}, u32[]{:S(2)}) collective-permute-start(f32[4,3072]{1,0:T(4,128)S(1)} %fusion.37), channel_id=1, source_target_pairs={{0,2},{2,0},{4,6},{6,4},{1,3},{3,1},{5,7},{7,5},{8,10},{10,8},{12,... | collective-permute-start | bytes 147464 | tf_op jit(solution)/shard_map/ppermute | solution.py:31
  242.1 6.7 %copy-start = (f32[4,2,128,128]{3,2,1,0:T(8,128)S(1)}, f32[4,2,128,128]{3,2,1,0:T(8,128)}, u32[]{:S(2)}) copy-start(f32[4,2,128,128]{3,2,1,0:T(8,128)} %param.6) | copy-start | bytes 1572868
  242.1 6.9 %copy-start.1 = (s32[128,128]{1,0:T(8,128)S(1)}, s32[128,128]{1,0:T(8,128)}, u32[]{:S(2)}) copy-start(s32[128,128]{1,0:T(8,128)} %param.7) | copy-start | bytes 196612
  248.7 2.0 collective-permute-start.6
  257.7 5.1 %collective-permute-start.9 = (f32[4,3072]{1,0:T(4,128)S(1)}, f32[4,3072]{1,0:T(4,128)S(1)}, u32[]{:S(2)}, u32[]{:S(2)}) collective-permute-start(f32[4,3072]{1,0:T(4,128)S(1)} %multiply_multiply_fusion.1), channel_id=1, source_target_pairs={{0,24},{8,16},{16,8},{24,0},{1,25},{9,17},{17,9},{25,1},{2,26},{10... | collective-permute-start | bytes 147464 | tf_op jit(solution)/shard_map/ppermute | solution.py:31
  260.1 4.1 %collective-permute-start.8 = (f32[4,3072]{1,0:T(4,128)S(1)}, f32[4,3072]{1,0:T(4,128)S(1)}, u32[]{:S(2)}, u32[]{:S(2)}) collective-permute-start(f32[4,3072]{1,0:T(4,128)S(1)} %multiply_multiply_fusion.1), channel_id=1, source_target_pairs={{0,16},{8,24},{16,0},{24,8},{1,17},{9,25},{17,1},{25,9},{2,18},{10... | collective-permute-start | bytes 147464 | tf_op jit(solution)/shard_map/ppermute | solution.py:31
  260.7 4.1 %collective-permute-start.7 = (f32[4,3072]{1,0:T(4,128)S(1)}, f32[4,3072]{1,0:T(4,128)S(1)}, u32[]{:S(2)}, u32[]{:S(2)}) collective-permute-start(f32[4,3072]{1,0:T(4,128)S(1)} %multiply_multiply_fusion.1), channel_id=1, source_target_pairs={{0,8},{8,0},{16,24},{24,16},{1,9},{9,1},{17,25},{25,17},{2,10},{10... | collective-permute-start | bytes 147464 | tf_op jit(solution)/shard_map/ppermute | solution.py:31
  264.9 6.0 %collective-permute-start.12 = (f32[4,3072]{1,0:T(4,128)S(1)}, f32[4,3072]{1,0:T(4,128)S(1)}, u32[]{:S(2)}, u32[]{:S(2)}) collective-permute-start(f32[4,3072]{1,0:T(4,128)S(1)} %fusion.36), channel_id=1, source_target_pairs={{0,6},{2,4},{4,2},{6,0},{1,7},{3,5},{5,3},{7,1},{8,14},{10,12},{12... | collective-permute-start | bytes 147464 | tf_op jit(solution)/shard_map/ppermute | solution.py:31
  266.1 5.7 %collective-permute-start.11 = (f32[4,3072]{1,0:T(4,128)S(1)}, f32[4,3072]{1,0:T(4,128)S(1)}, u32[]{:S(2)}, u32[]{:S(2)}) collective-permute-start(f32[4,3072]{1,0:T(4,128)S(1)} %fusion.36), channel_id=1, source_target_pairs={{0,4},{2,6},{4,0},{6,2},{1,5},{3,7},{5,1},{7,3},{8,12},{10,14},{12... | collective-permute-start | bytes 147464 | tf_op jit(solution)/shard_map/ppermute | solution.py:31
  266.3 5.6 %collective-permute-start.10 = (f32[4,3072]{1,0:T(4,128)S(1)}, f32[4,3072]{1,0:T(4,128)S(1)}, u32[]{:S(2)}, u32[]{:S(2)}) collective-permute-start(f32[4,3072]{1,0:T(4,128)S(1)} %fusion.36), channel_id=1, source_target_pairs={{0,2},{2,0},{4,6},{6,4},{1,3},{3,1},{5,7},{7,5},{8,10},{10,8},{12,... | collective-permute-start | bytes 147464 | tf_op jit(solution)/shard_map/ppermute | solution.py:31
  272.6 1.3 collective-permute-start.13
  275.2 11.6 %slice-start = ((s8[6291456]{0:T(1024)(128)(4,1)}), s8[2097152]{0:T(1024)(128)(4,1)S(1)}, s32[]{:S(2)}) async-start(s8[6291456]{0:T(1024)(128)(4,1)} %bitcast.69), calls=%async_computation.1 | async-start | bytes 4194304
  279.8 7.0 %slice-start.1 = ((s8[6291456]{0:T(1024)(128)(4,1)}), s8[4194304]{0:T(1024)(128)(4,1)S(1)}, s32[]{:S(2)}) async-start(s8[6291456]{0:T(1024)(128)(4,1)} %bitcast.69), calls=%async_computation.2 | async-start | bytes 8388608
  284.7 2.0 collective-permute-start.14
  292.3 5.1 %collective-permute-start.17 = (f32[4,3072]{1,0:T(4,128)S(1)}, f32[4,3072]{1,0:T(4,128)S(1)}, u32[]{:S(2)}, u32[]{:S(2)}) collective-permute-start(f32[4,3072]{1,0:T(4,128)S(1)} %multiply_multiply_fusion), channel_id=1, source_target_pairs={{0,24},{8,16},{16,8},{24,0},{1,25},{9,17},{17,9},{25,1},{2,26},{10... | collective-permute-start | bytes 147464 | tf_op jit(solution)/shard_map/ppermute | solution.py:31
  293.8 4.3 %collective-permute-start.16 = (f32[4,3072]{1,0:T(4,128)S(1)}, f32[4,3072]{1,0:T(4,128)S(1)}, u32[]{:S(2)}, u32[]{:S(2)}) collective-permute-start(f32[4,3072]{1,0:T(4,128)S(1)} %multiply_multiply_fusion), channel_id=1, source_target_pairs={{0,16},{8,24},{16,0},{24,8},{1,17},{9,25},{17,1},{25,9},{2,18},{10... | collective-permute-start | bytes 147464 | tf_op jit(solution)/shard_map/ppermute | solution.py:31
  294.4 4.1 %collective-permute-start.15 = (f32[4,3072]{1,0:T(4,128)S(1)}, f32[4,3072]{1,0:T(4,128)S(1)}, u32[]{:S(2)}, u32[]{:S(2)}) collective-permute-start(f32[4,3072]{1,0:T(4,128)S(1)} %multiply_multiply_fusion), channel_id=1, source_target_pairs={{0,8},{8,0},{16,24},{24,16},{1,9},{9,1},{17,25},{25,17},{2,10},{10... | collective-permute-start | bytes 147464 | tf_op jit(solution)/shard_map/ppermute | solution.py:31
  298.6 6.0 %collective-permute-start.20 = (f32[4,3072]{1,0:T(4,128)S(1)}, f32[4,3072]{1,0:T(4,128)S(1)}, u32[]{:S(2)}, u32[]{:S(2)}) collective-permute-start(f32[4,3072]{1,0:T(4,128)S(1)} %fusion.35), channel_id=1, source_target_pairs={{0,6},{2,4},{4,2},{6,0},{1,7},{3,5},{5,3},{7,1},{8,14},{10,12},{12... | collective-permute-start | bytes 147464 | tf_op jit(solution)/shard_map/ppermute | solution.py:31
  300.9 5.4 %collective-permute-start.19 = (f32[4,3072]{1,0:T(4,128)S(1)}, f32[4,3072]{1,0:T(4,128)S(1)}, u32[]{:S(2)}, u32[]{:S(2)}) collective-permute-start(f32[4,3072]{1,0:T(4,128)S(1)} %fusion.35), channel_id=1, source_target_pairs={{0,4},{2,6},{4,0},{6,2},{1,5},{3,7},{5,1},{7,3},{8,12},{10,14},{12... | collective-permute-start | bytes 147464 | tf_op jit(solution)/shard_map/ppermute | solution.py:31
  301.6 4.7 %collective-permute-start.18 = (f32[4,3072]{1,0:T(4,128)S(1)}, f32[4,3072]{1,0:T(4,128)S(1)}, u32[]{:S(2)}, u32[]{:S(2)}) collective-permute-start(f32[4,3072]{1,0:T(4,128)S(1)} %fusion.35), channel_id=1, source_target_pairs={{0,2},{2,0},{4,6},{6,4},{1,3},{3,1},{5,7},{7,5},{8,10},{10,8},{12,... | collective-permute-start | bytes 147464 | tf_op jit(solution)/shard_map/ppermute | solution.py:31
  307.1 1.3 collective-permute-start.21
Sparse Core Ops, SparseCore 0:
  12.5 229.6 all-reduce.1

commit v3 on v2

--- a/solution.py
+++ b/solution.py
@@ -71,7 +71,7 @@
     return quad_weight * psd_field * jnp.sum(left_rows * accumulated, axis=1)
 
 
-def body(green_panel, log_psd, observed, pair_weights):
+def broadcast_body(green_panel, log_psd, observed, pair_weights):
     freq_count, comp_count, span_j, local_pts = green_panel.shape
     span_i = observed.shape[2]
     piece = log_psd.shape[2]
@@ -110,9 +110,104 @@
     return own[None]
 
 
+PAIR_PLAN = ((0, 0, 1), (1, 2, 0), (2, 0, 3), (2, 2, 1), (1, 1, 3), (3, 3, 2))
+
+
+def pair_tables(blocks):
+    role = [0] * (blocks * blocks)
+    panel_moves = []
+    needs = []
+    for line, sender, receiver in PAIR_PLAN:
+        role[line * blocks + receiver] = 1
+        panel_moves.append((line * blocks + sender, line * blocks + receiver))
+        needs.append((line * blocks + receiver, 0, receiver * blocks + sender))
+        needs.append((line * blocks + receiver, 1, sender * blocks + receiver))
+    for plane in range(blocks):
+        role[plane * blocks + plane] = 2
+    rounds = []
+    moved = [[0, 0] for _ in range(blocks * blocks)]
+    for dest, which, owner in needs:
+        if owner == dest:
+            continue
+        for number, (pairs, whiches) in enumerate(rounds):
+            if all(s != owner and d != dest for s, d in pairs):
+                pairs.append((owner, dest))
+                whiches.append((dest, which))
+                moved[dest][which] = number + 1
+                break
+        else:
+            rounds.append(([(owner, dest)], [(dest, which)]))
+            moved[dest][which] = len(rounds)
+    return role, panel_moves, rounds, moved
+
+
+def pair_body(green_panel, log_psd, observed, pair_weights):
+    freq_count, comp_count, span_j, local_pts = green_panel.shape
+    piece = log_psd.shape[2]
+    blocks = lax.axis_size("col")
+    pts_count = lax.axis_size("pts")
+    quad_weight = 1.0 / (pts_count * local_pts)
+    entry_count = freq_count * pts_count * local_pts
+    role, panel_moves, rounds, moved = pair_tables(blocks)
+    slot = lax.axis_index("row") * blocks + lax.axis_index("col")
+    my_role = jnp.array(role, jnp.int32)[slot]
+    is_diag = my_role == 2
+    axes = ("row", "col")
+
+    received = lax.ppermute(green_panel, axes, panel_moves)
+    other = jnp.where(is_diag, green_panel, received)
+    mine_rows = green_panel.reshape(freq_count, 2 * span_j, local_pts)
+    other_rows = other.reshape(freq_count, 2 * span_j, local_pts)
+
+    own_block = jnp.concatenate(
+        [observed.reshape(-1, span_j, span_j), pair_weights.astype(jnp.float32)[None]], axis=0
+    )
+    arrived = [own_block]
+    for pairs, _ in rounds:
+        arrived.append(lax.ppermute(own_block, axes, pairs))
+    arrived = jnp.stack(arrived)
+    moved_table = jnp.array(moved, jnp.int32)[slot]
+    first_block = arrived[moved_table[0]]
+    second_block = arrived[moved_table[1]]
+    obs_first = first_block[:-1].reshape(observed.shape)
+    obs_second = second_block[:-1].reshape(observed.shape)
+    scale_first = first_block[-1]
+    scale_second = second_block[-1]
+    keep_first = my_role > 0
+    keep_second = my_role == 1
+
+    offset = slot * piece
+    placed = lax.dynamic_update_slice_in_dim(
+        jnp.zeros((freq_count, local_pts), jnp.float32), log_psd[0], offset, axis=1
+    )
+    log_field = butterfly_sum(placed, axes)
+
+    for _ in range(ITERS):
+        psd_field = jnp.exp(log_field)
+        spread = psd_field[:, None, None, :]
+        weighted_mine = (green_panel * spread).astype(jnp.bfloat16).reshape(mine_rows.shape)
+        weighted_other = (other * spread).astype(jnp.bfloat16).reshape(other_rows.shape)
+        corr_first = correlate(mine_rows, weighted_other)
+        corr_second = correlate(other_rows, weighted_mine)
+        both = swap_add(jnp.stack([corr_first, corr_second]), "pts")
+        adj_first = (scale_first * (quad_weight * both[0] - obs_first)).astype(jnp.bfloat16)
+        adj_second = (scale_second * (quad_weight * both[1] - obs_second)).astype(jnp.bfloat16)
+        term_first = point_terms(adj_first, other_rows, mine_rows, psd_field, quad_weight)
+        term_second = point_terms(adj_second, mine_rows, other_rows, psd_field, quad_weight)
+        point_part = jnp.where(keep_first, term_first, 0.0) + jnp.where(keep_second, term_second, 0.0)
+        gradient = butterfly_sum(point_part, axes)
+        squares = swap_add(jnp.sum(gradient * gradient), "pts")
+        log_field = log_field - descent * gradient / jnp.sqrt(squares / entry_count + epsilon)
+
+    own = lax.dynamic_slice_in_dim(log_field, offset, piece, axis=1)
+    return own[None]
+
+
 def solution(mesh):
+    shape = mesh.shape
+    plan_fits = shape["row"] == 4 and shape["col"] == 4 and shape["pts"] == 2
     return jax.shard_map(
-        body,
+        pair_body if plan_fits else broadcast_body,
         mesh=mesh,
         in_specs=(
             P(None, None, "col", "pts"),

time: 318 us -> 285 us (0.90)
  waiting for transfers between devices: 229 us -> 143 us
  starting transfers between devices: 26.5 us -> 62.9 us
  other arithmetic: 20.6 us -> 29.8 us
  local copies, waits for them, and re-layouts: 1.1 us -> 9.12 us
  between operations: 16.4 us -> 9.04 us
  matrix products: 23.4 us -> 30.6 us
    psum x1 -> x0, waiting for transfers between devices: 200 us -> none  [from_root(): return lax.psum(block, axis)]
    ppermute x18, waiting for transfers between devices: 23.1 us -> 138 us  [butterfly_sum(): got.append(lax.ppermute(value, axis, [(i, i ^ mask) for i in range(size)]))]
    ppermute x18, starting transfers between devices: 26.2 us -> 53.4 us  [butterfly_sum(): got.append(lax.ppermute(value, axis, [(i, i ^ mask) for i in range(size)]))]
    ppermute x0 -> x3, starting transfers between devices: none -> 9.22 us  [the longest x1 7.64 us: pair_body(): received = lax.ppermute(green_panel, axes, panel_moves)]
    convert_element_type x5 -> x4, other arithmetic: 12 us -> 18.3 us  [the longest x2 18 us: pair_body(): (other * spread).astype(jnp.bfloat16).reshape(other_rows.shape)]
    select_n x1 -> x0, other arithmetic: 5.8 us -> none  [from_root(): jnp.where(lax.axis_index(axis) == source, block, jnp.zeros_like(block))]
    dot_general x2 -> x4, matrix products: 11.2 us -> 16.2 us  [correlate(): jnp.einsum('fan,fbn->fab', left_rows, weighted, preferred_element_type=jn...]
    another operation x0 -> x7, other arithmetic: none -> 4.72 us  [the longest x5 3.24 us: pair_body(): both = swap_add(jnp.stack([corr_first, corr_second]), 'pts')]
  transfers between devices with their start and end apart: 23 -> 25, of which waited for: 21 -> 17; matrix products, arithmetic and copies ran while one was open for 2% -> 3% of each run, Pallas kernels for 0% -> 0%
where the time goes in v3:
time: 285 us; the launch traced here: 284 us
  waiting for transfers between devices  143 us (50%)
  starting transfers between devices  62.9 us (22%)
  matrix products  30.6 us (11%)
  other arithmetic  29.8 us (10%)
  local copies, waits for them, and re-layouts  9.12 us (3%)
  between operations  9.04 us (3%)
    ppermute x18, waiting for transfers between devices, butterfly_sum(): got.append(lax.ppermute(value, axis, [(i, i ^ mask) for i in range(size)]))  138 us
    ppermute x18, starting transfers between devices, butterfly_sum(): got.append(lax.ppermute(value, axis, [(i, i ^ mask) for i in range(size)]))  53.4 us
    convert_element_type x2, other arithmetic, pair_body(): (other * spread).astype(jnp.bfloat16).reshape(other_rows.shape)  18 us
    dot_general x4, matrix products, correlate(): jnp.einsum('fan,fbn->fab', left_rows, weighted, preferred_element_type=jn...  16.2 us
    dot_general x4, matrix products, point_terms(): jnp.einsum('fab,fbn->fan', adjoint_block(adjoint), right_rows, preferred_...  14.3 us
    ppermute x1, starting transfers between devices, pair_body(): received = lax.ppermute(green_panel, axes, panel_moves)  7.64 us
  transfers between devices with their start and end apart: 25, of which 17 were waited for; matrix products, arithmetic and copies ran while one was open for 3% of the time, Pallas kernels for 0%

profile of v3, /device:TPU:0, one launch (start us, length us, event | category | flops | bytes accessed | tf_op | source)
XLA Modules:
  0.0 284.2 jit_solution(11944265399318943438)
XLA Ops:
  0.0 7.6 %collective-permute-start.8 = (bf16[4,2,128,3072]{3,2,1,0:T(8,128)(2,1)}, bf16[4,2,128,3072]{3,2,1,0:T(8,128)(2,1)}, u32[]{:S(2)}, u32[]{:S(2)}) collective-permute-start(bf16[4,2,128,3072]{3,2,1,0:T(8,128)(2,1)} %param.6), channel_id=1, source_target_pairs={{0,2},{12,8},{16,22},{20,18},{10,14},{30,28},{1,3},{13,9},{17,23},... | collective-permute-start | bytes 18874376 | tf_op jit(solution)/shard_map/ppermute | solution.py:157
  8.6 3.6 %collective-permute-start.1 = (f32[4,3072]{1,0:T(4,128)S(1)}, f32[4,3072]{1,0:T(4,128)S(1)}, u32[]{:S(2)}, u32[]{:S(2)}) collective-permute-start(f32[4,3072]{1,0:T(4,128)S(1)} %dynamic_update_slice.3), channel_id=1, source_target_pairs={{0,16},{8,24},{16,0},{24,8},{1,17},{9,25},{17,1},{25,9},{2,18},{10... | collective-permute-start | bytes 147464 | tf_op jit(solution)/shard_map/ppermute | solution.py:31
  12.2 1.4 collective-permute-start.2
  17.9 1.9 collective-permute-start.4
  19.8 1.9 collective-permute-start.5
  21.7 120.3 %collective-permute-done.3 = f32[4,3072]{1,0:T(4,128)S(1)} collective-permute-done((f32[4,3072]{1,0:T(4,128)S(1)}, f32[4,3072]{1,0:T(4,128)S(1)}, u32[]{:S(2)}, u32[]{:S(2)}) %collective-permute-start.3) | collective-permute-done | bytes 49184 | tf_op jit(solution)/shard_map/ppermute | solution.py:31
  143.2 10.8 %fusion.2 = (bf16[4,2,128,3072]{3,2,1,0:T(8,128)(2,1)S(1)}, bf16[4,2,128,3072]{3,2,1,0:T(8,128)(2,1)S(1)}, bf16[4,2,128,3072]{3,2,1,0:T(8,128)(2,1)}) fusion(f32[4,3072]{1,0:T(4,128)S(1)} %get-tuple-element.13, bf16[4,2,128,3072]{3,2,1,0:T(8,128)(2,1)} %param.6, bf16[4,2,128,3072]{3,2,1,0:T(8,128)(2,1)} %collective-permute-done.8, pred[]{:T(512)} %bitcast.18), kind=kLoop, calls=%fused_computation.10 | loop fusion | flops 22020096 | bytes 31506432 | tf_op jit(solution)/shard_map/convert_element_type | solution.py:189
  154.0 6.9 %fusion.79 = f32[4,256,256]{1,2,0:T(8,128)S(1)} fusion(bf16[4,256,3072]{2,1,0:T(8,128)(2,1)S(1)} %bitcast.190, bf16[4,256,3072]{2,1,0:T(8,128)(2,1)} %bitcast.202), kind=kOutput, calls=%fused_computation.150 | convolution fusion | flops 1610612736 | bytes 13631488 | tf_op jit(solution)/shard_map/fan,fbn->fab/dot_general | solution.py:53
  161.0 1.8 convolution_bitcast_fusion.1
  164.6 2.2 pad_maximum_fusion.1
  180.0 1.6 fusion.77
  182.0 6.9 %fusion = f32[4,3072]{1,0:T(4,128)S(1)} fusion(bf16[4,256,3072]{2,1,0:T(8,128)(2,1)} %bitcast.178, bf16[4,256,3072]{2,1,0:T(8,128)(2,1)} %bitcast.191, bf16[4,128,128]{1,2,0:T(8,128)(2,1)S(1)} %get-tuple-element.39, bf16[4,128,128]{1,2,0:T(8,128)(2,1)S(1)} %get-tuple-element.38, bf16[4,128,128]{1,2,0:T(8,128)(2,1)S(1)} %fusion.71), kind=kOutput, calls=%fused_computation.8 | convolution fusion | flops 1622134784 | bytes 13025280 | tf_op jit(solution)/shard_map/fab,fbn->fan/dot_general | solution.py:68
  190.1 2.3 fusion.6
  192.4 22.4 %collective-permute-start.10 = (f32[4,3072]{1,0:T(4,128)S(1)}, f32[4,3072]{1,0:T(4,128)S(1)}, u32[]{:S(2)}, u32[]{:S(2)}) collective-permute-start(f32[4,3072]{1,0:T(4,128)S(1)} %select_add_fusion.1), channel_id=1, source_target_pairs={{0,8},{8,0},{16,24},{24,16},{1,9},{9,1},{17,25},{25,17},{2,10},{10... | collective-permute-start | bytes 147464 | tf_op jit(solution)/shard_map/ppermute | solution.py:31
  214.8 1.5 collective-permute-start.12
  216.9 2.0 collective-permute-done.11
  219.9 9.2 %collective-permute-start.13 = (f32[4,3072]{1,0:T(4,128)S(1)}, f32[4,3072]{1,0:T(4,128)S(1)}, u32[]{:S(2)}, u32[]{:S(2)}) collective-permute-start(f32[4,3072]{1,0:T(4,128)S(1)} %fusion.94), channel_id=1, source_target_pairs={{0,2},{2,0},{4,6},{6,4},{1,3},{3,1},{5,7},{7,5},{8,10},{10,8},{12,... | collective-permute-start | bytes 147464 | tf_op jit(solution)/shard_map/ppermute | solution.py:31
  229.1 2.8 collective-permute-start.14
  231.9 3.0 %collective-permute-done.14 = f32[4,3072]{1,0:T(4,128)S(1)} collective-permute-done((f32[4,3072]{1,0:T(4,128)S(1)}, f32[4,3072]{1,0:T(4,128)S(1)}, u32[]{:S(2)}, u32[]{:S(2)}) %collective-permute-start.14) | collective-permute-done | bytes 49184 | tf_op jit(solution)/shard_map/ppermute | solution.py:31
  235.0 2.8 collective-permute-done.15
  241.1 7.2 %fusion.3 = (bf16[4,2,128,3072]{3,2,1,0:T(8,128)(2,1)S(1)}, bf16[4,2,128,3072]{3,2,1,0:T(8,128)(2,1)S(1)}) fusion(bf16[4,2,128,3072]{3,2,1,0:T(8,128)(2,1)} %copy-done, f32[4,3072]{1,0:T(4,128)S(1)} %get-tuple-element.7, bf16[4,2,128,3072]{3,2,1,0:T(8,128)(2,1)} %param.6), kind=kLoop, calls=%fused_computation.11 | loop fusion | flops 18874368 | bytes 25214976 | tf_op jit(solution)/shard_map/convert_element_type | solution.py:189
  248.3 1.8 convolution_bitcast_fusion
  250.2 5.7 %fusion.80 = f32[4,256,256]{1,2,0:T(8,128)} fusion(bf16[4,256,3072]{2,1,0:T(8,128)(2,1)} %bitcast.192, bf16[4,256,3072]{2,1,0:T(8,128)(2,1)S(1)} %bitcast.201), kind=kOutput, calls=%fused_computation.151 | convolution fusion | flops 1610612736 | bytes 13631488 | tf_op jit(solution)/shard_map/fan,fbn->fab/dot_general | solution.py:53
  257.7 2.5 collective-permute-done.17
  260.6 2.6 fusion.1
  263.2 2.5 fusion.7
  266.4 1.5 collective-permute-start.19
  268.0 1.4 collective-permute-start.20
  270.5 2.4 collective-permute-done.20
  274.2 3.3 %collective-permute-start.23 = (f32[4,3072]{1,0:T(4,128)S(1)}, f32[4,3072]{1,0:T(4,128)S(1)}, u32[]{:S(2)}, u32[]{:S(2)}) collective-permute-start(f32[4,3072]{1,0:T(4,128)S(1)} %fusion.93), channel_id=1, source_target_pairs={{0,6},{2,4},{4,2},{6,0},{1,7},{3,5},{5,3},{7,1},{8,14},{10,12},{12... | collective-permute-start | bytes 147464 | tf_op jit(solution)/shard_map/ppermute | solution.py:31
  278.3 1.8 collective-permute-done.23
  280.8 1.4 collective-permute-done.24
  (119 shorter events, 27.9 us)
Async XLA Ops:
  0.0 143.2 %collective-permute-start.8 = (bf16[4,2,128,3072]{3,2,1,0:T(8,128)(2,1)}, bf16[4,2,128,3072]{3,2,1,0:T(8,128)(2,1)}, u32[]{:S(2)}, u32[]{:S(2)}) collective-permute-start(bf16[4,2,128,3072]{3,2,1,0:T(8,128)(2,1)} %param.6), channel_id=1, source_target_pairs={{0,2},{12,8},{16,22},{20,18},{10,14},{30,28},{1,3},{13,9},{17,23},... | collective-permute-start | bytes 18874376 | tf_op jit(solution)/shard_map/ppermute | solution.py:157
  8.5 7.8 %collective-permute-start = (f32[4,3072]{1,0:T(4,128)S(1)}, f32[4,3072]{1,0:T(4,128)S(1)}, u32[]{:S(2)}, u32[]{:S(2)}) collective-permute-start(f32[4,3072]{1,0:T(4,128)S(1)} %dynamic_update_slice.3), channel_id=1, source_target_pairs={{0,8},{8,0},{16,24},{24,16},{1,9},{9,1},{17,25},{25,17},{2,10},{10... | collective-permute-start | bytes 147464 | tf_op jit(solution)/shard_map/ppermute | solution.py:31
  8.6 7.7 %collective-permute-start.1 = (f32[4,3072]{1,0:T(4,128)S(1)}, f32[4,3072]{1,0:T(4,128)S(1)}, u32[]{:S(2)}, u32[]{:S(2)}) collective-permute-start(f32[4,3072]{1,0:T(4,128)S(1)} %dynamic_update_slice.3), channel_id=1, source_target_pairs={{0,16},{8,24},{16,0},{24,8},{1,17},{9,25},{17,1},{25,9},{2,18},{10... | collective-permute-start | bytes 147464 | tf_op jit(solution)/shard_map/ppermute | solution.py:31
  12.2 5.0 %collective-permute-start.2 = (f32[4,3072]{1,0:T(4,128)S(1)}, f32[4,3072]{1,0:T(4,128)S(1)}, u32[]{:S(2)}, u32[]{:S(2)}) collective-permute-start(f32[4,3072]{1,0:T(4,128)S(1)} %dynamic_update_slice.3), channel_id=1, source_target_pairs={{0,24},{8,16},{16,8},{24,0},{1,25},{9,17},{17,9},{25,1},{2,26},{10... | collective-permute-start | bytes 147464 | tf_op jit(solution)/shard_map/ppermute | solution.py:31
  17.3 124.8 %collective-permute-start.3 = (f32[4,3072]{1,0:T(4,128)S(1)}, f32[4,3072]{1,0:T(4,128)S(1)}, u32[]{:S(2)}, u32[]{:S(2)}) collective-permute-start(f32[4,3072]{1,0:T(4,128)S(1)} %fusion.95), channel_id=1, source_target_pairs={{0,2},{2,0},{4,6},{6,4},{1,3},{3,1},{5,7},{7,5},{8,10},{10,8},{12,... | collective-permute-start | bytes 147464 | tf_op jit(solution)/shard_map/ppermute | solution.py:31
  17.9 124.7 %collective-permute-start.4 = (f32[4,3072]{1,0:T(4,128)S(1)}, f32[4,3072]{1,0:T(4,128)S(1)}, u32[]{:S(2)}, u32[]{:S(2)}) collective-permute-start(f32[4,3072]{1,0:T(4,128)S(1)} %fusion.95), channel_id=1, source_target_pairs={{0,4},{2,6},{4,0},{6,2},{1,5},{3,7},{5,1},{7,3},{8,12},{10,14},{12... | collective-permute-start | bytes 147464 | tf_op jit(solution)/shard_map/ppermute | solution.py:31
  19.8 123.3 %collective-permute-start.5 = (f32[4,3072]{1,0:T(4,128)S(1)}, f32[4,3072]{1,0:T(4,128)S(1)}, u32[]{:S(2)}, u32[]{:S(2)}) collective-permute-start(f32[4,3072]{1,0:T(4,128)S(1)} %fusion.95), channel_id=1, source_target_pairs={{0,6},{2,4},{4,2},{6,0},{1,7},{3,5},{5,3},{7,1},{8,14},{10,12},{12... | collective-permute-start | bytes 147464 | tf_op jit(solution)/shard_map/ppermute | solution.py:31
  143.1 17.9 %slice-start = ((s8[6291456]{0:T(1024)(128)(4,1)}), s8[4194304]{0:T(1024)(128)(4,1)S(1)}, s32[]{:S(2)}) async-start(s8[6291456]{0:T(1024)(128)(4,1)} %bitcast.179), calls=%async_computation | async-start | bytes 8388608
  143.2 17.8 %slice-start.1 = ((s8[6291456]{0:T(1024)(128)(4,1)}), s8[2097152]{0:T(1024)(128)(4,1)S(1)}, s32[]{:S(2)}) async-start(s8[6291456]{0:T(1024)(128)(4,1)} %bitcast.179), calls=%async_computation.1 | async-start | bytes 4194304
  166.8 13.2 %collective-permute-start.9 = (f32[2,4,2,128,128]{3,4,1,2,0:T(8,128)}, f32[2,4,2,128,128]{3,4,1,2,0:T(8,128)}, u32[]{:S(2)}, u32[]{:S(2)}) collective-permute-start(f32[2,4,2,128,128]{3,4,1,2,0:T(8,128)} %pad_maximum_fusion.1), channel_id=1, source_target_pairs={{0,1},{1,0},{2,3},{3,2},{4,5},{5,4},{6,7},{7,6},{8,9},{9,8},{10,11... | collective-permute-start | bytes 3145736 | tf_op jit(solution)/shard_map/ppermute | solution.py:47
  166.9 8.1 %collective-permute-start.6 = (f32[9,128,128]{2,1,0:T(8,128)S(1)}, f32[9,128,128]{2,1,0:T(8,128)S(1)}, u32[]{:S(2)}, u32[]{:S(2)}) collective-permute-start(f32[9,128,128]{2,1,0:T(8,128)S(1)} %get-tuple-element.33), channel_id=1, source_target_pairs={{8,2},{4,8},{24,22},{12,18},{26,14},{22,28},{9,3},{5,9},{25,23},{1... | collective-permute-start | bytes 1769480 | tf_op jit(solution)/shard_map/ppermute | solution.py:167
  167.6 7.4 %collective-permute-start.7 = (f32[9,128,128]{2,1,0:T(8,128)S(1)}, f32[9,128,128]{2,1,0:T(8,128)S(1)}, u32[]{:S(2)}, u32[]{:S(2)}) collective-permute-start(f32[9,128,128]{2,1,0:T(8,128)S(1)} %get-tuple-element.33), channel_id=1, source_target_pairs={{16,8},{6,22},{17,9},{7,23}} | collective-permute-start | bytes 1769480 | tf_op jit(solution)/shard_map/ppermute | solution.py:167
  182.0 7.6 %slice-start.3 = ((s8[6291456]{0:T(1024)(128)(4,1)}), s8[2097152]{0:T(1024)(128)(4,1)S(1)}, s32[]{:S(2)}) async-start(s8[6291456]{0:T(1024)(128)(4,1)} %bitcast.182), calls=%async_computation.3 | async-start | bytes 4194304
  182.0 8.2 %slice-start.7 = ((s8[6291456]{0:T(1024)(128)(4,1)}), s8[2097152]{0:T(1024)(128)(4,1)S(1)}, s32[]{:S(2)}) async-start(s8[6291456]{0:T(1024)(128)(4,1)} %bitcast.193), calls=%async_computation.7 | async-start | bytes 4194304
  192.4 24.5 %collective-permute-start.10 = (f32[4,3072]{1,0:T(4,128)S(1)}, f32[4,3072]{1,0:T(4,128)S(1)}, u32[]{:S(2)}, u32[]{:S(2)}) collective-permute-start(f32[4,3072]{1,0:T(4,128)S(1)} %select_add_fusion.1), channel_id=1, source_target_pairs={{0,8},{8,0},{16,24},{24,16},{1,9},{9,1},{17,25},{25,17},{2,10},{10... | collective-permute-start | bytes 147464 | tf_op jit(solution)/shard_map/ppermute | solution.py:31
  214.8 4.1 %collective-permute-start.11 = (f32[4,3072]{1,0:T(4,128)S(1)}, f32[4,3072]{1,0:T(4,128)S(1)}, u32[]{:S(2)}, u32[]{:S(2)}) collective-permute-start(f32[4,3072]{1,0:T(4,128)S(1)} %select_add_fusion.1), channel_id=1, source_target_pairs={{0,16},{8,24},{16,0},{24,8},{1,17},{9,25},{17,1},{25,9},{2,18},{10... | collective-permute-start | bytes 147464 | tf_op jit(solution)/shard_map/ppermute | solution.py:31
  214.8 5.0 %collective-permute-start.12 = (f32[4,3072]{1,0:T(4,128)S(1)}, f32[4,3072]{1,0:T(4,128)S(1)}, u32[]{:S(2)}, u32[]{:S(2)}) collective-permute-start(f32[4,3072]{1,0:T(4,128)S(1)} %select_add_fusion.1), channel_id=1, source_target_pairs={{0,24},{8,16},{16,8},{24,0},{1,25},{9,17},{17,9},{25,1},{2,26},{10... | collective-permute-start | bytes 147464 | tf_op jit(solution)/shard_map/ppermute | solution.py:31
  219.8 28.5 %slice-start.4 = ((s8[6291456]{0:T(1024)(128)(4,1)}), s8[2097152]{0:T(1024)(128)(4,1)S(1)}, s32[]{:S(2)}) async-start(s8[6291456]{0:T(1024)(128)(4,1)} %bitcast.185), calls=%async_computation.4 | async-start | bytes 4194304
  219.9 12.1 %collective-permute-start.13 = (f32[4,3072]{1,0:T(4,128)S(1)}, f32[4,3072]{1,0:T(4,128)S(1)}, u32[]{:S(2)}, u32[]{:S(2)}) collective-permute-start(f32[4,3072]{1,0:T(4,128)S(1)} %fusion.94), channel_id=1, source_target_pairs={{0,2},{2,0},{4,6},{6,4},{1,3},{3,1},{5,7},{7,5},{8,10},{10,8},{12,... | collective-permute-start | bytes 147464 | tf_op jit(solution)/shard_map/ppermute | solution.py:31
  229.1 5.9 %collective-permute-start.14 = (f32[4,3072]{1,0:T(4,128)S(1)}, f32[4,3072]{1,0:T(4,128)S(1)}, u32[]{:S(2)}, u32[]{:S(2)}) collective-permute-start(f32[4,3072]{1,0:T(4,128)S(1)} %fusion.94), channel_id=1, source_target_pairs={{0,4},{2,6},{4,0},{6,2},{1,5},{3,7},{5,1},{7,3},{8,12},{10,14},{12... | collective-permute-start | bytes 147464 | tf_op jit(solution)/shard_map/ppermute | solution.py:31
  231.9 5.9 %collective-permute-start.15 = (f32[4,3072]{1,0:T(4,128)S(1)}, f32[4,3072]{1,0:T(4,128)S(1)}, u32[]{:S(2)}, u32[]{:S(2)}) collective-permute-start(f32[4,3072]{1,0:T(4,128)S(1)} %fusion.94), channel_id=1, source_target_pairs={{0,6},{2,4},{4,2},{6,0},{1,7},{3,5},{5,3},{7,1},{8,14},{10,12},{12... | collective-permute-start | bytes 147464 | tf_op jit(solution)/shard_map/ppermute | solution.py:31
  238.5 1.3 collective-permute-start.16
  250.2 10.4 %slice-start.8 = ((s8[6291456]{0:T(1024)(128)(4,1)}), s8[4194304]{0:T(1024)(128)(4,1)S(1)}, s32[]{:S(2)}) async-start(s8[6291456]{0:T(1024)(128)(4,1)} %bitcast.196), calls=%async_computation.8 | async-start | bytes 8388608
  250.2 10.4 %slice-start.9 = ((s8[6291456]{0:T(1024)(128)(4,1)}), s8[2097152]{0:T(1024)(128)(4,1)S(1)}, s32[]{:S(2)}) async-start(s8[6291456]{0:T(1024)(128)(4,1)} %bitcast.196), calls=%async_computation.9 | async-start | bytes 4194304
  257.4 2.7 collective-permute-start.17
  265.8 4.2 %collective-permute-start.18 = (f32[4,3072]{1,0:T(4,128)S(1)}, f32[4,3072]{1,0:T(4,128)S(1)}, u32[]{:S(2)}, u32[]{:S(2)}) collective-permute-start(f32[4,3072]{1,0:T(4,128)S(1)} %select_add_fusion), channel_id=1, source_target_pairs={{0,8},{8,0},{16,24},{24,16},{1,9},{9,1},{17,25},{25,17},{2,10},{10... | collective-permute-start | bytes 147464 | tf_op jit(solution)/shard_map/ppermute | solution.py:31
  266.4 4.1 %collective-permute-start.19 = (f32[4,3072]{1,0:T(4,128)S(1)}, f32[4,3072]{1,0:T(4,128)S(1)}, u32[]{:S(2)}, u32[]{:S(2)}) collective-permute-start(f32[4,3072]{1,0:T(4,128)S(1)} %select_add_fusion), channel_id=1, source_target_pairs={{0,16},{8,24},{16,0},{24,8},{1,17},{9,25},{17,1},{25,9},{2,18},{10... | collective-permute-start | bytes 147464 | tf_op jit(solution)/shard_map/ppermute | solution.py:31
  268.0 5.0 %collective-permute-start.20 = (f32[4,3072]{1,0:T(4,128)S(1)}, f32[4,3072]{1,0:T(4,128)S(1)}, u32[]{:S(2)}, u32[]{:S(2)}) collective-permute-start(f32[4,3072]{1,0:T(4,128)S(1)} %select_add_fusion), channel_id=1, source_target_pairs={{0,24},{8,16},{16,8},{24,0},{1,25},{9,17},{17,9},{25,1},{2,26},{10... | collective-permute-start | bytes 147464 | tf_op jit(solution)/shard_map/ppermute | solution.py:31
  273.1 4.5 %collective-permute-start.21 = (f32[4,3072]{1,0:T(4,128)S(1)}, f32[4,3072]{1,0:T(4,128)S(1)}, u32[]{:S(2)}, u32[]{:S(2)}) collective-permute-start(f32[4,3072]{1,0:T(4,128)S(1)} %fusion.93), channel_id=1, source_target_pairs={{0,2},{2,0},{4,6},{6,4},{1,3},{3,1},{5,7},{7,5},{8,10},{10,8},{12,... | collective-permute-start | bytes 147464 | tf_op jit(solution)/shard_map/ppermute | solution.py:31
  273.1 5.1 %collective-permute-start.22 = (f32[4,3072]{1,0:T(4,128)S(1)}, f32[4,3072]{1,0:T(4,128)S(1)}, u32[]{:S(2)}, u32[]{:S(2)}) collective-permute-start(f32[4,3072]{1,0:T(4,128)S(1)} %fusion.93), channel_id=1, source_target_pairs={{0,4},{2,6},{4,0},{6,2},{1,5},{3,7},{5,1},{7,3},{8,12},{10,14},{12... | collective-permute-start | bytes 147464 | tf_op jit(solution)/shard_map/ppermute | solution.py:31
  274.2 5.9 %collective-permute-start.23 = (f32[4,3072]{1,0:T(4,128)S(1)}, f32[4,3072]{1,0:T(4,128)S(1)}, u32[]{:S(2)}, u32[]{:S(2)}) collective-permute-start(f32[4,3072]{1,0:T(4,128)S(1)} %fusion.93), channel_id=1, source_target_pairs={{0,6},{2,4},{4,2},{6,0},{1,7},{3,5},{5,3},{7,1},{8,14},{10,12},{12... | collective-permute-start | bytes 147464 | tf_op jit(solution)/shard_map/ppermute | solution.py:31
  280.8 1.4 collective-permute-start.24
  (8 other events, 36.6 us)

commit v4 on v3

--- a/solution.py
+++ b/solution.py
@@ -155,9 +155,6 @@
     axes = ("row", "col")
 
     received = lax.ppermute(green_panel, axes, panel_moves)
-    other = jnp.where(is_diag, green_panel, received)
-    mine_rows = green_panel.reshape(freq_count, 2 * span_j, local_pts)
-    other_rows = other.reshape(freq_count, 2 * span_j, local_pts)
 
     own_block = jnp.concatenate(
         [observed.reshape(-1, span_j, span_j), pair_weights.astype(jnp.float32)[None]], axis=0
@@ -166,6 +163,10 @@
     for pairs, _ in rounds:
         arrived.append(lax.ppermute(own_block, axes, pairs))
     arrived = jnp.stack(arrived)
+    received, arrived = lax.optimization_barrier((received, arrived))
+    other = jnp.where(is_diag, green_panel, received)
+    mine_rows = green_panel.reshape(freq_count, 2 * span_j, local_pts)
+    other_rows = other.reshape(freq_count, 2 * span_j, local_pts)
     moved_table = jnp.array(moved, jnp.int32)[slot]
     first_block = arrived[moved_table[0]]
     second_block = arrived[moved_table[1]]

time: 285 us -> 267 us (0.937)
  starting transfers between devices: 62.9 us -> 51.9 us
  waiting for transfers between devices: 143 us -> 138 us
    ppermute x18, starting transfers between devices: 53.4 us -> 42.6 us  [butterfly_sum(): got.append(lax.ppermute(value, axis, [(i, i ^ mask) for i in range(size)]))]
    ppermute x18, waiting for transfers between devices: 138 us -> 133 us  [butterfly_sum(): got.append(lax.ppermute(value, axis, [(i, i ^ mask) for i in range(size)]))]
  transfers between devices with their start and end apart: 25 -> 25, of which waited for: 17 -> 13; matrix products, arithmetic and copies ran while one was open for 3% -> 4% of each run, Pallas kernels for 0% -> 0%
where the time goes in v4:
time: 267 us
  waiting for transfers between devices  138 us (52%)
  starting transfers between devices  51.9 us (19%)
  other arithmetic  29.6 us (11%)
  matrix products  29.6 us (11%)
  local copies, waits for them, and re-layouts  9.04 us (3%)
  between operations  9.02 us (3%)
    ppermute x18, waiting for transfers between devices, butterfly_sum(): got.append(lax.ppermute(value, axis, [(i, i ^ mask) for i in range(size)]))  133 us
    ppermute x18, starting transfers between devices, butterfly_sum(): got.append(lax.ppermute(value, axis, [(i, i ^ mask) for i in range(size)]))  42.6 us
    convert_element_type x2, other arithmetic, pair_body(): (other * spread).astype(jnp.bfloat16).reshape(other_rows.shape)  17.9 us
    dot_general x4, matrix products, correlate(): jnp.einsum('fan,fbn->fab', left_rows, weighted, preferred_element_type=jn...  15.3 us
    dot_general x4, matrix products, point_terms(): jnp.einsum('fab,fbn->fan', adjoint_block(adjoint), right_rows, preferred_...  14.3 us
    ppermute x1, starting transfers between devices, pair_body(): received = lax.ppermute(green_panel, axes, panel_moves)  7.63 us
  transfers between devices with their start and end apart: 25, of which 13 were waited for; matrix products, arithmetic and copies ran while one was open for 4% of the time, Pallas kernels for 0%

profile of v4, /device:TPU:0, one launch (start us, length us, event | category | flops | bytes accessed | tf_op | source)
XLA Modules:
  0.0 266.8 jit_solution(17126461982180882439)
XLA Ops:
  0.0 7.6 %collective-permute-start.6 = (bf16[4,2,128,3072]{3,2,1,0:T(8,128)(2,1)}, bf16[4,2,128,3072]{3,2,1,0:T(8,128)(2,1)}, u32[]{:S(2)}, u32[]{:S(2)}) collective-permute-start(bf16[4,2,128,3072]{3,2,1,0:T(8,128)(2,1)} %param.6), channel_id=1, source_target_pairs={{0,2},{12,8},{16,22},{20,18},{10,14},{30,28},{1,3},{13,9},{17,23},... | collective-permute-start | bytes 18874376 | tf_op jit(solution)/shard_map/ppermute | solution.py:157
  8.6 3.6 %collective-permute-start.1 = (f32[4,3072]{1,0:T(4,128)S(1)}, f32[4,3072]{1,0:T(4,128)S(1)}, u32[]{:S(2)}, u32[]{:S(2)}) collective-permute-start(f32[4,3072]{1,0:T(4,128)S(1)} %dynamic_update_slice.3), channel_id=1, source_target_pairs={{0,16},{8,24},{16,0},{24,8},{1,17},{9,25},{17,1},{25,9},{2,18},{10... | collective-permute-start | bytes 147464 | tf_op jit(solution)/shard_map/ppermute | solution.py:31
  19.1 3.7 %collective-permute-start.4 = (f32[4,3072]{1,0:T(4,128)S(1)}, f32[4,3072]{1,0:T(4,128)S(1)}, u32[]{:S(2)}, u32[]{:S(2)}) collective-permute-start(f32[4,3072]{1,0:T(4,128)S(1)} %fusion.95), channel_id=1, source_target_pairs={{0,4},{2,6},{4,0},{6,2},{1,5},{3,7},{5,1},{7,3},{8,12},{10,14},{12... | collective-permute-start | bytes 147464 | tf_op jit(solution)/shard_map/ppermute | solution.py:31
  23.3 118.8 %collective-permute-done.5 = f32[4,3072]{1,0:T(4,128)S(1)} collective-permute-done((f32[4,3072]{1,0:T(4,128)S(1)}, f32[4,3072]{1,0:T(4,128)S(1)}, u32[]{:S(2)}, u32[]{:S(2)}) %collective-permute-start.5) | collective-permute-done | bytes 49184 | tf_op jit(solution)/shard_map/ppermute | solution.py:31
  145.4 10.8 %fusion.2 = (bf16[4,2,128,3072]{3,2,1,0:T(8,128)(2,1)}, bf16[4,2,128,3072]{3,2,1,0:T(8,128)(2,1)S(1)}, bf16[4,2,128,3072]{3,2,1,0:T(8,128)(2,1)S(1)}) fusion(f32[4,3072]{1,0:T(4,128)S(1)} %get-tuple-element.17, bf16[4,2,128,3072]{3,2,1,0:T(8,128)(2,1)} %param.6, bf16[4,2,128,3072]{3,2,1,0:T(8,128)(2,1)} %collective-permute-done.6, pred[]{:T(512)} %bitcast.18), kind=kLoop, calls=%fused_computation.10 | loop fusion | flops 22020096 | bytes 31506432 | tf_op jit(solution)/shard_map/convert_element_type | solution.py:190
  156.2 6.9 %convolution_bitcast_fusion.1 = f32[4,256,256]{1,2,0:T(8,128)S(1)} fusion(bf16[4,256,3072]{2,1,0:T(8,128)(2,1)} %bitcast.202, bf16[4,256,3072]{2,1,0:T(8,128)(2,1)S(1)} %bitcast.181), kind=kOutput, calls=%fused_computation.19 | convolution fusion | flops 1610612736 | bytes 13631488 | tf_op jit(solution)/shard_map/fan,fbn->fab/dot_general | solution.py:53
  163.2 1.8 fusion.79
  166.7 2.2 pad_maximum_fusion.1
  176.4 1.4 copy.17
  178.0 1.6 fusion.77
  180.0 6.9 %fusion = f32[4,3072]{1,0:T(4,128)S(1)} fusion(bf16[4,256,3072]{2,1,0:T(8,128)(2,1)} %bitcast.178, bf16[4,256,3072]{2,1,0:T(8,128)(2,1)} %bitcast.191, bf16[4,128,128]{1,2,0:T(8,128)(2,1)S(1)} %get-tuple-element.43, bf16[4,128,128]{1,2,0:T(8,128)(2,1)S(1)} %get-tuple-element.42, bf16[4,128,128]{1,2,0:T(8,128)(2,1)S(1)} %fusion.71), kind=kOutput, calls=%fused_computation.8 | convolution fusion | flops 1622134784 | bytes 13025280 | tf_op jit(solution)/shard_map/fab,fbn->fan/dot_general | solution.py:68
  188.2 2.3 fusion.6
  190.5 6.8 %collective-permute-start.12 = (f32[4,3072]{1,0:T(4,128)S(1)}, f32[4,3072]{1,0:T(4,128)S(1)}, u32[]{:S(2)}, u32[]{:S(2)}) collective-permute-start(f32[4,3072]{1,0:T(4,128)S(1)} %select_add_fusion.1), channel_id=1, source_target_pairs={{0,24},{8,16},{16,8},{24,0},{1,25},{9,17},{17,9},{25,1},{2,26},{10... | collective-permute-start | bytes 147464 | tf_op jit(solution)/shard_map/ppermute | solution.py:31
  197.3 13.4 %collective-permute-start.11 = (f32[4,3072]{1,0:T(4,128)S(1)}, f32[4,3072]{1,0:T(4,128)S(1)}, u32[]{:S(2)}, u32[]{:S(2)}) collective-permute-start(f32[4,3072]{1,0:T(4,128)S(1)} %select_add_fusion.1), channel_id=1, source_target_pairs={{0,16},{8,24},{16,0},{24,8},{1,17},{9,25},{17,1},{25,9},{2,18},{10... | collective-permute-start | bytes 147464 | tf_op jit(solution)/shard_map/ppermute | solution.py:31
  210.8 2.1 collective-permute-done.11
  212.8 2.0 collective-permute-done.10
  214.9 3.2 %collective-permute-start.15 = (f32[4,3072]{1,0:T(4,128)S(1)}, f32[4,3072]{1,0:T(4,128)S(1)}, u32[]{:S(2)}, u32[]{:S(2)}) collective-permute-start(f32[4,3072]{1,0:T(4,128)S(1)} %fusion.94), channel_id=1, source_target_pairs={{0,6},{2,4},{4,2},{6,0},{1,7},{3,5},{5,3},{7,1},{8,14},{10,12},{12... | collective-permute-start | bytes 147464 | tf_op jit(solution)/shard_map/ppermute | solution.py:31
  219.4 1.6 collective-permute-done.15
  221.0 2.2 collective-permute-done.14
  223.8 1.4 collective-permute-done.16
  226.5 7.1 %fusion.3 = (bf16[4,2,128,3072]{3,2,1,0:T(8,128)(2,1)S(1)}, bf16[4,2,128,3072]{3,2,1,0:T(8,128)(2,1)S(1)}) fusion(bf16[4,2,128,3072]{3,2,1,0:T(8,128)(2,1)} %copy-done, f32[4,3072]{1,0:T(4,128)S(1)} %get-tuple-element.11, bf16[4,2,128,3072]{3,2,1,0:T(8,128)(2,1)} %param.6), kind=kLoop, calls=%fused_computation.11 | loop fusion | flops 18874368 | bytes 25214976 | tf_op jit(solution)/shard_map/convert_element_type | solution.py:190
  233.7 1.8 convolution_bitcast_fusion
  235.6 4.8 %fusion.80 = f32[4,256,256]{1,2,0:T(8,128)S(1)} fusion(bf16[4,256,3072]{2,1,0:T(8,128)(2,1)} %bitcast.192, bf16[4,256,3072]{2,1,0:T(8,128)(2,1)S(1)} %bitcast.201), kind=kOutput, calls=%fused_computation.151 | convolution fusion | flops 1610612736 | bytes 13631488 | tf_op jit(solution)/shard_map/fan,fbn->fab/dot_general | solution.py:53
  240.9 2.5 collective-permute-done.17
  243.9 2.6 fusion.1
  246.5 2.6 fusion.7
  249.1 2.4 collective-permute-start.20
  252.7 1.5 collective-permute-done.20
  254.2 1.4 collective-permute-done.19
  255.7 1.5 collective-permute-start.23
  257.9 2.3 collective-permute-start.21
  260.2 1.6 collective-permute-done.23
  (123 shorter events, 25.3 us)
Async XLA Ops:
  0.0 145.4 %collective-permute-start.6 = (bf16[4,2,128,3072]{3,2,1,0:T(8,128)(2,1)}, bf16[4,2,128,3072]{3,2,1,0:T(8,128)(2,1)}, u32[]{:S(2)}, u32[]{:S(2)}) collective-permute-start(bf16[4,2,128,3072]{3,2,1,0:T(8,128)(2,1)} %param.6), channel_id=1, source_target_pairs={{0,2},{12,8},{16,22},{20,18},{10,14},{30,28},{1,3},{13,9},{17,23},... | collective-permute-start | bytes 18874376 | tf_op jit(solution)/shard_map/ppermute | solution.py:157
  8.5 9.8 %collective-permute-start.2 = (f32[4,3072]{1,0:T(4,128)S(1)}, f32[4,3072]{1,0:T(4,128)S(1)}, u32[]{:S(2)}, u32[]{:S(2)}) collective-permute-start(f32[4,3072]{1,0:T(4,128)S(1)} %dynamic_update_slice.3), channel_id=1, source_target_pairs={{0,24},{8,16},{16,8},{24,0},{1,25},{9,17},{17,9},{25,1},{2,26},{10... | collective-permute-start | bytes 147464 | tf_op jit(solution)/shard_map/ppermute | solution.py:31
  8.6 9.7 %collective-permute-start.1 = (f32[4,3072]{1,0:T(4,128)S(1)}, f32[4,3072]{1,0:T(4,128)S(1)}, u32[]{:S(2)}, u32[]{:S(2)}) collective-permute-start(f32[4,3072]{1,0:T(4,128)S(1)} %dynamic_update_slice.3), channel_id=1, source_target_pairs={{0,16},{8,24},{16,0},{24,8},{1,17},{9,25},{17,1},{25,9},{2,18},{10... | collective-permute-start | bytes 147464 | tf_op jit(solution)/shard_map/ppermute | solution.py:31
  12.2 6.1 %collective-permute-start = (f32[4,3072]{1,0:T(4,128)S(1)}, f32[4,3072]{1,0:T(4,128)S(1)}, u32[]{:S(2)}, u32[]{:S(2)}) collective-permute-start(f32[4,3072]{1,0:T(4,128)S(1)} %dynamic_update_slice.3), channel_id=1, source_target_pairs={{0,8},{8,0},{16,24},{24,16},{1,9},{9,1},{17,25},{25,17},{2,10},{10... | collective-permute-start | bytes 147464 | tf_op jit(solution)/shard_map/ppermute | solution.py:31
  15.6 127.6 %collective-permute-start.7 = (f32[9,128,128]{2,1,0:T(8,128)S(1)}, f32[9,128,128]{2,1,0:T(8,128)S(1)}, u32[]{:S(2)}, u32[]{:S(2)}) collective-permute-start(f32[9,128,128]{2,1,0:T(8,128)S(1)} %get-tuple-element.37), channel_id=1, source_target_pairs={{8,2},{4,8},{24,22},{12,18},{26,14},{22,28},{9,3},{5,9},{25,23},{1... | collective-permute-start | bytes 1769480 | tf_op jit(solution)/shard_map/ppermute | solution.py:164
  18.4 123.7 %collective-permute-start.5 = (f32[4,3072]{1,0:T(4,128)S(1)}, f32[4,3072]{1,0:T(4,128)S(1)}, u32[]{:S(2)}, u32[]{:S(2)}) collective-permute-start(f32[4,3072]{1,0:T(4,128)S(1)} %fusion.95), channel_id=1, source_target_pairs={{0,6},{2,4},{4,2},{6,0},{1,7},{3,5},{5,3},{7,1},{8,14},{10,12},{12... | collective-permute-start | bytes 147464 | tf_op jit(solution)/shard_map/ppermute | solution.py:31
  19.1 123.7 %collective-permute-start.4 = (f32[4,3072]{1,0:T(4,128)S(1)}, f32[4,3072]{1,0:T(4,128)S(1)}, u32[]{:S(2)}, u32[]{:S(2)}) collective-permute-start(f32[4,3072]{1,0:T(4,128)S(1)} %fusion.95), channel_id=1, source_target_pairs={{0,4},{2,6},{4,0},{6,2},{1,5},{3,7},{5,1},{7,3},{8,12},{10,14},{12... | collective-permute-start | bytes 147464 | tf_op jit(solution)/shard_map/ppermute | solution.py:31
  22.8 120.3 %collective-permute-start.3 = (f32[4,3072]{1,0:T(4,128)S(1)}, f32[4,3072]{1,0:T(4,128)S(1)}, u32[]{:S(2)}, u32[]{:S(2)}) collective-permute-start(f32[4,3072]{1,0:T(4,128)S(1)} %fusion.95), channel_id=1, source_target_pairs={{0,2},{2,0},{4,6},{6,4},{1,3},{3,1},{5,7},{7,5},{8,10},{10,8},{12,... | collective-permute-start | bytes 147464 | tf_op jit(solution)/shard_map/ppermute | solution.py:31
  142.0 1.2 collective-permute-start.8
  144.0 12.2 %slice-start = ((s8[6291456]{0:T(1024)(128)(4,1)}), s8[4194304]{0:T(1024)(128)(4,1)S(1)}, s32[]{:S(2)}) async-start(s8[6291456]{0:T(1024)(128)(4,1)} %bitcast.179), calls=%async_computation | async-start | bytes 8388608
  145.4 10.8 %slice-start.1 = ((s8[6291456]{0:T(1024)(128)(4,1)}), s8[2097152]{0:T(1024)(128)(4,1)S(1)}, s32[]{:S(2)}) async-start(s8[6291456]{0:T(1024)(128)(4,1)} %bitcast.179), calls=%async_computation.1 | async-start | bytes 4194304
  168.9 9.1 %collective-permute-start.9 = (f32[2,4,2,128,128]{3,4,1,2,0:T(8,128)}, f32[2,4,2,128,128]{3,4,1,2,0:T(8,128)}, u32[]{:S(2)}, u32[]{:S(2)}) collective-permute-start(f32[2,4,2,128,128]{3,4,1,2,0:T(8,128)} %pad_maximum_fusion.1), channel_id=1, source_target_pairs={{0,1},{1,0},{2,3},{3,2},{4,5},{5,4},{6,7},{7,6},{8,9},{9,8},{10,11... | collective-permute-start | bytes 3145736 | tf_op jit(solution)/shard_map/ppermute | solution.py:47
  176.3 10.6 %copy-start.1 = (f32[4,2,128,128]{2,3,0,1:T(8,128)}, f32[4,2,128,128]{2,3,0,1:T(8,128)S(1)}, u32[]{:S(2)}) copy-start(f32[4,2,128,128]{2,3,0,1:T(8,128)S(1)} %copy.14) | copy-start | bytes 1572868
  177.8 9.1 %copy-start.3 = (f32[4,2,128,128]{2,3,0,1:T(8,128)}, f32[4,2,128,128]{2,3,0,1:T(8,128)S(1)}, u32[]{:S(2)}) copy-start(f32[4,2,128,128]{2,3,0,1:T(8,128)S(1)} %copy.17) | copy-start | bytes 1572868
  190.5 20.3 %collective-permute-start.12 = (f32[4,3072]{1,0:T(4,128)S(1)}, f32[4,3072]{1,0:T(4,128)S(1)}, u32[]{:S(2)}, u32[]{:S(2)}) collective-permute-start(f32[4,3072]{1,0:T(4,128)S(1)} %select_add_fusion.1), channel_id=1, source_target_pairs={{0,24},{8,16},{16,8},{24,0},{1,25},{9,17},{17,9},{25,1},{2,26},{10... | collective-permute-start | bytes 147464 | tf_op jit(solution)/shard_map/ppermute | solution.py:31
  197.3 15.5 %collective-permute-start.11 = (f32[4,3072]{1,0:T(4,128)S(1)}, f32[4,3072]{1,0:T(4,128)S(1)}, u32[]{:S(2)}, u32[]{:S(2)}) collective-permute-start(f32[4,3072]{1,0:T(4,128)S(1)} %select_add_fusion.1), channel_id=1, source_target_pairs={{0,16},{8,24},{16,0},{24,8},{1,17},{9,25},{17,1},{25,9},{2,18},{10... | collective-permute-start | bytes 147464 | tf_op jit(solution)/shard_map/ppermute | solution.py:31
  210.7 4.1 %collective-permute-start.10 = (f32[4,3072]{1,0:T(4,128)S(1)}, f32[4,3072]{1,0:T(4,128)S(1)}, u32[]{:S(2)}, u32[]{:S(2)}) collective-permute-start(f32[4,3072]{1,0:T(4,128)S(1)} %select_add_fusion.1), channel_id=1, source_target_pairs={{0,8},{8,0},{16,24},{24,16},{1,9},{9,1},{17,25},{25,17},{2,10},{10... | collective-permute-start | bytes 147464 | tf_op jit(solution)/shard_map/ppermute | solution.py:31
  214.8 18.9 %slice-start.4 = ((s8[6291456]{0:T(1024)(128)(4,1)}), s8[2097152]{0:T(1024)(128)(4,1)S(1)}, s32[]{:S(2)}) async-start(s8[6291456]{0:T(1024)(128)(4,1)} %bitcast.185), calls=%async_computation.4 | async-start | bytes 4194304
  214.9 6.1 %collective-permute-start.15 = (f32[4,3072]{1,0:T(4,128)S(1)}, f32[4,3072]{1,0:T(4,128)S(1)}, u32[]{:S(2)}, u32[]{:S(2)}) collective-permute-start(f32[4,3072]{1,0:T(4,128)S(1)} %fusion.94), channel_id=1, source_target_pairs={{0,6},{2,4},{4,2},{6,0},{1,7},{3,5},{5,3},{7,1},{8,14},{10,12},{12... | collective-permute-start | bytes 147464 | tf_op jit(solution)/shard_map/ppermute | solution.py:31
  218.1 5.0 %collective-permute-start.14 = (f32[4,3072]{1,0:T(4,128)S(1)}, f32[4,3072]{1,0:T(4,128)S(1)}, u32[]{:S(2)}, u32[]{:S(2)}) collective-permute-start(f32[4,3072]{1,0:T(4,128)S(1)} %fusion.94), channel_id=1, source_target_pairs={{0,4},{2,6},{4,0},{6,2},{1,5},{3,7},{5,1},{7,3},{8,12},{10,14},{12... | collective-permute-start | bytes 147464 | tf_op jit(solution)/shard_map/ppermute | solution.py:31
  218.1 5.0 %collective-permute-start.13 = (f32[4,3072]{1,0:T(4,128)S(1)}, f32[4,3072]{1,0:T(4,128)S(1)}, u32[]{:S(2)}, u32[]{:S(2)}) collective-permute-start(f32[4,3072]{1,0:T(4,128)S(1)} %fusion.94), channel_id=1, source_target_pairs={{0,2},{2,0},{4,6},{6,4},{1,3},{3,1},{5,7},{7,5},{8,10},{10,8},{12,... | collective-permute-start | bytes 147464 | tf_op jit(solution)/shard_map/ppermute | solution.py:31
  223.8 1.4 collective-permute-start.16
  235.6 8.2 %slice-start.8 = ((s8[6291456]{0:T(1024)(128)(4,1)}), s8[4194304]{0:T(1024)(128)(4,1)S(1)}, s32[]{:S(2)}) async-start(s8[6291456]{0:T(1024)(128)(4,1)} %bitcast.196), calls=%async_computation.8 | async-start | bytes 8388608
  235.6 8.2 %slice-start.9 = ((s8[6291456]{0:T(1024)(128)(4,1)}), s8[2097152]{0:T(1024)(128)(4,1)S(1)}, s32[]{:S(2)}) async-start(s8[6291456]{0:T(1024)(128)(4,1)} %bitcast.196), calls=%async_computation.9 | async-start | bytes 4194304
  240.7 2.7 %collective-permute-start.17 = (f32[2,4,2,128,128]{3,4,1,2,0:T(8,128)S(1)}, f32[2,4,2,128,128]{3,4,1,2,0:T(8,128)S(1)}, u32[]{:S(2)}, u32[]{:S(2)}) collective-permute-start(f32[2,4,2,128,128]{3,4,1,2,0:T(8,128)S(1)} %pad_maximum_fusion.2), channel_id=1, source_target_pairs={{0,1},{1,0},{2,3},{3,2},{4,5},{5,4},{6,7},{7,6},{8,9},{9,8},{10,11... | collective-permute-start | bytes 3145736 | tf_op jit(solution)/shard_map/ppermute | solution.py:47
  249.1 5.1 %collective-permute-start.20 = (f32[4,3072]{1,0:T(4,128)S(1)}, f32[4,3072]{1,0:T(4,128)S(1)}, u32[]{:S(2)}, u32[]{:S(2)}) collective-permute-start(f32[4,3072]{1,0:T(4,128)S(1)} %select_add_fusion), channel_id=1, source_target_pairs={{0,24},{8,16},{16,8},{24,0},{1,25},{9,17},{17,9},{25,1},{2,26},{10... | collective-permute-start | bytes 147464 | tf_op jit(solution)/shard_map/ppermute | solution.py:31
  251.5 4.1 %collective-permute-start.19 = (f32[4,3072]{1,0:T(4,128)S(1)}, f32[4,3072]{1,0:T(4,128)S(1)}, u32[]{:S(2)}, u32[]{:S(2)}) collective-permute-start(f32[4,3072]{1,0:T(4,128)S(1)} %select_add_fusion), channel_id=1, source_target_pairs={{0,16},{8,24},{16,0},{24,8},{1,17},{9,25},{17,1},{25,9},{2,18},{10... | collective-permute-start | bytes 147464 | tf_op jit(solution)/shard_map/ppermute | solution.py:31
  251.5 4.1 %collective-permute-start.18 = (f32[4,3072]{1,0:T(4,128)S(1)}, f32[4,3072]{1,0:T(4,128)S(1)}, u32[]{:S(2)}, u32[]{:S(2)}) collective-permute-start(f32[4,3072]{1,0:T(4,128)S(1)} %select_add_fusion), channel_id=1, source_target_pairs={{0,8},{8,0},{16,24},{24,16},{1,9},{9,1},{17,25},{25,17},{2,10},{10... | collective-permute-start | bytes 147464 | tf_op jit(solution)/shard_map/ppermute | solution.py:31
  255.7 6.1 %collective-permute-start.23 = (f32[4,3072]{1,0:T(4,128)S(1)}, f32[4,3072]{1,0:T(4,128)S(1)}, u32[]{:S(2)}, u32[]{:S(2)}) collective-permute-start(f32[4,3072]{1,0:T(4,128)S(1)} %fusion.93), channel_id=1, source_target_pairs={{0,6},{2,4},{4,2},{6,0},{1,7},{3,5},{5,3},{7,1},{8,14},{10,12},{12... | collective-permute-start | bytes 147464 | tf_op jit(solution)/shard_map/ppermute | solution.py:31
  257.2 5.6 %collective-permute-start.22 = (f32[4,3072]{1,0:T(4,128)S(1)}, f32[4,3072]{1,0:T(4,128)S(1)}, u32[]{:S(2)}, u32[]{:S(2)}) collective-permute-start(f32[4,3072]{1,0:T(4,128)S(1)} %fusion.93), channel_id=1, source_target_pairs={{0,4},{2,6},{4,0},{6,2},{1,5},{3,7},{5,1},{7,3},{8,12},{10,14},{12... | collective-permute-start | bytes 147464 | tf_op jit(solution)/shard_map/ppermute | solution.py:31
  257.9 5.0 %collective-permute-start.21 = (f32[4,3072]{1,0:T(4,128)S(1)}, f32[4,3072]{1,0:T(4,128)S(1)}, u32[]{:S(2)}, u32[]{:S(2)}) collective-permute-start(f32[4,3072]{1,0:T(4,128)S(1)} %fusion.93), channel_id=1, source_target_pairs={{0,2},{2,0},{4,6},{6,4},{1,3},{3,1},{5,7},{7,5},{8,10},{10,8},{12,... | collective-permute-start | bytes 147464 | tf_op jit(solution)/shard_map/ppermute | solution.py:31
  263.6 1.3 collective-permute-start.24
  (10 other events, 51.9 us)

commit v5 on v4

--- a/solution.py
+++ b/solution.py
@@ -122,8 +122,12 @@
         panel_moves.append((line * blocks + sender, line * blocks + receiver))
         needs.append((line * blocks + receiver, 0, receiver * blocks + sender))
         needs.append((line * blocks + receiver, 1, sender * blocks + receiver))
+    busy = {s for s, _ in panel_moves} | {d for _, d in panel_moves}
     for plane in range(blocks):
         role[plane * blocks + plane] = 2
+        free = [line for line in range(blocks) if line * blocks + plane not in busy]
+        panel_moves.append((free[0] * blocks + plane, plane * blocks + plane))
+        busy.add(free[0] * blocks + plane)
     rounds = []
     moved = [[0, 0] for _ in range(blocks * blocks)]
     for dest, which, owner in needs:
@@ -164,7 +168,7 @@
         arrived.append(lax.ppermute(own_block, axes, pairs))
     arrived = jnp.stack(arrived)
     received, arrived = lax.optimization_barrier((received, arrived))
-    other = jnp.where(is_diag, green_panel, received)
+    other = received
     mine_rows = green_panel.reshape(freq_count, 2 * span_j, local_pts)
     other_rows = other.reshape(freq_count, 2 * span_j, local_pts)
     moved_table = jnp.array(moved, jnp.int32)[slot]

time: 267 us -> 271 us (1.015)
  waiting for transfers between devices: 138 us -> 147 us
  matrix products: 29.6 us -> 34.8 us
  starting transfers between devices: 51.9 us -> 47.4 us
  other arithmetic: 29.6 us -> 26.4 us
  local copies, waits for them, and re-layouts: 9.04 us -> 6.22 us
    ppermute x18, waiting for transfers between devices: 133 us -> 142 us  [butterfly_sum(): got.append(lax.ppermute(value, axis, [(i, i ^ mask) for i in range(size)]))]
    dot_general x4, matrix products: 14.3 us -> 21.9 us  [point_terms(): jnp.einsum('fab,fbn->fan', adjoint_block(adjoint), right_rows, preferred_...]
    convert_element_type x2, other arithmetic: 17.9 us -> 14.4 us  [pair_body(): (other * spread).astype(jnp.bfloat16).reshape(other_rows.shape)]
  transfers between devices with their start and end apart: 25 -> 25, of which waited for: 13 -> 16; matrix products, arithmetic and copies ran while one was open for 4% -> 3% of each run, Pallas kernels for 0% -> 0%
where the time goes in v5:
time: 271 us; the launch traced here: 270 us
  waiting for transfers between devices  147 us (54%)
  starting transfers between devices  47.4 us (17%)
  matrix products  34.8 us (13%)
  other arithmetic  26.4 us (10%)
  between operations  8.27 us (3%)
  local copies, waits for them, and re-layouts  6.22 us (2%)
    ppermute x18, waiting for transfers between devices, butterfly_sum(): got.append(lax.ppermute(value, axis, [(i, i ^ mask) for i in range(size)]))  142 us
    ppermute x18, starting transfers between devices, butterfly_sum(): got.append(lax.ppermute(value, axis, [(i, i ^ mask) for i in range(size)]))  40.8 us
    dot_general x4, matrix products, point_terms(): jnp.einsum('fab,fbn->fan', adjoint_block(adjoint), right_rows, preferred_...  21.9 us
    convert_element_type x2, other arithmetic, pair_body(): (other * spread).astype(jnp.bfloat16).reshape(other_rows.shape)  14.4 us
    dot_general x4, matrix products, correlate(): jnp.einsum('fan,fbn->fab', left_rows, weighted, preferred_element_type=jn...  12.8 us
  transfers between devices with their start and end apart: 25, of which 16 were waited for; matrix products, arithmetic and copies ran while one was open for 3% of the time, Pallas kernels for 0%

profile of v5, /device:TPU:0, one launch (start us, length us, event | category | flops | bytes accessed | tf_op | source)
XLA Modules:
  0.0 270.2 jit_solution(5245164065703722406)
XLA Ops:
  0.0 5.0 %collective-permute-start.6 = (bf16[4,2,128,3072]{3,2,1,0:T(8,128)(2,1)}, bf16[4,2,128,3072]{3,2,1,0:T(8,128)(2,1)}, u32[]{:S(2)}, u32[]{:S(2)}) collective-permute-start(bf16[4,2,128,3072]{3,2,1,0:T(8,128)(2,1)} %param.6), channel_id=1, source_target_pairs={{0,2},{12,8},{16,22},{20,18},{10,14},{30,28},{24,0},{26,10},{4,20}... | collective-permute-start | bytes 18874376 | tf_op jit(solution)/shard_map/ppermute | solution.py:161
  5.8 2.9 %collective-permute-start.2 = (f32[4,3072]{1,0:T(4,128)S(1)}, f32[4,3072]{1,0:T(4,128)S(1)}, u32[]{:S(2)}, u32[]{:S(2)}) collective-permute-start(f32[4,3072]{1,0:T(4,128)S(1)} %dynamic_update_slice.3), channel_id=1, source_target_pairs={{0,24},{8,16},{16,8},{24,0},{1,25},{9,17},{17,9},{25,1},{2,26},{10... | collective-permute-start | bytes 147464 | tf_op jit(solution)/shard_map/ppermute | solution.py:31
  8.8 3.4 %collective-permute-start.1 = (f32[4,3072]{1,0:T(4,128)S(1)}, f32[4,3072]{1,0:T(4,128)S(1)}, u32[]{:S(2)}, u32[]{:S(2)}) collective-permute-start(f32[4,3072]{1,0:T(4,128)S(1)} %dynamic_update_slice.3), channel_id=1, source_target_pairs={{0,16},{8,24},{16,0},{24,8},{1,17},{9,25},{17,1},{25,9},{2,18},{10... | collective-permute-start | bytes 147464 | tf_op jit(solution)/shard_map/ppermute | solution.py:31
  16.3 126.2 %collective-permute-done.2 = f32[4,3072]{1,0:T(4,128)S(1)} collective-permute-done((f32[4,3072]{1,0:T(4,128)S(1)}, f32[4,3072]{1,0:T(4,128)S(1)}, u32[]{:S(2)}, u32[]{:S(2)}) %collective-permute-start.2) | collective-permute-done | bytes 49184 | tf_op jit(solution)/shard_map/ppermute | solution.py:31
  143.1 3.6 %collective-permute-start.5 = (f32[4,3072]{1,0:T(4,128)S(1)}, f32[4,3072]{1,0:T(4,128)S(1)}, u32[]{:S(2)}, u32[]{:S(2)}) collective-permute-start(f32[4,3072]{1,0:T(4,128)S(1)} %fusion.95), channel_id=1, source_target_pairs={{0,6},{2,4},{4,2},{6,0},{1,7},{3,5},{5,3},{7,1},{8,14},{10,12},{12... | collective-permute-start | bytes 147464 | tf_op jit(solution)/shard_map/ppermute | solution.py:31
  147.6 1.6 collective-permute-done.5
  149.9 1.8 collective-permute-done.4
  154.0 7.1 %fusion.2 = (bf16[4,2,128,3072]{3,2,1,0:T(8,128)(2,1)S(1)}, bf16[4,2,128,3072]{3,2,1,0:T(8,128)(2,1)S(1)}) fusion(bf16[4,2,128,3072]{3,2,1,0:T(8,128)(2,1)} %collective-permute-done.6, f32[4,3072]{1,0:T(4,128)S(1)} %get-tuple-element.15, bf16[4,2,128,3072]{3,2,1,0:T(8,128)(2,1)} %param.6), kind=kLoop, calls=%fused_computation.10 | loop fusion | flops 18874368 | bytes 25214976 | tf_op jit(solution)/shard_map/convert_element_type | solution.py:194
  161.2 1.8 convolution_bitcast_fusion.1
  163.1 4.6 %fusion.79 = f32[4,256,256]{1,2,0:T(8,128)S(1)} fusion(bf16[4,256,3072]{2,1,0:T(8,128)(2,1)} %bitcast.24, bf16[4,256,3072]{2,1,0:T(8,128)(2,1)S(1)} %bitcast.189), kind=kOutput, calls=%fused_computation.149 | convolution fusion | flops 1610612736 | bytes 13631488 | tf_op jit(solution)/shard_map/fan,fbn->fab/dot_general | solution.py:53
  168.8 2.4 pad_maximum_fusion.1
  180.7 1.6 fusion.77
  182.6 6.9 %fusion = f32[4,3072]{1,0:T(4,128)S(1)} fusion(bf16[4,256,3072]{2,1,0:T(8,128)(2,1)} %bitcast.177, bf16[4,256,3072]{2,1,0:T(8,128)(2,1)} %bitcast.24, bf16[4,128,128]{1,2,0:T(8,128)(2,1)S(1)} %get-tuple-element.40, bf16[4,128,128]{1,2,0:T(8,128)(2,1)S(1)} %get-tuple-element.39, bf16[4,128,128]{1,2,0:T(8,128)(2,1)S(1)} %fusion.71), kind=kOutput, calls=%fused_computation.8 | convolution fusion | flops 1622134784 | bytes 13025280 | tf_op jit(solution)/shard_map/fab,fbn->fan/dot_general | solution.py:68
  189.6 5.0 %fusion.6 = f32[4,3072]{1,0:T(4,128)S(1)} fusion(bf16[4,256,3072]{2,1,0:T(8,128)(2,1)} %bitcast.24, bf16[4,256,3072]{2,1,0:T(8,128)(2,1)S(1)} %bitcast.183, bf16[4,128,128]{1,2,0:T(8,128)(2,1)S(1)} %get-tuple-element.42, bf16[4,128,128]{1,2,0:T(8,128)(2,1)S(1)} %get-tuple-element.41, bf16[4,128,128]{1,2,0:T(8,128)(2,1)S(1)} %fusion.72), kind=kOutput, calls=%fused_computation.14 | convolution fusion | flops 1622134784 | bytes 13025280 | tf_op jit(solution)/shard_map/fab,fbn->fan/dot_general | solution.py:68
  194.6 3.4 %collective-permute-start.12 = (f32[4,3072]{1,0:T(4,128)S(1)}, f32[4,3072]{1,0:T(4,128)S(1)}, u32[]{:S(2)}, u32[]{:S(2)}) collective-permute-start(f32[4,3072]{1,0:T(4,128)S(1)} %select_add_fusion.1), channel_id=1, source_target_pairs={{0,24},{8,16},{16,8},{24,0},{1,25},{9,17},{17,9},{25,1},{2,26},{10... | collective-permute-start | bytes 147464 | tf_op jit(solution)/shard_map/ppermute | solution.py:31
  198.0 12.8 %collective-permute-start.11 = (f32[4,3072]{1,0:T(4,128)S(1)}, f32[4,3072]{1,0:T(4,128)S(1)}, u32[]{:S(2)}, u32[]{:S(2)}) collective-permute-start(f32[4,3072]{1,0:T(4,128)S(1)} %select_add_fusion.1), channel_id=1, source_target_pairs={{0,16},{8,24},{16,0},{24,8},{1,17},{9,25},{17,1},{25,9},{2,18},{10... | collective-permute-start | bytes 147464 | tf_op jit(solution)/shard_map/ppermute | solution.py:31
  210.9 2.1 collective-permute-done.11
  213.0 2.0 collective-permute-done.10
  215.2 4.3 %collective-permute-start.13 = (f32[4,3072]{1,0:T(4,128)S(1)}, f32[4,3072]{1,0:T(4,128)S(1)}, u32[]{:S(2)}, u32[]{:S(2)}) collective-permute-start(f32[4,3072]{1,0:T(4,128)S(1)} %fusion.94), channel_id=1, source_target_pairs={{0,2},{2,0},{4,6},{6,4},{1,3},{3,1},{5,7},{7,5},{8,10},{10,8},{12,... | collective-permute-start | bytes 147464 | tf_op jit(solution)/shard_map/ppermute | solution.py:31
  219.5 1.5 collective-permute-done.15
  224.9 7.3 %fusion.3 = (bf16[4,2,128,3072]{3,2,1,0:T(8,128)(2,1)S(1)}, bf16[4,2,128,3072]{3,2,1,0:T(8,128)(2,1)S(1)}) fusion(bf16[4,2,128,3072]{3,2,1,0:T(8,128)(2,1)} %collective-permute-done.6, f32[4,3072]{1,0:T(4,128)S(1)} %get-tuple-element.11, bf16[4,2,128,3072]{3,2,1,0:T(8,128)(2,1)} %param.6), kind=kLoop, calls=%fused_computation.11 | loop fusion | flops 18874368 | bytes 25214976 | tf_op jit(solution)/shard_map/convert_element_type | solution.py:194
  232.2 1.8 convolution_bitcast_fusion
  234.1 4.6 %fusion.80 = f32[4,256,256]{1,2,0:T(8,128)S(1)} fusion(bf16[4,256,3072]{2,1,0:T(8,128)(2,1)} %bitcast.24, bf16[4,256,3072]{2,1,0:T(8,128)(2,1)S(1)} %bitcast.190), kind=kOutput, calls=%fused_computation.150 | convolution fusion | flops 1610612736 | bytes 13631488 | tf_op jit(solution)/shard_map/fan,fbn->fab/dot_general | solution.py:53
  239.2 2.5 collective-permute-done.17
  242.1 5.0 %fusion.1 = f32[4,3072]{1,0:T(4,128)S(1)} fusion(bf16[4,256,3072]{2,1,0:T(8,128)(2,1)S(1)} %bitcast.187, bf16[4,256,3072]{2,1,0:T(8,128)(2,1)} %bitcast.24, bf16[4,128,128]{1,2,0:T(8,128)(2,1)S(1)} %get-tuple-element.36, bf16[4,128,128]{1,2,0:T(8,128)(2,1)S(1)} %get-tuple-element.35, bf16[4,128,128]{1,2,0:T(8,128)(2,1)S(1)} %fusion.73), kind=kOutput, calls=%fused_computation.9 | convolution fusion | flops 1622134784 | bytes 13025280 | tf_op jit(solution)/shard_map/fab,fbn->fan/dot_general | solution.py:68
  247.1 5.0 %fusion.7 = f32[4,3072]{1,0:T(4,128)S(1)} fusion(bf16[4,256,3072]{2,1,0:T(8,128)(2,1)} %bitcast.24, bf16[4,256,3072]{2,1,0:T(8,128)(2,1)S(1)} %bitcast.188, bf16[4,128,128]{1,2,0:T(8,128)(2,1)S(1)} %get-tuple-element.38, bf16[4,128,128]{1,2,0:T(8,128)(2,1)S(1)} %get-tuple-element.37, bf16[4,128,128]{1,2,0:T(8,128)(2,1)S(1)} %fusion.74), kind=kOutput, calls=%fused_computation.15 | convolution fusion | flops 1622134784 | bytes 13025280 | tf_op jit(solution)/shard_map/fab,fbn->fan/dot_general | solution.py:68
  253.7 2.0 collective-permute-start.18
  255.8 1.7 collective-permute-done.20
  258.0 2.4 collective-permute-start.23
  262.5 1.6 collective-permute-done.23
  264.1 1.7 collective-permute-done.22
  266.8 1.4 collective-permute-done.24
  (103 shorter events, 25.0 us)
Async XLA Ops:
  0.0 154.0 %collective-permute-start.6 = (bf16[4,2,128,3072]{3,2,1,0:T(8,128)(2,1)}, bf16[4,2,128,3072]{3,2,1,0:T(8,128)(2,1)}, u32[]{:S(2)}, u32[]{:S(2)}) collective-permute-start(bf16[4,2,128,3072]{3,2,1,0:T(8,128)(2,1)} %param.6), channel_id=1, source_target_pairs={{0,2},{12,8},{16,22},{20,18},{10,14},{30,28},{24,0},{26,10},{4,20}... | collective-permute-start | bytes 18874376 | tf_op jit(solution)/shard_map/ppermute | solution.py:161
  5.8 136.7 %collective-permute-start.2 = (f32[4,3072]{1,0:T(4,128)S(1)}, f32[4,3072]{1,0:T(4,128)S(1)}, u32[]{:S(2)}, u32[]{:S(2)}) collective-permute-start(f32[4,3072]{1,0:T(4,128)S(1)} %dynamic_update_slice.3), channel_id=1, source_target_pairs={{0,24},{8,16},{16,8},{24,0},{1,25},{9,17},{17,9},{25,1},{2,26},{10... | collective-permute-start | bytes 147464 | tf_op jit(solution)/shard_map/ppermute | solution.py:31
  8.8 134.2 %collective-permute-start.1 = (f32[4,3072]{1,0:T(4,128)S(1)}, f32[4,3072]{1,0:T(4,128)S(1)}, u32[]{:S(2)}, u32[]{:S(2)}) collective-permute-start(f32[4,3072]{1,0:T(4,128)S(1)} %dynamic_update_slice.3), channel_id=1, source_target_pairs={{0,16},{8,24},{16,0},{24,8},{1,17},{9,25},{17,1},{25,9},{2,18},{10... | collective-permute-start | bytes 147464 | tf_op jit(solution)/shard_map/ppermute | solution.py:31
  12.1 130.9 %collective-permute-start = (f32[4,3072]{1,0:T(4,128)S(1)}, f32[4,3072]{1,0:T(4,128)S(1)}, u32[]{:S(2)}, u32[]{:S(2)}) collective-permute-start(f32[4,3072]{1,0:T(4,128)S(1)} %dynamic_update_slice.3), channel_id=1, source_target_pairs={{0,8},{8,0},{16,24},{24,16},{1,9},{9,1},{17,25},{25,17},{2,10},{10... | collective-permute-start | bytes 147464 | tf_op jit(solution)/shard_map/ppermute | solution.py:31
  15.5 136.3 %collective-permute-start.7 = (f32[9,128,128]{2,1,0:T(8,128)S(1)}, f32[9,128,128]{2,1,0:T(8,128)S(1)}, u32[]{:S(2)}, u32[]{:S(2)}) collective-permute-start(f32[9,128,128]{2,1,0:T(8,128)S(1)} %get-tuple-element.34), channel_id=1, source_target_pairs={{8,2},{4,8},{24,22},{12,18},{26,14},{22,28},{9,3},{5,9},{25,23},{1... | collective-permute-start | bytes 1769480 | tf_op jit(solution)/shard_map/ppermute | solution.py:168
  143.1 6.1 %collective-permute-start.5 = (f32[4,3072]{1,0:T(4,128)S(1)}, f32[4,3072]{1,0:T(4,128)S(1)}, u32[]{:S(2)}, u32[]{:S(2)}) collective-permute-start(f32[4,3072]{1,0:T(4,128)S(1)} %fusion.95), channel_id=1, source_target_pairs={{0,6},{2,4},{4,2},{6,0},{1,7},{3,5},{5,3},{7,1},{8,14},{10,12},{12... | collective-permute-start | bytes 147464 | tf_op jit(solution)/shard_map/ppermute | solution.py:31
  146.7 5.0 %collective-permute-start.4 = (f32[4,3072]{1,0:T(4,128)S(1)}, f32[4,3072]{1,0:T(4,128)S(1)}, u32[]{:S(2)}, u32[]{:S(2)}) collective-permute-start(f32[4,3072]{1,0:T(4,128)S(1)} %fusion.95), channel_id=1, source_target_pairs={{0,4},{2,6},{4,0},{6,2},{1,5},{3,7},{5,1},{7,3},{8,12},{10,14},{12... | collective-permute-start | bytes 147464 | tf_op jit(solution)/shard_map/ppermute | solution.py:31
  146.7 5.0 %collective-permute-start.3 = (f32[4,3072]{1,0:T(4,128)S(1)}, f32[4,3072]{1,0:T(4,128)S(1)}, u32[]{:S(2)}, u32[]{:S(2)}) collective-permute-start(f32[4,3072]{1,0:T(4,128)S(1)} %fusion.95), channel_id=1, source_target_pairs={{0,2},{2,0},{4,6},{6,4},{1,3},{3,1},{5,7},{7,5},{8,10},{10,8},{12,... | collective-permute-start | bytes 147464 | tf_op jit(solution)/shard_map/ppermute | solution.py:31
  149.2 2.6 collective-permute-start.8
  152.6 8.5 %slice-start = ((s8[6291456]{0:T(1024)(128)(4,1)}), s8[4194304]{0:T(1024)(128)(4,1)S(1)}, s32[]{:S(2)}) async-start(s8[6291456]{0:T(1024)(128)(4,1)} %bitcast.178), calls=%async_computation | async-start | bytes 8388608
  154.0 7.1 %slice-start.1 = ((s8[6291456]{0:T(1024)(128)(4,1)}), s8[2097152]{0:T(1024)(128)(4,1)S(1)}, s32[]{:S(2)}) async-start(s8[6291456]{0:T(1024)(128)(4,1)} %bitcast.178), calls=%async_computation.1 | async-start | bytes 4194304
  163.0 12.0 %copy-start.1 = (s32[16]{0:T(128)S(1)}, s32[16]{0:T(128)}, u32[]{:S(2)}) copy-start(s32[16]{0:T(128)} %constant.93.clone) | copy-start | bytes 196
  171.2 9.5 %collective-permute-start.9 = (f32[2,4,2,128,128]{3,4,1,2,0:T(8,128)}, f32[2,4,2,128,128]{3,4,1,2,0:T(8,128)}, u32[]{:S(2)}, u32[]{:S(2)}) collective-permute-start(f32[2,4,2,128,128]{3,4,1,2,0:T(8,128)} %pad_maximum_fusion.1), channel_id=1, source_target_pairs={{0,1},{1,0},{2,3},{3,2},{4,5},{5,4},{6,7},{7,6},{8,9},{9,8},{10,11... | collective-permute-start | bytes 3145736 | tf_op jit(solution)/shard_map/ppermute | solution.py:47
  182.5 7.0 %slice-start.2 = ((s8[6291456]{0:T(1024)(128)(4,1)}), s8[4194304]{0:T(1024)(128)(4,1)S(1)}, s32[]{:S(2)}) async-start(s8[6291456]{0:T(1024)(128)(4,1)} %bitcast.181), calls=%async_computation.2 | async-start | bytes 8388608
  182.6 6.9 %slice-start.3 = ((s8[6291456]{0:T(1024)(128)(4,1)}), s8[2097152]{0:T(1024)(128)(4,1)S(1)}, s32[]{:S(2)}) async-start(s8[6291456]{0:T(1024)(128)(4,1)} %bitcast.181), calls=%async_computation.3 | async-start | bytes 4194304
  194.6 16.3 %collective-permute-start.12 = (f32[4,3072]{1,0:T(4,128)S(1)}, f32[4,3072]{1,0:T(4,128)S(1)}, u32[]{:S(2)}, u32[]{:S(2)}) collective-permute-start(f32[4,3072]{1,0:T(4,128)S(1)} %select_add_fusion.1), channel_id=1, source_target_pairs={{0,24},{8,16},{16,8},{24,0},{1,25},{9,17},{17,9},{25,1},{2,26},{10... | collective-permute-start | bytes 147464 | tf_op jit(solution)/shard_map/ppermute | solution.py:31
  198.0 14.9 %collective-permute-start.11 = (f32[4,3072]{1,0:T(4,128)S(1)}, f32[4,3072]{1,0:T(4,128)S(1)}, u32[]{:S(2)}, u32[]{:S(2)}) collective-permute-start(f32[4,3072]{1,0:T(4,128)S(1)} %select_add_fusion.1), channel_id=1, source_target_pairs={{0,16},{8,24},{16,0},{24,8},{1,17},{9,25},{17,1},{25,9},{2,18},{10... | collective-permute-start | bytes 147464 | tf_op jit(solution)/shard_map/ppermute | solution.py:31
  210.9 4.1 %collective-permute-start.10 = (f32[4,3072]{1,0:T(4,128)S(1)}, f32[4,3072]{1,0:T(4,128)S(1)}, u32[]{:S(2)}, u32[]{:S(2)}) collective-permute-start(f32[4,3072]{1,0:T(4,128)S(1)} %select_add_fusion.1), channel_id=1, source_target_pairs={{0,8},{8,0},{16,24},{24,16},{1,9},{9,1},{17,25},{25,17},{2,10},{10... | collective-permute-start | bytes 147464 | tf_op jit(solution)/shard_map/ppermute | solution.py:31
  214.9 17.2 %slice-start.4 = ((s8[6291456]{0:T(1024)(128)(4,1)}), s8[2097152]{0:T(1024)(128)(4,1)S(1)}, s32[]{:S(2)}) async-start(s8[6291456]{0:T(1024)(128)(4,1)} %bitcast.184), calls=%async_computation.4 | async-start | bytes 4194304
  215.0 6.0 %collective-permute-start.15 = (f32[4,3072]{1,0:T(4,128)S(1)}, f32[4,3072]{1,0:T(4,128)S(1)}, u32[]{:S(2)}, u32[]{:S(2)}) collective-permute-start(f32[4,3072]{1,0:T(4,128)S(1)} %fusion.94), channel_id=1, source_target_pairs={{0,6},{2,4},{4,2},{6,0},{1,7},{3,5},{5,3},{7,1},{8,14},{10,12},{12... | collective-permute-start | bytes 147464 | tf_op jit(solution)/shard_map/ppermute | solution.py:31
  215.1 5.9 %collective-permute-start.14 = (f32[4,3072]{1,0:T(4,128)S(1)}, f32[4,3072]{1,0:T(4,128)S(1)}, u32[]{:S(2)}, u32[]{:S(2)}) collective-permute-start(f32[4,3072]{1,0:T(4,128)S(1)} %fusion.94), channel_id=1, source_target_pairs={{0,4},{2,6},{4,0},{6,2},{1,5},{3,7},{5,1},{7,3},{8,12},{10,14},{12... | collective-permute-start | bytes 147464 | tf_op jit(solution)/shard_map/ppermute | solution.py:31
  215.2 6.4 %collective-permute-start.13 = (f32[4,3072]{1,0:T(4,128)S(1)}, f32[4,3072]{1,0:T(4,128)S(1)}, u32[]{:S(2)}, u32[]{:S(2)}) collective-permute-start(f32[4,3072]{1,0:T(4,128)S(1)} %fusion.94), channel_id=1, source_target_pairs={{0,2},{2,0},{4,6},{6,4},{1,3},{3,1},{5,7},{7,5},{8,10},{10,8},{12,... | collective-permute-start | bytes 147464 | tf_op jit(solution)/shard_map/ppermute | solution.py:31
  222.3 1.3 collective-permute-start.16
  224.9 7.3 %slice-start.5 = ((s8[6291456]{0:T(1024)(128)(4,1)}), s8[4194304]{0:T(1024)(128)(4,1)S(1)}, s32[]{:S(2)}) async-start(s8[6291456]{0:T(1024)(128)(4,1)} %bitcast.184), calls=%async_computation.5 | async-start | bytes 8388608
  239.0 2.7 %collective-permute-start.17 = (f32[2,4,2,128,128]{3,4,1,2,0:T(8,128)S(1)}, f32[2,4,2,128,128]{3,4,1,2,0:T(8,128)S(1)}, u32[]{:S(2)}, u32[]{:S(2)}) collective-permute-start(f32[2,4,2,128,128]{3,4,1,2,0:T(8,128)S(1)} %pad_maximum_fusion.2), channel_id=1, source_target_pairs={{0,1},{1,0},{2,3},{3,2},{4,5},{5,4},{6,7},{7,6},{8,9},{9,8},{10,11... | collective-permute-start | bytes 3145736 | tf_op jit(solution)/shard_map/ppermute | solution.py:47
  252.2 5.3 %collective-permute-start.20 = (f32[4,3072]{1,0:T(4,128)S(1)}, f32[4,3072]{1,0:T(4,128)S(1)}, u32[]{:S(2)}, u32[]{:S(2)}) collective-permute-start(f32[4,3072]{1,0:T(4,128)S(1)} %select_add_fusion), channel_id=1, source_target_pairs={{0,24},{8,16},{16,8},{24,0},{1,25},{9,17},{17,9},{25,1},{2,26},{10... | collective-permute-start | bytes 147464 | tf_op jit(solution)/shard_map/ppermute | solution.py:31
  253.3 4.6 %collective-permute-start.19 = (f32[4,3072]{1,0:T(4,128)S(1)}, f32[4,3072]{1,0:T(4,128)S(1)}, u32[]{:S(2)}, u32[]{:S(2)}) collective-permute-start(f32[4,3072]{1,0:T(4,128)S(1)} %select_add_fusion), channel_id=1, source_target_pairs={{0,16},{8,24},{16,0},{24,8},{1,17},{9,25},{17,1},{25,9},{2,18},{10... | collective-permute-start | bytes 147464 | tf_op jit(solution)/shard_map/ppermute | solution.py:31
  253.7 4.2 %collective-permute-start.18 = (f32[4,3072]{1,0:T(4,128)S(1)}, f32[4,3072]{1,0:T(4,128)S(1)}, u32[]{:S(2)}, u32[]{:S(2)}) collective-permute-start(f32[4,3072]{1,0:T(4,128)S(1)} %select_add_fusion), channel_id=1, source_target_pairs={{0,8},{8,0},{16,24},{24,16},{1,9},{9,1},{17,25},{25,17},{2,10},{10... | collective-permute-start | bytes 147464 | tf_op jit(solution)/shard_map/ppermute | solution.py:31
  258.0 6.1 %collective-permute-start.23 = (f32[4,3072]{1,0:T(4,128)S(1)}, f32[4,3072]{1,0:T(4,128)S(1)}, u32[]{:S(2)}, u32[]{:S(2)}) collective-permute-start(f32[4,3072]{1,0:T(4,128)S(1)} %fusion.93), channel_id=1, source_target_pairs={{0,6},{2,4},{4,2},{6,0},{1,7},{3,5},{5,3},{7,1},{8,14},{10,12},{12... | collective-permute-start | bytes 147464 | tf_op jit(solution)/shard_map/ppermute | solution.py:31
  260.3 5.4 %collective-permute-start.22 = (f32[4,3072]{1,0:T(4,128)S(1)}, f32[4,3072]{1,0:T(4,128)S(1)}, u32[]{:S(2)}, u32[]{:S(2)}) collective-permute-start(f32[4,3072]{1,0:T(4,128)S(1)} %fusion.93), channel_id=1, source_target_pairs={{0,4},{2,6},{4,0},{6,2},{1,5},{3,7},{5,1},{7,3},{8,12},{10,14},{12... | collective-permute-start | bytes 147464 | tf_op jit(solution)/shard_map/ppermute | solution.py:31
  261.5 4.7 %collective-permute-start.21 = (f32[4,3072]{1,0:T(4,128)S(1)}, f32[4,3072]{1,0:T(4,128)S(1)}, u32[]{:S(2)}, u32[]{:S(2)}) collective-permute-start(f32[4,3072]{1,0:T(4,128)S(1)} %fusion.93), channel_id=1, source_target_pairs={{0,2},{2,0},{4,6},{6,4},{1,3},{3,1},{5,7},{7,5},{8,10},{10,8},{12,... | collective-permute-start | bytes 147464 | tf_op jit(solution)/shard_map/ppermute | solution.py:31
  266.8 1.4 collective-permute-start.24
  (1 other events, 0.8 us)

commit v6 on v4

--- a/solution.py
+++ b/solution.py
@@ -183,7 +183,7 @@
     )
     log_field = butterfly_sum(placed, axes)
 
-    for _ in range(ITERS):
+    def run_sweep(sweep_idx, log_field):
         psd_field = jnp.exp(log_field)
         spread = psd_field[:, None, None, :]
         weighted_mine = (green_panel * spread).astype(jnp.bfloat16).reshape(mine_rows.shape)
@@ -198,8 +198,9 @@
         point_part = jnp.where(keep_first, term_first, 0.0) + jnp.where(keep_second, term_second, 0.0)
         gradient = butterfly_sum(point_part, axes)
         squares = swap_add(jnp.sum(gradient * gradient), "pts")
-        log_field = log_field - descent * gradient / jnp.sqrt(squares / entry_count + epsilon)
-
+        return log_field - descent * gradient / jnp.sqrt(squares / entry_count + epsilon)
+
+    log_field = lax.fori_loop(0, ITERS, run_sweep, log_field)
     own = lax.dynamic_slice_in_dim(log_field, offset, piece, axis=1)
     return own[None]
 

time: 267 us -> 253 us (0.948)
  other arithmetic: 29.6 us -> 11.6 us
  matrix products: 29.6 us -> 39.4 us
  local copies, waits for them, and re-layouts: 9.04 us -> 4.93 us
  loops' own time: 0 us -> 3.04 us
  between operations: 9.02 us -> 5.98 us
  waiting for transfers between devices: 138 us -> 135 us
    convert_element_type x4 -> x2, other arithmetic: 18.3 us -> 0.4 us  [run_sweep(): (scale_first * (quad_weight * both[0] - obs_first)).astype(jnp.bfloat16)]
    dot_general x4, matrix products: 15.3 us -> 23.6 us  [correlate(): jnp.einsum('fan,fbn->fab', left_rows, weighted, preferred_element_type=jn...]
    select_n x0 -> x1, other arithmetic: none -> 6.06 us  [pair_body(): other = jnp.where(is_diag, green_panel, received)]
    ppermute x18, waiting for transfers between devices: 133 us -> 127 us  [butterfly_sum(): got.append(lax.ppermute(value, axis, [(i, i ^ mask) for i in range(size)]))]
    another operation x0 -> x1, loops' own time: none -> 3.04 us  [pair_body(): log_field = lax.fori_loop(0, ITERS, run_sweep, log_field)]
    unnamed x34 -> x0, local copies, waits for them, and re-layouts: 2.89 us -> none
    another operation x5 -> x4, other arithmetic: 3.22 us -> 0.36 us  [run_sweep(): both = swap_add(jnp.stack([corr_first, corr_second]), 'pts')]
  transfers between devices with their start and end apart: 25 -> 25, of which waited for: 13 -> 15; matrix products, arithmetic and copies ran while one was open for 4% -> 2% of each run, Pallas kernels for 0% -> 0%
where the time goes in v6:
time: 253 us; the launch traced here: 252 us
  waiting for transfers between devices  135 us (53%)
  starting transfers between devices  52.1 us (21%)
  matrix products  39.4 us (16%)
  other arithmetic  11.6 us (5%)
  between operations  5.98 us (2%)
  local copies, waits for them, and re-layouts  4.93 us (2%)
  loops' own time  3.04 us (1%)
    ppermute x18, waiting for transfers between devices, butterfly_sum(): got.append(lax.ppermute(value, axis, [(i, i ^ mask) for i in range(size)]))  127 us
    ppermute x18, starting transfers between devices, butterfly_sum(): got.append(lax.ppermute(value, axis, [(i, i ^ mask) for i in range(size)]))  42.8 us
    dot_general x4, matrix products, correlate(): jnp.einsum('fan,fbn->fab', left_rows, weighted, preferred_element_type=jn...  23.6 us
    dot_general x4, matrix products, point_terms(): jnp.einsum('fab,fbn->fan', adjoint_block(adjoint), right_rows, preferred_...  15.9 us
    ppermute x4, waiting for transfers between devices, swap_add(): return value + lax.ppermute(value, axis, [(0, 1), (1, 0)])  7.83 us
    ppermute x1, starting transfers between devices, pair_body(): received = lax.ppermute(green_panel, axes, panel_moves)  7.61 us
    select_n x1, other arithmetic, pair_body(): other = jnp.where(is_diag, green_panel, received)  6.06 us
  transfers between devices with their start and end apart: 25, of which 15 were waited for; matrix products, arithmetic and copies ran while one was open for 2% of the time, Pallas kernels for 0%

profile of v6, /device:TPU:0, one launch (start us, length us, event | category | flops | bytes accessed | tf_op | source)
XLA Modules:
  0.0 252.4 jit_solution(12195668634696865618)
XLA Ops:
  0.0 7.6 %collective-permute-start.14 = (bf16[4,2,128,3072]{3,2,1,0:T(8,128)(2,1)}, bf16[4,2,128,3072]{3,2,1,0:T(8,128)(2,1)}, u32[]{:S(2)}, u32[]{:S(2)}) collective-permute-start(bf16[4,2,128,3072]{3,2,1,0:T(8,128)(2,1)} %param.8), channel_id=1, source_target_pairs={{0,2},{12,8},{16,22},{20,18},{10,14},{30,28},{1,3},{13,9},{17,23},... | collective-permute-start | bytes 18874376 | tf_op jit(solution)/shard_map/ppermute | solution.py:157
  8.5 3.6 %collective-permute-start.9 = (f32[4,3072]{1,0:T(4,128)S(1)}, f32[4,3072]{1,0:T(4,128)S(1)}, u32[]{:S(2)}, u32[]{:S(2)}) collective-permute-start(f32[4,3072]{1,0:T(4,128)S(1)} %dynamic_update_slice.3), channel_id=1, source_target_pairs={{0,16},{8,24},{16,0},{24,8},{1,17},{9,25},{17,1},{25,9},{2,18},{10... | collective-permute-start | bytes 147464 | tf_op jit(solution)/shard_map/ppermute | solution.py:31
  12.2 1.4 collective-permute-start.10
  25.2 3.3 %collective-permute-start.13 = (f32[4,3072]{1,0:T(4,128)S(1)}, f32[4,3072]{1,0:T(4,128)S(1)}, u32[]{:S(2)}, u32[]{:S(2)}) collective-permute-start(f32[4,3072]{1,0:T(4,128)S(1)} %fusion.52), channel_id=1, source_target_pairs={{0,6},{2,4},{4,2},{6,0},{1,7},{3,5},{5,3},{7,1},{8,14},{10,12},{12... | collective-permute-start | bytes 147464 | tf_op jit(solution)/shard_map/ppermute | solution.py:31
  29.2 112.8 %collective-permute-done.11 = f32[4,3072]{1,0:T(4,128)S(1)} collective-permute-done((f32[4,3072]{1,0:T(4,128)S(1)}, f32[4,3072]{1,0:T(4,128)S(1)}, u32[]{:S(2)}, u32[]{:S(2)}) %collective-permute-start.11) | collective-permute-done | bytes 49184 | tf_op jit(solution)/shard_map/ppermute | solution.py:31
  144.1 6.1 %broadcast_select_fusion = bf16[4,2,128,3072]{3,2,1,0:T(8,128)(2,1)} fusion(bf16[4,2,128,3072]{3,2,1,0:T(8,128)(2,1)} %param.8, bf16[4,2,128,3072]{3,2,1,0:T(8,128)(2,1)} %collective-permute-done.14, pred[]{:T(512)} %bitcast.46), kind=kLoop, calls=%fused_computation.63 | loop fusion | flops 3145728 | bytes 18874368 | tf_op jit(solution)/shard_map/jit(_where)/select_n | solution.py:167
  150.2 101.6 %while.13 = (s32[]{:T(128)}, f32[4,3072]{1,0:T(4,128)S(1)}, pred[]{:T(512)}, bf16[4,256,3072]{2,1,0:T(8,128)(2,1)}, f32[1,128,128]{1,2,0:T(8,128)S(1)}, /*index=...) while((s32[]{:T(128)}, f32[4,3072]{1,0:T(4,128)S(1)}, ...), condition=%wide.region_4.5_spmd, body=%wide.region_0.4_spmd.sunk | while | flops 6487400448 | bytes 119604528 | solution.py:203
  150.2 6.6 %fusion.78 = f32[4,256,256]{1,2,0:T(8,128)S(1)} fusion(bf16[4,256,3072]{2,1,0:T(8,128)(2,1)} %bitcast.154, bf16[4,256,3072]{2,1,0:T(8,128)(2,1)} %get-tuple-element.412, f32[4,3072]{1,0:T(4,128)S(1)} %exp.11), kind=kOutput, calls=%fused_computation.11.clone.1 | convolution fusion | flops 1620049920 | bytes 13680640 | tf_op jit(solution)/shard_map/while/body/eval_jaxpr/fan,fbn->fab/dot_general | solution.py:53
  156.9 5.2 %fusion.80 = f32[4,256,256]{1,2,0:T(8,128)S(1)} fusion(bf16[4,256,3072]{2,1,0:T(8,128)(2,1)} %get-tuple-element.412, bf16[4,256,3072]{2,1,0:T(8,128)(2,1)S(1)} %bitcast.156, f32[4,3072]{1,0:T(4,128)S(1)} %exp.11), kind=kOutput, calls=%fused_computation.10.clone.1 | convolution fusion | flops 1620049920 | bytes 13680640 | tf_op jit(solution)/shard_map/while/body/eval_jaxpr/fan,fbn->fab/dot_general | solution.py:53
  162.4 2.6 %collective-permute-done = f32[2,4,2,128,128]{3,4,1,2,0:T(8,128)S(1)} collective-permute-done((f32[2,4,2,128,128]{3,4,1,2,0:T(8,128)S(1)}, f32[2,4,2,128,128]{3,4,1,2,0:T(8,128)S(1)}, u32[]{:S(2)}, u32[]{:S(2)}) %collective-permute-start) | collective-permute-done | bytes 1048608 | tf_op jit(solution)/shard_map/while/body/eval_jaxpr/ppermute | solution.py:47
  165.5 5.4 %multiply_reduce_fusion.7 = f32[4,3072]{1,0:T(4,128)S(1)} fusion(bf16[4,256,3072]{2,1,0:T(8,128)(2,1)S(1)} %bitcast.157, bf16[4,256,3072]{2,1,0:T(8,128)(2,1)} %get-tuple-element.412, bf16[4,128,128]{1,2,0:T(8,128)(2,1)S(1)} %get-tuple-element.359, bf16[4,128,128]{1,2,0:T(8,128)(2,1)S(1)} %get-tuple-element.360, bf16[4,128,128]{1,2,0:T(8,128)(2,1)S(1)} %fusion.85), kind=kOutput, calls=%fused_computation.5.clone.1 | convolution fusion | flops 1622134784 | bytes 13025280 | tf_op jit(solution)/shard_map/while/body/eval_jaxpr/fab,fbn->fan/dot_general | solution.py:68
  171.0 2.5 %multiply_reduce_fusion.6 = f32[4,3072]{1,0:T(4,128)S(1)} fusion(bf16[4,256,3072]{2,1,0:T(8,128)(2,1)S(1)} %bitcast.162, bf16[4,256,3072]{2,1,0:T(8,128)(2,1)S(1)} %bitcast.158, bf16[4,128,128]{1,2,0:T(8,128)(2,1)S(1)} %get-tuple-element.356, bf16[4,128,128]{1,2,0:T(8,128)(2,1)S(1)} %get-tuple-element.357, bf16[4,128,128]{1,2,0:T(8,128)(2,1)S(1)} %fusion.84), kind=kOutput, calls=%fused_computation.4.clone.1 | convolution fusion | flops 1622134784 | bytes 13025280 | tf_op jit(solution)/shard_map/while/body/eval_jaxpr/fab,fbn->fan/dot_general | solution.py:68
  173.6 5.4 %collective-permute-start.1 = (f32[4,3072]{1,0:T(4,128)S(1)}, f32[4,3072]{1,0:T(4,128)S(1)}, u32[]{:S(2)}, u32[]{:S(2)}) collective-permute-start(f32[4,3072]{1,0:T(4,128)S(1)} %select_add_fusion.2), channel_id=1, source_target_pairs={{0,24},{8,16},{16,8},{24,0},{1,25},{9,17},{17,9},{25,1},{2,26},{10... | collective-permute-start | bytes 147464 | tf_op jit(solution)/shard_map/while/body/eval_jaxpr/ppermute | solution.py:31
  179.0 12.7 %collective-permute-start.2 = (f32[4,3072]{1,0:T(4,128)S(1)}, f32[4,3072]{1,0:T(4,128)S(1)}, u32[]{:S(2)}, u32[]{:S(2)}) collective-permute-start(f32[4,3072]{1,0:T(4,128)S(1)} %select_add_fusion.2), channel_id=1, source_target_pairs={{0,16},{8,24},{16,0},{24,8},{1,17},{9,25},{17,1},{25,9},{2,18},{10... | collective-permute-start | bytes 147464 | tf_op jit(solution)/shard_map/while/body/eval_jaxpr/ppermute | solution.py:31
  191.7 2.1 collective-permute-done.2
  193.8 2.0 collective-permute-done.3
  195.9 6.5 %collective-permute-start.4 = (f32[4,3072]{1,0:T(4,128)S(1)}, f32[4,3072]{1,0:T(4,128)S(1)}, u32[]{:S(2)}, u32[]{:S(2)}) collective-permute-start(f32[4,3072]{1,0:T(4,128)S(1)} %fusion.86), channel_id=1, source_target_pairs={{0,6},{2,4},{4,2},{6,0},{1,7},{3,5},{5,3},{7,1},{8,14},{10,12},{12... | collective-permute-start | bytes 147464 | tf_op jit(solution)/shard_map/while/body/eval_jaxpr/ppermute | solution.py:31
  203.0 1.5 collective-permute-done.4
  204.5 2.8 %collective-permute-done.5 = f32[4,3072]{1,0:T(4,128)S(1)} collective-permute-done((f32[4,3072]{1,0:T(4,128)S(1)}, f32[4,3072]{1,0:T(4,128)S(1)}, u32[]{:S(2)}, u32[]{:S(2)}) %collective-permute-start.5) | collective-permute-done | bytes 49184 | tf_op jit(solution)/shard_map/while/body/eval_jaxpr/ppermute | solution.py:31
  208.1 1.3 collective-permute-done.7
  210.9 6.6 %fusion.78 = f32[4,256,256]{1,2,0:T(8,128)S(1)} fusion(bf16[4,256,3072]{2,1,0:T(8,128)(2,1)} %bitcast.154, bf16[4,256,3072]{2,1,0:T(8,128)(2,1)} %get-tuple-element.412, f32[4,3072]{1,0:T(4,128)S(1)} %exp.11), kind=kOutput, calls=%fused_computation.11.clone.1 | convolution fusion | flops 1620049920 | bytes 13680640 | tf_op jit(solution)/shard_map/while/body/eval_jaxpr/fan,fbn->fab/dot_general | solution.py:53
  217.5 5.2 %fusion.80 = f32[4,256,256]{1,2,0:T(8,128)S(1)} fusion(bf16[4,256,3072]{2,1,0:T(8,128)(2,1)} %get-tuple-element.412, bf16[4,256,3072]{2,1,0:T(8,128)(2,1)S(1)} %bitcast.156, f32[4,3072]{1,0:T(4,128)S(1)} %exp.11), kind=kOutput, calls=%fused_computation.10.clone.1 | convolution fusion | flops 1620049920 | bytes 13680640 | tf_op jit(solution)/shard_map/while/body/eval_jaxpr/fan,fbn->fab/dot_general | solution.py:53
  223.2 2.5 collective-permute-done
  226.2 5.4 %multiply_reduce_fusion.7 = f32[4,3072]{1,0:T(4,128)S(1)} fusion(bf16[4,256,3072]{2,1,0:T(8,128)(2,1)S(1)} %bitcast.157, bf16[4,256,3072]{2,1,0:T(8,128)(2,1)} %get-tuple-element.412, bf16[4,128,128]{1,2,0:T(8,128)(2,1)S(1)} %get-tuple-element.359, bf16[4,128,128]{1,2,0:T(8,128)(2,1)S(1)} %get-tuple-element.360, bf16[4,128,128]{1,2,0:T(8,128)(2,1)S(1)} %fusion.85), kind=kOutput, calls=%fused_computation.5.clone.1 | convolution fusion | flops 1622134784 | bytes 13025280 | tf_op jit(solution)/shard_map/while/body/eval_jaxpr/fab,fbn->fan/dot_general | solution.py:68
  231.6 2.5 %multiply_reduce_fusion.6 = f32[4,3072]{1,0:T(4,128)S(1)} fusion(bf16[4,256,3072]{2,1,0:T(8,128)(2,1)S(1)} %bitcast.162, bf16[4,256,3072]{2,1,0:T(8,128)(2,1)S(1)} %bitcast.158, bf16[4,128,128]{1,2,0:T(8,128)(2,1)S(1)} %get-tuple-element.356, bf16[4,128,128]{1,2,0:T(8,128)(2,1)S(1)} %get-tuple-element.357, bf16[4,128,128]{1,2,0:T(8,128)(2,1)S(1)} %fusion.84), kind=kOutput, calls=%fused_computation.4.clone.1 | convolution fusion | flops 1622134784 | bytes 13025280 | tf_op jit(solution)/shard_map/while/body/eval_jaxpr/fab,fbn->fan/dot_general | solution.py:68
  234.2 2.8 %collective-permute-start.1 = (f32[4,3072]{1,0:T(4,128)S(1)}, f32[4,3072]{1,0:T(4,128)S(1)}, u32[]{:S(2)}, u32[]{:S(2)}) collective-permute-start(f32[4,3072]{1,0:T(4,128)S(1)} %select_add_fusion.2), channel_id=1, source_target_pairs={{0,24},{8,16},{16,8},{24,0},{1,25},{9,17},{17,9},{25,1},{2,26},{10... | collective-permute-start | bytes 147464 | tf_op jit(solution)/shard_map/while/body/eval_jaxpr/ppermute | solution.py:31
  237.8 1.5 collective-permute-done.1
  239.3 1.8 collective-permute-done.2
  241.2 1.5 collective-permute-start.4
  243.4 2.3 collective-permute-start.6
  245.7 1.5 collective-permute-done.4
  249.0 1.3 collective-permute-done.7
  (98 shorter events, 17.0 us)
Async XLA Ops:
  0.0 143.4 %collective-permute-start.14 = (bf16[4,2,128,3072]{3,2,1,0:T(8,128)(2,1)}, bf16[4,2,128,3072]{3,2,1,0:T(8,128)(2,1)}, u32[]{:S(2)}, u32[]{:S(2)}) collective-permute-start(bf16[4,2,128,3072]{3,2,1,0:T(8,128)(2,1)} %param.8), channel_id=1, source_target_pairs={{0,2},{12,8},{16,22},{20,18},{10,14},{30,28},{1,3},{13,9},{17,23},... | collective-permute-start | bytes 18874376 | tf_op jit(solution)/shard_map/ppermute | solution.py:157
  8.5 15.5 %collective-permute-start.8 = (f32[4,3072]{1,0:T(4,128)S(1)}, f32[4,3072]{1,0:T(4,128)S(1)}, u32[]{:S(2)}, u32[]{:S(2)}) collective-permute-start(f32[4,3072]{1,0:T(4,128)S(1)} %dynamic_update_slice.3), channel_id=1, source_target_pairs={{0,8},{8,0},{16,24},{24,16},{1,9},{9,1},{17,25},{25,17},{2,10},{10... | collective-permute-start | bytes 147464 | tf_op jit(solution)/shard_map/ppermute | solution.py:31
  8.5 15.4 %collective-permute-start.9 = (f32[4,3072]{1,0:T(4,128)S(1)}, f32[4,3072]{1,0:T(4,128)S(1)}, u32[]{:S(2)}, u32[]{:S(2)}) collective-permute-start(f32[4,3072]{1,0:T(4,128)S(1)} %dynamic_update_slice.3), channel_id=1, source_target_pairs={{0,16},{8,24},{16,0},{24,8},{1,17},{9,25},{17,1},{25,9},{2,18},{10... | collective-permute-start | bytes 147464 | tf_op jit(solution)/shard_map/ppermute | solution.py:31
  12.2 11.8 %collective-permute-start.10 = (f32[4,3072]{1,0:T(4,128)S(1)}, f32[4,3072]{1,0:T(4,128)S(1)}, u32[]{:S(2)}, u32[]{:S(2)}) collective-permute-start(f32[4,3072]{1,0:T(4,128)S(1)} %dynamic_update_slice.3), channel_id=1, source_target_pairs={{0,24},{8,16},{16,8},{24,0},{1,25},{9,17},{17,9},{25,1},{2,26},{10... | collective-permute-start | bytes 147464 | tf_op jit(solution)/shard_map/ppermute | solution.py:31
  24.1 118.0 %collective-permute-start.11 = (f32[4,3072]{1,0:T(4,128)S(1)}, f32[4,3072]{1,0:T(4,128)S(1)}, u32[]{:S(2)}, u32[]{:S(2)}) collective-permute-start(f32[4,3072]{1,0:T(4,128)S(1)} %fusion.52), channel_id=1, source_target_pairs={{0,2},{2,0},{4,6},{6,4},{1,3},{3,1},{5,7},{7,5},{8,10},{10,8},{12,... | collective-permute-start | bytes 147464 | tf_op jit(solution)/shard_map/ppermute | solution.py:31
  24.8 117.9 %collective-permute-start.12 = (f32[4,3072]{1,0:T(4,128)S(1)}, f32[4,3072]{1,0:T(4,128)S(1)}, u32[]{:S(2)}, u32[]{:S(2)}) collective-permute-start(f32[4,3072]{1,0:T(4,128)S(1)} %fusion.52), channel_id=1, source_target_pairs={{0,4},{2,6},{4,0},{6,2},{1,5},{3,7},{5,1},{7,3},{8,12},{10,14},{12... | collective-permute-start | bytes 147464 | tf_op jit(solution)/shard_map/ppermute | solution.py:31
  25.2 117.9 %collective-permute-start.13 = (f32[4,3072]{1,0:T(4,128)S(1)}, f32[4,3072]{1,0:T(4,128)S(1)}, u32[]{:S(2)}, u32[]{:S(2)}) collective-permute-start(f32[4,3072]{1,0:T(4,128)S(1)} %fusion.52), channel_id=1, source_target_pairs={{0,6},{2,4},{4,2},{6,0},{1,7},{3,5},{5,3},{7,1},{8,14},{10,12},{12... | collective-permute-start | bytes 147464 | tf_op jit(solution)/shard_map/ppermute | solution.py:31
  28.5 114.6 %collective-permute-start.15 = (f32[9,128,128]{2,1,0:T(8,128)S(1)}, f32[9,128,128]{2,1,0:T(8,128)S(1)}, u32[]{:S(2)}, u32[]{:S(2)}) collective-permute-start(f32[9,128,128]{2,1,0:T(8,128)S(1)} %get-tuple-element.259), channel_id=1, source_target_pairs={{8,2},{4,8},{24,22},{12,18},{26,14},{22,28},{9,3},{5,9},{25,23},{1... | collective-permute-start | bytes 1769480 | tf_op jit(solution)/shard_map/ppermute | solution.py:164
  142.0 1.2 collective-permute-start.16
  150.2 6.7 %copy-start = (bf16[4,2,128,3072]{3,2,1,0:T(8,128)(2,1)S(1)}, bf16[4,2,128,3072]{3,2,1,0:T(8,128)(2,1)}, u32[]{:S(2)}) copy-start(bf16[4,2,128,3072]{3,2,1,0:T(8,128)(2,1)} %get-tuple-element.411) | copy-start | bytes 18874372 | tf_op jit(solution)/shard_map/while
  162.3 2.7 %collective-permute-start = (f32[2,4,2,128,128]{3,4,1,2,0:T(8,128)S(1)}, f32[2,4,2,128,128]{3,4,1,2,0:T(8,128)S(1)}, u32[]{:S(2)}, u32[]{:S(2)}) collective-permute-start(f32[2,4,2,128,128]{3,4,1,2,0:T(8,128)S(1)} %pad_maximum_fusion.10), channel_id=1, source_target_pairs={{0,1},{1,0},{2,3},{3,2},{4,5},{5,4},{6,7},{7,6},{8,9},{9,8},{10,11... | collective-permute-start | bytes 3145736 | tf_op jit(solution)/shard_map/while/body/eval_jaxpr/ppermute | solution.py:47
  165.4 5.5 %slice-start = ((s8[6291456]{0:T(1024)(128)(4,1)}), s8[2097152]{0:T(1024)(128)(4,1)S(1)}, s32[]{:S(2)}) async-start(s8[6291456]{0:T(1024)(128)(4,1)} %bitcast.161), calls=%async_computation | async-start | bytes 4194304 | tf_op jit(solution)/shard_map/while
  165.5 5.4 %slice-start.1 = ((s8[6291456]{0:T(1024)(128)(4,1)}), s8[4194304]{0:T(1024)(128)(4,1)S(1)}, s32[]{:S(2)}) async-start(s8[6291456]{0:T(1024)(128)(4,1)} %bitcast.161), calls=%async_computation.1 | async-start | bytes 8388608 | tf_op jit(solution)/shard_map/while
  173.6 18.1 %collective-permute-start.1 = (f32[4,3072]{1,0:T(4,128)S(1)}, f32[4,3072]{1,0:T(4,128)S(1)}, u32[]{:S(2)}, u32[]{:S(2)}) collective-permute-start(f32[4,3072]{1,0:T(4,128)S(1)} %select_add_fusion.2), channel_id=1, source_target_pairs={{0,24},{8,16},{16,8},{24,0},{1,25},{9,17},{17,9},{25,1},{2,26},{10... | collective-permute-start | bytes 147464 | tf_op jit(solution)/shard_map/while/body/eval_jaxpr/ppermute | solution.py:31
  179.0 14.8 %collective-permute-start.2 = (f32[4,3072]{1,0:T(4,128)S(1)}, f32[4,3072]{1,0:T(4,128)S(1)}, u32[]{:S(2)}, u32[]{:S(2)}) collective-permute-start(f32[4,3072]{1,0:T(4,128)S(1)} %select_add_fusion.2), channel_id=1, source_target_pairs={{0,16},{8,24},{16,0},{24,8},{1,17},{9,25},{17,1},{25,9},{2,18},{10... | collective-permute-start | bytes 147464 | tf_op jit(solution)/shard_map/while/body/eval_jaxpr/ppermute | solution.py:31
  191.7 4.1 %collective-permute-start.3 = (f32[4,3072]{1,0:T(4,128)S(1)}, f32[4,3072]{1,0:T(4,128)S(1)}, u32[]{:S(2)}, u32[]{:S(2)}) collective-permute-start(f32[4,3072]{1,0:T(4,128)S(1)} %select_add_fusion.2), channel_id=1, source_target_pairs={{0,8},{8,0},{16,24},{24,16},{1,9},{9,1},{17,25},{25,17},{2,10},{10... | collective-permute-start | bytes 147464 | tf_op jit(solution)/shard_map/while/body/eval_jaxpr/ppermute | solution.py:31
  195.9 8.6 %collective-permute-start.4 = (f32[4,3072]{1,0:T(4,128)S(1)}, f32[4,3072]{1,0:T(4,128)S(1)}, u32[]{:S(2)}, u32[]{:S(2)}) collective-permute-start(f32[4,3072]{1,0:T(4,128)S(1)} %fusion.86), channel_id=1, source_target_pairs={{0,6},{2,4},{4,2},{6,0},{1,7},{3,5},{5,3},{7,1},{8,14},{10,12},{12... | collective-permute-start | bytes 147464 | tf_op jit(solution)/shard_map/while/body/eval_jaxpr/ppermute | solution.py:31
  202.4 5.0 %collective-permute-start.5 = (f32[4,3072]{1,0:T(4,128)S(1)}, f32[4,3072]{1,0:T(4,128)S(1)}, u32[]{:S(2)}, u32[]{:S(2)}) collective-permute-start(f32[4,3072]{1,0:T(4,128)S(1)} %fusion.86), channel_id=1, source_target_pairs={{0,4},{2,6},{4,0},{6,2},{1,5},{3,7},{5,1},{7,3},{8,12},{10,14},{12... | collective-permute-start | bytes 147464 | tf_op jit(solution)/shard_map/while/body/eval_jaxpr/ppermute | solution.py:31
  202.4 5.0 %collective-permute-start.6 = (f32[4,3072]{1,0:T(4,128)S(1)}, f32[4,3072]{1,0:T(4,128)S(1)}, u32[]{:S(2)}, u32[]{:S(2)}) collective-permute-start(f32[4,3072]{1,0:T(4,128)S(1)} %fusion.86), channel_id=1, source_target_pairs={{0,2},{2,0},{4,6},{6,4},{1,3},{3,1},{5,7},{7,5},{8,10},{10,8},{12,... | collective-permute-start | bytes 147464 | tf_op jit(solution)/shard_map/while/body/eval_jaxpr/ppermute | solution.py:31
  208.1 1.4 collective-permute-start.7
  210.9 6.7 %copy-start = (bf16[4,2,128,3072]{3,2,1,0:T(8,128)(2,1)S(1)}, bf16[4,2,128,3072]{3,2,1,0:T(8,128)(2,1)}, u32[]{:S(2)}) copy-start(bf16[4,2,128,3072]{3,2,1,0:T(8,128)(2,1)} %get-tuple-element.411) | copy-start | bytes 18874372 | tf_op jit(solution)/shard_map/while
  223.0 2.7 %collective-permute-start = (f32[2,4,2,128,128]{3,4,1,2,0:T(8,128)S(1)}, f32[2,4,2,128,128]{3,4,1,2,0:T(8,128)S(1)}, u32[]{:S(2)}, u32[]{:S(2)}) collective-permute-start(f32[2,4,2,128,128]{3,4,1,2,0:T(8,128)S(1)} %pad_maximum_fusion.10), channel_id=1, source_target_pairs={{0,1},{1,0},{2,3},{3,2},{4,5},{5,4},{6,7},{7,6},{8,9},{9,8},{10,11... | collective-permute-start | bytes 3145736 | tf_op jit(solution)/shard_map/while/body/eval_jaxpr/ppermute | solution.py:47
  226.1 5.5 %slice-start = ((s8[6291456]{0:T(1024)(128)(4,1)}), s8[2097152]{0:T(1024)(128)(4,1)S(1)}, s32[]{:S(2)}) async-start(s8[6291456]{0:T(1024)(128)(4,1)} %bitcast.161), calls=%async_computation | async-start | bytes 4194304 | tf_op jit(solution)/shard_map/while
  226.2 5.4 %slice-start.1 = ((s8[6291456]{0:T(1024)(128)(4,1)}), s8[4194304]{0:T(1024)(128)(4,1)S(1)}, s32[]{:S(2)}) async-start(s8[6291456]{0:T(1024)(128)(4,1)} %bitcast.161), calls=%async_computation.1 | async-start | bytes 8388608 | tf_op jit(solution)/shard_map/while
  234.2 5.1 %collective-permute-start.1 = (f32[4,3072]{1,0:T(4,128)S(1)}, f32[4,3072]{1,0:T(4,128)S(1)}, u32[]{:S(2)}, u32[]{:S(2)}) collective-permute-start(f32[4,3072]{1,0:T(4,128)S(1)} %select_add_fusion.2), channel_id=1, source_target_pairs={{0,24},{8,16},{16,8},{24,0},{1,25},{9,17},{17,9},{25,1},{2,26},{10... | collective-permute-start | bytes 147464 | tf_op jit(solution)/shard_map/while/body/eval_jaxpr/ppermute | solution.py:31
  237.0 4.1 %collective-permute-start.2 = (f32[4,3072]{1,0:T(4,128)S(1)}, f32[4,3072]{1,0:T(4,128)S(1)}, u32[]{:S(2)}, u32[]{:S(2)}) collective-permute-start(f32[4,3072]{1,0:T(4,128)S(1)} %select_add_fusion.2), channel_id=1, source_target_pairs={{0,16},{8,24},{16,0},{24,8},{1,17},{9,25},{17,1},{25,9},{2,18},{10... | collective-permute-start | bytes 147464 | tf_op jit(solution)/shard_map/while/body/eval_jaxpr/ppermute | solution.py:31
  237.0 4.1 %collective-permute-start.3 = (f32[4,3072]{1,0:T(4,128)S(1)}, f32[4,3072]{1,0:T(4,128)S(1)}, u32[]{:S(2)}, u32[]{:S(2)}) collective-permute-start(f32[4,3072]{1,0:T(4,128)S(1)} %select_add_fusion.2), channel_id=1, source_target_pairs={{0,8},{8,0},{16,24},{24,16},{1,9},{9,1},{17,25},{25,17},{2,10},{10... | collective-permute-start | bytes 147464 | tf_op jit(solution)/shard_map/while/body/eval_jaxpr/ppermute | solution.py:31
  241.2 6.0 %collective-permute-start.4 = (f32[4,3072]{1,0:T(4,128)S(1)}, f32[4,3072]{1,0:T(4,128)S(1)}, u32[]{:S(2)}, u32[]{:S(2)}) collective-permute-start(f32[4,3072]{1,0:T(4,128)S(1)} %fusion.86), channel_id=1, source_target_pairs={{0,6},{2,4},{4,2},{6,0},{1,7},{3,5},{5,3},{7,1},{8,14},{10,12},{12... | collective-permute-start | bytes 147464 | tf_op jit(solution)/shard_map/while/body/eval_jaxpr/ppermute | solution.py:31
  242.8 5.1 %collective-permute-start.5 = (f32[4,3072]{1,0:T(4,128)S(1)}, f32[4,3072]{1,0:T(4,128)S(1)}, u32[]{:S(2)}, u32[]{:S(2)}) collective-permute-start(f32[4,3072]{1,0:T(4,128)S(1)} %fusion.86), channel_id=1, source_target_pairs={{0,4},{2,6},{4,0},{6,2},{1,5},{3,7},{5,1},{7,3},{8,12},{10,14},{12... | collective-permute-start | bytes 147464 | tf_op jit(solution)/shard_map/while/body/eval_jaxpr/ppermute | solution.py:31
  243.4 4.9 %collective-permute-start.6 = (f32[4,3072]{1,0:T(4,128)S(1)}, f32[4,3072]{1,0:T(4,128)S(1)}, u32[]{:S(2)}, u32[]{:S(2)}) collective-permute-start(f32[4,3072]{1,0:T(4,128)S(1)} %fusion.86), channel_id=1, source_target_pairs={{0,2},{2,0},{4,6},{6,4},{1,3},{3,1},{5,7},{7,5},{8,10},{10,8},{12,... | collective-permute-start | bytes 147464 | tf_op jit(solution)/shard_map/while/body/eval_jaxpr/ppermute | solution.py:31
  249.0 1.4 collective-permute-start.7

commit v7 on v6

--- a/solution.py
+++ b/solution.py
@@ -159,10 +159,21 @@
     own_block = jnp.concatenate(
         [observed.reshape(-1, span_j, span_j), pair_weights.astype(jnp.float32)[None]], axis=0
     )
-    arrived = [own_block]
-    for pairs, _ in rounds:
-        arrived.append(lax.ppermute(own_block, axes, pairs))
-    arrived = jnp.stack(arrived)
+    planes = own_block.shape[0]
+    half_planes = (planes + 1) // 2
+    padded = jnp.concatenate(
+        [own_block, jnp.zeros((2 * half_planes - planes,) + own_block.shape[1:], own_block.dtype)], axis=0
+    )
+    core = lax.axis_index("pts")
+    own_half = lax.dynamic_slice_in_dim(padded, core * half_planes, half_planes, axis=0)
+    halves = jnp.stack([lax.ppermute(own_half, axes, pairs) for pairs, _ in rounds])
+    partner_halves = lax.ppermute(halves, "pts", [(0, 1), (1, 0)])
+    joined = jnp.where(
+        core == 0,
+        jnp.concatenate([halves, partner_halves], axis=1),
+        jnp.concatenate([partner_halves, halves], axis=1),
+    )[:, :planes]
+    arrived = jnp.concatenate([own_block[None], joined], axis=0)
     received, arrived = lax.optimization_barrier((received, arrived))
     other = jnp.where(is_diag, green_panel, received)
     mine_rows = green_panel.reshape(freq_count, 2 * span_j, local_pts)

time: 253 us -> 245 us (0.968)
  starting transfers between devices: 52.1 us -> 46 us
  waiting for transfers between devices: 135 us -> 132 us
    ppermute x18, starting transfers between devices: 42.8 us -> 36.6 us  [butterfly_sum(): got.append(lax.ppermute(value, axis, [(i, i ^ mask) for i in range(size)]))]
    ppermute x18, waiting for transfers between devices: 127 us -> 125 us  [butterfly_sum(): got.append(lax.ppermute(value, axis, [(i, i ^ mask) for i in range(size)]))]
  transfers between devices with their start and end apart: 25 -> 26, of which waited for: 15 -> 16; matrix products, arithmetic and copies ran while one was open for 2% -> 3% of each run, Pallas kernels for 0% -> 0%
where the time goes in v7:
time: 245 us
  waiting for transfers between devices  132 us (54%)
  starting transfers between devices  46 us (19%)
  matrix products  39.4 us (16%)
  other arithmetic  12.7 us (5%)
  between operations  5.99 us (2%)
  local copies, waits for them, and re-layouts  5.08 us (2%)
  loops' own time  3.04 us (1%)
    ppermute x18, waiting for transfers between devices, butterfly_sum(): got.append(lax.ppermute(value, axis, [(i, i ^ mask) for i in range(size)]))  125 us
    ppermute x18, starting transfers between devices, butterfly_sum(): got.append(lax.ppermute(value, axis, [(i, i ^ mask) for i in range(size)]))  36.6 us
    dot_general x4, matrix products, correlate(): jnp.einsum('fan,fbn->fab', left_rows, weighted, preferred_element_type=jn...  23.5 us
    dot_general x4, matrix products, point_terms(): jnp.einsum('fab,fbn->fan', adjoint_block(adjoint), right_rows, preferred_...  15.9 us
    ppermute x4, waiting for transfers between devices, swap_add(): return value + lax.ppermute(value, axis, [(0, 1), (1, 0)])  7.84 us
    ppermute x1, starting transfers between devices, pair_body(): received = lax.ppermute(green_panel, axes, panel_moves)  7.61 us
    select_n x1, other arithmetic, pair_body(): other = jnp.where(is_diag, green_panel, received)  6.06 us
  transfers between devices with their start and end apart: 26, of which 16 were waited for; matrix products, arithmetic and copies ran while one was open for 3% of the time, Pallas kernels for 0%

profile of v7, /device:TPU:0, one launch (start us, length us, event | category | flops | bytes accessed | tf_op | source)
XLA Modules:
  0.0 244.6 jit_solution(13372955702850316892)
XLA Ops:
  0.0 7.6 %collective-permute-start.14 = (bf16[4,2,128,3072]{3,2,1,0:T(8,128)(2,1)}, bf16[4,2,128,3072]{3,2,1,0:T(8,128)(2,1)}, u32[]{:S(2)}, u32[]{:S(2)}) collective-permute-start(bf16[4,2,128,3072]{3,2,1,0:T(8,128)(2,1)} %param.8), channel_id=1, source_target_pairs={{0,2},{12,8},{16,22},{20,18},{10,14},{30,28},{1,3},{13,9},{17,23},... | collective-permute-start | bytes 18874376 | tf_op jit(solution)/shard_map/ppermute | solution.py:157
  8.5 3.6 %collective-permute-start.9 = (f32[4,3072]{1,0:T(4,128)S(1)}, f32[4,3072]{1,0:T(4,128)S(1)}, u32[]{:S(2)}, u32[]{:S(2)}) collective-permute-start(f32[4,3072]{1,0:T(4,128)S(1)} %dynamic_update_slice.3), channel_id=1, source_target_pairs={{0,16},{8,24},{16,0},{24,8},{1,17},{9,25},{17,1},{25,9},{2,18},{10... | collective-permute-start | bytes 147464 | tf_op jit(solution)/shard_map/ppermute | solution.py:31
  12.2 1.4 collective-permute-start.10
  20.7 1.3 dynamic_slice.106
  26.6 1.4 collective-permute-start.11
  28.0 4.2 %collective-permute-start.12 = (f32[4,3072]{1,0:T(4,128)S(1)}, f32[4,3072]{1,0:T(4,128)S(1)}, u32[]{:S(2)}, u32[]{:S(2)}) collective-permute-start(f32[4,3072]{1,0:T(4,128)S(1)} %fusion.54), channel_id=1, source_target_pairs={{0,4},{2,6},{4,0},{6,2},{1,5},{3,7},{5,1},{7,3},{8,12},{10,14},{12... | collective-permute-start | bytes 147464 | tf_op jit(solution)/shard_map/ppermute | solution.py:31
  32.6 109.4 %collective-permute-done.11 = f32[4,3072]{1,0:T(4,128)S(1)} collective-permute-done((f32[4,3072]{1,0:T(4,128)S(1)}, f32[4,3072]{1,0:T(4,128)S(1)}, u32[]{:S(2)}, u32[]{:S(2)}) %collective-permute-start.11) | collective-permute-done | bytes 49184 | tf_op jit(solution)/shard_map/ppermute | solution.py:31
  144.2 6.1 %broadcast_select_fusion = bf16[4,2,128,3072]{3,2,1,0:T(8,128)(2,1)} fusion(bf16[4,2,128,3072]{3,2,1,0:T(8,128)(2,1)} %param.8, bf16[4,2,128,3072]{3,2,1,0:T(8,128)(2,1)} %collective-permute-done.14, pred[]{:T(512)} %bitcast.46), kind=kLoop, calls=%fused_computation.63 | loop fusion | flops 3145728 | bytes 18874368 | tf_op jit(solution)/shard_map/jit(_where)/select_n | solution.py:178
  150.2 93.7 %while.13 = (s32[]{:T(128)}, f32[4,3072]{1,0:T(4,128)S(1)}, pred[]{:T(512)}, bf16[4,256,3072]{2,1,0:T(8,128)(2,1)}, f32[1,128,128]{1,2,0:T(8,128)S(1)}, /*index=...) while((s32[]{:T(128)}, f32[4,3072]{1,0:T(4,128)S(1)}, ...), condition=%wide.region_4.5_spmd, body=%wide.region_0.4_spmd.sunk | while | flops 6487400448 | bytes 119604528 | solution.py:214
  150.3 6.6 %fusion.80 = f32[4,256,256]{1,2,0:T(8,128)S(1)} fusion(bf16[4,256,3072]{2,1,0:T(8,128)(2,1)} %bitcast.155, bf16[4,256,3072]{2,1,0:T(8,128)(2,1)} %get-tuple-element.410, f32[4,3072]{1,0:T(4,128)S(1)} %exp.11), kind=kOutput, calls=%fused_computation.11.clone.1 | convolution fusion | flops 1620049920 | bytes 13680640 | tf_op jit(solution)/shard_map/while/body/eval_jaxpr/fan,fbn->fab/dot_general | solution.py:53
  156.9 5.2 %fusion.82 = f32[4,256,256]{1,2,0:T(8,128)S(1)} fusion(bf16[4,256,3072]{2,1,0:T(8,128)(2,1)} %get-tuple-element.410, bf16[4,256,3072]{2,1,0:T(8,128)(2,1)S(1)} %bitcast.157, f32[4,3072]{1,0:T(4,128)S(1)} %exp.11), kind=kOutput, calls=%fused_computation.10.clone.1 | convolution fusion | flops 1620049920 | bytes 13680640 | tf_op jit(solution)/shard_map/while/body/eval_jaxpr/fan,fbn->fab/dot_general | solution.py:53
  162.5 2.6 %collective-permute-done = f32[2,4,2,128,128]{3,4,1,2,0:T(8,128)S(1)} collective-permute-done((f32[2,4,2,128,128]{3,4,1,2,0:T(8,128)S(1)}, f32[2,4,2,128,128]{3,4,1,2,0:T(8,128)S(1)}, u32[]{:S(2)}, u32[]{:S(2)}) %collective-permute-start) | collective-permute-done | bytes 1048608 | tf_op jit(solution)/shard_map/while/body/eval_jaxpr/ppermute | solution.py:47
  165.6 5.4 %multiply_reduce_fusion.7 = f32[4,3072]{1,0:T(4,128)S(1)} fusion(bf16[4,256,3072]{2,1,0:T(8,128)(2,1)S(1)} %bitcast.158, bf16[4,256,3072]{2,1,0:T(8,128)(2,1)} %get-tuple-element.410, bf16[4,128,128]{1,2,0:T(8,128)(2,1)S(1)} %get-tuple-element.357, bf16[4,128,128]{1,2,0:T(8,128)(2,1)S(1)} %get-tuple-element.358, bf16[4,128,128]{1,2,0:T(8,128)(2,1)S(1)} %fusion.87), kind=kOutput, calls=%fused_computation.5.clone.1 | convolution fusion | flops 1622134784 | bytes 13025280 | tf_op jit(solution)/shard_map/while/body/eval_jaxpr/fab,fbn->fan/dot_general | solution.py:68
  171.0 2.5 %multiply_reduce_fusion.6 = f32[4,3072]{1,0:T(4,128)S(1)} fusion(bf16[4,256,3072]{2,1,0:T(8,128)(2,1)S(1)} %bitcast.163, bf16[4,256,3072]{2,1,0:T(8,128)(2,1)S(1)} %bitcast.159, bf16[4,128,128]{1,2,0:T(8,128)(2,1)S(1)} %get-tuple-element.354, bf16[4,128,128]{1,2,0:T(8,128)(2,1)S(1)} %get-tuple-element.355, bf16[4,128,128]{1,2,0:T(8,128)(2,1)S(1)} %fusion.86), kind=kOutput, calls=%fused_computation.4.clone.1 | convolution fusion | flops 1622134784 | bytes 13025280 | tf_op jit(solution)/shard_map/while/body/eval_jaxpr/fab,fbn->fan/dot_general | solution.py:68
  173.6 5.4 %collective-permute-start.1 = (f32[4,3072]{1,0:T(4,128)S(1)}, f32[4,3072]{1,0:T(4,128)S(1)}, u32[]{:S(2)}, u32[]{:S(2)}) collective-permute-start(f32[4,3072]{1,0:T(4,128)S(1)} %select_add_fusion.2), channel_id=1, source_target_pairs={{0,24},{8,16},{16,8},{24,0},{1,25},{9,17},{17,9},{25,1},{2,26},{10... | collective-permute-start | bytes 147464 | tf_op jit(solution)/shard_map/while/body/eval_jaxpr/ppermute | solution.py:31
  179.1 7.0 %collective-permute-start.2 = (f32[4,3072]{1,0:T(4,128)S(1)}, f32[4,3072]{1,0:T(4,128)S(1)}, u32[]{:S(2)}, u32[]{:S(2)}) collective-permute-start(f32[4,3072]{1,0:T(4,128)S(1)} %select_add_fusion.2), channel_id=1, source_target_pairs={{0,16},{8,24},{16,0},{24,8},{1,17},{9,25},{17,1},{25,9},{2,18},{10... | collective-permute-start | bytes 147464 | tf_op jit(solution)/shard_map/while/body/eval_jaxpr/ppermute | solution.py:31
  186.1 2.1 collective-permute-done.2
  188.1 2.0 collective-permute-done.3
  190.3 5.2 %collective-permute-start.5 = (f32[4,3072]{1,0:T(4,128)S(1)}, f32[4,3072]{1,0:T(4,128)S(1)}, u32[]{:S(2)}, u32[]{:S(2)}) collective-permute-start(f32[4,3072]{1,0:T(4,128)S(1)} %fusion.88), channel_id=1, source_target_pairs={{0,4},{2,6},{4,0},{6,2},{1,5},{3,7},{5,1},{7,3},{8,12},{10,14},{12... | collective-permute-start | bytes 147464 | tf_op jit(solution)/shard_map/while/body/eval_jaxpr/ppermute | solution.py:31
  196.4 2.3 collective-permute-done.5
  200.4 1.3 collective-permute-done.7
  203.1 6.6 %fusion.80 = f32[4,256,256]{1,2,0:T(8,128)S(1)} fusion(bf16[4,256,3072]{2,1,0:T(8,128)(2,1)} %bitcast.155, bf16[4,256,3072]{2,1,0:T(8,128)(2,1)} %get-tuple-element.410, f32[4,3072]{1,0:T(4,128)S(1)} %exp.11), kind=kOutput, calls=%fused_computation.11.clone.1 | convolution fusion | flops 1620049920 | bytes 13680640 | tf_op jit(solution)/shard_map/while/body/eval_jaxpr/fan,fbn->fab/dot_general | solution.py:53
  209.8 5.2 %fusion.82 = f32[4,256,256]{1,2,0:T(8,128)S(1)} fusion(bf16[4,256,3072]{2,1,0:T(8,128)(2,1)} %get-tuple-element.410, bf16[4,256,3072]{2,1,0:T(8,128)(2,1)S(1)} %bitcast.157, f32[4,3072]{1,0:T(4,128)S(1)} %exp.11), kind=kOutput, calls=%fused_computation.10.clone.1 | convolution fusion | flops 1620049920 | bytes 13680640 | tf_op jit(solution)/shard_map/while/body/eval_jaxpr/fan,fbn->fab/dot_general | solution.py:53
  215.5 2.5 %collective-permute-done = f32[2,4,2,128,128]{3,4,1,2,0:T(8,128)S(1)} collective-permute-done((f32[2,4,2,128,128]{3,4,1,2,0:T(8,128)S(1)}, f32[2,4,2,128,128]{3,4,1,2,0:T(8,128)S(1)}, u32[]{:S(2)}, u32[]{:S(2)}) %collective-permute-start) | collective-permute-done | bytes 1048608 | tf_op jit(solution)/shard_map/while/body/eval_jaxpr/ppermute | solution.py:47
  218.4 5.4 %multiply_reduce_fusion.7 = f32[4,3072]{1,0:T(4,128)S(1)} fusion(bf16[4,256,3072]{2,1,0:T(8,128)(2,1)S(1)} %bitcast.158, bf16[4,256,3072]{2,1,0:T(8,128)(2,1)} %get-tuple-element.410, bf16[4,128,128]{1,2,0:T(8,128)(2,1)S(1)} %get-tuple-element.357, bf16[4,128,128]{1,2,0:T(8,128)(2,1)S(1)} %get-tuple-element.358, bf16[4,128,128]{1,2,0:T(8,128)(2,1)S(1)} %fusion.87), kind=kOutput, calls=%fused_computation.5.clone.1 | convolution fusion | flops 1622134784 | bytes 13025280 | tf_op jit(solution)/shard_map/while/body/eval_jaxpr/fab,fbn->fan/dot_general | solution.py:68
  223.9 2.5 %multiply_reduce_fusion.6 = f32[4,3072]{1,0:T(4,128)S(1)} fusion(bf16[4,256,3072]{2,1,0:T(8,128)(2,1)S(1)} %bitcast.163, bf16[4,256,3072]{2,1,0:T(8,128)(2,1)S(1)} %bitcast.159, bf16[4,128,128]{1,2,0:T(8,128)(2,1)S(1)} %get-tuple-element.354, bf16[4,128,128]{1,2,0:T(8,128)(2,1)S(1)} %get-tuple-element.355, bf16[4,128,128]{1,2,0:T(8,128)(2,1)S(1)} %fusion.86), kind=kOutput, calls=%fused_computation.4.clone.1 | convolution fusion | flops 1622134784 | bytes 13025280 | tf_op jit(solution)/shard_map/while/body/eval_jaxpr/fab,fbn->fan/dot_general | solution.py:68
  226.5 2.8 %collective-permute-start.1 = (f32[4,3072]{1,0:T(4,128)S(1)}, f32[4,3072]{1,0:T(4,128)S(1)}, u32[]{:S(2)}, u32[]{:S(2)}) collective-permute-start(f32[4,3072]{1,0:T(4,128)S(1)} %select_add_fusion.2), channel_id=1, source_target_pairs={{0,24},{8,16},{16,8},{24,0},{1,25},{9,17},{17,9},{25,1},{2,26},{10... | collective-permute-start | bytes 147464 | tf_op jit(solution)/shard_map/while/body/eval_jaxpr/ppermute | solution.py:31
  230.0 1.5 collective-permute-done.1
  231.5 1.9 collective-permute-done.2
  235.5 2.4 collective-permute-start.6
  238.0 1.5 collective-permute-done.4
  241.3 1.3 collective-permute-done.7
  (105 shorter events, 19.3 us)
Async XLA Ops:
  0.0 143.4 %collective-permute-start.14 = (bf16[4,2,128,3072]{3,2,1,0:T(8,128)(2,1)}, bf16[4,2,128,3072]{3,2,1,0:T(8,128)(2,1)}, u32[]{:S(2)}, u32[]{:S(2)}) collective-permute-start(bf16[4,2,128,3072]{3,2,1,0:T(8,128)(2,1)} %param.8), channel_id=1, source_target_pairs={{0,2},{12,8},{16,22},{20,18},{10,14},{30,28},{1,3},{13,9},{17,23},... | collective-permute-start | bytes 18874376 | tf_op jit(solution)/shard_map/ppermute | solution.py:157
  8.5 17.3 %collective-permute-start.8 = (f32[4,3072]{1,0:T(4,128)S(1)}, f32[4,3072]{1,0:T(4,128)S(1)}, u32[]{:S(2)}, u32[]{:S(2)}) collective-permute-start(f32[4,3072]{1,0:T(4,128)S(1)} %dynamic_update_slice.3), channel_id=1, source_target_pairs={{0,8},{8,0},{16,24},{24,16},{1,9},{9,1},{17,25},{25,17},{2,10},{10... | collective-permute-start | bytes 147464 | tf_op jit(solution)/shard_map/ppermute | solution.py:31
  8.5 17.9 %collective-permute-start.9 = (f32[4,3072]{1,0:T(4,128)S(1)}, f32[4,3072]{1,0:T(4,128)S(1)}, u32[]{:S(2)}, u32[]{:S(2)}) collective-permute-start(f32[4,3072]{1,0:T(4,128)S(1)} %dynamic_update_slice.3), channel_id=1, source_target_pairs={{0,16},{8,24},{16,0},{24,8},{1,17},{9,25},{17,1},{25,9},{2,18},{10... | collective-permute-start | bytes 147464 | tf_op jit(solution)/shard_map/ppermute | solution.py:31
  12.2 14.3 %collective-permute-start.10 = (f32[4,3072]{1,0:T(4,128)S(1)}, f32[4,3072]{1,0:T(4,128)S(1)}, u32[]{:S(2)}, u32[]{:S(2)}) collective-permute-start(f32[4,3072]{1,0:T(4,128)S(1)} %dynamic_update_slice.3), channel_id=1, source_target_pairs={{0,24},{8,16},{16,8},{24,0},{1,25},{9,17},{17,9},{25,1},{2,26},{10... | collective-permute-start | bytes 147464 | tf_op jit(solution)/shard_map/ppermute | solution.py:31
  25.1 7.1 %collective-permute-start.15 = (f32[5,128,128]{2,1,0:T(8,128)S(1)}, f32[5,128,128]{2,1,0:T(8,128)S(1)}, u32[]{:S(2)}, u32[]{:S(2)}) collective-permute-start(f32[5,128,128]{2,1,0:T(8,128)S(1)} %fusion.47), channel_id=1, source_target_pairs={{8,2},{4,8},{24,22},{12,18},{26,14},{22,28},{9,3},{5,9},{25,23},{1... | collective-permute-start | bytes 983048 | tf_op jit(solution)/shard_map/ppermute | solution.py:169
  25.8 6.7 %collective-permute-start.16 = (f32[5,128,128]{2,1,0:T(8,128)S(1)}, f32[5,128,128]{2,1,0:T(8,128)S(1)}, u32[]{:S(2)}, u32[]{:S(2)}) collective-permute-start(f32[5,128,128]{2,1,0:T(8,128)S(1)} %fusion.47), channel_id=1, source_target_pairs={{16,8},{6,22},{17,9},{7,23}} | collective-permute-start | bytes 983048 | tf_op jit(solution)/shard_map/ppermute | solution.py:169
  26.6 115.5 %collective-permute-start.11 = (f32[4,3072]{1,0:T(4,128)S(1)}, f32[4,3072]{1,0:T(4,128)S(1)}, u32[]{:S(2)}, u32[]{:S(2)}) collective-permute-start(f32[4,3072]{1,0:T(4,128)S(1)} %fusion.54), channel_id=1, source_target_pairs={{0,2},{2,0},{4,6},{6,4},{1,3},{3,1},{5,7},{7,5},{8,10},{10,8},{12,... | collective-permute-start | bytes 147464 | tf_op jit(solution)/shard_map/ppermute | solution.py:31
  28.0 114.6 %collective-permute-start.12 = (f32[4,3072]{1,0:T(4,128)S(1)}, f32[4,3072]{1,0:T(4,128)S(1)}, u32[]{:S(2)}, u32[]{:S(2)}) collective-permute-start(f32[4,3072]{1,0:T(4,128)S(1)} %fusion.54), channel_id=1, source_target_pairs={{0,4},{2,6},{4,0},{6,2},{1,5},{3,7},{5,1},{7,3},{8,12},{10,14},{12... | collective-permute-start | bytes 147464 | tf_op jit(solution)/shard_map/ppermute | solution.py:31
  32.2 110.9 %collective-permute-start.13 = (f32[4,3072]{1,0:T(4,128)S(1)}, f32[4,3072]{1,0:T(4,128)S(1)}, u32[]{:S(2)}, u32[]{:S(2)}) collective-permute-start(f32[4,3072]{1,0:T(4,128)S(1)} %fusion.54), channel_id=1, source_target_pairs={{0,6},{2,4},{4,2},{6,0},{1,7},{3,5},{5,3},{7,1},{8,14},{10,12},{12... | collective-permute-start | bytes 147464 | tf_op jit(solution)/shard_map/ppermute | solution.py:31
  32.5 110.7 %collective-permute-start.17 = (f32[2,5,128,128]{3,2,1,0:T(8,128)S(1)}, f32[2,5,128,128]{3,2,1,0:T(8,128)S(1)}, u32[]{:S(2)}, u32[]{:S(2)}) collective-permute-start(f32[2,5,128,128]{3,2,1,0:T(8,128)S(1)} %pad_maximum_fusion.8), channel_id=1, source_target_pairs={{0,1},{1,0},{2,3},{3,2},{4,5},{5,4},{6,7},{7,6},{8,9},{9,8},{10,11... | collective-permute-start | bytes 1966088 | tf_op jit(solution)/shard_map/ppermute | solution.py:170
  150.3 6.7 %copy-start = (bf16[4,2,128,3072]{3,2,1,0:T(8,128)(2,1)S(1)}, bf16[4,2,128,3072]{3,2,1,0:T(8,128)(2,1)}, u32[]{:S(2)}) copy-start(bf16[4,2,128,3072]{3,2,1,0:T(8,128)(2,1)} %get-tuple-element.409) | copy-start | bytes 18874372 | tf_op jit(solution)/shard_map/while
  162.4 2.7 %collective-permute-start = (f32[2,4,2,128,128]{3,4,1,2,0:T(8,128)S(1)}, f32[2,4,2,128,128]{3,4,1,2,0:T(8,128)S(1)}, u32[]{:S(2)}, u32[]{:S(2)}) collective-permute-start(f32[2,4,2,128,128]{3,4,1,2,0:T(8,128)S(1)} %pad_maximum_fusion.14), channel_id=1, source_target_pairs={{0,1},{1,0},{2,3},{3,2},{4,5},{5,4},{6,7},{7,6},{8,9},{9,8},{10,11... | collective-permute-start | bytes 3145736 | tf_op jit(solution)/shard_map/while/body/eval_jaxpr/ppermute | solution.py:47
  165.5 5.5 %slice-start = ((s8[6291456]{0:T(1024)(128)(4,1)}), s8[2097152]{0:T(1024)(128)(4,1)S(1)}, s32[]{:S(2)}) async-start(s8[6291456]{0:T(1024)(128)(4,1)} %bitcast.162), calls=%async_computation | async-start | bytes 4194304 | tf_op jit(solution)/shard_map/while
  165.6 5.4 %slice-start.1 = ((s8[6291456]{0:T(1024)(128)(4,1)}), s8[4194304]{0:T(1024)(128)(4,1)S(1)}, s32[]{:S(2)}) async-start(s8[6291456]{0:T(1024)(128)(4,1)} %bitcast.162), calls=%async_computation.1 | async-start | bytes 8388608 | tf_op jit(solution)/shard_map/while
  173.6 12.4 %collective-permute-start.1 = (f32[4,3072]{1,0:T(4,128)S(1)}, f32[4,3072]{1,0:T(4,128)S(1)}, u32[]{:S(2)}, u32[]{:S(2)}) collective-permute-start(f32[4,3072]{1,0:T(4,128)S(1)} %select_add_fusion.2), channel_id=1, source_target_pairs={{0,24},{8,16},{16,8},{24,0},{1,25},{9,17},{17,9},{25,1},{2,26},{10... | collective-permute-start | bytes 147464 | tf_op jit(solution)/shard_map/while/body/eval_jaxpr/ppermute | solution.py:31
  179.1 9.0 %collective-permute-start.2 = (f32[4,3072]{1,0:T(4,128)S(1)}, f32[4,3072]{1,0:T(4,128)S(1)}, u32[]{:S(2)}, u32[]{:S(2)}) collective-permute-start(f32[4,3072]{1,0:T(4,128)S(1)} %select_add_fusion.2), channel_id=1, source_target_pairs={{0,16},{8,24},{16,0},{24,8},{1,17},{9,25},{17,1},{25,9},{2,18},{10... | collective-permute-start | bytes 147464 | tf_op jit(solution)/shard_map/while/body/eval_jaxpr/ppermute | solution.py:31
  186.0 4.1 %collective-permute-start.3 = (f32[4,3072]{1,0:T(4,128)S(1)}, f32[4,3072]{1,0:T(4,128)S(1)}, u32[]{:S(2)}, u32[]{:S(2)}) collective-permute-start(f32[4,3072]{1,0:T(4,128)S(1)} %select_add_fusion.2), channel_id=1, source_target_pairs={{0,8},{8,0},{16,24},{24,16},{1,9},{9,1},{17,25},{25,17},{2,10},{10... | collective-permute-start | bytes 147464 | tf_op jit(solution)/shard_map/while/body/eval_jaxpr/ppermute | solution.py:31
  190.2 6.2 %collective-permute-start.4 = (f32[4,3072]{1,0:T(4,128)S(1)}, f32[4,3072]{1,0:T(4,128)S(1)}, u32[]{:S(2)}, u32[]{:S(2)}) collective-permute-start(f32[4,3072]{1,0:T(4,128)S(1)} %fusion.88), channel_id=1, source_target_pairs={{0,6},{2,4},{4,2},{6,0},{1,7},{3,5},{5,3},{7,1},{8,14},{10,12},{12... | collective-permute-start | bytes 147464 | tf_op jit(solution)/shard_map/while/body/eval_jaxpr/ppermute | solution.py:31
  190.3 8.4 %collective-permute-start.5 = (f32[4,3072]{1,0:T(4,128)S(1)}, f32[4,3072]{1,0:T(4,128)S(1)}, u32[]{:S(2)}, u32[]{:S(2)}) collective-permute-start(f32[4,3072]{1,0:T(4,128)S(1)} %fusion.88), channel_id=1, source_target_pairs={{0,4},{2,6},{4,0},{6,2},{1,5},{3,7},{5,1},{7,3},{8,12},{10,14},{12... | collective-permute-start | bytes 147464 | tf_op jit(solution)/shard_map/while/body/eval_jaxpr/ppermute | solution.py:31
  195.5 4.1 %collective-permute-start.6 = (f32[4,3072]{1,0:T(4,128)S(1)}, f32[4,3072]{1,0:T(4,128)S(1)}, u32[]{:S(2)}, u32[]{:S(2)}) collective-permute-start(f32[4,3072]{1,0:T(4,128)S(1)} %fusion.88), channel_id=1, source_target_pairs={{0,2},{2,0},{4,6},{6,4},{1,3},{3,1},{5,7},{7,5},{8,10},{10,8},{12,... | collective-permute-start | bytes 147464 | tf_op jit(solution)/shard_map/while/body/eval_jaxpr/ppermute | solution.py:31
  200.4 1.4 collective-permute-start.7
  203.1 6.7 %copy-start = (bf16[4,2,128,3072]{3,2,1,0:T(8,128)(2,1)S(1)}, bf16[4,2,128,3072]{3,2,1,0:T(8,128)(2,1)}, u32[]{:S(2)}) copy-start(bf16[4,2,128,3072]{3,2,1,0:T(8,128)(2,1)} %get-tuple-element.409) | copy-start | bytes 18874372 | tf_op jit(solution)/shard_map/while
  215.2 2.7 %collective-permute-start = (f32[2,4,2,128,128]{3,4,1,2,0:T(8,128)S(1)}, f32[2,4,2,128,128]{3,4,1,2,0:T(8,128)S(1)}, u32[]{:S(2)}, u32[]{:S(2)}) collective-permute-start(f32[2,4,2,128,128]{3,4,1,2,0:T(8,128)S(1)} %pad_maximum_fusion.14), channel_id=1, source_target_pairs={{0,1},{1,0},{2,3},{3,2},{4,5},{5,4},{6,7},{7,6},{8,9},{9,8},{10,11... | collective-permute-start | bytes 3145736 | tf_op jit(solution)/shard_map/while/body/eval_jaxpr/ppermute | solution.py:47
  218.3 5.5 %slice-start = ((s8[6291456]{0:T(1024)(128)(4,1)}), s8[2097152]{0:T(1024)(128)(4,1)S(1)}, s32[]{:S(2)}) async-start(s8[6291456]{0:T(1024)(128)(4,1)} %bitcast.162), calls=%async_computation | async-start | bytes 4194304 | tf_op jit(solution)/shard_map/while
  218.4 5.4 %slice-start.1 = ((s8[6291456]{0:T(1024)(128)(4,1)}), s8[4194304]{0:T(1024)(128)(4,1)S(1)}, s32[]{:S(2)}) async-start(s8[6291456]{0:T(1024)(128)(4,1)} %bitcast.162), calls=%async_computation.1 | async-start | bytes 8388608 | tf_op jit(solution)/shard_map/while
  226.5 5.1 %collective-permute-start.1 = (f32[4,3072]{1,0:T(4,128)S(1)}, f32[4,3072]{1,0:T(4,128)S(1)}, u32[]{:S(2)}, u32[]{:S(2)}) collective-permute-start(f32[4,3072]{1,0:T(4,128)S(1)} %select_add_fusion.2), channel_id=1, source_target_pairs={{0,24},{8,16},{16,8},{24,0},{1,25},{9,17},{17,9},{25,1},{2,26},{10... | collective-permute-start | bytes 147464 | tf_op jit(solution)/shard_map/while/body/eval_jaxpr/ppermute | solution.py:31
  229.3 4.1 %collective-permute-start.2 = (f32[4,3072]{1,0:T(4,128)S(1)}, f32[4,3072]{1,0:T(4,128)S(1)}, u32[]{:S(2)}, u32[]{:S(2)}) collective-permute-start(f32[4,3072]{1,0:T(4,128)S(1)} %select_add_fusion.2), channel_id=1, source_target_pairs={{0,16},{8,24},{16,0},{24,8},{1,17},{9,25},{17,1},{25,9},{2,18},{10... | collective-permute-start | bytes 147464 | tf_op jit(solution)/shard_map/while/body/eval_jaxpr/ppermute | solution.py:31
  229.3 4.1 %collective-permute-start.3 = (f32[4,3072]{1,0:T(4,128)S(1)}, f32[4,3072]{1,0:T(4,128)S(1)}, u32[]{:S(2)}, u32[]{:S(2)}) collective-permute-start(f32[4,3072]{1,0:T(4,128)S(1)} %select_add_fusion.2), channel_id=1, source_target_pairs={{0,8},{8,0},{16,24},{24,16},{1,9},{9,1},{17,25},{25,17},{2,10},{10... | collective-permute-start | bytes 147464 | tf_op jit(solution)/shard_map/while/body/eval_jaxpr/ppermute | solution.py:31
  233.5 6.0 %collective-permute-start.4 = (f32[4,3072]{1,0:T(4,128)S(1)}, f32[4,3072]{1,0:T(4,128)S(1)}, u32[]{:S(2)}, u32[]{:S(2)}) collective-permute-start(f32[4,3072]{1,0:T(4,128)S(1)} %fusion.88), channel_id=1, source_target_pairs={{0,6},{2,4},{4,2},{6,0},{1,7},{3,5},{5,3},{7,1},{8,14},{10,12},{12... | collective-permute-start | bytes 147464 | tf_op jit(solution)/shard_map/while/body/eval_jaxpr/ppermute | solution.py:31
  234.5 6.0 %collective-permute-start.5 = (f32[4,3072]{1,0:T(4,128)S(1)}, f32[4,3072]{1,0:T(4,128)S(1)}, u32[]{:S(2)}, u32[]{:S(2)}) collective-permute-start(f32[4,3072]{1,0:T(4,128)S(1)} %fusion.88), channel_id=1, source_target_pairs={{0,4},{2,6},{4,0},{6,2},{1,5},{3,7},{5,1},{7,3},{8,12},{10,14},{12... | collective-permute-start | bytes 147464 | tf_op jit(solution)/shard_map/while/body/eval_jaxpr/ppermute | solution.py:31
  235.5 5.0 %collective-permute-start.6 = (f32[4,3072]{1,0:T(4,128)S(1)}, f32[4,3072]{1,0:T(4,128)S(1)}, u32[]{:S(2)}, u32[]{:S(2)}) collective-permute-start(f32[4,3072]{1,0:T(4,128)S(1)} %fusion.88), channel_id=1, source_target_pairs={{0,2},{2,0},{4,6},{6,4},{1,3},{3,1},{5,7},{7,5},{8,10},{10,8},{12,... | collective-permute-start | bytes 147464 | tf_op jit(solution)/shard_map/while/body/eval_jaxpr/ppermute | solution.py:31
  241.3 1.4 collective-permute-start.7

commit v8 on v7

--- a/solution.py
+++ b/solution.py
@@ -110,7 +110,7 @@
     return own[None]
 
 
-PAIR_PLAN = ((0, 0, 1), (1, 2, 0), (2, 0, 3), (2, 2, 1), (1, 1, 3), (3, 3, 2))
+PAIR_PLAN = ((2, 0, 1), (1, 0, 2), (1, 3, 0), (0, 1, 2), (2, 1, 3), (0, 2, 3))
 
 
 def pair_tables(blocks):
@@ -124,6 +124,7 @@
         needs.append((line * blocks + receiver, 1, sender * blocks + receiver))
     for plane in range(blocks):
         role[plane * blocks + plane] = 2
+        panel_moves.append((plane * blocks + plane, plane * blocks + plane))
     rounds = []
     moved = [[0, 0] for _ in range(blocks * blocks)]
     for dest, which, owner in needs:
@@ -175,7 +176,7 @@
     )[:, :planes]
     arrived = jnp.concatenate([own_block[None], joined], axis=0)
     received, arrived = lax.optimization_barrier((received, arrived))
-    other = jnp.where(is_diag, green_panel, received)
+    other = received
     mine_rows = green_panel.reshape(freq_count, 2 * span_j, local_pts)
     other_rows = other.reshape(freq_count, 2 * span_j, local_pts)
     moved_table = jnp.array(moved, jnp.int32)[slot]

time: 245 us -> 257 us (1.049); the launches traced: 245 us -> 253 us
  starting transfers between devices: 46 us -> 163 us
  waiting for transfers between devices: 132 us -> 24.9 us
  other arithmetic: 12.7 us -> 6.57 us
  matrix products: 39.4 us -> 44.8 us
    ppermute x18, waiting for transfers between devices: 125 us -> 17.1 us  [butterfly_sum(): got.append(lax.ppermute(value, axis, [(i, i ^ mask) for i in range(size)]))]
    ppermute x18, starting transfers between devices: 36.6 us -> 113 us  [butterfly_sum(): got.append(lax.ppermute(value, axis, [(i, i ^ mask) for i in range(size)]))]
    ppermute x1, starting transfers between devices: 7.61 us -> 48.5 us  [pair_body(): received = lax.ppermute(green_panel, axes, panel_moves)]
    select_n x1 -> x0, other arithmetic: 6.06 us -> none  [pair_body(): other = jnp.where(is_diag, green_panel, received)]
    dot_general x4, matrix products: 15.9 us -> 21.1 us  [point_terms(): jnp.einsum('fab,fbn->fan', adjoint_block(adjoint), right_rows, preferred_...]
  transfers between devices with their start and end apart: 26 -> 26, of which waited for: 16 -> 15; matrix products, arithmetic and copies ran while one was open for 3% -> 3% of each run, Pallas kernels for 0% -> 0%
where the time goes in v8:
time: 257 us; the launch traced here: 253 us
  starting transfers between devices  163 us (63%)
  matrix products  44.8 us (17%)
  waiting for transfers between devices  24.9 us (10%)
  other arithmetic  6.57 us (3%)
  between operations  5.57 us (2%)
  local copies, waits for them, and re-layouts  5.15 us (2%)
  loops' own time  3.12 us (1%)
    ppermute x18, starting transfers between devices, butterfly_sum(): got.append(lax.ppermute(value, axis, [(i, i ^ mask) for i in range(size)]))  113 us
    ppermute x1, starting transfers between devices, pair_body(): received = lax.ppermute(green_panel, axes, panel_moves)  48.5 us
    dot_general x4, matrix products, correlate(): jnp.einsum('fan,fbn->fab', left_rows, weighted, preferred_element_type=jn...  23.7 us
    dot_general x4, matrix products, point_terms(): jnp.einsum('fab,fbn->fan', adjoint_block(adjoint), right_rows, preferred_...  21.1 us
    ppermute x18, waiting for transfers between devices, butterfly_sum(): got.append(lax.ppermute(value, axis, [(i, i ^ mask) for i in range(size)]))  17.1 us
    ppermute x4, waiting for transfers between devices, swap_add(): return value + lax.ppermute(value, axis, [(0, 1), (1, 0)])  7.72 us
  transfers between devices with their start and end apart: 26, of which 15 were waited for; matrix products, arithmetic and copies ran while one was open for 3% of the time, Pallas kernels for 0%

profile of v8, /device:TPU:0, one launch (start us, length us, event | category | flops | bytes accessed | tf_op | source)
XLA Modules:
  0.0 253.1 jit_solution(11963279721130169428)
XLA Ops:
  0.0 48.5 %collective-permute-start.14 = (bf16[4,2,128,3072]{3,2,1,0:T(8,128)(2,1)}, bf16[4,2,128,3072]{3,2,1,0:T(8,128)(2,1)}, u32[]{:S(2)}, u32[]{:S(2)}) collective-permute-start(bf16[4,2,128,3072]{3,2,1,0:T(8,128)(2,1)} %param.8), channel_id=1, source_target_pairs={{16,18},{8,12},{14,8},{2,4},{18,22},{4,6},{0,0},{10,10},{20,20},{3... | collective-permute-start | bytes 18874376 | tf_op jit(solution)/shard_map/ppermute | solution.py:158
  49.5 3.4 %collective-permute-start.10 = (f32[4,3072]{1,0:T(4,128)S(1)}, f32[4,3072]{1,0:T(4,128)S(1)}, u32[]{:S(2)}, u32[]{:S(2)}) collective-permute-start(f32[4,3072]{1,0:T(4,128)S(1)} %dynamic_update_slice.3), channel_id=1, source_target_pairs={{0,24},{8,16},{16,8},{24,0},{1,25},{9,17},{17,9},{25,1},{2,26},{10... | collective-permute-start | bytes 147464 | tf_op jit(solution)/shard_map/ppermute | solution.py:31
  65.6 8.1 %collective-permute-start.11 = (f32[4,3072]{1,0:T(4,128)S(1)}, f32[4,3072]{1,0:T(4,128)S(1)}, u32[]{:S(2)}, u32[]{:S(2)}) collective-permute-start(f32[4,3072]{1,0:T(4,128)S(1)} %fusion.54), channel_id=1, source_target_pairs={{0,2},{2,0},{4,6},{6,4},{1,3},{3,1},{5,7},{7,5},{8,10},{10,8},{12,... | collective-permute-start | bytes 147464 | tf_op jit(solution)/shard_map/ppermute | solution.py:31
  73.8 17.1 %collective-permute-start.13 = (f32[4,3072]{1,0:T(4,128)S(1)}, f32[4,3072]{1,0:T(4,128)S(1)}, u32[]{:S(2)}, u32[]{:S(2)}) collective-permute-start(f32[4,3072]{1,0:T(4,128)S(1)} %fusion.54), channel_id=1, source_target_pairs={{0,6},{2,4},{4,2},{6,0},{1,7},{3,5},{5,3},{7,1},{8,14},{10,12},{12... | collective-permute-start | bytes 147464 | tf_op jit(solution)/shard_map/ppermute | solution.py:31
  91.1 1.9 collective-permute-done.13
  94.2 158.3 %while.13 = (s32[]{:T(128)}, f32[4,3072]{1,0:T(4,128)S(1)}, pred[]{:T(512)}, bf16[4,256,3072]{2,1,0:T(8,128)(2,1)}, f32[1,128,128]{1,2,0:T(8,128)S(1)}, /*index=...) while((s32[]{:T(128)}, f32[4,3072]{1,0:T(4,128)S(1)}, ...), condition=%wide.region_4.5_spmd, body=%wide.region_0.4_spmd.sunk | while | flops 6487400448 | bytes 100730112 | solution.py:215
  94.2 6.6 %fusion.80 = f32[4,256,256]{1,2,0:T(8,128)S(1)} fusion(bf16[4,256,3072]{2,1,0:T(8,128)(2,1)} %bitcast.179, bf16[4,256,3072]{2,1,0:T(8,128)(2,1)} %bitcast.142, f32[4,3072]{1,0:T(4,128)S(1)} %exp.11), kind=kOutput, calls=%fused_computation.11.clone.1 | convolution fusion | flops 1620049920 | bytes 13680640 | tf_op jit(solution)/shard_map/while/body/eval_jaxpr/fan,fbn->fab/dot_general | solution.py:53
  100.9 5.2 %fusion.82 = f32[4,256,256]{1,2,0:T(8,128)S(1)} fusion(bf16[4,256,3072]{2,1,0:T(8,128)(2,1)} %get-tuple-element.410, bf16[4,256,3072]{2,1,0:T(8,128)(2,1)S(1)} %bitcast.181, f32[4,3072]{1,0:T(4,128)S(1)} %exp.11), kind=kOutput, calls=%fused_computation.10.clone.1 | convolution fusion | flops 1620049920 | bytes 13680640 | tf_op jit(solution)/shard_map/while/body/eval_jaxpr/fan,fbn->fab/dot_general | solution.py:53
  106.6 2.5 collective-permute-done
  109.5 5.2 %multiply_reduce_fusion.7 = f32[4,3072]{1,0:T(4,128)S(1)} fusion(bf16[4,256,3072]{2,1,0:T(8,128)(2,1)S(1)} %bitcast.182, bf16[4,256,3072]{2,1,0:T(8,128)(2,1)} %get-tuple-element.410, bf16[4,128,128]{1,2,0:T(8,128)(2,1)S(1)} %get-tuple-element.357, bf16[4,128,128]{1,2,0:T(8,128)(2,1)S(1)} %get-tuple-element.358, bf16[4,128,128]{1,2,0:T(8,128)(2,1)S(1)} %fusion.87), kind=kOutput, calls=%fused_computation.5.clone.1 | convolution fusion | flops 1622134784 | bytes 13025280 | tf_op jit(solution)/shard_map/while/body/eval_jaxpr/fab,fbn->fan/dot_general | solution.py:68
  114.8 5.3 %multiply_reduce_fusion.6 = f32[4,3072]{1,0:T(4,128)S(1)} fusion(bf16[4,256,3072]{2,1,0:T(8,128)(2,1)} %get-tuple-element.410, bf16[4,256,3072]{2,1,0:T(8,128)(2,1)S(1)} %bitcast.183, bf16[4,128,128]{1,2,0:T(8,128)(2,1)S(1)} %get-tuple-element.354, bf16[4,128,128]{1,2,0:T(8,128)(2,1)S(1)} %get-tuple-element.355, bf16[4,128,128]{1,2,0:T(8,128)(2,1)S(1)} %fusion.86), kind=kOutput, calls=%fused_computation.4.clone.1 | convolution fusion | flops 1622134784 | bytes 13025280 | tf_op jit(solution)/shard_map/while/body/eval_jaxpr/fab,fbn->fan/dot_general | solution.py:68
  120.2 64.9 %collective-permute-start.2 = (f32[4,3072]{1,0:T(4,128)S(1)}, f32[4,3072]{1,0:T(4,128)S(1)}, u32[]{:S(2)}, u32[]{:S(2)}) collective-permute-start(f32[4,3072]{1,0:T(4,128)S(1)} %select_add_fusion.2), channel_id=1, source_target_pairs={{0,16},{8,24},{16,0},{24,8},{1,17},{9,25},{17,1},{25,9},{2,18},{10... | collective-permute-start | bytes 147464 | tf_op jit(solution)/shard_map/while/body/eval_jaxpr/ppermute | solution.py:31
  185.1 2.1 collective-permute-done.2
  187.2 2.0 collective-permute-done.3
  189.3 6.9 %collective-permute-start.4 = (f32[4,3072]{1,0:T(4,128)S(1)}, f32[4,3072]{1,0:T(4,128)S(1)}, u32[]{:S(2)}, u32[]{:S(2)}) collective-permute-start(f32[4,3072]{1,0:T(4,128)S(1)} %fusion.88), channel_id=1, source_target_pairs={{0,6},{2,4},{4,2},{6,0},{1,7},{3,5},{5,3},{7,1},{8,14},{10,12},{12... | collective-permute-start | bytes 147464 | tf_op jit(solution)/shard_map/while/body/eval_jaxpr/ppermute | solution.py:31
  196.2 3.5 %collective-permute-start.5 = (f32[4,3072]{1,0:T(4,128)S(1)}, f32[4,3072]{1,0:T(4,128)S(1)}, u32[]{:S(2)}, u32[]{:S(2)}) collective-permute-start(f32[4,3072]{1,0:T(4,128)S(1)} %fusion.88), channel_id=1, source_target_pairs={{0,4},{2,6},{4,0},{6,2},{1,5},{3,7},{5,1},{7,3},{8,12},{10,14},{12... | collective-permute-start | bytes 147464 | tf_op jit(solution)/shard_map/while/body/eval_jaxpr/ppermute | solution.py:31
  200.2 2.6 %collective-permute-done.5 = f32[4,3072]{1,0:T(4,128)S(1)} collective-permute-done((f32[4,3072]{1,0:T(4,128)S(1)}, f32[4,3072]{1,0:T(4,128)S(1)}, u32[]{:S(2)}, u32[]{:S(2)}) %collective-permute-start.5) | collective-permute-done | bytes 49184 | tf_op jit(solution)/shard_map/while/body/eval_jaxpr/ppermute | solution.py:31
  204.5 1.3 collective-permute-done.7
  207.3 6.6 %fusion.80 = f32[4,256,256]{1,2,0:T(8,128)S(1)} fusion(bf16[4,256,3072]{2,1,0:T(8,128)(2,1)} %bitcast.179, bf16[4,256,3072]{2,1,0:T(8,128)(2,1)} %bitcast.142, f32[4,3072]{1,0:T(4,128)S(1)} %exp.11), kind=kOutput, calls=%fused_computation.11.clone.1 | convolution fusion | flops 1620049920 | bytes 13680640 | tf_op jit(solution)/shard_map/while/body/eval_jaxpr/fan,fbn->fab/dot_general | solution.py:53
  214.0 5.2 %fusion.82 = f32[4,256,256]{1,2,0:T(8,128)S(1)} fusion(bf16[4,256,3072]{2,1,0:T(8,128)(2,1)} %get-tuple-element.410, bf16[4,256,3072]{2,1,0:T(8,128)(2,1)S(1)} %bitcast.181, f32[4,3072]{1,0:T(4,128)S(1)} %exp.11), kind=kOutput, calls=%fused_computation.10.clone.1 | convolution fusion | flops 1620049920 | bytes 13680640 | tf_op jit(solution)/shard_map/while/body/eval_jaxpr/fan,fbn->fab/dot_general | solution.py:53
  219.7 2.5 collective-permute-done
  222.7 5.2 %multiply_reduce_fusion.7 = f32[4,3072]{1,0:T(4,128)S(1)} fusion(bf16[4,256,3072]{2,1,0:T(8,128)(2,1)S(1)} %bitcast.182, bf16[4,256,3072]{2,1,0:T(8,128)(2,1)} %get-tuple-element.410, bf16[4,128,128]{1,2,0:T(8,128)(2,1)S(1)} %get-tuple-element.357, bf16[4,128,128]{1,2,0:T(8,128)(2,1)S(1)} %get-tuple-element.358, bf16[4,128,128]{1,2,0:T(8,128)(2,1)S(1)} %fusion.87), kind=kOutput, calls=%fused_computation.5.clone.1 | convolution fusion | flops 1622134784 | bytes 13025280 | tf_op jit(solution)/shard_map/while/body/eval_jaxpr/fab,fbn->fan/dot_general | solution.py:68
  227.9 5.3 %multiply_reduce_fusion.6 = f32[4,3072]{1,0:T(4,128)S(1)} fusion(bf16[4,256,3072]{2,1,0:T(8,128)(2,1)} %get-tuple-element.410, bf16[4,256,3072]{2,1,0:T(8,128)(2,1)S(1)} %bitcast.183, bf16[4,128,128]{1,2,0:T(8,128)(2,1)S(1)} %get-tuple-element.354, bf16[4,128,128]{1,2,0:T(8,128)(2,1)S(1)} %get-tuple-element.355, bf16[4,128,128]{1,2,0:T(8,128)(2,1)S(1)} %fusion.86), kind=kOutput, calls=%fused_computation.4.clone.1 | convolution fusion | flops 1622134784 | bytes 13025280 | tf_op jit(solution)/shard_map/while/body/eval_jaxpr/fab,fbn->fan/dot_general | solution.py:68
  233.3 1.5 collective-permute-start.1
  234.8 2.0 collective-permute-start.2
  236.8 1.6 collective-permute-done.1
  239.1 1.8 collective-permute-done.3
  241.0 2.9 %collective-permute-start.4 = (f32[4,3072]{1,0:T(4,128)S(1)}, f32[4,3072]{1,0:T(4,128)S(1)}, u32[]{:S(2)}, u32[]{:S(2)}) collective-permute-start(f32[4,3072]{1,0:T(4,128)S(1)} %fusion.88), channel_id=1, source_target_pairs={{0,6},{2,4},{4,2},{6,0},{1,7},{3,5},{5,3},{7,1},{8,14},{10,12},{12... | collective-permute-start | bytes 147464 | tf_op jit(solution)/shard_map/while/body/eval_jaxpr/ppermute | solution.py:31
  243.9 1.5 collective-permute-start.6
  245.5 1.7 collective-permute-done.4
  247.1 1.8 collective-permute-done.5
  249.7 1.3 collective-permute-done.7
  (94 shorter events, 16.2 us)
Async XLA Ops:
  0.0 93.4 %collective-permute-start.14 = (bf16[4,2,128,3072]{3,2,1,0:T(8,128)(2,1)}, bf16[4,2,128,3072]{3,2,1,0:T(8,128)(2,1)}, u32[]{:S(2)}, u32[]{:S(2)}) collective-permute-start(bf16[4,2,128,3072]{3,2,1,0:T(8,128)(2,1)} %param.8), channel_id=1, source_target_pairs={{16,18},{8,12},{14,8},{2,4},{18,22},{4,6},{0,0},{10,10},{20,20},{3... | collective-permute-start | bytes 18874376 | tf_op jit(solution)/shard_map/ppermute | solution.py:158
  49.4 15.4 %collective-permute-start.8 = (f32[4,3072]{1,0:T(4,128)S(1)}, f32[4,3072]{1,0:T(4,128)S(1)}, u32[]{:S(2)}, u32[]{:S(2)}) collective-permute-start(f32[4,3072]{1,0:T(4,128)S(1)} %dynamic_update_slice.3), channel_id=1, source_target_pairs={{0,8},{8,0},{16,24},{24,16},{1,9},{9,1},{17,25},{25,17},{2,10},{10... | collective-permute-start | bytes 147464 | tf_op jit(solution)/shard_map/ppermute | solution.py:31
  49.5 16.0 %collective-permute-start.9 = (f32[4,3072]{1,0:T(4,128)S(1)}, f32[4,3072]{1,0:T(4,128)S(1)}, u32[]{:S(2)}, u32[]{:S(2)}) collective-permute-start(f32[4,3072]{1,0:T(4,128)S(1)} %dynamic_update_slice.3), channel_id=1, source_target_pairs={{0,16},{8,24},{16,0},{24,8},{1,17},{9,25},{17,1},{25,9},{2,18},{10... | collective-permute-start | bytes 147464 | tf_op jit(solution)/shard_map/ppermute | solution.py:31
  49.5 15.9 %collective-permute-start.10 = (f32[4,3072]{1,0:T(4,128)S(1)}, f32[4,3072]{1,0:T(4,128)S(1)}, u32[]{:S(2)}, u32[]{:S(2)}) collective-permute-start(f32[4,3072]{1,0:T(4,128)S(1)} %dynamic_update_slice.3), channel_id=1, source_target_pairs={{0,24},{8,16},{16,8},{24,0},{1,25},{9,17},{17,9},{25,1},{2,26},{10... | collective-permute-start | bytes 147464 | tf_op jit(solution)/shard_map/ppermute | solution.py:31
  64.1 9.7 %collective-permute-start.15 = (f32[5,128,128]{2,1,0:T(8,128)S(1)}, f32[5,128,128]{2,1,0:T(8,128)S(1)}, u32[]{:S(2)}, u32[]{:S(2)}) collective-permute-start(f32[5,128,128]{2,1,0:T(8,128)S(1)} %fusion.47), channel_id=1, source_target_pairs={{8,18},{16,12},{6,8},{18,4},{26,22},{28,6},{9,19},{17,13},{7,9},{1... | collective-permute-start | bytes 983048 | tf_op jit(solution)/shard_map/ppermute | solution.py:170
  64.8 26.2 %collective-permute-start.16 = (f32[5,128,128]{2,1,0:T(8,128)S(1)}, f32[5,128,128]{2,1,0:T(8,128)S(1)}, u32[]{:S(2)}, u32[]{:S(2)}) collective-permute-start(f32[5,128,128]{2,1,0:T(8,128)S(1)} %fusion.47), channel_id=1, source_target_pairs={{2,18},{4,12},{24,8},{12,4},{14,22},{22,6},{3,19},{5,13},{25,9},{1... | collective-permute-start | bytes 983048 | tf_op jit(solution)/shard_map/ppermute | solution.py:170
  65.6 25.5 %collective-permute-start.11 = (f32[4,3072]{1,0:T(4,128)S(1)}, f32[4,3072]{1,0:T(4,128)S(1)}, u32[]{:S(2)}, u32[]{:S(2)}) collective-permute-start(f32[4,3072]{1,0:T(4,128)S(1)} %fusion.54), channel_id=1, source_target_pairs={{0,2},{2,0},{4,6},{6,4},{1,3},{3,1},{5,7},{7,5},{8,10},{10,8},{12,... | collective-permute-start | bytes 147464 | tf_op jit(solution)/shard_map/ppermute | solution.py:31
  73.7 17.4 %collective-permute-start.12 = (f32[4,3072]{1,0:T(4,128)S(1)}, f32[4,3072]{1,0:T(4,128)S(1)}, u32[]{:S(2)}, u32[]{:S(2)}) collective-permute-start(f32[4,3072]{1,0:T(4,128)S(1)} %fusion.54), channel_id=1, source_target_pairs={{0,4},{2,6},{4,0},{6,2},{1,5},{3,7},{5,1},{7,3},{8,12},{10,14},{12... | collective-permute-start | bytes 147464 | tf_op jit(solution)/shard_map/ppermute | solution.py:31
  73.8 19.2 %collective-permute-start.13 = (f32[4,3072]{1,0:T(4,128)S(1)}, f32[4,3072]{1,0:T(4,128)S(1)}, u32[]{:S(2)}, u32[]{:S(2)}) collective-permute-start(f32[4,3072]{1,0:T(4,128)S(1)} %fusion.54), channel_id=1, source_target_pairs={{0,6},{2,4},{4,2},{6,0},{1,7},{3,5},{5,3},{7,1},{8,14},{10,12},{12... | collective-permute-start | bytes 147464 | tf_op jit(solution)/shard_map/ppermute | solution.py:31
  91.0 2.2 collective-permute-start.17
  94.2 6.7 %copy-start = (bf16[4,2,128,3072]{3,2,1,0:T(8,128)(2,1)S(1)}, bf16[4,2,128,3072]{3,2,1,0:T(8,128)(2,1)}, u32[]{:S(2)}) copy-start(bf16[4,2,128,3072]{3,2,1,0:T(8,128)(2,1)} %get-tuple-element.409) | copy-start | bytes 18874372 | tf_op jit(solution)/shard_map/while
  106.4 2.7 %collective-permute-start = (f32[2,4,2,128,128]{3,4,1,2,0:T(8,128)S(1)}, f32[2,4,2,128,128]{3,4,1,2,0:T(8,128)S(1)}, u32[]{:S(2)}, u32[]{:S(2)}) collective-permute-start(f32[2,4,2,128,128]{3,4,1,2,0:T(8,128)S(1)} %pad_maximum_fusion.14), channel_id=1, source_target_pairs={{0,1},{1,0},{2,3},{3,2},{4,5},{5,4},{6,7},{7,6},{8,9},{9,8},{10,11... | collective-permute-start | bytes 3145736 | tf_op jit(solution)/shard_map/while/body/eval_jaxpr/ppermute | solution.py:47
  120.1 65.0 %collective-permute-start.1 = (f32[4,3072]{1,0:T(4,128)S(1)}, f32[4,3072]{1,0:T(4,128)S(1)}, u32[]{:S(2)}, u32[]{:S(2)}) collective-permute-start(f32[4,3072]{1,0:T(4,128)S(1)} %select_add_fusion.2), channel_id=1, source_target_pairs={{0,24},{8,16},{16,8},{24,0},{1,25},{9,17},{17,9},{25,1},{2,26},{10... | collective-permute-start | bytes 147464 | tf_op jit(solution)/shard_map/while/body/eval_jaxpr/ppermute | solution.py:31
  120.2 67.0 %collective-permute-start.2 = (f32[4,3072]{1,0:T(4,128)S(1)}, f32[4,3072]{1,0:T(4,128)S(1)}, u32[]{:S(2)}, u32[]{:S(2)}) collective-permute-start(f32[4,3072]{1,0:T(4,128)S(1)} %select_add_fusion.2), channel_id=1, source_target_pairs={{0,16},{8,24},{16,0},{24,8},{1,17},{9,25},{17,1},{25,9},{2,18},{10... | collective-permute-start | bytes 147464 | tf_op jit(solution)/shard_map/while/body/eval_jaxpr/ppermute | solution.py:31
  185.1 4.1 %collective-permute-start.3 = (f32[4,3072]{1,0:T(4,128)S(1)}, f32[4,3072]{1,0:T(4,128)S(1)}, u32[]{:S(2)}, u32[]{:S(2)}) collective-permute-start(f32[4,3072]{1,0:T(4,128)S(1)} %select_add_fusion.2), channel_id=1, source_target_pairs={{0,8},{8,0},{16,24},{24,16},{1,9},{9,1},{17,25},{25,17},{2,10},{10... | collective-permute-start | bytes 147464 | tf_op jit(solution)/shard_map/while/body/eval_jaxpr/ppermute | solution.py:31
  189.3 10.9 %collective-permute-start.4 = (f32[4,3072]{1,0:T(4,128)S(1)}, f32[4,3072]{1,0:T(4,128)S(1)}, u32[]{:S(2)}, u32[]{:S(2)}) collective-permute-start(f32[4,3072]{1,0:T(4,128)S(1)} %fusion.88), channel_id=1, source_target_pairs={{0,6},{2,4},{4,2},{6,0},{1,7},{3,5},{5,3},{7,1},{8,14},{10,12},{12... | collective-permute-start | bytes 147464 | tf_op jit(solution)/shard_map/while/body/eval_jaxpr/ppermute | solution.py:31
  196.2 6.5 %collective-permute-start.5 = (f32[4,3072]{1,0:T(4,128)S(1)}, f32[4,3072]{1,0:T(4,128)S(1)}, u32[]{:S(2)}, u32[]{:S(2)}) collective-permute-start(f32[4,3072]{1,0:T(4,128)S(1)} %fusion.88), channel_id=1, source_target_pairs={{0,4},{2,6},{4,0},{6,2},{1,5},{3,7},{5,1},{7,3},{8,12},{10,14},{12... | collective-permute-start | bytes 147464 | tf_op jit(solution)/shard_map/while/body/eval_jaxpr/ppermute | solution.py:31
  199.7 4.1 %collective-permute-start.6 = (f32[4,3072]{1,0:T(4,128)S(1)}, f32[4,3072]{1,0:T(4,128)S(1)}, u32[]{:S(2)}, u32[]{:S(2)}) collective-permute-start(f32[4,3072]{1,0:T(4,128)S(1)} %fusion.88), channel_id=1, source_target_pairs={{0,2},{2,0},{4,6},{6,4},{1,3},{3,1},{5,7},{7,5},{8,10},{10,8},{12,... | collective-permute-start | bytes 147464 | tf_op jit(solution)/shard_map/while/body/eval_jaxpr/ppermute | solution.py:31
  204.5 1.4 collective-permute-start.7
  207.3 6.7 %copy-start = (bf16[4,2,128,3072]{3,2,1,0:T(8,128)(2,1)S(1)}, bf16[4,2,128,3072]{3,2,1,0:T(8,128)(2,1)}, u32[]{:S(2)}) copy-start(bf16[4,2,128,3072]{3,2,1,0:T(8,128)(2,1)} %get-tuple-element.409) | copy-start | bytes 18874372 | tf_op jit(solution)/shard_map/while
  219.5 2.7 %collective-permute-start = (f32[2,4,2,128,128]{3,4,1,2,0:T(8,128)S(1)}, f32[2,4,2,128,128]{3,4,1,2,0:T(8,128)S(1)}, u32[]{:S(2)}, u32[]{:S(2)}) collective-permute-start(f32[2,4,2,128,128]{3,4,1,2,0:T(8,128)S(1)} %pad_maximum_fusion.14), channel_id=1, source_target_pairs={{0,1},{1,0},{2,3},{3,2},{4,5},{5,4},{6,7},{7,6},{8,9},{9,8},{10,11... | collective-permute-start | bytes 3145736 | tf_op jit(solution)/shard_map/while/body/eval_jaxpr/ppermute | solution.py:47
  233.3 5.2 %collective-permute-start.1 = (f32[4,3072]{1,0:T(4,128)S(1)}, f32[4,3072]{1,0:T(4,128)S(1)}, u32[]{:S(2)}, u32[]{:S(2)}) collective-permute-start(f32[4,3072]{1,0:T(4,128)S(1)} %select_add_fusion.2), channel_id=1, source_target_pairs={{0,24},{8,16},{16,8},{24,0},{1,25},{9,17},{17,9},{25,1},{2,26},{10... | collective-permute-start | bytes 147464 | tf_op jit(solution)/shard_map/while/body/eval_jaxpr/ppermute | solution.py:31
  234.8 4.3 %collective-permute-start.2 = (f32[4,3072]{1,0:T(4,128)S(1)}, f32[4,3072]{1,0:T(4,128)S(1)}, u32[]{:S(2)}, u32[]{:S(2)}) collective-permute-start(f32[4,3072]{1,0:T(4,128)S(1)} %select_add_fusion.2), channel_id=1, source_target_pairs={{0,16},{8,24},{16,0},{24,8},{1,17},{9,25},{17,1},{25,9},{2,18},{10... | collective-permute-start | bytes 147464 | tf_op jit(solution)/shard_map/while/body/eval_jaxpr/ppermute | solution.py:31
  236.8 4.1 %collective-permute-start.3 = (f32[4,3072]{1,0:T(4,128)S(1)}, f32[4,3072]{1,0:T(4,128)S(1)}, u32[]{:S(2)}, u32[]{:S(2)}) collective-permute-start(f32[4,3072]{1,0:T(4,128)S(1)} %select_add_fusion.2), channel_id=1, source_target_pairs={{0,8},{8,0},{16,24},{24,16},{1,9},{9,1},{17,25},{25,17},{2,10},{10... | collective-permute-start | bytes 147464 | tf_op jit(solution)/shard_map/while/body/eval_jaxpr/ppermute | solution.py:31
  241.0 6.1 %collective-permute-start.4 = (f32[4,3072]{1,0:T(4,128)S(1)}, f32[4,3072]{1,0:T(4,128)S(1)}, u32[]{:S(2)}, u32[]{:S(2)}) collective-permute-start(f32[4,3072]{1,0:T(4,128)S(1)} %fusion.88), channel_id=1, source_target_pairs={{0,6},{2,4},{4,2},{6,0},{1,7},{3,5},{5,3},{7,1},{8,14},{10,12},{12... | collective-permute-start | bytes 147464 | tf_op jit(solution)/shard_map/while/body/eval_jaxpr/ppermute | solution.py:31
  243.9 5.0 %collective-permute-start.5 = (f32[4,3072]{1,0:T(4,128)S(1)}, f32[4,3072]{1,0:T(4,128)S(1)}, u32[]{:S(2)}, u32[]{:S(2)}) collective-permute-start(f32[4,3072]{1,0:T(4,128)S(1)} %fusion.88), channel_id=1, source_target_pairs={{0,4},{2,6},{4,0},{6,2},{1,5},{3,7},{5,1},{7,3},{8,12},{10,14},{12... | collective-permute-start | bytes 147464 | tf_op jit(solution)/shard_map/while/body/eval_jaxpr/ppermute | solution.py:31
  243.9 5.0 %collective-permute-start.6 = (f32[4,3072]{1,0:T(4,128)S(1)}, f32[4,3072]{1,0:T(4,128)S(1)}, u32[]{:S(2)}, u32[]{:S(2)}) collective-permute-start(f32[4,3072]{1,0:T(4,128)S(1)} %fusion.88), channel_id=1, source_target_pairs={{0,2},{2,0},{4,6},{6,4},{1,3},{3,1},{5,7},{7,5},{8,10},{10,8},{12,... | collective-permute-start | bytes 147464 | tf_op jit(solution)/shard_map/while/body/eval_jaxpr/ppermute | solution.py:31
  249.7 1.4 collective-permute-start.7

commit v9 on v7

--- a/solution.py
+++ b/solution.py
@@ -1,6 +1,8 @@
 import jax
 import jax.numpy as jnp
 from jax import lax
+from jax.experimental import pallas as pl
+from jax.experimental.pallas import tpu as pltpu
 from jax.sharding import PartitionSpec as P
 
 ITERS = 2
@@ -51,6 +53,40 @@
     half_a = left_rows.shape[1] // 2
     half_b = weighted.shape[1] // 2
     products = jnp.einsum("fan,fbn->fab", left_rows, weighted, preferred_element_type=jnp.float32)
+    corr_real = products[:, :half_a, :half_b] + products[:, half_a:, half_b:]
+    corr_imag = products[:, half_a:, :half_b] - products[:, :half_a, half_b:]
+    return jnp.stack([corr_real, corr_imag], axis=1)
+
+
+def pair_products(mine, other, field, tile=512):
+    freq, rows, points = mine.shape
+    def kernel(mine_ref, other_ref, field_ref, first_ref, second_ref):
+        step = pl.program_id(1)
+        @pl.when(step == 0)
+        def _():
+            first_ref[...] = jnp.zeros_like(first_ref)
+            second_ref[...] = jnp.zeros_like(second_ref)
+        spread = field_ref[0]
+        mine_tile = mine_ref[0]
+        other_tile = other_ref[0]
+        weighted_other = (other_tile.astype(jnp.float32) * spread).astype(jnp.bfloat16)
+        weighted_mine = (mine_tile.astype(jnp.float32) * spread).astype(jnp.bfloat16)
+        dims = (((1,), (1,)), ((), ()))
+        first_ref[0] += jax.lax.dot_general(mine_tile, weighted_other, dims, preferred_element_type=jnp.float32)
+        second_ref[0] += jax.lax.dot_general(other_tile, weighted_mine, dims, preferred_element_type=jnp.float32)
+    spec = pl.BlockSpec((1, rows, tile), lambda f, t: (f, 0, t))
+    out_spec = pl.BlockSpec((1, rows, rows), lambda f, t: (f, 0, 0))
+    return pl.pallas_call(
+        kernel,
+        grid=(freq, points // tile),
+        in_specs=[spec, spec, pl.BlockSpec((1, 1, tile), lambda f, t: (f, 0, t))],
+        out_specs=[out_spec, out_spec],
+        out_shape=[jax.ShapeDtypeStruct((freq, rows, rows), jnp.float32)] * 2,
+        compiler_params=pltpu.CompilerParams(dimension_semantics=("parallel", "arbitrary")),
+    )(mine, other, field[:, None, :])
+
+
+def combine(products, half_a, half_b):
     corr_real = products[:, :half_a, :half_b] + products[:, half_a:, half_b:]
     corr_imag = products[:, half_a:, :half_b] - products[:, :half_a, half_b:]
     return jnp.stack([corr_real, corr_imag], axis=1)
@@ -197,10 +233,9 @@
     def run_sweep(sweep_idx, log_field):
         psd_field = jnp.exp(log_field)
         spread = psd_field[:, None, None, :]
-        weighted_mine = (green_panel * spread).astype(jnp.bfloat16).reshape(mine_rows.shape)
-        weighted_other = (other * spread).astype(jnp.bfloat16).reshape(other_rows.shape)
-        corr_first = correlate(mine_rows, weighted_other)
-        corr_second = correlate(other_rows, weighted_mine)
+        product_first, product_second = pair_products(mine_rows, other_rows, psd_field)
+        corr_first = combine(product_first, span_j, span_j)
+        corr_second = combine(product_second, span_j, span_j)
         both = swap_add(jnp.stack([corr_first, corr_second]), "pts")
         adj_first = (scale_first * (quad_weight * both[0] - obs_first)).astype(jnp.bfloat16)
         adj_second = (scale_second * (quad_weight * both[1] - obs_second)).astype(jnp.bfloat16)

time: 245 us -> 265 us (1.082)
  Pallas kernels: 0 us -> 38.2 us
  matrix products: 39.4 us -> 13.2 us
  other arithmetic: 12.7 us -> 15.5 us
  starting transfers between devices: 46 us -> 48.7 us
    pallas_call x0 -> x2, Pallas kernels: none -> 38.2 us  [pair_products(): pl.pallas_call(kernel, grid=(freq, points // tile), in_specs=[spec, spec,...]
    dot_general x4 -> x0, matrix products: 23.5 us -> none  [correlate(): jnp.einsum('fan,fbn->fab', left_rows, weighted, preferred_element_type=jn...]
    another operation x4 -> x2, other arithmetic: 0.22 us -> 3.62 us  [combine(): return jnp.stack([corr_real, corr_imag], axis=1)]
    ppermute x18, starting transfers between devices: 36.6 us -> 39.4 us  [butterfly_sum(): got.append(lax.ppermute(value, axis, [(i, i ^ mask) for i in range(size)]))]
    dot_general x4, matrix products: 15.9 us -> 13.2 us  [point_terms(): jnp.einsum('fab,fbn->fan', adjoint_block(adjoint), right_rows, preferred_...]
where the time goes in v9:
time: 265 us; the launch traced here: 264 us
  waiting for transfers between devices  131 us (49%)
  starting transfers between devices  48.7 us (18%)
  Pallas kernels  38.2 us (14%)
  other arithmetic  15.5 us (6%)
  matrix products  13.2 us (5%)
  local copies, waits for them, and re-layouts  7.52 us (3%)
  between operations  6.1 us (2%)
  loops' own time  3.05 us (1%)
    ppermute x18, waiting for transfers between devices, butterfly_sum(): got.append(lax.ppermute(value, axis, [(i, i ^ mask) for i in range(size)]))  124 us
    ppermute x18, starting transfers between devices, butterfly_sum(): got.append(lax.ppermute(value, axis, [(i, i ^ mask) for i in range(size)]))  39.4 us
    pallas_call x2, Pallas kernels, pair_products(): pl.pallas_call(kernel, grid=(freq, points // tile), in_specs=[spec, spec,...  38.2 us
    dot_general x4, matrix products, point_terms(): jnp.einsum('fab,fbn->fan', adjoint_block(adjoint), right_rows, preferred_...  13.2 us
    ppermute x4, waiting for transfers between devices, swap_add(): return value + lax.ppermute(value, axis, [(0, 1), (1, 0)])  7.87 us
    ppermute x1, starting transfers between devices, pair_body(): received = lax.ppermute(green_panel, axes, panel_moves)  7.58 us
  transfers between devices with their start and end apart: 26, of which 16 were waited for; matrix products, arithmetic and copies ran while one was open for 3% of the time, Pallas kernels for 0%

profile of v9, /device:TPU:0, one launch (start us, length us, event | category | flops | bytes accessed | tf_op | source)
XLA Modules:
  0.0 263.7 jit_solution(6320213803502880035)
XLA Ops:
  0.0 7.6 %collective-permute-start.14 = (bf16[4,2,128,3072]{3,2,1,0:T(8,128)(2,1)}, bf16[4,2,128,3072]{3,2,1,0:T(8,128)(2,1)}, u32[]{:S(2)}, u32[]{:S(2)}) collective-permute-start(bf16[4,2,128,3072]{3,2,1,0:T(8,128)(2,1)} %param.8), channel_id=1, source_target_pairs={{0,2},{12,8},{16,22},{20,18},{10,14},{30,28},{1,3},{13,9},{17,23},... | collective-permute-start | bytes 18874376 | tf_op jit(solution)/shard_map/ppermute | solution.py:193
  8.5 3.6 %collective-permute-start.9 = (f32[4,3072]{1,0:T(4,128)S(1)}, f32[4,3072]{1,0:T(4,128)S(1)}, u32[]{:S(2)}, u32[]{:S(2)}) collective-permute-start(f32[4,3072]{1,0:T(4,128)S(1)} %dynamic_update_slice.3), channel_id=1, source_target_pairs={{0,16},{8,24},{16,0},{24,8},{1,17},{9,25},{17,1},{25,9},{2,18},{10... | collective-permute-start | bytes 147464 | tf_op jit(solution)/shard_map/ppermute | solution.py:33
  12.1 1.4 collective-permute-start.10
  15.2 1.9 maximum_bitcast_fusion.2
  27.5 1.4 collective-permute-start.11
  28.9 4.2 %collective-permute-start.12 = (f32[4,3072]{1,0:T(4,128)S(1)}, f32[4,3072]{1,0:T(4,128)S(1)}, u32[]{:S(2)}, u32[]{:S(2)}) collective-permute-start(f32[4,3072]{1,0:T(4,128)S(1)} %fusion.34), channel_id=1, source_target_pairs={{0,4},{2,6},{4,0},{6,2},{1,5},{3,7},{5,1},{7,3},{8,12},{10,14},{12... | collective-permute-start | bytes 147464 | tf_op jit(solution)/shard_map/ppermute | solution.py:33
  33.5 108.5 %collective-permute-done.11 = f32[4,3072]{1,0:T(4,128)S(1)} collective-permute-done((f32[4,3072]{1,0:T(4,128)S(1)}, f32[4,3072]{1,0:T(4,128)S(1)}, u32[]{:S(2)}, u32[]{:S(2)}) %collective-permute-start.11) | collective-permute-done | bytes 49184 | tf_op jit(solution)/shard_map/ppermute | solution.py:33
  143.3 1.4 pad_maximum_fusion.3
  146.5 3.5 %broadcast_select_fusion = bf16[4,2,128,3072]{3,2,1,0:T(8,128)(2,1)} fusion(bf16[4,2,128,3072]{3,2,1,0:T(8,128)(2,1)S(1)} %bitcast.134, bf16[4,2,128,3072]{3,2,1,0:T(8,128)(2,1)} %collective-permute-done.14, pred[]{:T(512)} %bitcast.42), kind=kLoop, calls=%fused_computation.49 | loop fusion | flops 3145728 | bytes 18874368 | tf_op jit(solution)/shard_map/jit(_where)/select_n | solution.py:214
  150.0 113.0 %while.13 = (s32[]{:T(128)}, f32[4,3072]{1,0:T(4,128)S(1)}, pred[]{:T(512)}, bf16[4,256,3072]{2,1,0:T(8,128)(2,1)}, f32[1,128,128]{2,1,0:T(8,128)S(1)}, /*index=...) while((s32[]{:T(128)}, f32[4,3072]{1,0:T(4,128)S(1)}, ...), condition=%wide.region_4.5_spmd, body=%wide.region_0.4_spmd.sunk | while | flops 3247300608 | bytes 90244464 | solution.py:249
  150.6 19.1 %eval_jaxpr.5 = (f32[4,256,256]{2,1,0:T(8,128)}, f32[4,256,256]{2,1,0:T(8,128)}) custom-call(bf16[4,256,3072]{2,1,0:T(8,128)(2,1)} %get-tuple-element.356.mine_ref, bf16[4,256,3072]{2,1,0:T(8,128)(2,1)} %get-tuple-element.358.other_ref, f32[4,1,3072]{2,1,0:T(1,128)} %broadcast_in_dim.36.field_ref), custom_call_target="tpu_custom_call" | custom-call | tf_op jit(solution)/shard_map/while/body/eval_jaxpr/pallas_call | solution.py:79
  169.7 1.8 add_bitcast_fusion.4
  171.8 2.6 %collective-permute-done = f32[2,4,2,128,128]{4,3,1,2,0:T(8,128)S(1)} collective-permute-done((f32[2,4,2,128,128]{4,3,1,2,0:T(8,128)S(1)}, f32[2,4,2,128,128]{4,3,1,2,0:T(8,128)S(1)}, u32[]{:S(2)}, u32[]{:S(2)}) %collective-permute-start) | collective-permute-done | bytes 1048608 | tf_op jit(solution)/shard_map/while/body/eval_jaxpr/ppermute | solution.py:49
  175.0 4.8 %multiply_reduce_fusion.7 = f32[4,3072]{1,0:T(4,128)S(1)} fusion(bf16[4,256,3072]{2,1,0:T(8,128)(2,1)S(1)} %bitcast.136, bf16[4,256,3072]{2,1,0:T(8,128)(2,1)} %get-tuple-element.358.other_ref, bf16[4,128,128]{2,1,0:T(8,128)(2,1)S(1)} %get-tuple-element.311, bf16[4,128,128]{2,1,0:T(8,128)(2,1)S(1)} %get-tuple-element.312, ...), kind=kOutput, calls=%fused_computation.1.clone.1 | convolution fusion | flops 1622134784 | bytes 13025280 | tf_op jit(solution)/shard_map/while/body/eval_jaxpr/fab,fbn->fan/dot_general | solution.py:104
  179.8 1.8 multiply_reduce_fusion.6
  181.7 8.2 %collective-permute-start.1 = (f32[4,3072]{1,0:T(4,128)S(1)}, f32[4,3072]{1,0:T(4,128)S(1)}, u32[]{:S(2)}, u32[]{:S(2)}) collective-permute-start(f32[4,3072]{1,0:T(4,128)S(1)} %select_add_fusion.2), channel_id=1, source_target_pairs={{0,24},{8,16},{16,8},{24,0},{1,25},{9,17},{17,9},{25,1},{2,26},{10... | collective-permute-start | bytes 147464 | tf_op jit(solution)/shard_map/while/body/eval_jaxpr/ppermute | solution.py:33
  189.9 7.0 %collective-permute-start.2 = (f32[4,3072]{1,0:T(4,128)S(1)}, f32[4,3072]{1,0:T(4,128)S(1)}, u32[]{:S(2)}, u32[]{:S(2)}) collective-permute-start(f32[4,3072]{1,0:T(4,128)S(1)} %select_add_fusion.2), channel_id=1, source_target_pairs={{0,16},{8,24},{16,0},{24,8},{1,17},{9,25},{17,1},{25,9},{2,18},{10... | collective-permute-start | bytes 147464 | tf_op jit(solution)/shard_map/while/body/eval_jaxpr/ppermute | solution.py:33
  196.9 2.1 collective-permute-done.2
  198.9 2.0 collective-permute-done.3
  201.1 5.2 %collective-permute-start.5 = (f32[4,3072]{1,0:T(4,128)S(1)}, f32[4,3072]{1,0:T(4,128)S(1)}, u32[]{:S(2)}, u32[]{:S(2)}) collective-permute-start(f32[4,3072]{1,0:T(4,128)S(1)} %fusion.52), channel_id=1, source_target_pairs={{0,4},{2,6},{4,0},{6,2},{1,5},{3,7},{5,1},{7,3},{8,12},{10,14},{12... | collective-permute-start | bytes 147464 | tf_op jit(solution)/shard_map/while/body/eval_jaxpr/ppermute | solution.py:33
  207.3 2.3 collective-permute-done.5
  211.2 1.3 collective-permute-done.7
  214.5 19.1 %eval_jaxpr.5 = (f32[4,256,256]{2,1,0:T(8,128)}, f32[4,256,256]{2,1,0:T(8,128)}) custom-call(bf16[4,256,3072]{2,1,0:T(8,128)(2,1)} %get-tuple-element.356.mine_ref, bf16[4,256,3072]{2,1,0:T(8,128)(2,1)} %get-tuple-element.358.other_ref, f32[4,1,3072]{2,1,0:T(1,128)} %broadcast_in_dim.36.field_ref), custom_call_target="tpu_custom_call" | custom-call | tf_op jit(solution)/shard_map/while/body/eval_jaxpr/pallas_call | solution.py:79
  233.7 1.8 add_bitcast_fusion.4
  235.9 2.5 collective-permute-done
  238.9 4.8 %multiply_reduce_fusion.7 = f32[4,3072]{1,0:T(4,128)S(1)} fusion(bf16[4,256,3072]{2,1,0:T(8,128)(2,1)S(1)} %bitcast.136, bf16[4,256,3072]{2,1,0:T(8,128)(2,1)} %get-tuple-element.358.other_ref, bf16[4,128,128]{2,1,0:T(8,128)(2,1)S(1)} %get-tuple-element.311, bf16[4,128,128]{2,1,0:T(8,128)(2,1)S(1)} %get-tuple-element.312, ...), kind=kOutput, calls=%fused_computation.1.clone.1 | convolution fusion | flops 1622134784 | bytes 13025280 | tf_op jit(solution)/shard_map/while/body/eval_jaxpr/fab,fbn->fan/dot_general | solution.py:104
  243.7 1.8 multiply_reduce_fusion.6
  245.6 2.8 %collective-permute-start.1 = (f32[4,3072]{1,0:T(4,128)S(1)}, f32[4,3072]{1,0:T(4,128)S(1)}, u32[]{:S(2)}, u32[]{:S(2)}) collective-permute-start(f32[4,3072]{1,0:T(4,128)S(1)} %select_add_fusion.2), channel_id=1, source_target_pairs={{0,24},{8,16},{16,8},{24,0},{1,25},{9,17},{17,9},{25,1},{2,26},{10... | collective-permute-start | bytes 147464 | tf_op jit(solution)/shard_map/while/body/eval_jaxpr/ppermute | solution.py:33
  249.1 1.5 collective-permute-done.1
  250.6 1.8 collective-permute-done.2
  254.6 2.4 collective-permute-start.6
  257.0 1.5 collective-permute-done.4
  (122 shorter events, 22.8 us)
Async XLA Ops:
  0.0 144.7 %collective-permute-start.14 = (bf16[4,2,128,3072]{3,2,1,0:T(8,128)(2,1)}, bf16[4,2,128,3072]{3,2,1,0:T(8,128)(2,1)}, u32[]{:S(2)}, u32[]{:S(2)}) collective-permute-start(bf16[4,2,128,3072]{3,2,1,0:T(8,128)(2,1)} %param.8), channel_id=1, source_target_pairs={{0,2},{12,8},{16,22},{20,18},{10,14},{30,28},{1,3},{13,9},{17,23},... | collective-permute-start | bytes 18874376 | tf_op jit(solution)/shard_map/ppermute | solution.py:193
  8.4 18.2 %collective-permute-start.8 = (f32[4,3072]{1,0:T(4,128)S(1)}, f32[4,3072]{1,0:T(4,128)S(1)}, u32[]{:S(2)}, u32[]{:S(2)}) collective-permute-start(f32[4,3072]{1,0:T(4,128)S(1)} %dynamic_update_slice.3), channel_id=1, source_target_pairs={{0,8},{8,0},{16,24},{24,16},{1,9},{9,1},{17,25},{25,17},{2,10},{10... | collective-permute-start | bytes 147464 | tf_op jit(solution)/shard_map/ppermute | solution.py:33
  8.5 18.8 %collective-permute-start.9 = (f32[4,3072]{1,0:T(4,128)S(1)}, f32[4,3072]{1,0:T(4,128)S(1)}, u32[]{:S(2)}, u32[]{:S(2)}) collective-permute-start(f32[4,3072]{1,0:T(4,128)S(1)} %dynamic_update_slice.3), channel_id=1, source_target_pairs={{0,16},{8,24},{16,0},{24,8},{1,17},{9,25},{17,1},{25,9},{2,18},{10... | collective-permute-start | bytes 147464 | tf_op jit(solution)/shard_map/ppermute | solution.py:33
  12.1 15.2 %collective-permute-start.10 = (f32[4,3072]{1,0:T(4,128)S(1)}, f32[4,3072]{1,0:T(4,128)S(1)}, u32[]{:S(2)}, u32[]{:S(2)}) collective-permute-start(f32[4,3072]{1,0:T(4,128)S(1)} %dynamic_update_slice.3), channel_id=1, source_target_pairs={{0,24},{8,16},{16,8},{24,0},{1,25},{9,17},{17,9},{25,1},{2,26},{10... | collective-permute-start | bytes 147464 | tf_op jit(solution)/shard_map/ppermute | solution.py:33
  26.0 7.2 %collective-permute-start.15 = (f32[5,128,128]{2,1,0:T(8,128)S(1)}, f32[5,128,128]{2,1,0:T(8,128)S(1)}, u32[]{:S(2)}, u32[]{:S(2)}) collective-permute-start(f32[5,128,128]{2,1,0:T(8,128)S(1)} %fusion.29), channel_id=1, source_target_pairs={{8,2},{4,8},{24,22},{12,18},{26,14},{22,28},{9,3},{5,9},{25,23},{1... | collective-permute-start | bytes 983048 | tf_op jit(solution)/shard_map/ppermute | solution.py:205
  26.7 6.7 %collective-permute-start.16 = (f32[5,128,128]{2,1,0:T(8,128)S(1)}, f32[5,128,128]{2,1,0:T(8,128)S(1)}, u32[]{:S(2)}, u32[]{:S(2)}) collective-permute-start(f32[5,128,128]{2,1,0:T(8,128)S(1)} %fusion.29), channel_id=1, source_target_pairs={{16,8},{6,22},{17,9},{7,23}} | collective-permute-start | bytes 983048 | tf_op jit(solution)/shard_map/ppermute | solution.py:205
  27.5 114.6 %collective-permute-start.11 = (f32[4,3072]{1,0:T(4,128)S(1)}, f32[4,3072]{1,0:T(4,128)S(1)}, u32[]{:S(2)}, u32[]{:S(2)}) collective-permute-start(f32[4,3072]{1,0:T(4,128)S(1)} %fusion.34), channel_id=1, source_target_pairs={{0,2},{2,0},{4,6},{6,4},{1,3},{3,1},{5,7},{7,5},{8,10},{10,8},{12,... | collective-permute-start | bytes 147464 | tf_op jit(solution)/shard_map/ppermute | solution.py:33
  28.9 117.6 %slice-start = ((s8[6291456]{0:T(1024)(128)(4,1)}), s8[4194304]{0:T(1024)(128)(4,1)S(1)}, s32[]{:S(2)}) async-start(s8[6291456]{0:T(1024)(128)(4,1)} %bitcast.133), calls=%async_computation | async-start | bytes 8388608
  28.9 113.7 %collective-permute-start.12 = (f32[4,3072]{1,0:T(4,128)S(1)}, f32[4,3072]{1,0:T(4,128)S(1)}, u32[]{:S(2)}, u32[]{:S(2)}) collective-permute-start(f32[4,3072]{1,0:T(4,128)S(1)} %fusion.34), channel_id=1, source_target_pairs={{0,4},{2,6},{4,0},{6,2},{1,5},{3,7},{5,1},{7,3},{8,12},{10,14},{12... | collective-permute-start | bytes 147464 | tf_op jit(solution)/shard_map/ppermute | solution.py:33
  33.1 110.0 %collective-permute-start.13 = (f32[4,3072]{1,0:T(4,128)S(1)}, f32[4,3072]{1,0:T(4,128)S(1)}, u32[]{:S(2)}, u32[]{:S(2)}) collective-permute-start(f32[4,3072]{1,0:T(4,128)S(1)} %fusion.34), channel_id=1, source_target_pairs={{0,6},{2,4},{4,2},{6,0},{1,7},{3,5},{5,3},{7,1},{8,14},{10,12},{12... | collective-permute-start | bytes 147464 | tf_op jit(solution)/shard_map/ppermute | solution.py:33
  33.4 109.8 %collective-permute-start.17 = (f32[2,5,128,128]{3,2,1,0:T(8,128)S(1)}, f32[2,5,128,128]{3,2,1,0:T(8,128)S(1)}, u32[]{:S(2)}, u32[]{:S(2)}) collective-permute-start(f32[2,5,128,128]{3,2,1,0:T(8,128)S(1)} %pad_maximum_fusion.8), channel_id=1, source_target_pairs={{0,1},{1,0},{2,3},{3,2},{4,5},{5,4},{6,7},{7,6},{8,9},{9,8},{10,11... | collective-permute-start | bytes 1966088 | tf_op jit(solution)/shard_map/ppermute | solution.py:206
  150.6 24.3 %slice-start.2 = ((s8[6291456]{0:T(1024)(128)(4,1)}), s8[2097152]{0:T(1024)(128)(4,1)S(1)}, s32[]{:S(2)}) async-start(s8[6291456]{0:T(1024)(128)(4,1)} %bitcast.135), calls=%async_computation.2 | async-start | bytes 4194304 | tf_op jit(solution)/shard_map/while
  169.7 4.9 %copy-start.1 = (f32[4,2,128,128]{3,2,0,1:T(8,128)S(1)}, f32[4,2,128,128]{3,2,0,1:T(8,128)}, u32[]{:S(2)}) copy-start(f32[4,2,128,128]{3,2,0,1:T(8,128)} %get-tuple-element.362) | copy-start | bytes 1572868 | tf_op jit(solution)/shard_map/while
  169.7 5.2 %slice-start.3 = ((s8[6291456]{0:T(1024)(128)(4,1)}), s8[4194304]{0:T(1024)(128)(4,1)S(1)}, s32[]{:S(2)}) async-start(s8[6291456]{0:T(1024)(128)(4,1)} %bitcast.135), calls=%async_computation.3 | async-start | bytes 8388608 | tf_op jit(solution)/shard_map/while
  171.7 2.7 %collective-permute-start = (f32[2,4,2,128,128]{4,3,1,2,0:T(8,128)S(1)}, f32[2,4,2,128,128]{4,3,1,2,0:T(8,128)S(1)}, u32[]{:S(2)}, u32[]{:S(2)}) collective-permute-start(f32[2,4,2,128,128]{4,3,1,2,0:T(8,128)S(1)} %pad_maximum_fusion.14), channel_id=1, source_target_pairs={{0,1},{1,0},{2,3},{3,2},{4,5},{5,4},{6,7},{7,6},{8,9},{9,8},{10,11... | collective-permute-start | bytes 3145736 | tf_op jit(solution)/shard_map/while/body/eval_jaxpr/ppermute | solution.py:49
  181.7 15.2 %collective-permute-start.1 = (f32[4,3072]{1,0:T(4,128)S(1)}, f32[4,3072]{1,0:T(4,128)S(1)}, u32[]{:S(2)}, u32[]{:S(2)}) collective-permute-start(f32[4,3072]{1,0:T(4,128)S(1)} %select_add_fusion.2), channel_id=1, source_target_pairs={{0,24},{8,16},{16,8},{24,0},{1,25},{9,17},{17,9},{25,1},{2,26},{10... | collective-permute-start | bytes 147464 | tf_op jit(solution)/shard_map/while/body/eval_jaxpr/ppermute | solution.py:33
  189.9 9.0 %collective-permute-start.2 = (f32[4,3072]{1,0:T(4,128)S(1)}, f32[4,3072]{1,0:T(4,128)S(1)}, u32[]{:S(2)}, u32[]{:S(2)}) collective-permute-start(f32[4,3072]{1,0:T(4,128)S(1)} %select_add_fusion.2), channel_id=1, source_target_pairs={{0,16},{8,24},{16,0},{24,8},{1,17},{9,25},{17,1},{25,9},{2,18},{10... | collective-permute-start | bytes 147464 | tf_op jit(solution)/shard_map/while/body/eval_jaxpr/ppermute | solution.py:33
  196.9 4.1 %collective-permute-start.3 = (f32[4,3072]{1,0:T(4,128)S(1)}, f32[4,3072]{1,0:T(4,128)S(1)}, u32[]{:S(2)}, u32[]{:S(2)}) collective-permute-start(f32[4,3072]{1,0:T(4,128)S(1)} %select_add_fusion.2), channel_id=1, source_target_pairs={{0,8},{8,0},{16,24},{24,16},{1,9},{9,1},{17,25},{25,17},{2,10},{10... | collective-permute-start | bytes 147464 | tf_op jit(solution)/shard_map/while/body/eval_jaxpr/ppermute | solution.py:33
  201.0 6.2 %collective-permute-start.4 = (f32[4,3072]{1,0:T(4,128)S(1)}, f32[4,3072]{1,0:T(4,128)S(1)}, u32[]{:S(2)}, u32[]{:S(2)}) collective-permute-start(f32[4,3072]{1,0:T(4,128)S(1)} %fusion.52), channel_id=1, source_target_pairs={{0,6},{2,4},{4,2},{6,0},{1,7},{3,5},{5,3},{7,1},{8,14},{10,12},{12... | collective-permute-start | bytes 147464 | tf_op jit(solution)/shard_map/while/body/eval_jaxpr/ppermute | solution.py:33
  201.1 8.4 %collective-permute-start.5 = (f32[4,3072]{1,0:T(4,128)S(1)}, f32[4,3072]{1,0:T(4,128)S(1)}, u32[]{:S(2)}, u32[]{:S(2)}) collective-permute-start(f32[4,3072]{1,0:T(4,128)S(1)} %fusion.52), channel_id=1, source_target_pairs={{0,4},{2,6},{4,0},{6,2},{1,5},{3,7},{5,1},{7,3},{8,12},{10,14},{12... | collective-permute-start | bytes 147464 | tf_op jit(solution)/shard_map/while/body/eval_jaxpr/ppermute | solution.py:33
  206.3 4.1 %collective-permute-start.6 = (f32[4,3072]{1,0:T(4,128)S(1)}, f32[4,3072]{1,0:T(4,128)S(1)}, u32[]{:S(2)}, u32[]{:S(2)}) collective-permute-start(f32[4,3072]{1,0:T(4,128)S(1)} %fusion.52), channel_id=1, source_target_pairs={{0,2},{2,0},{4,6},{6,4},{1,3},{3,1},{5,7},{7,5},{8,10},{10,8},{12,... | collective-permute-start | bytes 147464 | tf_op jit(solution)/shard_map/while/body/eval_jaxpr/ppermute | solution.py:33
  211.1 1.4 collective-permute-start.7
  214.5 24.3 %slice-start.2 = ((s8[6291456]{0:T(1024)(128)(4,1)}), s8[2097152]{0:T(1024)(128)(4,1)S(1)}, s32[]{:S(2)}) async-start(s8[6291456]{0:T(1024)(128)(4,1)} %bitcast.135), calls=%async_computation.2 | async-start | bytes 4194304 | tf_op jit(solution)/shard_map/while
  233.6 5.2 %slice-start.3 = ((s8[6291456]{0:T(1024)(128)(4,1)}), s8[4194304]{0:T(1024)(128)(4,1)S(1)}, s32[]{:S(2)}) async-start(s8[6291456]{0:T(1024)(128)(4,1)} %bitcast.135), calls=%async_computation.3 | async-start | bytes 8388608 | tf_op jit(solution)/shard_map/while
  235.7 2.7 %collective-permute-start = (f32[2,4,2,128,128]{4,3,1,2,0:T(8,128)S(1)}, f32[2,4,2,128,128]{4,3,1,2,0:T(8,128)S(1)}, u32[]{:S(2)}, u32[]{:S(2)}) collective-permute-start(f32[2,4,2,128,128]{4,3,1,2,0:T(8,128)S(1)} %pad_maximum_fusion.14), channel_id=1, source_target_pairs={{0,1},{1,0},{2,3},{3,2},{4,5},{5,4},{6,7},{7,6},{8,9},{9,8},{10,11... | collective-permute-start | bytes 3145736 | tf_op jit(solution)/shard_map/while/body/eval_jaxpr/ppermute | solution.py:49
  245.6 5.1 %collective-permute-start.1 = (f32[4,3072]{1,0:T(4,128)S(1)}, f32[4,3072]{1,0:T(4,128)S(1)}, u32[]{:S(2)}, u32[]{:S(2)}) collective-permute-start(f32[4,3072]{1,0:T(4,128)S(1)} %select_add_fusion.2), channel_id=1, source_target_pairs={{0,24},{8,16},{16,8},{24,0},{1,25},{9,17},{17,9},{25,1},{2,26},{10... | collective-permute-start | bytes 147464 | tf_op jit(solution)/shard_map/while/body/eval_jaxpr/ppermute | solution.py:33
  248.4 4.1 %collective-permute-start.2 = (f32[4,3072]{1,0:T(4,128)S(1)}, f32[4,3072]{1,0:T(4,128)S(1)}, u32[]{:S(2)}, u32[]{:S(2)}) collective-permute-start(f32[4,3072]{1,0:T(4,128)S(1)} %select_add_fusion.2), channel_id=1, source_target_pairs={{0,16},{8,24},{16,0},{24,8},{1,17},{9,25},{17,1},{25,9},{2,18},{10... | collective-permute-start | bytes 147464 | tf_op jit(solution)/shard_map/while/body/eval_jaxpr/ppermute | solution.py:33
  248.4 4.1 %collective-permute-start.3 = (f32[4,3072]{1,0:T(4,128)S(1)}, f32[4,3072]{1,0:T(4,128)S(1)}, u32[]{:S(2)}, u32[]{:S(2)}) collective-permute-start(f32[4,3072]{1,0:T(4,128)S(1)} %select_add_fusion.2), channel_id=1, source_target_pairs={{0,8},{8,0},{16,24},{24,16},{1,9},{9,1},{17,25},{25,17},{2,10},{10... | collective-permute-start | bytes 147464 | tf_op jit(solution)/shard_map/while/body/eval_jaxpr/ppermute | solution.py:33
  252.6 6.0 %collective-permute-start.4 = (f32[4,3072]{1,0:T(4,128)S(1)}, f32[4,3072]{1,0:T(4,128)S(1)}, u32[]{:S(2)}, u32[]{:S(2)}) collective-permute-start(f32[4,3072]{1,0:T(4,128)S(1)} %fusion.52), channel_id=1, source_target_pairs={{0,6},{2,4},{4,2},{6,0},{1,7},{3,5},{5,3},{7,1},{8,14},{10,12},{12... | collective-permute-start | bytes 147464 | tf_op jit(solution)/shard_map/while/body/eval_jaxpr/ppermute | solution.py:33
  253.6 6.0 %collective-permute-start.5 = (f32[4,3072]{1,0:T(4,128)S(1)}, f32[4,3072]{1,0:T(4,128)S(1)}, u32[]{:S(2)}, u32[]{:S(2)}) collective-permute-start(f32[4,3072]{1,0:T(4,128)S(1)} %fusion.52), channel_id=1, source_target_pairs={{0,4},{2,6},{4,0},{6,2},{1,5},{3,7},{5,1},{7,3},{8,12},{10,14},{12... | collective-permute-start | bytes 147464 | tf_op jit(solution)/shard_map/while/body/eval_jaxpr/ppermute | solution.py:33
  254.6 5.0 %collective-permute-start.6 = (f32[4,3072]{1,0:T(4,128)S(1)}, f32[4,3072]{1,0:T(4,128)S(1)}, u32[]{:S(2)}, u32[]{:S(2)}) collective-permute-start(f32[4,3072]{1,0:T(4,128)S(1)} %fusion.52), channel_id=1, source_target_pairs={{0,2},{2,0},{4,6},{6,4},{1,3},{3,1},{5,7},{7,5},{8,10},{10,8},{12,... | collective-permute-start | bytes 147464 | tf_op jit(solution)/shard_map/while/body/eval_jaxpr/ppermute | solution.py:33
  260.3 1.4 collective-permute-start.7
  (8 other events, 37.2 us)

commit v10 on v9

--- a/solution.py
+++ b/solution.py
@@ -58,7 +58,7 @@
     return jnp.stack([corr_real, corr_imag], axis=1)
 
 
-def pair_products(mine, other, field, tile=512):
+def pair_products(mine, other, field, tile=1536):
     freq, rows, points = mine.shape
     def kernel(mine_ref, other_ref, field_ref, first_ref, second_ref):
         step = pl.program_id(1)

time: 265 us -> 247 us (0.932)
  Pallas kernels: 38.2 us -> 21.1 us
    pallas_call x2, Pallas kernels: 38.2 us -> 21.1 us  [pair_products(): pl.pallas_call(kernel, grid=(freq, points // tile), in_specs=[spec, spec,...]
  transfers between devices with their start and end apart: 26 -> 26, of which waited for: 16 -> 16; matrix products, arithmetic and copies ran while one was open for 3% -> 4% of each run, Pallas kernels for 0% -> 0%
where the time goes in v10:
time: 247 us
  waiting for transfers between devices  131 us (53%)
  starting transfers between devices  48.7 us (20%)
  Pallas kernels  21.1 us (9%)
  other arithmetic  15.5 us (6%)
  matrix products  13.2 us (5%)
  local copies, waits for them, and re-layouts  7.52 us (3%)
  between operations  6.1 us (2%)
  loops' own time  3.05 us (1%)
    ppermute x18, waiting for transfers between devices, butterfly_sum(): got.append(lax.ppermute(value, axis, [(i, i ^ mask) for i in range(size)]))  124 us
    ppermute x18, starting transfers between devices, butterfly_sum(): got.append(lax.ppermute(value, axis, [(i, i ^ mask) for i in range(size)]))  39.4 us
    pallas_call x2, Pallas kernels, pair_products(): pl.pallas_call(kernel, grid=(freq, points // tile), in_specs=[spec, spec,...  21.1 us
    dot_general x4, matrix products, point_terms(): jnp.einsum('fab,fbn->fan', adjoint_block(adjoint), right_rows, preferred_...  13.2 us
    ppermute x4, waiting for transfers between devices, swap_add(): return value + lax.ppermute(value, axis, [(0, 1), (1, 0)])  7.83 us
    ppermute x1, starting transfers between devices, pair_body(): received = lax.ppermute(green_panel, axes, panel_moves)  7.58 us
  transfers between devices with their start and end apart: 26, of which 16 were waited for; matrix products, arithmetic and copies ran while one was open for 4% of the time, Pallas kernels for 0%

profile of v10, /device:TPU:0, one launch (start us, length us, event | category | flops | bytes accessed | tf_op | source)
XLA Modules:
  0.0 246.6 jit_solution(555620260134642802)
XLA Ops:
  0.0 7.6 %collective-permute-start.14 = (bf16[4,2,128,3072]{3,2,1,0:T(8,128)(2,1)}, bf16[4,2,128,3072]{3,2,1,0:T(8,128)(2,1)}, u32[]{:S(2)}, u32[]{:S(2)}) collective-permute-start(bf16[4,2,128,3072]{3,2,1,0:T(8,128)(2,1)} %param.8), channel_id=1, source_target_pairs={{0,2},{12,8},{16,22},{20,18},{10,14},{30,28},{1,3},{13,9},{17,23},... | collective-permute-start | bytes 18874376 | tf_op jit(solution)/shard_map/ppermute | solution.py:193
  8.5 3.6 %collective-permute-start.9 = (f32[4,3072]{1,0:T(4,128)S(1)}, f32[4,3072]{1,0:T(4,128)S(1)}, u32[]{:S(2)}, u32[]{:S(2)}) collective-permute-start(f32[4,3072]{1,0:T(4,128)S(1)} %dynamic_update_slice.3), channel_id=1, source_target_pairs={{0,16},{8,24},{16,0},{24,8},{1,17},{9,25},{17,1},{25,9},{2,18},{10... | collective-permute-start | bytes 147464 | tf_op jit(solution)/shard_map/ppermute | solution.py:33
  12.1 1.4 collective-permute-start.10
  15.2 1.9 maximum_bitcast_fusion.2
  27.5 1.4 collective-permute-start.11
  28.9 4.2 %collective-permute-start.12 = (f32[4,3072]{1,0:T(4,128)S(1)}, f32[4,3072]{1,0:T(4,128)S(1)}, u32[]{:S(2)}, u32[]{:S(2)}) collective-permute-start(f32[4,3072]{1,0:T(4,128)S(1)} %fusion.34), channel_id=1, source_target_pairs={{0,4},{2,6},{4,0},{6,2},{1,5},{3,7},{5,1},{7,3},{8,12},{10,14},{12... | collective-permute-start | bytes 147464 | tf_op jit(solution)/shard_map/ppermute | solution.py:33
  33.5 108.5 %collective-permute-done.11 = f32[4,3072]{1,0:T(4,128)S(1)} collective-permute-done((f32[4,3072]{1,0:T(4,128)S(1)}, f32[4,3072]{1,0:T(4,128)S(1)}, u32[]{:S(2)}, u32[]{:S(2)}) %collective-permute-start.11) | collective-permute-done | bytes 49184 | tf_op jit(solution)/shard_map/ppermute | solution.py:33
  143.3 1.4 pad_maximum_fusion.3
  146.5 3.5 %broadcast_select_fusion = bf16[4,2,128,3072]{3,2,1,0:T(8,128)(2,1)} fusion(bf16[4,2,128,3072]{3,2,1,0:T(8,128)(2,1)S(1)} %bitcast.134, bf16[4,2,128,3072]{3,2,1,0:T(8,128)(2,1)} %collective-permute-done.14, pred[]{:T(512)} %bitcast.42), kind=kLoop, calls=%fused_computation.49 | loop fusion | flops 3145728 | bytes 18874368 | tf_op jit(solution)/shard_map/jit(_where)/select_n | solution.py:214
  150.0 95.9 %while.13 = (s32[]{:T(128)}, f32[4,3072]{1,0:T(4,128)S(1)}, pred[]{:T(512)}, bf16[4,256,3072]{2,1,0:T(8,128)(2,1)}, f32[1,128,128]{2,1,0:T(8,128)S(1)}, /*index=...) while((s32[]{:T(128)}, f32[4,3072]{1,0:T(4,128)S(1)}, ...), condition=%wide.region_4.5_spmd, body=%wide.region_0.4_spmd.sunk | while | flops 3247300608 | bytes 90244464 | solution.py:249
  150.6 10.5 %eval_jaxpr.5 = (f32[4,256,256]{2,1,0:T(8,128)}, f32[4,256,256]{2,1,0:T(8,128)}) custom-call(bf16[4,256,3072]{2,1,0:T(8,128)(2,1)} %get-tuple-element.356.mine_ref, bf16[4,256,3072]{2,1,0:T(8,128)(2,1)} %get-tuple-element.358.other_ref, f32[4,1,3072]{2,1,0:T(1,128)} %broadcast_in_dim.36.field_ref), custom_call_target="tpu_custom_call" | custom-call | tf_op jit(solution)/shard_map/while/body/eval_jaxpr/pallas_call | solution.py:79
  161.2 1.8 add_bitcast_fusion.4
  163.3 2.6 %collective-permute-done = f32[2,4,2,128,128]{4,3,1,2,0:T(8,128)S(1)} collective-permute-done((f32[2,4,2,128,128]{4,3,1,2,0:T(8,128)S(1)}, f32[2,4,2,128,128]{4,3,1,2,0:T(8,128)S(1)}, u32[]{:S(2)}, u32[]{:S(2)}) %collective-permute-start) | collective-permute-done | bytes 1048608 | tf_op jit(solution)/shard_map/while/body/eval_jaxpr/ppermute | solution.py:49
  166.4 4.8 %multiply_reduce_fusion.7 = f32[4,3072]{1,0:T(4,128)S(1)} fusion(bf16[4,256,3072]{2,1,0:T(8,128)(2,1)S(1)} %bitcast.136, bf16[4,256,3072]{2,1,0:T(8,128)(2,1)} %get-tuple-element.358.other_ref, bf16[4,128,128]{2,1,0:T(8,128)(2,1)S(1)} %get-tuple-element.311, bf16[4,128,128]{2,1,0:T(8,128)(2,1)S(1)} %get-tuple-element.312, ...), kind=kOutput, calls=%fused_computation.1.clone.1 | convolution fusion | flops 1622134784 | bytes 13025280 | tf_op jit(solution)/shard_map/while/body/eval_jaxpr/fab,fbn->fan/dot_general | solution.py:104
  171.2 1.8 multiply_reduce_fusion.6
  173.1 8.2 %collective-permute-start.1 = (f32[4,3072]{1,0:T(4,128)S(1)}, f32[4,3072]{1,0:T(4,128)S(1)}, u32[]{:S(2)}, u32[]{:S(2)}) collective-permute-start(f32[4,3072]{1,0:T(4,128)S(1)} %select_add_fusion.2), channel_id=1, source_target_pairs={{0,24},{8,16},{16,8},{24,0},{1,25},{9,17},{17,9},{25,1},{2,26},{10... | collective-permute-start | bytes 147464 | tf_op jit(solution)/shard_map/while/body/eval_jaxpr/ppermute | solution.py:33
  181.3 7.0 %collective-permute-start.2 = (f32[4,3072]{1,0:T(4,128)S(1)}, f32[4,3072]{1,0:T(4,128)S(1)}, u32[]{:S(2)}, u32[]{:S(2)}) collective-permute-start(f32[4,3072]{1,0:T(4,128)S(1)} %select_add_fusion.2), channel_id=1, source_target_pairs={{0,16},{8,24},{16,0},{24,8},{1,17},{9,25},{17,1},{25,9},{2,18},{10... | collective-permute-start | bytes 147464 | tf_op jit(solution)/shard_map/while/body/eval_jaxpr/ppermute | solution.py:33
  188.3 2.1 collective-permute-done.2
  190.4 2.0 collective-permute-done.3
  192.6 5.2 %collective-permute-start.5 = (f32[4,3072]{1,0:T(4,128)S(1)}, f32[4,3072]{1,0:T(4,128)S(1)}, u32[]{:S(2)}, u32[]{:S(2)}) collective-permute-start(f32[4,3072]{1,0:T(4,128)S(1)} %fusion.52), channel_id=1, source_target_pairs={{0,4},{2,6},{4,0},{6,2},{1,5},{3,7},{5,1},{7,3},{8,12},{10,14},{12... | collective-permute-start | bytes 147464 | tf_op jit(solution)/shard_map/while/body/eval_jaxpr/ppermute | solution.py:33
  198.7 2.3 collective-permute-done.5
  206.0 10.5 %eval_jaxpr.5 = (f32[4,256,256]{2,1,0:T(8,128)}, f32[4,256,256]{2,1,0:T(8,128)}) custom-call(bf16[4,256,3072]{2,1,0:T(8,128)(2,1)} %get-tuple-element.356.mine_ref, bf16[4,256,3072]{2,1,0:T(8,128)(2,1)} %get-tuple-element.358.other_ref, f32[4,1,3072]{2,1,0:T(1,128)} %broadcast_in_dim.36.field_ref), custom_call_target="tpu_custom_call" | custom-call | tf_op jit(solution)/shard_map/while/body/eval_jaxpr/pallas_call | solution.py:79
  216.6 1.8 add_bitcast_fusion.4
  218.8 2.5 %collective-permute-done = f32[2,4,2,128,128]{4,3,1,2,0:T(8,128)S(1)} collective-permute-done((f32[2,4,2,128,128]{4,3,1,2,0:T(8,128)S(1)}, f32[2,4,2,128,128]{4,3,1,2,0:T(8,128)S(1)}, u32[]{:S(2)}, u32[]{:S(2)}) %collective-permute-start) | collective-permute-done | bytes 1048608 | tf_op jit(solution)/shard_map/while/body/eval_jaxpr/ppermute | solution.py:49
  221.8 4.8 %multiply_reduce_fusion.7 = f32[4,3072]{1,0:T(4,128)S(1)} fusion(bf16[4,256,3072]{2,1,0:T(8,128)(2,1)S(1)} %bitcast.136, bf16[4,256,3072]{2,1,0:T(8,128)(2,1)} %get-tuple-element.358.other_ref, bf16[4,128,128]{2,1,0:T(8,128)(2,1)S(1)} %get-tuple-element.311, bf16[4,128,128]{2,1,0:T(8,128)(2,1)S(1)} %get-tuple-element.312, ...), kind=kOutput, calls=%fused_computation.1.clone.1 | convolution fusion | flops 1622134784 | bytes 13025280 | tf_op jit(solution)/shard_map/while/body/eval_jaxpr/fab,fbn->fan/dot_general | solution.py:104
  226.6 1.8 multiply_reduce_fusion.6
  228.5 2.8 %collective-permute-start.1 = (f32[4,3072]{1,0:T(4,128)S(1)}, f32[4,3072]{1,0:T(4,128)S(1)}, u32[]{:S(2)}, u32[]{:S(2)}) collective-permute-start(f32[4,3072]{1,0:T(4,128)S(1)} %select_add_fusion.2), channel_id=1, source_target_pairs={{0,24},{8,16},{16,8},{24,0},{1,25},{9,17},{17,9},{25,1},{2,26},{10... | collective-permute-start | bytes 147464 | tf_op jit(solution)/shard_map/while/body/eval_jaxpr/ppermute | solution.py:33
  232.0 1.5 collective-permute-done.1
  233.5 1.8 collective-permute-done.2
  237.5 2.4 collective-permute-start.6
  239.9 1.5 collective-permute-done.4
  243.2 1.3 collective-permute-done.7
  (122 shorter events, 22.8 us)
Async XLA Ops:
  0.0 144.7 %collective-permute-start.14 = (bf16[4,2,128,3072]{3,2,1,0:T(8,128)(2,1)}, bf16[4,2,128,3072]{3,2,1,0:T(8,128)(2,1)}, u32[]{:S(2)}, u32[]{:S(2)}) collective-permute-start(bf16[4,2,128,3072]{3,2,1,0:T(8,128)(2,1)} %param.8), channel_id=1, source_target_pairs={{0,2},{12,8},{16,22},{20,18},{10,14},{30,28},{1,3},{13,9},{17,23},... | collective-permute-start | bytes 18874376 | tf_op jit(solution)/shard_map/ppermute | solution.py:193
  8.4 18.2 %collective-permute-start.8 = (f32[4,3072]{1,0:T(4,128)S(1)}, f32[4,3072]{1,0:T(4,128)S(1)}, u32[]{:S(2)}, u32[]{:S(2)}) collective-permute-start(f32[4,3072]{1,0:T(4,128)S(1)} %dynamic_update_slice.3), channel_id=1, source_target_pairs={{0,8},{8,0},{16,24},{24,16},{1,9},{9,1},{17,25},{25,17},{2,10},{10... | collective-permute-start | bytes 147464 | tf_op jit(solution)/shard_map/ppermute | solution.py:33
  8.5 18.8 %collective-permute-start.9 = (f32[4,3072]{1,0:T(4,128)S(1)}, f32[4,3072]{1,0:T(4,128)S(1)}, u32[]{:S(2)}, u32[]{:S(2)}) collective-permute-start(f32[4,3072]{1,0:T(4,128)S(1)} %dynamic_update_slice.3), channel_id=1, source_target_pairs={{0,16},{8,24},{16,0},{24,8},{1,17},{9,25},{17,1},{25,9},{2,18},{10... | collective-permute-start | bytes 147464 | tf_op jit(solution)/shard_map/ppermute | solution.py:33
  12.1 15.2 %collective-permute-start.10 = (f32[4,3072]{1,0:T(4,128)S(1)}, f32[4,3072]{1,0:T(4,128)S(1)}, u32[]{:S(2)}, u32[]{:S(2)}) collective-permute-start(f32[4,3072]{1,0:T(4,128)S(1)} %dynamic_update_slice.3), channel_id=1, source_target_pairs={{0,24},{8,16},{16,8},{24,0},{1,25},{9,17},{17,9},{25,1},{2,26},{10... | collective-permute-start | bytes 147464 | tf_op jit(solution)/shard_map/ppermute | solution.py:33
  26.0 7.2 %collective-permute-start.15 = (f32[5,128,128]{2,1,0:T(8,128)S(1)}, f32[5,128,128]{2,1,0:T(8,128)S(1)}, u32[]{:S(2)}, u32[]{:S(2)}) collective-permute-start(f32[5,128,128]{2,1,0:T(8,128)S(1)} %fusion.29), channel_id=1, source_target_pairs={{8,2},{4,8},{24,22},{12,18},{26,14},{22,28},{9,3},{5,9},{25,23},{1... | collective-permute-start | bytes 983048 | tf_op jit(solution)/shard_map/ppermute | solution.py:205
  26.7 6.7 %collective-permute-start.16 = (f32[5,128,128]{2,1,0:T(8,128)S(1)}, f32[5,128,128]{2,1,0:T(8,128)S(1)}, u32[]{:S(2)}, u32[]{:S(2)}) collective-permute-start(f32[5,128,128]{2,1,0:T(8,128)S(1)} %fusion.29), channel_id=1, source_target_pairs={{16,8},{6,22},{17,9},{7,23}} | collective-permute-start | bytes 983048 | tf_op jit(solution)/shard_map/ppermute | solution.py:205
  27.5 114.6 %collective-permute-start.11 = (f32[4,3072]{1,0:T(4,128)S(1)}, f32[4,3072]{1,0:T(4,128)S(1)}, u32[]{:S(2)}, u32[]{:S(2)}) collective-permute-start(f32[4,3072]{1,0:T(4,128)S(1)} %fusion.34), channel_id=1, source_target_pairs={{0,2},{2,0},{4,6},{6,4},{1,3},{3,1},{5,7},{7,5},{8,10},{10,8},{12,... | collective-permute-start | bytes 147464 | tf_op jit(solution)/shard_map/ppermute | solution.py:33
  28.9 117.6 %slice-start = ((s8[6291456]{0:T(1024)(128)(4,1)}), s8[4194304]{0:T(1024)(128)(4,1)S(1)}, s32[]{:S(2)}) async-start(s8[6291456]{0:T(1024)(128)(4,1)} %bitcast.133), calls=%async_computation | async-start | bytes 8388608
  28.9 113.7 %collective-permute-start.12 = (f32[4,3072]{1,0:T(4,128)S(1)}, f32[4,3072]{1,0:T(4,128)S(1)}, u32[]{:S(2)}, u32[]{:S(2)}) collective-permute-start(f32[4,3072]{1,0:T(4,128)S(1)} %fusion.34), channel_id=1, source_target_pairs={{0,4},{2,6},{4,0},{6,2},{1,5},{3,7},{5,1},{7,3},{8,12},{10,14},{12... | collective-permute-start | bytes 147464 | tf_op jit(solution)/shard_map/ppermute | solution.py:33
  33.1 110.0 %collective-permute-start.13 = (f32[4,3072]{1,0:T(4,128)S(1)}, f32[4,3072]{1,0:T(4,128)S(1)}, u32[]{:S(2)}, u32[]{:S(2)}) collective-permute-start(f32[4,3072]{1,0:T(4,128)S(1)} %fusion.34), channel_id=1, source_target_pairs={{0,6},{2,4},{4,2},{6,0},{1,7},{3,5},{5,3},{7,1},{8,14},{10,12},{12... | collective-permute-start | bytes 147464 | tf_op jit(solution)/shard_map/ppermute | solution.py:33
  33.4 109.8 %collective-permute-start.17 = (f32[2,5,128,128]{3,2,1,0:T(8,128)S(1)}, f32[2,5,128,128]{3,2,1,0:T(8,128)S(1)}, u32[]{:S(2)}, u32[]{:S(2)}) collective-permute-start(f32[2,5,128,128]{3,2,1,0:T(8,128)S(1)} %pad_maximum_fusion.8), channel_id=1, source_target_pairs={{0,1},{1,0},{2,3},{3,2},{4,5},{5,4},{6,7},{7,6},{8,9},{9,8},{10,11... | collective-permute-start | bytes 1966088 | tf_op jit(solution)/shard_map/ppermute | solution.py:206
  150.6 15.7 %slice-start.2 = ((s8[6291456]{0:T(1024)(128)(4,1)}), s8[2097152]{0:T(1024)(128)(4,1)S(1)}, s32[]{:S(2)}) async-start(s8[6291456]{0:T(1024)(128)(4,1)} %bitcast.135), calls=%async_computation.2 | async-start | bytes 4194304 | tf_op jit(solution)/shard_map/while
  161.2 4.9 %copy-start.1 = (f32[4,2,128,128]{3,2,0,1:T(8,128)S(1)}, f32[4,2,128,128]{3,2,0,1:T(8,128)}, u32[]{:S(2)}) copy-start(f32[4,2,128,128]{3,2,0,1:T(8,128)} %get-tuple-element.362) | copy-start | bytes 1572868 | tf_op jit(solution)/shard_map/while
  161.2 5.2 %slice-start.3 = ((s8[6291456]{0:T(1024)(128)(4,1)}), s8[4194304]{0:T(1024)(128)(4,1)S(1)}, s32[]{:S(2)}) async-start(s8[6291456]{0:T(1024)(128)(4,1)} %bitcast.135), calls=%async_computation.3 | async-start | bytes 8388608 | tf_op jit(solution)/shard_map/while
  163.2 2.7 %collective-permute-start = (f32[2,4,2,128,128]{4,3,1,2,0:T(8,128)S(1)}, f32[2,4,2,128,128]{4,3,1,2,0:T(8,128)S(1)}, u32[]{:S(2)}, u32[]{:S(2)}) collective-permute-start(f32[2,4,2,128,128]{4,3,1,2,0:T(8,128)S(1)} %pad_maximum_fusion.14), channel_id=1, source_target_pairs={{0,1},{1,0},{2,3},{3,2},{4,5},{5,4},{6,7},{7,6},{8,9},{9,8},{10,11... | collective-permute-start | bytes 3145736 | tf_op jit(solution)/shard_map/while/body/eval_jaxpr/ppermute | solution.py:49
  173.1 15.2 %collective-permute-start.1 = (f32[4,3072]{1,0:T(4,128)S(1)}, f32[4,3072]{1,0:T(4,128)S(1)}, u32[]{:S(2)}, u32[]{:S(2)}) collective-permute-start(f32[4,3072]{1,0:T(4,128)S(1)} %select_add_fusion.2), channel_id=1, source_target_pairs={{0,24},{8,16},{16,8},{24,0},{1,25},{9,17},{17,9},{25,1},{2,26},{10... | collective-permute-start | bytes 147464 | tf_op jit(solution)/shard_map/while/body/eval_jaxpr/ppermute | solution.py:33
  181.3 9.0 %collective-permute-start.2 = (f32[4,3072]{1,0:T(4,128)S(1)}, f32[4,3072]{1,0:T(4,128)S(1)}, u32[]{:S(2)}, u32[]{:S(2)}) collective-permute-start(f32[4,3072]{1,0:T(4,128)S(1)} %select_add_fusion.2), channel_id=1, source_target_pairs={{0,16},{8,24},{16,0},{24,8},{1,17},{9,25},{17,1},{25,9},{2,18},{10... | collective-permute-start | bytes 147464 | tf_op jit(solution)/shard_map/while/body/eval_jaxpr/ppermute | solution.py:33
  188.3 4.1 %collective-permute-start.3 = (f32[4,3072]{1,0:T(4,128)S(1)}, f32[4,3072]{1,0:T(4,128)S(1)}, u32[]{:S(2)}, u32[]{:S(2)}) collective-permute-start(f32[4,3072]{1,0:T(4,128)S(1)} %select_add_fusion.2), channel_id=1, source_target_pairs={{0,8},{8,0},{16,24},{24,16},{1,9},{9,1},{17,25},{25,17},{2,10},{10... | collective-permute-start | bytes 147464 | tf_op jit(solution)/shard_map/while/body/eval_jaxpr/ppermute | solution.py:33
  192.5 6.2 %collective-permute-start.4 = (f32[4,3072]{1,0:T(4,128)S(1)}, f32[4,3072]{1,0:T(4,128)S(1)}, u32[]{:S(2)}, u32[]{:S(2)}) collective-permute-start(f32[4,3072]{1,0:T(4,128)S(1)} %fusion.52), channel_id=1, source_target_pairs={{0,6},{2,4},{4,2},{6,0},{1,7},{3,5},{5,3},{7,1},{8,14},{10,12},{12... | collective-permute-start | bytes 147464 | tf_op jit(solution)/shard_map/while/body/eval_jaxpr/ppermute | solution.py:33
  192.6 8.4 %collective-permute-start.5 = (f32[4,3072]{1,0:T(4,128)S(1)}, f32[4,3072]{1,0:T(4,128)S(1)}, u32[]{:S(2)}, u32[]{:S(2)}) collective-permute-start(f32[4,3072]{1,0:T(4,128)S(1)} %fusion.52), channel_id=1, source_target_pairs={{0,4},{2,6},{4,0},{6,2},{1,5},{3,7},{5,1},{7,3},{8,12},{10,14},{12... | collective-permute-start | bytes 147464 | tf_op jit(solution)/shard_map/while/body/eval_jaxpr/ppermute | solution.py:33
  197.8 4.1 %collective-permute-start.6 = (f32[4,3072]{1,0:T(4,128)S(1)}, f32[4,3072]{1,0:T(4,128)S(1)}, u32[]{:S(2)}, u32[]{:S(2)}) collective-permute-start(f32[4,3072]{1,0:T(4,128)S(1)} %fusion.52), channel_id=1, source_target_pairs={{0,2},{2,0},{4,6},{6,4},{1,3},{3,1},{5,7},{7,5},{8,10},{10,8},{12,... | collective-permute-start | bytes 147464 | tf_op jit(solution)/shard_map/while/body/eval_jaxpr/ppermute | solution.py:33
  202.6 1.4 collective-permute-start.7
  206.0 15.8 %slice-start.2 = ((s8[6291456]{0:T(1024)(128)(4,1)}), s8[2097152]{0:T(1024)(128)(4,1)S(1)}, s32[]{:S(2)}) async-start(s8[6291456]{0:T(1024)(128)(4,1)} %bitcast.135), calls=%async_computation.2 | async-start | bytes 4194304 | tf_op jit(solution)/shard_map/while
  216.5 5.2 %slice-start.3 = ((s8[6291456]{0:T(1024)(128)(4,1)}), s8[4194304]{0:T(1024)(128)(4,1)S(1)}, s32[]{:S(2)}) async-start(s8[6291456]{0:T(1024)(128)(4,1)} %bitcast.135), calls=%async_computation.3 | async-start | bytes 8388608 | tf_op jit(solution)/shard_map/while
  218.6 2.7 %collective-permute-start = (f32[2,4,2,128,128]{4,3,1,2,0:T(8,128)S(1)}, f32[2,4,2,128,128]{4,3,1,2,0:T(8,128)S(1)}, u32[]{:S(2)}, u32[]{:S(2)}) collective-permute-start(f32[2,4,2,128,128]{4,3,1,2,0:T(8,128)S(1)} %pad_maximum_fusion.14), channel_id=1, source_target_pairs={{0,1},{1,0},{2,3},{3,2},{4,5},{5,4},{6,7},{7,6},{8,9},{9,8},{10,11... | collective-permute-start | bytes 3145736 | tf_op jit(solution)/shard_map/while/body/eval_jaxpr/ppermute | solution.py:49
  228.5 5.1 %collective-permute-start.1 = (f32[4,3072]{1,0:T(4,128)S(1)}, f32[4,3072]{1,0:T(4,128)S(1)}, u32[]{:S(2)}, u32[]{:S(2)}) collective-permute-start(f32[4,3072]{1,0:T(4,128)S(1)} %select_add_fusion.2), channel_id=1, source_target_pairs={{0,24},{8,16},{16,8},{24,0},{1,25},{9,17},{17,9},{25,1},{2,26},{10... | collective-permute-start | bytes 147464 | tf_op jit(solution)/shard_map/while/body/eval_jaxpr/ppermute | solution.py:33
  231.3 4.1 %collective-permute-start.2 = (f32[4,3072]{1,0:T(4,128)S(1)}, f32[4,3072]{1,0:T(4,128)S(1)}, u32[]{:S(2)}, u32[]{:S(2)}) collective-permute-start(f32[4,3072]{1,0:T(4,128)S(1)} %select_add_fusion.2), channel_id=1, source_target_pairs={{0,16},{8,24},{16,0},{24,8},{1,17},{9,25},{17,1},{25,9},{2,18},{10... | collective-permute-start | bytes 147464 | tf_op jit(solution)/shard_map/while/body/eval_jaxpr/ppermute | solution.py:33
  231.3 4.1 %collective-permute-start.3 = (f32[4,3072]{1,0:T(4,128)S(1)}, f32[4,3072]{1,0:T(4,128)S(1)}, u32[]{:S(2)}, u32[]{:S(2)}) collective-permute-start(f32[4,3072]{1,0:T(4,128)S(1)} %select_add_fusion.2), channel_id=1, source_target_pairs={{0,8},{8,0},{16,24},{24,16},{1,9},{9,1},{17,25},{25,17},{2,10},{10... | collective-permute-start | bytes 147464 | tf_op jit(solution)/shard_map/while/body/eval_jaxpr/ppermute | solution.py:33
  235.5 6.0 %collective-permute-start.4 = (f32[4,3072]{1,0:T(4,128)S(1)}, f32[4,3072]{1,0:T(4,128)S(1)}, u32[]{:S(2)}, u32[]{:S(2)}) collective-permute-start(f32[4,3072]{1,0:T(4,128)S(1)} %fusion.52), channel_id=1, source_target_pairs={{0,6},{2,4},{4,2},{6,0},{1,7},{3,5},{5,3},{7,1},{8,14},{10,12},{12... | collective-permute-start | bytes 147464 | tf_op jit(solution)/shard_map/while/body/eval_jaxpr/ppermute | solution.py:33
  236.5 6.0 %collective-permute-start.5 = (f32[4,3072]{1,0:T(4,128)S(1)}, f32[4,3072]{1,0:T(4,128)S(1)}, u32[]{:S(2)}, u32[]{:S(2)}) collective-permute-start(f32[4,3072]{1,0:T(4,128)S(1)} %fusion.52), channel_id=1, source_target_pairs={{0,4},{2,6},{4,0},{6,2},{1,5},{3,7},{5,1},{7,3},{8,12},{10,14},{12... | collective-permute-start | bytes 147464 | tf_op jit(solution)/shard_map/while/body/eval_jaxpr/ppermute | solution.py:33
  237.5 5.0 %collective-permute-start.6 = (f32[4,3072]{1,0:T(4,128)S(1)}, f32[4,3072]{1,0:T(4,128)S(1)}, u32[]{:S(2)}, u32[]{:S(2)}) collective-permute-start(f32[4,3072]{1,0:T(4,128)S(1)} %fusion.52), channel_id=1, source_target_pairs={{0,2},{2,0},{4,6},{6,4},{1,3},{3,1},{5,7},{7,5},{8,10},{10,8},{12,... | collective-permute-start | bytes 147464 | tf_op jit(solution)/shard_map/while/body/eval_jaxpr/ppermute | solution.py:33
  243.2 1.4 collective-permute-start.7
  (8 other events, 37.2 us)

commit v11 on v10

--- a/solution.py
+++ b/solution.py
@@ -58,7 +58,7 @@
     return jnp.stack([corr_real, corr_imag], axis=1)
 
 
-def pair_products(mine, other, field, tile=1536):
+def pair_products(mine, other, field, tile=3072):
     freq, rows, points = mine.shape
     def kernel(mine_ref, other_ref, field_ref, first_ref, second_ref):
         step = pl.program_id(1)

time: 247 us -> 243 us (0.984)
  Pallas kernels: 21.1 us -> 16.6 us
    pallas_call x2, Pallas kernels: 21.1 us -> 16.6 us  [pair_products(): pl.pallas_call(kernel, grid=(freq, points // tile), in_specs=[spec, spec,...]
where the time goes in v11:
time: 243 us; the launch traced here: 242 us
  waiting for transfers between devices  131 us (54%)
  starting transfers between devices  48.7 us (20%)
  Pallas kernels  16.6 us (7%)
  other arithmetic  15.5 us (6%)
  matrix products  13.2 us (5%)
  local copies, waits for them, and re-layouts  7.52 us (3%)
  between operations  6.1 us (3%)
  loops' own time  3.05 us (1%)
    ppermute x18, waiting for transfers between devices, butterfly_sum(): got.append(lax.ppermute(value, axis, [(i, i ^ mask) for i in range(size)]))  124 us
    ppermute x18, starting transfers between devices, butterfly_sum(): got.append(lax.ppermute(value, axis, [(i, i ^ mask) for i in range(size)]))  39.4 us
    pallas_call x2, Pallas kernels, pair_products(): pl.pallas_call(kernel, grid=(freq, points // tile), in_specs=[spec, spec,...  16.6 us
    dot_general x4, matrix products, point_terms(): jnp.einsum('fab,fbn->fan', adjoint_block(adjoint), right_rows, preferred_...  13.2 us
    ppermute x4, waiting for transfers between devices, swap_add(): return value + lax.ppermute(value, axis, [(0, 1), (1, 0)])  7.83 us
    ppermute x1, starting transfers between devices, pair_body(): received = lax.ppermute(green_panel, axes, panel_moves)  7.58 us
  transfers between devices with their start and end apart: 26, of which 16 were waited for; matrix products, arithmetic and copies ran while one was open for 4% of the time, Pallas kernels for 0%

profile of v11, /device:TPU:0, one launch (start us, length us, event | category | flops | bytes accessed | tf_op | source)
XLA Modules:
  0.0 242.1 jit_solution(14547693161630426235)
XLA Ops:
  0.0 7.6 %collective-permute-start.14 = (bf16[4,2,128,3072]{3,2,1,0:T(8,128)(2,1)}, bf16[4,2,128,3072]{3,2,1,0:T(8,128)(2,1)}, u32[]{:S(2)}, u32[]{:S(2)}) collective-permute-start(bf16[4,2,128,3072]{3,2,1,0:T(8,128)(2,1)} %param.8), channel_id=1, source_target_pairs={{0,2},{12,8},{16,22},{20,18},{10,14},{30,28},{1,3},{13,9},{17,23},... | collective-permute-start | bytes 18874376 | tf_op jit(solution)/shard_map/ppermute | solution.py:193
  8.5 3.6 %collective-permute-start.9 = (f32[4,3072]{1,0:T(4,128)S(1)}, f32[4,3072]{1,0:T(4,128)S(1)}, u32[]{:S(2)}, u32[]{:S(2)}) collective-permute-start(f32[4,3072]{1,0:T(4,128)S(1)} %dynamic_update_slice.3), channel_id=1, source_target_pairs={{0,16},{8,24},{16,0},{24,8},{1,17},{9,25},{17,1},{25,9},{2,18},{10... | collective-permute-start | bytes 147464 | tf_op jit(solution)/shard_map/ppermute | solution.py:33
  12.1 1.4 collective-permute-start.10
  15.2 1.9 maximum_bitcast_fusion.2
  27.5 1.4 collective-permute-start.11
  28.9 4.2 %collective-permute-start.12 = (f32[4,3072]{1,0:T(4,128)S(1)}, f32[4,3072]{1,0:T(4,128)S(1)}, u32[]{:S(2)}, u32[]{:S(2)}) collective-permute-start(f32[4,3072]{1,0:T(4,128)S(1)} %fusion.34), channel_id=1, source_target_pairs={{0,4},{2,6},{4,0},{6,2},{1,5},{3,7},{5,1},{7,3},{8,12},{10,14},{12... | collective-permute-start | bytes 147464 | tf_op jit(solution)/shard_map/ppermute | solution.py:33
  33.5 108.5 %collective-permute-done.11 = f32[4,3072]{1,0:T(4,128)S(1)} collective-permute-done((f32[4,3072]{1,0:T(4,128)S(1)}, f32[4,3072]{1,0:T(4,128)S(1)}, u32[]{:S(2)}, u32[]{:S(2)}) %collective-permute-start.11) | collective-permute-done | bytes 49184 | tf_op jit(solution)/shard_map/ppermute | solution.py:33
  143.3 1.4 pad_maximum_fusion.3
  146.5 3.5 %broadcast_select_fusion = bf16[4,2,128,3072]{3,2,1,0:T(8,128)(2,1)} fusion(bf16[4,2,128,3072]{3,2,1,0:T(8,128)(2,1)S(1)} %bitcast.134, bf16[4,2,128,3072]{3,2,1,0:T(8,128)(2,1)} %collective-permute-done.14, pred[]{:T(512)} %bitcast.42), kind=kLoop, calls=%fused_computation.49 | loop fusion | flops 3145728 | bytes 18874368 | tf_op jit(solution)/shard_map/jit(_where)/select_n | solution.py:214
  150.0 91.4 %while.13 = (s32[]{:T(128)}, f32[4,3072]{1,0:T(4,128)S(1)}, pred[]{:T(512)}, bf16[4,256,3072]{2,1,0:T(8,128)(2,1)}, f32[1,128,128]{2,1,0:T(8,128)S(1)}, /*index=...) while((s32[]{:T(128)}, f32[4,3072]{1,0:T(4,128)S(1)}, ...), condition=%wide.region_4.5_spmd, body=%wide.region_0.4_spmd.sunk | while | flops 3247300608 | bytes 90244464 | solution.py:249
  150.6 8.3 %eval_jaxpr.5 = (f32[4,256,256]{2,1,0:T(8,128)}, f32[4,256,256]{2,1,0:T(8,128)}) custom-call(bf16[4,256,3072]{2,1,0:T(8,128)(2,1)} %get-tuple-element.356.mine_ref, bf16[4,256,3072]{2,1,0:T(8,128)(2,1)} %get-tuple-element.358.other_ref, f32[4,1,3072]{2,1,0:T(1,128)} %broadcast_in_dim.36.field_ref), custom_call_target="tpu_custom_call" | custom-call | tf_op jit(solution)/shard_map/while/body/eval_jaxpr/pallas_call | solution.py:79
  158.9 1.8 add_bitcast_fusion.4
  161.0 2.6 %collective-permute-done = f32[2,4,2,128,128]{4,3,1,2,0:T(8,128)S(1)} collective-permute-done((f32[2,4,2,128,128]{4,3,1,2,0:T(8,128)S(1)}, f32[2,4,2,128,128]{4,3,1,2,0:T(8,128)S(1)}, u32[]{:S(2)}, u32[]{:S(2)}) %collective-permute-start) | collective-permute-done | bytes 1048608 | tf_op jit(solution)/shard_map/while/body/eval_jaxpr/ppermute | solution.py:49
  164.2 4.8 %multiply_reduce_fusion.7 = f32[4,3072]{1,0:T(4,128)S(1)} fusion(bf16[4,256,3072]{2,1,0:T(8,128)(2,1)S(1)} %bitcast.136, bf16[4,256,3072]{2,1,0:T(8,128)(2,1)} %get-tuple-element.358.other_ref, bf16[4,128,128]{2,1,0:T(8,128)(2,1)S(1)} %get-tuple-element.311, bf16[4,128,128]{2,1,0:T(8,128)(2,1)S(1)} %get-tuple-element.312, ...), kind=kOutput, calls=%fused_computation.1.clone.1 | convolution fusion | flops 1622134784 | bytes 13025280 | tf_op jit(solution)/shard_map/while/body/eval_jaxpr/fab,fbn->fan/dot_general | solution.py:104
  169.0 1.8 multiply_reduce_fusion.6
  170.9 8.2 %collective-permute-start.1 = (f32[4,3072]{1,0:T(4,128)S(1)}, f32[4,3072]{1,0:T(4,128)S(1)}, u32[]{:S(2)}, u32[]{:S(2)}) collective-permute-start(f32[4,3072]{1,0:T(4,128)S(1)} %select_add_fusion.2), channel_id=1, source_target_pairs={{0,24},{8,16},{16,8},{24,0},{1,25},{9,17},{17,9},{25,1},{2,26},{10... | collective-permute-start | bytes 147464 | tf_op jit(solution)/shard_map/while/body/eval_jaxpr/ppermute | solution.py:33
  179.1 7.0 %collective-permute-start.2 = (f32[4,3072]{1,0:T(4,128)S(1)}, f32[4,3072]{1,0:T(4,128)S(1)}, u32[]{:S(2)}, u32[]{:S(2)}) collective-permute-start(f32[4,3072]{1,0:T(4,128)S(1)} %select_add_fusion.2), channel_id=1, source_target_pairs={{0,16},{8,24},{16,0},{24,8},{1,17},{9,25},{17,1},{25,9},{2,18},{10... | collective-permute-start | bytes 147464 | tf_op jit(solution)/shard_map/while/body/eval_jaxpr/ppermute | solution.py:33
  186.1 2.1 collective-permute-done.2
  188.1 2.0 collective-permute-done.3
  190.3 5.2 %collective-permute-start.5 = (f32[4,3072]{1,0:T(4,128)S(1)}, f32[4,3072]{1,0:T(4,128)S(1)}, u32[]{:S(2)}, u32[]{:S(2)}) collective-permute-start(f32[4,3072]{1,0:T(4,128)S(1)} %fusion.52), channel_id=1, source_target_pairs={{0,4},{2,6},{4,0},{6,2},{1,5},{3,7},{5,1},{7,3},{8,12},{10,14},{12... | collective-permute-start | bytes 147464 | tf_op jit(solution)/shard_map/while/body/eval_jaxpr/ppermute | solution.py:33
  196.4 2.3 collective-permute-done.5
  200.4 1.3 collective-permute-done.7
  203.7 8.3 %eval_jaxpr.5 = (f32[4,256,256]{2,1,0:T(8,128)}, f32[4,256,256]{2,1,0:T(8,128)}) custom-call(bf16[4,256,3072]{2,1,0:T(8,128)(2,1)} %get-tuple-element.356.mine_ref, bf16[4,256,3072]{2,1,0:T(8,128)(2,1)} %get-tuple-element.358.other_ref, f32[4,1,3072]{2,1,0:T(1,128)} %broadcast_in_dim.36.field_ref), custom_call_target="tpu_custom_call" | custom-call | tf_op jit(solution)/shard_map/while/body/eval_jaxpr/pallas_call | solution.py:79
  212.0 1.8 add_bitcast_fusion.4
  214.3 2.5 %collective-permute-done = f32[2,4,2,128,128]{4,3,1,2,0:T(8,128)S(1)} collective-permute-done((f32[2,4,2,128,128]{4,3,1,2,0:T(8,128)S(1)}, f32[2,4,2,128,128]{4,3,1,2,0:T(8,128)S(1)}, u32[]{:S(2)}, u32[]{:S(2)}) %collective-permute-start) | collective-permute-done | bytes 1048608 | tf_op jit(solution)/shard_map/while/body/eval_jaxpr/ppermute | solution.py:49
  217.2 4.8 %multiply_reduce_fusion.7 = f32[4,3072]{1,0:T(4,128)S(1)} fusion(bf16[4,256,3072]{2,1,0:T(8,128)(2,1)S(1)} %bitcast.136, bf16[4,256,3072]{2,1,0:T(8,128)(2,1)} %get-tuple-element.358.other_ref, bf16[4,128,128]{2,1,0:T(8,128)(2,1)S(1)} %get-tuple-element.311, bf16[4,128,128]{2,1,0:T(8,128)(2,1)S(1)} %get-tuple-element.312, ...), kind=kOutput, calls=%fused_computation.1.clone.1 | convolution fusion | flops 1622134784 | bytes 13025280 | tf_op jit(solution)/shard_map/while/body/eval_jaxpr/fab,fbn->fan/dot_general | solution.py:104
  222.1 1.8 multiply_reduce_fusion.6
  223.9 2.8 %collective-permute-start.1 = (f32[4,3072]{1,0:T(4,128)S(1)}, f32[4,3072]{1,0:T(4,128)S(1)}, u32[]{:S(2)}, u32[]{:S(2)}) collective-permute-start(f32[4,3072]{1,0:T(4,128)S(1)} %select_add_fusion.2), channel_id=1, source_target_pairs={{0,24},{8,16},{16,8},{24,0},{1,25},{9,17},{17,9},{25,1},{2,26},{10... | collective-permute-start | bytes 147464 | tf_op jit(solution)/shard_map/while/body/eval_jaxpr/ppermute | solution.py:33
  227.5 1.5 collective-permute-done.1
  229.0 1.8 collective-permute-done.2
  233.0 2.4 collective-permute-start.6
  235.4 1.5 collective-permute-done.4
  (122 shorter events, 22.8 us)
Async XLA Ops:
  0.0 144.7 %collective-permute-start.14 = (bf16[4,2,128,3072]{3,2,1,0:T(8,128)(2,1)}, bf16[4,2,128,3072]{3,2,1,0:T(8,128)(2,1)}, u32[]{:S(2)}, u32[]{:S(2)}) collective-permute-start(bf16[4,2,128,3072]{3,2,1,0:T(8,128)(2,1)} %param.8), channel_id=1, source_target_pairs={{0,2},{12,8},{16,22},{20,18},{10,14},{30,28},{1,3},{13,9},{17,23},... | collective-permute-start | bytes 18874376 | tf_op jit(solution)/shard_map/ppermute | solution.py:193
  8.4 18.2 %collective-permute-start.8 = (f32[4,3072]{1,0:T(4,128)S(1)}, f32[4,3072]{1,0:T(4,128)S(1)}, u32[]{:S(2)}, u32[]{:S(2)}) collective-permute-start(f32[4,3072]{1,0:T(4,128)S(1)} %dynamic_update_slice.3), channel_id=1, source_target_pairs={{0,8},{8,0},{16,24},{24,16},{1,9},{9,1},{17,25},{25,17},{2,10},{10... | collective-permute-start | bytes 147464 | tf_op jit(solution)/shard_map/ppermute | solution.py:33
  8.5 18.8 %collective-permute-start.9 = (f32[4,3072]{1,0:T(4,128)S(1)}, f32[4,3072]{1,0:T(4,128)S(1)}, u32[]{:S(2)}, u32[]{:S(2)}) collective-permute-start(f32[4,3072]{1,0:T(4,128)S(1)} %dynamic_update_slice.3), channel_id=1, source_target_pairs={{0,16},{8,24},{16,0},{24,8},{1,17},{9,25},{17,1},{25,9},{2,18},{10... | collective-permute-start | bytes 147464 | tf_op jit(solution)/shard_map/ppermute | solution.py:33
  12.1 15.2 %collective-permute-start.10 = (f32[4,3072]{1,0:T(4,128)S(1)}, f32[4,3072]{1,0:T(4,128)S(1)}, u32[]{:S(2)}, u32[]{:S(2)}) collective-permute-start(f32[4,3072]{1,0:T(4,128)S(1)} %dynamic_update_slice.3), channel_id=1, source_target_pairs={{0,24},{8,16},{16,8},{24,0},{1,25},{9,17},{17,9},{25,1},{2,26},{10... | collective-permute-start | bytes 147464 | tf_op jit(solution)/shard_map/ppermute | solution.py:33
  26.0 7.2 %collective-permute-start.15 = (f32[5,128,128]{2,1,0:T(8,128)S(1)}, f32[5,128,128]{2,1,0:T(8,128)S(1)}, u32[]{:S(2)}, u32[]{:S(2)}) collective-permute-start(f32[5,128,128]{2,1,0:T(8,128)S(1)} %fusion.29), channel_id=1, source_target_pairs={{8,2},{4,8},{24,22},{12,18},{26,14},{22,28},{9,3},{5,9},{25,23},{1... | collective-permute-start | bytes 983048 | tf_op jit(solution)/shard_map/ppermute | solution.py:205
  26.7 6.7 %collective-permute-start.16 = (f32[5,128,128]{2,1,0:T(8,128)S(1)}, f32[5,128,128]{2,1,0:T(8,128)S(1)}, u32[]{:S(2)}, u32[]{:S(2)}) collective-permute-start(f32[5,128,128]{2,1,0:T(8,128)S(1)} %fusion.29), channel_id=1, source_target_pairs={{16,8},{6,22},{17,9},{7,23}} | collective-permute-start | bytes 983048 | tf_op jit(solution)/shard_map/ppermute | solution.py:205
  27.5 114.6 %collective-permute-start.11 = (f32[4,3072]{1,0:T(4,128)S(1)}, f32[4,3072]{1,0:T(4,128)S(1)}, u32[]{:S(2)}, u32[]{:S(2)}) collective-permute-start(f32[4,3072]{1,0:T(4,128)S(1)} %fusion.34), channel_id=1, source_target_pairs={{0,2},{2,0},{4,6},{6,4},{1,3},{3,1},{5,7},{7,5},{8,10},{10,8},{12,... | collective-permute-start | bytes 147464 | tf_op jit(solution)/shard_map/ppermute | solution.py:33
  28.9 117.6 %slice-start = ((s8[6291456]{0:T(1024)(128)(4,1)}), s8[4194304]{0:T(1024)(128)(4,1)S(1)}, s32[]{:S(2)}) async-start(s8[6291456]{0:T(1024)(128)(4,1)} %bitcast.133), calls=%async_computation | async-start | bytes 8388608
  28.9 113.7 %collective-permute-start.12 = (f32[4,3072]{1,0:T(4,128)S(1)}, f32[4,3072]{1,0:T(4,128)S(1)}, u32[]{:S(2)}, u32[]{:S(2)}) collective-permute-start(f32[4,3072]{1,0:T(4,128)S(1)} %fusion.34), channel_id=1, source_target_pairs={{0,4},{2,6},{4,0},{6,2},{1,5},{3,7},{5,1},{7,3},{8,12},{10,14},{12... | collective-permute-start | bytes 147464 | tf_op jit(solution)/shard_map/ppermute | solution.py:33
  33.1 110.0 %collective-permute-start.13 = (f32[4,3072]{1,0:T(4,128)S(1)}, f32[4,3072]{1,0:T(4,128)S(1)}, u32[]{:S(2)}, u32[]{:S(2)}) collective-permute-start(f32[4,3072]{1,0:T(4,128)S(1)} %fusion.34), channel_id=1, source_target_pairs={{0,6},{2,4},{4,2},{6,0},{1,7},{3,5},{5,3},{7,1},{8,14},{10,12},{12... | collective-permute-start | bytes 147464 | tf_op jit(solution)/shard_map/ppermute | solution.py:33
  33.4 109.8 %collective-permute-start.17 = (f32[2,5,128,128]{3,2,1,0:T(8,128)S(1)}, f32[2,5,128,128]{3,2,1,0:T(8,128)S(1)}, u32[]{:S(2)}, u32[]{:S(2)}) collective-permute-start(f32[2,5,128,128]{3,2,1,0:T(8,128)S(1)} %pad_maximum_fusion.8), channel_id=1, source_target_pairs={{0,1},{1,0},{2,3},{3,2},{4,5},{5,4},{6,7},{7,6},{8,9},{9,8},{10,11... | collective-permute-start | bytes 1966088 | tf_op jit(solution)/shard_map/ppermute | solution.py:206
  150.6 13.5 %slice-start.2 = ((s8[6291456]{0:T(1024)(128)(4,1)}), s8[2097152]{0:T(1024)(128)(4,1)S(1)}, s32[]{:S(2)}) async-start(s8[6291456]{0:T(1024)(128)(4,1)} %bitcast.135), calls=%async_computation.2 | async-start | bytes 4194304 | tf_op jit(solution)/shard_map/while
  158.9 5.2 %slice-start.3 = ((s8[6291456]{0:T(1024)(128)(4,1)}), s8[4194304]{0:T(1024)(128)(4,1)S(1)}, s32[]{:S(2)}) async-start(s8[6291456]{0:T(1024)(128)(4,1)} %bitcast.135), calls=%async_computation.3 | async-start | bytes 8388608 | tf_op jit(solution)/shard_map/while
  160.9 2.7 %collective-permute-start = (f32[2,4,2,128,128]{4,3,1,2,0:T(8,128)S(1)}, f32[2,4,2,128,128]{4,3,1,2,0:T(8,128)S(1)}, u32[]{:S(2)}, u32[]{:S(2)}) collective-permute-start(f32[2,4,2,128,128]{4,3,1,2,0:T(8,128)S(1)} %pad_maximum_fusion.14), channel_id=1, source_target_pairs={{0,1},{1,0},{2,3},{3,2},{4,5},{5,4},{6,7},{7,6},{8,9},{9,8},{10,11... | collective-permute-start | bytes 3145736 | tf_op jit(solution)/shard_map/while/body/eval_jaxpr/ppermute | solution.py:49
  170.9 15.2 %collective-permute-start.1 = (f32[4,3072]{1,0:T(4,128)S(1)}, f32[4,3072]{1,0:T(4,128)S(1)}, u32[]{:S(2)}, u32[]{:S(2)}) collective-permute-start(f32[4,3072]{1,0:T(4,128)S(1)} %select_add_fusion.2), channel_id=1, source_target_pairs={{0,24},{8,16},{16,8},{24,0},{1,25},{9,17},{17,9},{25,1},{2,26},{10... | collective-permute-start | bytes 147464 | tf_op jit(solution)/shard_map/while/body/eval_jaxpr/ppermute | solution.py:33
  179.1 9.1 %collective-permute-start.2 = (f32[4,3072]{1,0:T(4,128)S(1)}, f32[4,3072]{1,0:T(4,128)S(1)}, u32[]{:S(2)}, u32[]{:S(2)}) collective-permute-start(f32[4,3072]{1,0:T(4,128)S(1)} %select_add_fusion.2), channel_id=1, source_target_pairs={{0,16},{8,24},{16,0},{24,8},{1,17},{9,25},{17,1},{25,9},{2,18},{10... | collective-permute-start | bytes 147464 | tf_op jit(solution)/shard_map/while/body/eval_jaxpr/ppermute | solution.py:33
  186.1 4.1 %collective-permute-start.3 = (f32[4,3072]{1,0:T(4,128)S(1)}, f32[4,3072]{1,0:T(4,128)S(1)}, u32[]{:S(2)}, u32[]{:S(2)}) collective-permute-start(f32[4,3072]{1,0:T(4,128)S(1)} %select_add_fusion.2), channel_id=1, source_target_pairs={{0,8},{8,0},{16,24},{24,16},{1,9},{9,1},{17,25},{25,17},{2,10},{10... | collective-permute-start | bytes 147464 | tf_op jit(solution)/shard_map/while/body/eval_jaxpr/ppermute | solution.py:33
  190.2 6.2 %collective-permute-start.4 = (f32[4,3072]{1,0:T(4,128)S(1)}, f32[4,3072]{1,0:T(4,128)S(1)}, u32[]{:S(2)}, u32[]{:S(2)}) collective-permute-start(f32[4,3072]{1,0:T(4,128)S(1)} %fusion.52), channel_id=1, source_target_pairs={{0,6},{2,4},{4,2},{6,0},{1,7},{3,5},{5,3},{7,1},{8,14},{10,12},{12... | collective-permute-start | bytes 147464 | tf_op jit(solution)/shard_map/while/body/eval_jaxpr/ppermute | solution.py:33
  190.3 8.4 %collective-permute-start.5 = (f32[4,3072]{1,0:T(4,128)S(1)}, f32[4,3072]{1,0:T(4,128)S(1)}, u32[]{:S(2)}, u32[]{:S(2)}) collective-permute-start(f32[4,3072]{1,0:T(4,128)S(1)} %fusion.52), channel_id=1, source_target_pairs={{0,4},{2,6},{4,0},{6,2},{1,5},{3,7},{5,1},{7,3},{8,12},{10,14},{12... | collective-permute-start | bytes 147464 | tf_op jit(solution)/shard_map/while/body/eval_jaxpr/ppermute | solution.py:33
  195.5 4.1 %collective-permute-start.6 = (f32[4,3072]{1,0:T(4,128)S(1)}, f32[4,3072]{1,0:T(4,128)S(1)}, u32[]{:S(2)}, u32[]{:S(2)}) collective-permute-start(f32[4,3072]{1,0:T(4,128)S(1)} %fusion.52), channel_id=1, source_target_pairs={{0,2},{2,0},{4,6},{6,4},{1,3},{3,1},{5,7},{7,5},{8,10},{10,8},{12,... | collective-permute-start | bytes 147464 | tf_op jit(solution)/shard_map/while/body/eval_jaxpr/ppermute | solution.py:33
  200.3 1.4 collective-permute-start.7
  203.7 13.5 %slice-start.2 = ((s8[6291456]{0:T(1024)(128)(4,1)}), s8[2097152]{0:T(1024)(128)(4,1)S(1)}, s32[]{:S(2)}) async-start(s8[6291456]{0:T(1024)(128)(4,1)} %bitcast.135), calls=%async_computation.2 | async-start | bytes 4194304 | tf_op jit(solution)/shard_map/while
  212.0 4.9 %copy-start.1 = (f32[4,2,128,128]{3,2,0,1:T(8,128)S(1)}, f32[4,2,128,128]{3,2,0,1:T(8,128)}, u32[]{:S(2)}) copy-start(f32[4,2,128,128]{3,2,0,1:T(8,128)} %get-tuple-element.362) | copy-start | bytes 1572868 | tf_op jit(solution)/shard_map/while
  212.0 5.2 %slice-start.3 = ((s8[6291456]{0:T(1024)(128)(4,1)}), s8[4194304]{0:T(1024)(128)(4,1)S(1)}, s32[]{:S(2)}) async-start(s8[6291456]{0:T(1024)(128)(4,1)} %bitcast.135), calls=%async_computation.3 | async-start | bytes 8388608 | tf_op jit(solution)/shard_map/while
  214.0 2.7 %collective-permute-start = (f32[2,4,2,128,128]{4,3,1,2,0:T(8,128)S(1)}, f32[2,4,2,128,128]{4,3,1,2,0:T(8,128)S(1)}, u32[]{:S(2)}, u32[]{:S(2)}) collective-permute-start(f32[2,4,2,128,128]{4,3,1,2,0:T(8,128)S(1)} %pad_maximum_fusion.14), channel_id=1, source_target_pairs={{0,1},{1,0},{2,3},{3,2},{4,5},{5,4},{6,7},{7,6},{8,9},{9,8},{10,11... | collective-permute-start | bytes 3145736 | tf_op jit(solution)/shard_map/while/body/eval_jaxpr/ppermute | solution.py:49
  223.9 5.1 %collective-permute-start.1 = (f32[4,3072]{1,0:T(4,128)S(1)}, f32[4,3072]{1,0:T(4,128)S(1)}, u32[]{:S(2)}, u32[]{:S(2)}) collective-permute-start(f32[4,3072]{1,0:T(4,128)S(1)} %select_add_fusion.2), channel_id=1, source_target_pairs={{0,24},{8,16},{16,8},{24,0},{1,25},{9,17},{17,9},{25,1},{2,26},{10... | collective-permute-start | bytes 147464 | tf_op jit(solution)/shard_map/while/body/eval_jaxpr/ppermute | solution.py:33
  226.7 4.1 %collective-permute-start.2 = (f32[4,3072]{1,0:T(4,128)S(1)}, f32[4,3072]{1,0:T(4,128)S(1)}, u32[]{:S(2)}, u32[]{:S(2)}) collective-permute-start(f32[4,3072]{1,0:T(4,128)S(1)} %select_add_fusion.2), channel_id=1, source_target_pairs={{0,16},{8,24},{16,0},{24,8},{1,17},{9,25},{17,1},{25,9},{2,18},{10... | collective-permute-start | bytes 147464 | tf_op jit(solution)/shard_map/while/body/eval_jaxpr/ppermute | solution.py:33
  226.7 4.1 %collective-permute-start.3 = (f32[4,3072]{1,0:T(4,128)S(1)}, f32[4,3072]{1,0:T(4,128)S(1)}, u32[]{:S(2)}, u32[]{:S(2)}) collective-permute-start(f32[4,3072]{1,0:T(4,128)S(1)} %select_add_fusion.2), channel_id=1, source_target_pairs={{0,8},{8,0},{16,24},{24,16},{1,9},{9,1},{17,25},{25,17},{2,10},{10... | collective-permute-start | bytes 147464 | tf_op jit(solution)/shard_map/while/body/eval_jaxpr/ppermute | solution.py:33
  230.9 6.0 %collective-permute-start.4 = (f32[4,3072]{1,0:T(4,128)S(1)}, f32[4,3072]{1,0:T(4,128)S(1)}, u32[]{:S(2)}, u32[]{:S(2)}) collective-permute-start(f32[4,3072]{1,0:T(4,128)S(1)} %fusion.52), channel_id=1, source_target_pairs={{0,6},{2,4},{4,2},{6,0},{1,7},{3,5},{5,3},{7,1},{8,14},{10,12},{12... | collective-permute-start | bytes 147464 | tf_op jit(solution)/shard_map/while/body/eval_jaxpr/ppermute | solution.py:33
  232.0 6.0 %collective-permute-start.5 = (f32[4,3072]{1,0:T(4,128)S(1)}, f32[4,3072]{1,0:T(4,128)S(1)}, u32[]{:S(2)}, u32[]{:S(2)}) collective-permute-start(f32[4,3072]{1,0:T(4,128)S(1)} %fusion.52), channel_id=1, source_target_pairs={{0,4},{2,6},{4,0},{6,2},{1,5},{3,7},{5,1},{7,3},{8,12},{10,14},{12... | collective-permute-start | bytes 147464 | tf_op jit(solution)/shard_map/while/body/eval_jaxpr/ppermute | solution.py:33
  233.0 5.0 %collective-permute-start.6 = (f32[4,3072]{1,0:T(4,128)S(1)}, f32[4,3072]{1,0:T(4,128)S(1)}, u32[]{:S(2)}, u32[]{:S(2)}) collective-permute-start(f32[4,3072]{1,0:T(4,128)S(1)} %fusion.52), channel_id=1, source_target_pairs={{0,2},{2,0},{4,6},{6,4},{1,3},{3,1},{5,7},{7,5},{8,10},{10,8},{12,... | collective-permute-start | bytes 147464 | tf_op jit(solution)/shard_map/while/body/eval_jaxpr/ppermute | solution.py:33
  238.7 1.4 collective-permute-start.7
  (8 other events, 37.2 us)

commit v12 on v11

--- a/solution.py
+++ b/solution.py
@@ -211,7 +211,7 @@
     )[:, :planes]
     arrived = jnp.concatenate([own_block[None], joined], axis=0)
     received, arrived = lax.optimization_barrier((received, arrived))
-    other = jnp.where(is_diag, green_panel, received)
+    other = lax.cond(is_diag, lambda: green_panel, lambda: received)
     mine_rows = green_panel.reshape(freq_count, 2 * span_j, local_pts)
     other_rows = other.reshape(freq_count, 2 * span_j, local_pts)
     moved_table = jnp.array(moved, jnp.int32)[slot]

time: 243 us -> 242 us (level)
  other arithmetic: 15.5 us -> 8.87 us
  matrix products: 13.2 us -> 18.5 us
  starting transfers between devices: 48.7 us -> 44.7 us
  waiting for transfers between devices: 131 us -> 134 us
    dot_general x4, matrix products: 13.2 us -> 18.5 us  [point_terms(): jnp.einsum('fab,fbn->fan', adjoint_block(adjoint), right_rows, preferred_...]
    ppermute x18, starting transfers between devices: 39.4 us -> 35.2 us  [butterfly_sum(): got.append(lax.ppermute(value, axis, [(i, i ^ mask) for i in range(size)]))]
    select_n x1 -> x0, other arithmetic: 3.46 us -> none  [pair_body(): other = jnp.where(is_diag, green_panel, received)]
    ppermute x18, waiting for transfers between devices: 124 us -> 127 us  [butterfly_sum(): got.append(lax.ppermute(value, axis, [(i, i ^ mask) for i in range(size)]))]
    cond x0 -> x1, local copies, waits for them, and re-layouts: none -> 2.63 us
  transfers between devices with their start and end apart: 26 -> 26, of which waited for: 16 -> 15; matrix products, arithmetic and copies ran while one was open for 4% -> 2% of each run, Pallas kernels for 0% -> 0%
where the time goes in v12:
time: 242 us; the launch traced here: 241 us
  waiting for transfers between devices  134 us (55%)
  starting transfers between devices  44.7 us (18%)
  matrix products  18.5 us (8%)
  Pallas kernels  16.6 us (7%)
  local copies, waits for them, and re-layouts  9.12 us (4%)
  other arithmetic  8.87 us (4%)
  between operations  5.94 us (2%)
  loops' own time  3.07 us (1%)
    ppermute x18, waiting for transfers between devices, butterfly_sum(): got.append(lax.ppermute(value, axis, [(i, i ^ mask) for i in range(size)]))  127 us
    ppermute x18, starting transfers between devices, butterfly_sum(): got.append(lax.ppermute(value, axis, [(i, i ^ mask) for i in range(size)]))  35.2 us
    dot_general x4, matrix products, point_terms(): jnp.einsum('fab,fbn->fan', adjoint_block(adjoint), right_rows, preferred_...  18.5 us
    pallas_call x2, Pallas kernels, pair_products(): pl.pallas_call(kernel, grid=(freq, points // tile), in_specs=[spec, spec,...  16.6 us
    ppermute x4, waiting for transfers between devices, swap_add(): return value + lax.ppermute(value, axis, [(0, 1), (1, 0)])  7.81 us
    ppermute x1, starting transfers between devices, pair_body(): received = lax.ppermute(green_panel, axes, panel_moves)  7.72 us
  transfers between devices with their start and end apart: 26, of which 15 were waited for; matrix products, arithmetic and copies ran while one was open for 2% of the time, Pallas kernels for 0%

profile of v12, /device:TPU:0, one launch (start us, length us, event | category | flops | bytes accessed | tf_op | source)
XLA Modules:
  0.0 241.2 jit_solution(1966364021978823314)
XLA Ops:
  0.0 7.7 %collective-permute-start.14 = (bf16[4,2,128,3072]{3,2,1,0:T(8,128)(2,1)}, bf16[4,2,128,3072]{3,2,1,0:T(8,128)(2,1)}, u32[]{:S(2)}, u32[]{:S(2)}) collective-permute-start(bf16[4,2,128,3072]{3,2,1,0:T(8,128)(2,1)} %param.10), channel_id=1, source_target_pairs={{0,2},{12,8},{16,22},{20,18},{10,14},{30,28},{1,3},{13,9},{17,23},... | collective-permute-start | bytes 18874376 | tf_op jit(solution)/shard_map/ppermute | solution.py:193
  8.7 3.6 %collective-permute-start.9 = (f32[4,3072]{1,0:T(4,128)S(1)}, f32[4,3072]{1,0:T(4,128)S(1)}, u32[]{:S(2)}, u32[]{:S(2)}) collective-permute-start(f32[4,3072]{1,0:T(4,128)S(1)} %dynamic_update_slice.3), channel_id=1, source_target_pairs={{0,16},{8,24},{16,0},{24,8},{1,17},{9,25},{17,1},{25,9},{2,18},{10... | collective-permute-start | bytes 147464 | tf_op jit(solution)/shard_map/ppermute | solution.py:33
  12.3 1.4 collective-permute-start.10
  25.1 1.4 collective-permute-start.11
  26.5 4.2 %collective-permute-start.12 = (f32[4,3072]{1,0:T(4,128)S(1)}, f32[4,3072]{1,0:T(4,128)S(1)}, u32[]{:S(2)}, u32[]{:S(2)}) collective-permute-start(f32[4,3072]{1,0:T(4,128)S(1)} %fusion.34), channel_id=1, source_target_pairs={{0,4},{2,6},{4,0},{6,2},{1,5},{3,7},{5,1},{7,3},{8,12},{10,14},{12... | collective-permute-start | bytes 147464 | tf_op jit(solution)/shard_map/ppermute | solution.py:33
  31.1 111.1 %collective-permute-done.11 = f32[4,3072]{1,0:T(4,128)S(1)} collective-permute-done((f32[4,3072]{1,0:T(4,128)S(1)}, f32[4,3072]{1,0:T(4,128)S(1)}, u32[]{:S(2)}, u32[]{:S(2)}) %collective-permute-start.11) | collective-permute-done | bytes 49184 | tf_op jit(solution)/shard_map/ppermute | solution.py:33
  145.0 2.6 %conditional.1 = (bf16[4,256,3072]{2,1,0:T(8,128)(2,1)}) conditional(s32[]{:T(128)} %bitcast.44, bf16[4,2,128,3072]{3,2,1,0:T(8,128)(2,1)} %collective-permute-done.14, bf16[4,2,128,3072]{3,2,1,0:T(8,128)(2,1)S(1)} %bitcast.135), branch_computations={%region_0.1_spmd, %region_1.2_spmd} | conditional | bytes 12582920 | solution.py:214
  145.0 2.6 %copy.11 = bf16[4,256,3072]{2,1,0:T(8,128)(2,1)} copy(bf16[4,256,3072]{2,1,0:T(8,128)(2,1)S(1)} %bitcast.136) | data formatting | bytes 12582912 | tf_op jit(solution)/shard_map/cond
  147.7 92.8 %while.13 = (s32[]{:T(128)}, f32[4,3072]{1,0:T(4,128)S(1)}, pred[]{:T(512)}, bf16[4,256,3072]{2,1,0:T(8,128)(2,1)}, f32[1,128,128]{2,1,0:T(8,128)S(1)}, /*index=...) while((s32[]{:T(128)}, f32[4,3072]{1,0:T(4,128)S(1)}, ...), condition=%wide.region_6.7_spmd, body=%wide.region_2.6_spmd.sunk | while | flops 3247300608 | bytes 67175664 | solution.py:249
  148.3 8.3 %eval_jaxpr.5 = (f32[4,256,256]{2,1,0:T(8,128)}, f32[4,256,256]{2,1,0:T(8,128)}) custom-call(bf16[4,256,3072]{2,1,0:T(8,128)(2,1)} %get-tuple-element.372.mine_ref, bf16[4,256,3072]{2,1,0:T(8,128)(2,1)} %get-tuple-element.374.other_ref, f32[4,1,3072]{2,1,0:T(1,128)} %broadcast_in_dim.36.field_ref), custom_call_target="tpu_custom_call" | custom-call | tf_op jit(solution)/shard_map/while/body/eval_jaxpr/pallas_call | solution.py:79
  156.6 1.8 add_bitcast_fusion.4
  158.7 2.6 %collective-permute-done = f32[2,4,2,128,128]{4,3,1,2,0:T(8,128)S(1)} collective-permute-done((f32[2,4,2,128,128]{4,3,1,2,0:T(8,128)S(1)}, f32[2,4,2,128,128]{4,3,1,2,0:T(8,128)S(1)}, u32[]{:S(2)}, u32[]{:S(2)}) %collective-permute-start) | collective-permute-done | bytes 1048608 | tf_op jit(solution)/shard_map/while/body/eval_jaxpr/ppermute | solution.py:49
  161.8 4.6 %multiply_reduce_fusion.7 = f32[4,3072]{1,0:T(4,128)S(1)} fusion(bf16[4,256,3072]{2,1,0:T(8,128)(2,1)S(1)} %bitcast.138, bf16[4,256,3072]{2,1,0:T(8,128)(2,1)} %get-tuple-element.374.other_ref, bf16[4,128,128]{2,1,0:T(8,128)(2,1)S(1)} %get-tuple-element.325, bf16[4,128,128]{2,1,0:T(8,128)(2,1)S(1)} %get-tuple-element.326, ...), kind=kOutput, calls=%fused_computation.1.clone.1 | convolution fusion | flops 1622134784 | bytes 13025280 | tf_op jit(solution)/shard_map/while/body/eval_jaxpr/fab,fbn->fan/dot_general | solution.py:104
  166.4 4.6 %multiply_reduce_fusion.6 = f32[4,3072]{1,0:T(4,128)S(1)} fusion(bf16[4,256,3072]{2,1,0:T(8,128)(2,1)} %get-tuple-element.374.other_ref, bf16[4,256,3072]{2,1,0:T(8,128)(2,1)S(1)} %bitcast.138, bf16[4,128,128]{2,1,0:T(8,128)(2,1)S(1)} %get-tuple-element.322, bf16[4,128,128]{2,1,0:T(8,128)(2,1)S(1)} %get-tuple-element.323, ...), kind=kOutput, calls=%fused_computation.clone.1 | convolution fusion | flops 1622134784 | bytes 13025280 | tf_op jit(solution)/shard_map/while/body/eval_jaxpr/fab,fbn->fan/dot_general | solution.py:104
  171.1 2.8 %collective-permute-start.1 = (f32[4,3072]{1,0:T(4,128)S(1)}, f32[4,3072]{1,0:T(4,128)S(1)}, u32[]{:S(2)}, u32[]{:S(2)}) collective-permute-start(f32[4,3072]{1,0:T(4,128)S(1)} %select_add_fusion.2), channel_id=1, source_target_pairs={{0,24},{8,16},{16,8},{24,0},{1,25},{9,17},{17,9},{25,1},{2,26},{10... | collective-permute-start | bytes 147464 | tf_op jit(solution)/shard_map/while/body/eval_jaxpr/ppermute | solution.py:33
  173.9 7.0 %collective-permute-start.2 = (f32[4,3072]{1,0:T(4,128)S(1)}, f32[4,3072]{1,0:T(4,128)S(1)}, u32[]{:S(2)}, u32[]{:S(2)}) collective-permute-start(f32[4,3072]{1,0:T(4,128)S(1)} %select_add_fusion.2), channel_id=1, source_target_pairs={{0,16},{8,24},{16,0},{24,8},{1,17},{9,25},{17,1},{25,9},{2,18},{10... | collective-permute-start | bytes 147464 | tf_op jit(solution)/shard_map/while/body/eval_jaxpr/ppermute | solution.py:33
  180.9 2.1 collective-permute-done.2
  183.0 2.0 collective-permute-done.3
  185.2 5.9 %collective-permute-start.5 = (f32[4,3072]{1,0:T(4,128)S(1)}, f32[4,3072]{1,0:T(4,128)S(1)}, u32[]{:S(2)}, u32[]{:S(2)}) collective-permute-start(f32[4,3072]{1,0:T(4,128)S(1)} %fusion.52), channel_id=1, source_target_pairs={{0,4},{2,6},{4,0},{6,2},{1,5},{3,7},{5,1},{7,3},{8,12},{10,14},{12... | collective-permute-start | bytes 147464 | tf_op jit(solution)/shard_map/while/body/eval_jaxpr/ppermute | solution.py:33
  191.6 2.5 %collective-permute-done.5 = f32[4,3072]{1,0:T(4,128)S(1)} collective-permute-done((f32[4,3072]{1,0:T(4,128)S(1)}, f32[4,3072]{1,0:T(4,128)S(1)}, u32[]{:S(2)}, u32[]{:S(2)}) %collective-permute-start.5) | collective-permute-done | bytes 49184 | tf_op jit(solution)/shard_map/while/body/eval_jaxpr/ppermute | solution.py:33
  199.3 8.3 %eval_jaxpr.5 = (f32[4,256,256]{2,1,0:T(8,128)}, f32[4,256,256]{2,1,0:T(8,128)}) custom-call(bf16[4,256,3072]{2,1,0:T(8,128)(2,1)} %get-tuple-element.372.mine_ref, bf16[4,256,3072]{2,1,0:T(8,128)(2,1)} %get-tuple-element.374.other_ref, f32[4,1,3072]{2,1,0:T(1,128)} %broadcast_in_dim.36.field_ref), custom_call_target="tpu_custom_call" | custom-call | tf_op jit(solution)/shard_map/while/body/eval_jaxpr/pallas_call | solution.py:79
  207.7 1.8 add_bitcast_fusion.4
  209.9 2.5 %collective-permute-done = f32[2,4,2,128,128]{4,3,1,2,0:T(8,128)S(1)} collective-permute-done((f32[2,4,2,128,128]{4,3,1,2,0:T(8,128)S(1)}, f32[2,4,2,128,128]{4,3,1,2,0:T(8,128)S(1)}, u32[]{:S(2)}, u32[]{:S(2)}) %collective-permute-start) | collective-permute-done | bytes 1048608 | tf_op jit(solution)/shard_map/while/body/eval_jaxpr/ppermute | solution.py:49
  212.8 4.6 %multiply_reduce_fusion.7 = f32[4,3072]{1,0:T(4,128)S(1)} fusion(bf16[4,256,3072]{2,1,0:T(8,128)(2,1)S(1)} %bitcast.138, bf16[4,256,3072]{2,1,0:T(8,128)(2,1)} %get-tuple-element.374.other_ref, bf16[4,128,128]{2,1,0:T(8,128)(2,1)S(1)} %get-tuple-element.325, bf16[4,128,128]{2,1,0:T(8,128)(2,1)S(1)} %get-tuple-element.326, ...), kind=kOutput, calls=%fused_computation.1.clone.1 | convolution fusion | flops 1622134784 | bytes 13025280 | tf_op jit(solution)/shard_map/while/body/eval_jaxpr/fab,fbn->fan/dot_general | solution.py:104
  217.5 4.6 %multiply_reduce_fusion.6 = f32[4,3072]{1,0:T(4,128)S(1)} fusion(bf16[4,256,3072]{2,1,0:T(8,128)(2,1)} %get-tuple-element.374.other_ref, bf16[4,256,3072]{2,1,0:T(8,128)(2,1)S(1)} %bitcast.138, bf16[4,128,128]{2,1,0:T(8,128)(2,1)S(1)} %get-tuple-element.322, bf16[4,128,128]{2,1,0:T(8,128)(2,1)S(1)} %get-tuple-element.323, ...), kind=kOutput, calls=%fused_computation.clone.1 | convolution fusion | flops 1622134784 | bytes 13025280 | tf_op jit(solution)/shard_map/while/body/eval_jaxpr/fab,fbn->fan/dot_general | solution.py:104
  222.1 2.8 %collective-permute-start.1 = (f32[4,3072]{1,0:T(4,128)S(1)}, f32[4,3072]{1,0:T(4,128)S(1)}, u32[]{:S(2)}, u32[]{:S(2)}) collective-permute-start(f32[4,3072]{1,0:T(4,128)S(1)} %select_add_fusion.2), channel_id=1, source_target_pairs={{0,24},{8,16},{16,8},{24,0},{1,25},{9,17},{17,9},{25,1},{2,26},{10... | collective-permute-start | bytes 147464 | tf_op jit(solution)/shard_map/while/body/eval_jaxpr/ppermute | solution.py:33
  225.7 1.5 collective-permute-done.1
  227.2 1.8 collective-permute-done.2
  229.1 2.9 %collective-permute-start.4 = (f32[4,3072]{1,0:T(4,128)S(1)}, f32[4,3072]{1,0:T(4,128)S(1)}, u32[]{:S(2)}, u32[]{:S(2)}) collective-permute-start(f32[4,3072]{1,0:T(4,128)S(1)} %fusion.52), channel_id=1, source_target_pairs={{0,6},{2,4},{4,2},{6,0},{1,7},{3,5},{5,3},{7,1},{8,14},{10,12},{12... | collective-permute-start | bytes 147464 | tf_op jit(solution)/shard_map/while/body/eval_jaxpr/ppermute | solution.py:33
  232.0 1.5 collective-permute-start.6
  233.6 1.6 collective-permute-done.4
  235.2 1.9 collective-permute-done.5
  (109 shorter events, 20.0 us)
Async XLA Ops:
  0.0 19.8 %copy-start.1 = (s32[16]{0:T(128)S(1)}, s32[16]{0:T(128)}, u32[]{:S(2)}) copy-start(s32[16]{0:T(128)} %constant.200.clone) | copy-start | bytes 196
  0.0 16.4 %copy-start = (f32[4,2,128,128]{3,2,1,0:T(8,128)S(1)}, f32[4,2,128,128]{3,2,1,0:T(8,128)}, u32[]{:S(2)}) copy-start(f32[4,2,128,128]{3,2,1,0:T(8,128)} %param.12) | copy-start | bytes 1572868
  0.0 143.6 %collective-permute-start.14 = (bf16[4,2,128,3072]{3,2,1,0:T(8,128)(2,1)}, bf16[4,2,128,3072]{3,2,1,0:T(8,128)(2,1)}, u32[]{:S(2)}, u32[]{:S(2)}) collective-permute-start(bf16[4,2,128,3072]{3,2,1,0:T(8,128)(2,1)} %param.10), channel_id=1, source_target_pairs={{0,2},{12,8},{16,22},{20,18},{10,14},{30,28},{1,3},{13,9},{17,23},... | collective-permute-start | bytes 18874376 | tf_op jit(solution)/shard_map/ppermute | solution.py:193
  8.6 15.7 %collective-permute-start.8 = (f32[4,3072]{1,0:T(4,128)S(1)}, f32[4,3072]{1,0:T(4,128)S(1)}, u32[]{:S(2)}, u32[]{:S(2)}) collective-permute-start(f32[4,3072]{1,0:T(4,128)S(1)} %dynamic_update_slice.3), channel_id=1, source_target_pairs={{0,8},{8,0},{16,24},{24,16},{1,9},{9,1},{17,25},{25,17},{2,10},{10... | collective-permute-start | bytes 147464 | tf_op jit(solution)/shard_map/ppermute | solution.py:33
  8.7 16.3 %collective-permute-start.9 = (f32[4,3072]{1,0:T(4,128)S(1)}, f32[4,3072]{1,0:T(4,128)S(1)}, u32[]{:S(2)}, u32[]{:S(2)}) collective-permute-start(f32[4,3072]{1,0:T(4,128)S(1)} %dynamic_update_slice.3), channel_id=1, source_target_pairs={{0,16},{8,24},{16,0},{24,8},{1,17},{9,25},{17,1},{25,9},{2,18},{10... | collective-permute-start | bytes 147464 | tf_op jit(solution)/shard_map/ppermute | solution.py:33
  12.3 12.7 %collective-permute-start.10 = (f32[4,3072]{1,0:T(4,128)S(1)}, f32[4,3072]{1,0:T(4,128)S(1)}, u32[]{:S(2)}, u32[]{:S(2)}) collective-permute-start(f32[4,3072]{1,0:T(4,128)S(1)} %dynamic_update_slice.3), channel_id=1, source_target_pairs={{0,24},{8,16},{16,8},{24,0},{1,25},{9,17},{17,9},{25,1},{2,26},{10... | collective-permute-start | bytes 147464 | tf_op jit(solution)/shard_map/ppermute | solution.py:33
  23.6 7.1 %collective-permute-start.15 = (f32[5,128,128]{2,1,0:T(8,128)S(1)}, f32[5,128,128]{2,1,0:T(8,128)S(1)}, u32[]{:S(2)}, u32[]{:S(2)}) collective-permute-start(f32[5,128,128]{2,1,0:T(8,128)S(1)} %fusion.29), channel_id=1, source_target_pairs={{8,2},{4,8},{24,22},{12,18},{26,14},{22,28},{9,3},{5,9},{25,23},{1... | collective-permute-start | bytes 983048 | tf_op jit(solution)/shard_map/ppermute | solution.py:205
  24.3 6.7 %collective-permute-start.16 = (f32[5,128,128]{2,1,0:T(8,128)S(1)}, f32[5,128,128]{2,1,0:T(8,128)S(1)}, u32[]{:S(2)}, u32[]{:S(2)}) collective-permute-start(f32[5,128,128]{2,1,0:T(8,128)S(1)} %fusion.29), channel_id=1, source_target_pairs={{16,8},{6,22},{17,9},{7,23}} | collective-permute-start | bytes 983048 | tf_op jit(solution)/shard_map/ppermute | solution.py:205
  25.1 117.1 %collective-permute-start.11 = (f32[4,3072]{1,0:T(4,128)S(1)}, f32[4,3072]{1,0:T(4,128)S(1)}, u32[]{:S(2)}, u32[]{:S(2)}) collective-permute-start(f32[4,3072]{1,0:T(4,128)S(1)} %fusion.34), channel_id=1, source_target_pairs={{0,2},{2,0},{4,6},{6,4},{1,3},{3,1},{5,7},{7,5},{8,10},{10,8},{12,... | collective-permute-start | bytes 147464 | tf_op jit(solution)/shard_map/ppermute | solution.py:33
  26.5 116.2 %collective-permute-start.12 = (f32[4,3072]{1,0:T(4,128)S(1)}, f32[4,3072]{1,0:T(4,128)S(1)}, u32[]{:S(2)}, u32[]{:S(2)}) collective-permute-start(f32[4,3072]{1,0:T(4,128)S(1)} %fusion.34), channel_id=1, source_target_pairs={{0,4},{2,6},{4,0},{6,2},{1,5},{3,7},{5,1},{7,3},{8,12},{10,14},{12... | collective-permute-start | bytes 147464 | tf_op jit(solution)/shard_map/ppermute | solution.py:33
  30.7 112.5 %collective-permute-start.13 = (f32[4,3072]{1,0:T(4,128)S(1)}, f32[4,3072]{1,0:T(4,128)S(1)}, u32[]{:S(2)}, u32[]{:S(2)}) collective-permute-start(f32[4,3072]{1,0:T(4,128)S(1)} %fusion.34), channel_id=1, source_target_pairs={{0,6},{2,4},{4,2},{6,0},{1,7},{3,5},{5,3},{7,1},{8,14},{10,12},{12... | collective-permute-start | bytes 147464 | tf_op jit(solution)/shard_map/ppermute | solution.py:33
  31.0 112.8 %slice-start = ((s8[6291456]{0:T(1024)(128)(4,1)}), s8[4194304]{0:T(1024)(128)(4,1)S(1)}, s32[]{:S(2)}) async-start(s8[6291456]{0:T(1024)(128)(4,1)} %bitcast.134), calls=%async_computation | async-start | bytes 8388608
  31.0 112.3 %collective-permute-start.17 = (f32[2,5,128,128]{3,2,1,0:T(8,128)S(1)}, f32[2,5,128,128]{3,2,1,0:T(8,128)S(1)}, u32[]{:S(2)}, u32[]{:S(2)}) collective-permute-start(f32[2,5,128,128]{3,2,1,0:T(8,128)S(1)} %pad_maximum_fusion.8), channel_id=1, source_target_pairs={{0,1},{1,0},{2,3},{3,2},{4,5},{5,4},{6,7},{7,6},{8,9},{9,8},{10,11... | collective-permute-start | bytes 1966088 | tf_op jit(solution)/shard_map/ppermute | solution.py:206
  148.3 13.5 %slice-start.2 = ((s8[6291456]{0:T(1024)(128)(4,1)}), s8[2097152]{0:T(1024)(128)(4,1)S(1)}, s32[]{:S(2)}) async-start(s8[6291456]{0:T(1024)(128)(4,1)} %bitcast.137), calls=%async_computation.2 | async-start | bytes 4194304 | tf_op jit(solution)/shard_map/while
  156.6 5.2 %slice-start.3 = ((s8[6291456]{0:T(1024)(128)(4,1)}), s8[4194304]{0:T(1024)(128)(4,1)S(1)}, s32[]{:S(2)}) async-start(s8[6291456]{0:T(1024)(128)(4,1)} %bitcast.137), calls=%async_computation.3 | async-start | bytes 8388608 | tf_op jit(solution)/shard_map/while
  158.6 2.7 %collective-permute-start = (f32[2,4,2,128,128]{4,3,1,2,0:T(8,128)S(1)}, f32[2,4,2,128,128]{4,3,1,2,0:T(8,128)S(1)}, u32[]{:S(2)}, u32[]{:S(2)}) collective-permute-start(f32[2,4,2,128,128]{4,3,1,2,0:T(8,128)S(1)} %pad_maximum_fusion.14), channel_id=1, source_target_pairs={{0,1},{1,0},{2,3},{3,2},{4,5},{5,4},{6,7},{7,6},{8,9},{9,8},{10,11... | collective-permute-start | bytes 3145736 | tf_op jit(solution)/shard_map/while/body/eval_jaxpr/ppermute | solution.py:49
  171.1 9.8 %collective-permute-start.1 = (f32[4,3072]{1,0:T(4,128)S(1)}, f32[4,3072]{1,0:T(4,128)S(1)}, u32[]{:S(2)}, u32[]{:S(2)}) collective-permute-start(f32[4,3072]{1,0:T(4,128)S(1)} %select_add_fusion.2), channel_id=1, source_target_pairs={{0,24},{8,16},{16,8},{24,0},{1,25},{9,17},{17,9},{25,1},{2,26},{10... | collective-permute-start | bytes 147464 | tf_op jit(solution)/shard_map/while/body/eval_jaxpr/ppermute | solution.py:33
  173.9 9.0 %collective-permute-start.2 = (f32[4,3072]{1,0:T(4,128)S(1)}, f32[4,3072]{1,0:T(4,128)S(1)}, u32[]{:S(2)}, u32[]{:S(2)}) collective-permute-start(f32[4,3072]{1,0:T(4,128)S(1)} %select_add_fusion.2), channel_id=1, source_target_pairs={{0,16},{8,24},{16,0},{24,8},{1,17},{9,25},{17,1},{25,9},{2,18},{10... | collective-permute-start | bytes 147464 | tf_op jit(solution)/shard_map/while/body/eval_jaxpr/ppermute | solution.py:33
  180.9 4.1 %collective-permute-start.3 = (f32[4,3072]{1,0:T(4,128)S(1)}, f32[4,3072]{1,0:T(4,128)S(1)}, u32[]{:S(2)}, u32[]{:S(2)}) collective-permute-start(f32[4,3072]{1,0:T(4,128)S(1)} %select_add_fusion.2), channel_id=1, source_target_pairs={{0,8},{8,0},{16,24},{24,16},{1,9},{9,1},{17,25},{25,17},{2,10},{10... | collective-permute-start | bytes 147464 | tf_op jit(solution)/shard_map/while/body/eval_jaxpr/ppermute | solution.py:33
  185.1 6.5 %collective-permute-start.4 = (f32[4,3072]{1,0:T(4,128)S(1)}, f32[4,3072]{1,0:T(4,128)S(1)}, u32[]{:S(2)}, u32[]{:S(2)}) collective-permute-start(f32[4,3072]{1,0:T(4,128)S(1)} %fusion.52), channel_id=1, source_target_pairs={{0,6},{2,4},{4,2},{6,0},{1,7},{3,5},{5,3},{7,1},{8,14},{10,12},{12... | collective-permute-start | bytes 147464 | tf_op jit(solution)/shard_map/while/body/eval_jaxpr/ppermute | solution.py:33
  185.2 9.0 %collective-permute-start.5 = (f32[4,3072]{1,0:T(4,128)S(1)}, f32[4,3072]{1,0:T(4,128)S(1)}, u32[]{:S(2)}, u32[]{:S(2)}) collective-permute-start(f32[4,3072]{1,0:T(4,128)S(1)} %fusion.52), channel_id=1, source_target_pairs={{0,4},{2,6},{4,0},{6,2},{1,5},{3,7},{5,1},{7,3},{8,12},{10,14},{12... | collective-permute-start | bytes 147464 | tf_op jit(solution)/shard_map/while/body/eval_jaxpr/ppermute | solution.py:33
  191.1 4.1 %collective-permute-start.6 = (f32[4,3072]{1,0:T(4,128)S(1)}, f32[4,3072]{1,0:T(4,128)S(1)}, u32[]{:S(2)}, u32[]{:S(2)}) collective-permute-start(f32[4,3072]{1,0:T(4,128)S(1)} %fusion.52), channel_id=1, source_target_pairs={{0,2},{2,0},{4,6},{6,4},{1,3},{3,1},{5,7},{7,5},{8,10},{10,8},{12,... | collective-permute-start | bytes 147464 | tf_op jit(solution)/shard_map/while/body/eval_jaxpr/ppermute | solution.py:33
  195.9 1.4 collective-permute-start.7
  199.3 13.5 %slice-start.2 = ((s8[6291456]{0:T(1024)(128)(4,1)}), s8[2097152]{0:T(1024)(128)(4,1)S(1)}, s32[]{:S(2)}) async-start(s8[6291456]{0:T(1024)(128)(4,1)} %bitcast.137), calls=%async_computation.2 | async-start | bytes 4194304 | tf_op jit(solution)/shard_map/while
  209.6 2.7 %collective-permute-start = (f32[2,4,2,128,128]{4,3,1,2,0:T(8,128)S(1)}, f32[2,4,2,128,128]{4,3,1,2,0:T(8,128)S(1)}, u32[]{:S(2)}, u32[]{:S(2)}) collective-permute-start(f32[2,4,2,128,128]{4,3,1,2,0:T(8,128)S(1)} %pad_maximum_fusion.14), channel_id=1, source_target_pairs={{0,1},{1,0},{2,3},{3,2},{4,5},{5,4},{6,7},{7,6},{8,9},{9,8},{10,11... | collective-permute-start | bytes 3145736 | tf_op jit(solution)/shard_map/while/body/eval_jaxpr/ppermute | solution.py:49
  222.1 5.1 %collective-permute-start.1 = (f32[4,3072]{1,0:T(4,128)S(1)}, f32[4,3072]{1,0:T(4,128)S(1)}, u32[]{:S(2)}, u32[]{:S(2)}) collective-permute-start(f32[4,3072]{1,0:T(4,128)S(1)} %select_add_fusion.2), channel_id=1, source_target_pairs={{0,24},{8,16},{16,8},{24,0},{1,25},{9,17},{17,9},{25,1},{2,26},{10... | collective-permute-start | bytes 147464 | tf_op jit(solution)/shard_map/while/body/eval_jaxpr/ppermute | solution.py:33
  224.9 4.1 %collective-permute-start.2 = (f32[4,3072]{1,0:T(4,128)S(1)}, f32[4,3072]{1,0:T(4,128)S(1)}, u32[]{:S(2)}, u32[]{:S(2)}) collective-permute-start(f32[4,3072]{1,0:T(4,128)S(1)} %select_add_fusion.2), channel_id=1, source_target_pairs={{0,16},{8,24},{16,0},{24,8},{1,17},{9,25},{17,1},{25,9},{2,18},{10... | collective-permute-start | bytes 147464 | tf_op jit(solution)/shard_map/while/body/eval_jaxpr/ppermute | solution.py:33
  224.9 4.1 %collective-permute-start.3 = (f32[4,3072]{1,0:T(4,128)S(1)}, f32[4,3072]{1,0:T(4,128)S(1)}, u32[]{:S(2)}, u32[]{:S(2)}) collective-permute-start(f32[4,3072]{1,0:T(4,128)S(1)} %select_add_fusion.2), channel_id=1, source_target_pairs={{0,8},{8,0},{16,24},{24,16},{1,9},{9,1},{17,25},{25,17},{2,10},{10... | collective-permute-start | bytes 147464 | tf_op jit(solution)/shard_map/while/body/eval_jaxpr/ppermute | solution.py:33
  229.1 6.0 %collective-permute-start.4 = (f32[4,3072]{1,0:T(4,128)S(1)}, f32[4,3072]{1,0:T(4,128)S(1)}, u32[]{:S(2)}, u32[]{:S(2)}) collective-permute-start(f32[4,3072]{1,0:T(4,128)S(1)} %fusion.52), channel_id=1, source_target_pairs={{0,6},{2,4},{4,2},{6,0},{1,7},{3,5},{5,3},{7,1},{8,14},{10,12},{12... | collective-permute-start | bytes 147464 | tf_op jit(solution)/shard_map/while/body/eval_jaxpr/ppermute | solution.py:33
  232.0 5.0 %collective-permute-start.5 = (f32[4,3072]{1,0:T(4,128)S(1)}, f32[4,3072]{1,0:T(4,128)S(1)}, u32[]{:S(2)}, u32[]{:S(2)}) collective-permute-start(f32[4,3072]{1,0:T(4,128)S(1)} %fusion.52), channel_id=1, source_target_pairs={{0,4},{2,6},{4,0},{6,2},{1,5},{3,7},{5,1},{7,3},{8,12},{10,14},{12... | collective-permute-start | bytes 147464 | tf_op jit(solution)/shard_map/while/body/eval_jaxpr/ppermute | solution.py:33
  232.0 5.0 %collective-permute-start.6 = (f32[4,3072]{1,0:T(4,128)S(1)}, f32[4,3072]{1,0:T(4,128)S(1)}, u32[]{:S(2)}, u32[]{:S(2)}) collective-permute-start(f32[4,3072]{1,0:T(4,128)S(1)} %fusion.52), channel_id=1, source_target_pairs={{0,2},{2,0},{4,6},{6,4},{1,3},{3,1},{5,7},{7,5},{8,10},{10,8},{12,... | collective-permute-start | bytes 147464 | tf_op jit(solution)/shard_map/while/body/eval_jaxpr/ppermute | solution.py:33
  237.7 1.4 collective-permute-start.7
  (2 other events, 6.8 us)

commit v13 on v12

--- a/solution.py
+++ b/solution.py
@@ -242,7 +242,7 @@
         term_first = point_terms(adj_first, other_rows, mine_rows, psd_field, quad_weight)
         term_second = point_terms(adj_second, mine_rows, other_rows, psd_field, quad_weight)
         point_part = jnp.where(keep_first, term_first, 0.0) + jnp.where(keep_second, term_second, 0.0)
-        gradient = butterfly_sum(point_part, axes)
+        gradient = butterfly_sum(point_part, ("col", "row"))
         squares = swap_add(jnp.sum(gradient * gradient), "pts")
         return log_field - descent * gradient / jnp.sqrt(squares / entry_count + epsilon)
 

time: 242 us -> 242 us (level)
  transfers between devices with their start and end apart: 26 -> 26, of which waited for: 15 -> 16; matrix products, arithmetic and copies ran while one was open for 2% -> 2% of each run, Pallas kernels for 0% -> 0%
where the time goes in v13:
time: 242 us
  waiting for transfers between devices  133 us (55%)
  starting transfers between devices  46.3 us (19%)
  matrix products  18.5 us (8%)
  Pallas kernels  16.6 us (7%)
  local copies, waits for them, and re-layouts  9.12 us (4%)
  other arithmetic  8.87 us (4%)
  between operations  5.94 us (2%)
  loops' own time  3.06 us (1%)
    ppermute x18, waiting for transfers between devices, butterfly_sum(): got.append(lax.ppermute(value, axis, [(i, i ^ mask) for i in range(size)]))  125 us
    ppermute x18, starting transfers between devices, butterfly_sum(): got.append(lax.ppermute(value, axis, [(i, i ^ mask) for i in range(size)]))  36.8 us
    dot_general x4, matrix products, point_terms(): jnp.einsum('fab,fbn->fan', adjoint_block(adjoint), right_rows, preferred_...  18.5 us
    pallas_call x2, Pallas kernels, pair_products(): pl.pallas_call(kernel, grid=(freq, points // tile), in_specs=[spec, spec,...  16.6 us
    ppermute x4, waiting for transfers between devices, swap_add(): return value + lax.ppermute(value, axis, [(0, 1), (1, 0)])  7.81 us
    ppermute x1, starting transfers between devices, pair_body(): received = lax.ppermute(green_panel, axes, panel_moves)  7.72 us
  transfers between devices with their start and end apart: 26, of which 16 were waited for; matrix products, arithmetic and copies ran while one was open for 2% of the time, Pallas kernels for 0%

profile of v13, /device:TPU:0, one launch (start us, length us, event | category | flops | bytes accessed | tf_op | source)
XLA Modules:
  0.0 241.6 jit_solution(1778091313651974021)
XLA Ops:
  0.0 7.7 %collective-permute-start.14 = (bf16[4,2,128,3072]{3,2,1,0:T(8,128)(2,1)}, bf16[4,2,128,3072]{3,2,1,0:T(8,128)(2,1)}, u32[]{:S(2)}, u32[]{:S(2)}) collective-permute-start(bf16[4,2,128,3072]{3,2,1,0:T(8,128)(2,1)} %param.10), channel_id=1, source_target_pairs={{0,2},{12,8},{16,22},{20,18},{10,14},{30,28},{1,3},{13,9},{17,23},... | collective-permute-start | bytes 18874376 | tf_op jit(solution)/shard_map/ppermute | solution.py:193
  8.7 3.6 %collective-permute-start.9 = (f32[4,3072]{1,0:T(4,128)S(1)}, f32[4,3072]{1,0:T(4,128)S(1)}, u32[]{:S(2)}, u32[]{:S(2)}) collective-permute-start(f32[4,3072]{1,0:T(4,128)S(1)} %dynamic_update_slice.3), channel_id=1, source_target_pairs={{0,16},{8,24},{16,0},{24,8},{1,17},{9,25},{17,1},{25,9},{2,18},{10... | collective-permute-start | bytes 147464 | tf_op jit(solution)/shard_map/ppermute | solution.py:33
  12.3 1.4 collective-permute-start.10
  26.5 4.2 %collective-permute-start.12 = (f32[4,3072]{1,0:T(4,128)S(1)}, f32[4,3072]{1,0:T(4,128)S(1)}, u32[]{:S(2)}, u32[]{:S(2)}) collective-permute-start(f32[4,3072]{1,0:T(4,128)S(1)} %fusion.34), channel_id=1, source_target_pairs={{0,4},{2,6},{4,0},{6,2},{1,5},{3,7},{5,1},{7,3},{8,12},{10,14},{12... | collective-permute-start | bytes 147464 | tf_op jit(solution)/shard_map/ppermute | solution.py:33
  31.1 111.1 %collective-permute-done.11 = f32[4,3072]{1,0:T(4,128)S(1)} collective-permute-done((f32[4,3072]{1,0:T(4,128)S(1)}, f32[4,3072]{1,0:T(4,128)S(1)}, u32[]{:S(2)}, u32[]{:S(2)}) %collective-permute-start.11) | collective-permute-done | bytes 49184 | tf_op jit(solution)/shard_map/ppermute | solution.py:33
  145.0 2.6 %conditional.1 = (bf16[4,256,3072]{2,1,0:T(8,128)(2,1)}) conditional(s32[]{:T(128)} %bitcast.44, bf16[4,2,128,3072]{3,2,1,0:T(8,128)(2,1)} %collective-permute-done.14, bf16[4,2,128,3072]{3,2,1,0:T(8,128)(2,1)S(1)} %bitcast.135), branch_computations={%region_0.1_spmd, %region_1.2_spmd} | conditional | bytes 12582920 | solution.py:214
  145.0 2.6 %copy.11 = bf16[4,256,3072]{2,1,0:T(8,128)(2,1)} copy(bf16[4,256,3072]{2,1,0:T(8,128)(2,1)S(1)} %bitcast.136) | data formatting | bytes 12582912 | tf_op jit(solution)/shard_map/cond
  147.7 93.3 %while.13 = (s32[]{:T(128)}, f32[4,3072]{1,0:T(4,128)S(1)}, pred[]{:T(512)}, bf16[4,256,3072]{2,1,0:T(8,128)(2,1)}, f32[1,128,128]{2,1,0:T(8,128)S(1)}, /*index=...) while((s32[]{:T(128)}, f32[4,3072]{1,0:T(4,128)S(1)}, ...), condition=%wide.region_6.7_spmd, body=%wide.region_2.6_spmd.sunk | while | flops 3247300608 | bytes 67175664 | solution.py:249
  148.3 8.3 %eval_jaxpr.5 = (f32[4,256,256]{2,1,0:T(8,128)}, f32[4,256,256]{2,1,0:T(8,128)}) custom-call(bf16[4,256,3072]{2,1,0:T(8,128)(2,1)} %get-tuple-element.372.mine_ref, bf16[4,256,3072]{2,1,0:T(8,128)(2,1)} %get-tuple-element.374.other_ref, f32[4,1,3072]{2,1,0:T(1,128)} %broadcast_in_dim.36.field_ref), custom_call_target="tpu_custom_call" | custom-call | tf_op jit(solution)/shard_map/while/body/eval_jaxpr/pallas_call | solution.py:79
  156.6 1.8 add_bitcast_fusion.4
  158.7 2.6 %collective-permute-done = f32[2,4,2,128,128]{4,3,1,2,0:T(8,128)S(1)} collective-permute-done((f32[2,4,2,128,128]{4,3,1,2,0:T(8,128)S(1)}, f32[2,4,2,128,128]{4,3,1,2,0:T(8,128)S(1)}, u32[]{:S(2)}, u32[]{:S(2)}) %collective-permute-start) | collective-permute-done | bytes 1048608 | tf_op jit(solution)/shard_map/while/body/eval_jaxpr/ppermute | solution.py:49
  161.8 4.6 %multiply_reduce_fusion.7 = f32[4,3072]{1,0:T(4,128)S(1)} fusion(bf16[4,256,3072]{2,1,0:T(8,128)(2,1)S(1)} %bitcast.138, bf16[4,256,3072]{2,1,0:T(8,128)(2,1)} %get-tuple-element.374.other_ref, bf16[4,128,128]{2,1,0:T(8,128)(2,1)S(1)} %get-tuple-element.325, bf16[4,128,128]{2,1,0:T(8,128)(2,1)S(1)} %get-tuple-element.326, ...), kind=kOutput, calls=%fused_computation.1.clone.1 | convolution fusion | flops 1622134784 | bytes 13025280 | tf_op jit(solution)/shard_map/while/body/eval_jaxpr/fab,fbn->fan/dot_general | solution.py:104
  166.4 4.6 %multiply_reduce_fusion.6 = f32[4,3072]{1,0:T(4,128)S(1)} fusion(bf16[4,256,3072]{2,1,0:T(8,128)(2,1)} %get-tuple-element.374.other_ref, bf16[4,256,3072]{2,1,0:T(8,128)(2,1)S(1)} %bitcast.138, bf16[4,128,128]{2,1,0:T(8,128)(2,1)S(1)} %get-tuple-element.322, bf16[4,128,128]{2,1,0:T(8,128)(2,1)S(1)} %get-tuple-element.323, ...), kind=kOutput, calls=%fused_computation.clone.1 | convolution fusion | flops 1622134784 | bytes 13025280 | tf_op jit(solution)/shard_map/while/body/eval_jaxpr/fab,fbn->fan/dot_general | solution.py:104
  171.1 1.7 collective-permute-start.1
  172.8 2.7 %collective-permute-start.3 = (f32[4,3072]{1,0:T(4,128)S(1)}, f32[4,3072]{1,0:T(4,128)S(1)}, u32[]{:S(2)}, u32[]{:S(2)}) collective-permute-start(f32[4,3072]{1,0:T(4,128)S(1)} %select_add_fusion.2), channel_id=1, source_target_pairs={{0,2},{2,0},{4,6},{6,4},{1,3},{3,1},{5,7},{7,5},{8,10},{10,8},{12,... | collective-permute-start | bytes 147464 | tf_op jit(solution)/shard_map/while/body/eval_jaxpr/ppermute | solution.py:33
  175.6 1.8 collective-permute-done.1
  177.4 1.5 collective-permute-done.2
  179.0 2.8 %collective-permute-start.4 = (f32[4,3072]{1,0:T(4,128)S(1)}, f32[4,3072]{1,0:T(4,128)S(1)}, u32[]{:S(2)}, u32[]{:S(2)}) collective-permute-start(f32[4,3072]{1,0:T(4,128)S(1)} %fusion.52), channel_id=1, source_target_pairs={{0,24},{8,16},{16,8},{24,0},{1,25},{9,17},{17,9},{25,1},{2,26},{10... | collective-permute-start | bytes 147464 | tf_op jit(solution)/shard_map/while/body/eval_jaxpr/ppermute | solution.py:33
  181.8 9.5 %collective-permute-start.5 = (f32[4,3072]{1,0:T(4,128)S(1)}, f32[4,3072]{1,0:T(4,128)S(1)}, u32[]{:S(2)}, u32[]{:S(2)}) collective-permute-start(f32[4,3072]{1,0:T(4,128)S(1)} %fusion.52), channel_id=1, source_target_pairs={{0,16},{8,24},{16,0},{24,8},{1,17},{9,25},{17,1},{25,9},{2,18},{10... | collective-permute-start | bytes 147464 | tf_op jit(solution)/shard_map/while/body/eval_jaxpr/ppermute | solution.py:33
  193.3 2.0 collective-permute-done.6
  199.5 8.3 %eval_jaxpr.5 = (f32[4,256,256]{2,1,0:T(8,128)}, f32[4,256,256]{2,1,0:T(8,128)}) custom-call(bf16[4,256,3072]{2,1,0:T(8,128)(2,1)} %get-tuple-element.372.mine_ref, bf16[4,256,3072]{2,1,0:T(8,128)(2,1)} %get-tuple-element.374.other_ref, f32[4,1,3072]{2,1,0:T(1,128)} %broadcast_in_dim.36.field_ref), custom_call_target="tpu_custom_call" | custom-call | tf_op jit(solution)/shard_map/while/body/eval_jaxpr/pallas_call | solution.py:79
  207.8 1.8 add_bitcast_fusion.4
  210.1 2.5 %collective-permute-done = f32[2,4,2,128,128]{4,3,1,2,0:T(8,128)S(1)} collective-permute-done((f32[2,4,2,128,128]{4,3,1,2,0:T(8,128)S(1)}, f32[2,4,2,128,128]{4,3,1,2,0:T(8,128)S(1)}, u32[]{:S(2)}, u32[]{:S(2)}) %collective-permute-start) | collective-permute-done | bytes 1048608 | tf_op jit(solution)/shard_map/while/body/eval_jaxpr/ppermute | solution.py:49
  213.0 4.6 %multiply_reduce_fusion.7 = f32[4,3072]{1,0:T(4,128)S(1)} fusion(bf16[4,256,3072]{2,1,0:T(8,128)(2,1)S(1)} %bitcast.138, bf16[4,256,3072]{2,1,0:T(8,128)(2,1)} %get-tuple-element.374.other_ref, bf16[4,128,128]{2,1,0:T(8,128)(2,1)S(1)} %get-tuple-element.325, bf16[4,128,128]{2,1,0:T(8,128)(2,1)S(1)} %get-tuple-element.326, ...), kind=kOutput, calls=%fused_computation.1.clone.1 | convolution fusion | flops 1622134784 | bytes 13025280 | tf_op jit(solution)/shard_map/while/body/eval_jaxpr/fab,fbn->fan/dot_general | solution.py:104
  217.6 4.6 %multiply_reduce_fusion.6 = f32[4,3072]{1,0:T(4,128)S(1)} fusion(bf16[4,256,3072]{2,1,0:T(8,128)(2,1)} %get-tuple-element.374.other_ref, bf16[4,256,3072]{2,1,0:T(8,128)(2,1)S(1)} %bitcast.138, bf16[4,128,128]{2,1,0:T(8,128)(2,1)S(1)} %get-tuple-element.322, bf16[4,128,128]{2,1,0:T(8,128)(2,1)S(1)} %get-tuple-element.323, ...), kind=kOutput, calls=%fused_computation.clone.1 | convolution fusion | flops 1622134784 | bytes 13025280 | tf_op jit(solution)/shard_map/while/body/eval_jaxpr/fab,fbn->fan/dot_general | solution.py:104
  222.3 3.0 %collective-permute-start.1 = (f32[4,3072]{1,0:T(4,128)S(1)}, f32[4,3072]{1,0:T(4,128)S(1)}, u32[]{:S(2)}, u32[]{:S(2)}) collective-permute-start(f32[4,3072]{1,0:T(4,128)S(1)} %select_add_fusion.2), channel_id=1, source_target_pairs={{0,6},{2,4},{4,2},{6,0},{1,7},{3,5},{5,3},{7,1},{8,14},{10,12},{12... | collective-permute-start | bytes 147464 | tf_op jit(solution)/shard_map/while/body/eval_jaxpr/ppermute | solution.py:33
  225.2 1.5 collective-permute-start.3
  226.7 2.0 collective-permute-done.1
  228.7 1.5 collective-permute-done.2
  230.5 2.9 %collective-permute-start.4 = (f32[4,3072]{1,0:T(4,128)S(1)}, f32[4,3072]{1,0:T(4,128)S(1)}, u32[]{:S(2)}, u32[]{:S(2)}) collective-permute-start(f32[4,3072]{1,0:T(4,128)S(1)} %fusion.52), channel_id=1, source_target_pairs={{0,24},{8,16},{16,8},{24,0},{1,25},{9,17},{17,9},{25,1},{2,26},{10... | collective-permute-start | bytes 147464 | tf_op jit(solution)/shard_map/while/body/eval_jaxpr/ppermute | solution.py:33
  234.1 1.6 collective-permute-done.4
  235.6 1.9 collective-permute-done.5
  (109 shorter events, 21.8 us)
Async XLA Ops:
  0.0 19.8 %copy-start.1 = (s32[16]{0:T(128)S(1)}, s32[16]{0:T(128)}, u32[]{:S(2)}) copy-start(s32[16]{0:T(128)} %constant.200.clone) | copy-start | bytes 196
  0.0 16.4 %copy-start = (f32[4,2,128,128]{3,2,1,0:T(8,128)S(1)}, f32[4,2,128,128]{3,2,1,0:T(8,128)}, u32[]{:S(2)}) copy-start(f32[4,2,128,128]{3,2,1,0:T(8,128)} %param.12) | copy-start | bytes 1572868
  0.0 143.6 %collective-permute-start.14 = (bf16[4,2,128,3072]{3,2,1,0:T(8,128)(2,1)}, bf16[4,2,128,3072]{3,2,1,0:T(8,128)(2,1)}, u32[]{:S(2)}, u32[]{:S(2)}) collective-permute-start(bf16[4,2,128,3072]{3,2,1,0:T(8,128)(2,1)} %param.10), channel_id=1, source_target_pairs={{0,2},{12,8},{16,22},{20,18},{10,14},{30,28},{1,3},{13,9},{17,23},... | collective-permute-start | bytes 18874376 | tf_op jit(solution)/shard_map/ppermute | solution.py:193
  8.6 15.7 %collective-permute-start.8 = (f32[4,3072]{1,0:T(4,128)S(1)}, f32[4,3072]{1,0:T(4,128)S(1)}, u32[]{:S(2)}, u32[]{:S(2)}) collective-permute-start(f32[4,3072]{1,0:T(4,128)S(1)} %dynamic_update_slice.3), channel_id=1, source_target_pairs={{0,8},{8,0},{16,24},{24,16},{1,9},{9,1},{17,25},{25,17},{2,10},{10... | collective-permute-start | bytes 147464 | tf_op jit(solution)/shard_map/ppermute | solution.py:33
  8.7 16.3 %collective-permute-start.9 = (f32[4,3072]{1,0:T(4,128)S(1)}, f32[4,3072]{1,0:T(4,128)S(1)}, u32[]{:S(2)}, u32[]{:S(2)}) collective-permute-start(f32[4,3072]{1,0:T(4,128)S(1)} %dynamic_update_slice.3), channel_id=1, source_target_pairs={{0,16},{8,24},{16,0},{24,8},{1,17},{9,25},{17,1},{25,9},{2,18},{10... | collective-permute-start | bytes 147464 | tf_op jit(solution)/shard_map/ppermute | solution.py:33
  12.3 12.7 %collective-permute-start.10 = (f32[4,3072]{1,0:T(4,128)S(1)}, f32[4,3072]{1,0:T(4,128)S(1)}, u32[]{:S(2)}, u32[]{:S(2)}) collective-permute-start(f32[4,3072]{1,0:T(4,128)S(1)} %dynamic_update_slice.3), channel_id=1, source_target_pairs={{0,24},{8,16},{16,8},{24,0},{1,25},{9,17},{17,9},{25,1},{2,26},{10... | collective-permute-start | bytes 147464 | tf_op jit(solution)/shard_map/ppermute | solution.py:33
  23.6 7.1 %collective-permute-start.15 = (f32[5,128,128]{2,1,0:T(8,128)S(1)}, f32[5,128,128]{2,1,0:T(8,128)S(1)}, u32[]{:S(2)}, u32[]{:S(2)}) collective-permute-start(f32[5,128,128]{2,1,0:T(8,128)S(1)} %fusion.29), channel_id=1, source_target_pairs={{8,2},{4,8},{24,22},{12,18},{26,14},{22,28},{9,3},{5,9},{25,23},{1... | collective-permute-start | bytes 983048 | tf_op jit(solution)/shard_map/ppermute | solution.py:205
  24.3 6.7 %collective-permute-start.16 = (f32[5,128,128]{2,1,0:T(8,128)S(1)}, f32[5,128,128]{2,1,0:T(8,128)S(1)}, u32[]{:S(2)}, u32[]{:S(2)}) collective-permute-start(f32[5,128,128]{2,1,0:T(8,128)S(1)} %fusion.29), channel_id=1, source_target_pairs={{16,8},{6,22},{17,9},{7,23}} | collective-permute-start | bytes 983048 | tf_op jit(solution)/shard_map/ppermute | solution.py:205
  25.1 117.1 %collective-permute-start.11 = (f32[4,3072]{1,0:T(4,128)S(1)}, f32[4,3072]{1,0:T(4,128)S(1)}, u32[]{:S(2)}, u32[]{:S(2)}) collective-permute-start(f32[4,3072]{1,0:T(4,128)S(1)} %fusion.34), channel_id=1, source_target_pairs={{0,2},{2,0},{4,6},{6,4},{1,3},{3,1},{5,7},{7,5},{8,10},{10,8},{12,... | collective-permute-start | bytes 147464 | tf_op jit(solution)/shard_map/ppermute | solution.py:33
  26.5 116.2 %collective-permute-start.12 = (f32[4,3072]{1,0:T(4,128)S(1)}, f32[4,3072]{1,0:T(4,128)S(1)}, u32[]{:S(2)}, u32[]{:S(2)}) collective-permute-start(f32[4,3072]{1,0:T(4,128)S(1)} %fusion.34), channel_id=1, source_target_pairs={{0,4},{2,6},{4,0},{6,2},{1,5},{3,7},{5,1},{7,3},{8,12},{10,14},{12... | collective-permute-start | bytes 147464 | tf_op jit(solution)/shard_map/ppermute | solution.py:33
  30.7 112.5 %collective-permute-start.13 = (f32[4,3072]{1,0:T(4,128)S(1)}, f32[4,3072]{1,0:T(4,128)S(1)}, u32[]{:S(2)}, u32[]{:S(2)}) collective-permute-start(f32[4,3072]{1,0:T(4,128)S(1)} %fusion.34), channel_id=1, source_target_pairs={{0,6},{2,4},{4,2},{6,0},{1,7},{3,5},{5,3},{7,1},{8,14},{10,12},{12... | collective-permute-start | bytes 147464 | tf_op jit(solution)/shard_map/ppermute | solution.py:33
  31.0 112.8 %slice-start = ((s8[6291456]{0:T(1024)(128)(4,1)}), s8[4194304]{0:T(1024)(128)(4,1)S(1)}, s32[]{:S(2)}) async-start(s8[6291456]{0:T(1024)(128)(4,1)} %bitcast.134), calls=%async_computation | async-start | bytes 8388608
  31.0 112.3 %collective-permute-start.17 = (f32[2,5,128,128]{3,2,1,0:T(8,128)S(1)}, f32[2,5,128,128]{3,2,1,0:T(8,128)S(1)}, u32[]{:S(2)}, u32[]{:S(2)}) collective-permute-start(f32[2,5,128,128]{3,2,1,0:T(8,128)S(1)} %pad_maximum_fusion.8), channel_id=1, source_target_pairs={{0,1},{1,0},{2,3},{3,2},{4,5},{5,4},{6,7},{7,6},{8,9},{9,8},{10,11... | collective-permute-start | bytes 1966088 | tf_op jit(solution)/shard_map/ppermute | solution.py:206
  148.3 13.5 %slice-start.2 = ((s8[6291456]{0:T(1024)(128)(4,1)}), s8[2097152]{0:T(1024)(128)(4,1)S(1)}, s32[]{:S(2)}) async-start(s8[6291456]{0:T(1024)(128)(4,1)} %bitcast.137), calls=%async_computation.2 | async-start | bytes 4194304 | tf_op jit(solution)/shard_map/while
  156.6 5.2 %slice-start.3 = ((s8[6291456]{0:T(1024)(128)(4,1)}), s8[4194304]{0:T(1024)(128)(4,1)S(1)}, s32[]{:S(2)}) async-start(s8[6291456]{0:T(1024)(128)(4,1)} %bitcast.137), calls=%async_computation.3 | async-start | bytes 8388608 | tf_op jit(solution)/shard_map/while
  158.6 2.7 %collective-permute-start = (f32[2,4,2,128,128]{4,3,1,2,0:T(8,128)S(1)}, f32[2,4,2,128,128]{4,3,1,2,0:T(8,128)S(1)}, u32[]{:S(2)}, u32[]{:S(2)}) collective-permute-start(f32[2,4,2,128,128]{4,3,1,2,0:T(8,128)S(1)} %pad_maximum_fusion.14), channel_id=1, source_target_pairs={{0,1},{1,0},{2,3},{3,2},{4,5},{5,4},{6,7},{7,6},{8,9},{9,8},{10,11... | collective-permute-start | bytes 3145736 | tf_op jit(solution)/shard_map/while/body/eval_jaxpr/ppermute | solution.py:49
  171.1 6.3 %collective-permute-start.1 = (f32[4,3072]{1,0:T(4,128)S(1)}, f32[4,3072]{1,0:T(4,128)S(1)}, u32[]{:S(2)}, u32[]{:S(2)}) collective-permute-start(f32[4,3072]{1,0:T(4,128)S(1)} %select_add_fusion.2), channel_id=1, source_target_pairs={{0,6},{2,4},{4,2},{6,0},{1,7},{3,5},{5,3},{7,1},{8,14},{10,12},{12... | collective-permute-start | bytes 147464 | tf_op jit(solution)/shard_map/while/body/eval_jaxpr/ppermute | solution.py:33
  172.8 6.0 %collective-permute-start.2 = (f32[4,3072]{1,0:T(4,128)S(1)}, f32[4,3072]{1,0:T(4,128)S(1)}, u32[]{:S(2)}, u32[]{:S(2)}) collective-permute-start(f32[4,3072]{1,0:T(4,128)S(1)} %select_add_fusion.2), channel_id=1, source_target_pairs={{0,4},{2,6},{4,0},{6,2},{1,5},{3,7},{5,1},{7,3},{8,12},{10,14},{12... | collective-permute-start | bytes 147464 | tf_op jit(solution)/shard_map/while/body/eval_jaxpr/ppermute | solution.py:33
  172.8 6.0 %collective-permute-start.3 = (f32[4,3072]{1,0:T(4,128)S(1)}, f32[4,3072]{1,0:T(4,128)S(1)}, u32[]{:S(2)}, u32[]{:S(2)}) collective-permute-start(f32[4,3072]{1,0:T(4,128)S(1)} %select_add_fusion.2), channel_id=1, source_target_pairs={{0,2},{2,0},{4,6},{6,4},{1,3},{3,1},{5,7},{7,5},{8,10},{10,8},{12,... | collective-permute-start | bytes 147464 | tf_op jit(solution)/shard_map/while/body/eval_jaxpr/ppermute | solution.py:33
  179.0 13.4 %collective-permute-start.4 = (f32[4,3072]{1,0:T(4,128)S(1)}, f32[4,3072]{1,0:T(4,128)S(1)}, u32[]{:S(2)}, u32[]{:S(2)}) collective-permute-start(f32[4,3072]{1,0:T(4,128)S(1)} %fusion.52), channel_id=1, source_target_pairs={{0,24},{8,16},{16,8},{24,0},{1,25},{9,17},{17,9},{25,1},{2,26},{10... | collective-permute-start | bytes 147464 | tf_op jit(solution)/shard_map/while/body/eval_jaxpr/ppermute | solution.py:33
  181.8 11.5 %collective-permute-start.5 = (f32[4,3072]{1,0:T(4,128)S(1)}, f32[4,3072]{1,0:T(4,128)S(1)}, u32[]{:S(2)}, u32[]{:S(2)}) collective-permute-start(f32[4,3072]{1,0:T(4,128)S(1)} %fusion.52), channel_id=1, source_target_pairs={{0,16},{8,24},{16,0},{24,8},{1,17},{9,25},{17,1},{25,9},{2,18},{10... | collective-permute-start | bytes 147464 | tf_op jit(solution)/shard_map/while/body/eval_jaxpr/ppermute | solution.py:33
  191.3 4.1 %collective-permute-start.6 = (f32[4,3072]{1,0:T(4,128)S(1)}, f32[4,3072]{1,0:T(4,128)S(1)}, u32[]{:S(2)}, u32[]{:S(2)}) collective-permute-start(f32[4,3072]{1,0:T(4,128)S(1)} %fusion.52), channel_id=1, source_target_pairs={{0,8},{8,0},{16,24},{24,16},{1,9},{9,1},{17,25},{25,17},{2,10},{10... | collective-permute-start | bytes 147464 | tf_op jit(solution)/shard_map/while/body/eval_jaxpr/ppermute | solution.py:33
  196.0 1.4 collective-permute-start.7
  199.5 13.5 %slice-start.2 = ((s8[6291456]{0:T(1024)(128)(4,1)}), s8[2097152]{0:T(1024)(128)(4,1)S(1)}, s32[]{:S(2)}) async-start(s8[6291456]{0:T(1024)(128)(4,1)} %bitcast.137), calls=%async_computation.2 | async-start | bytes 4194304 | tf_op jit(solution)/shard_map/while
  209.8 2.7 %collective-permute-start = (f32[2,4,2,128,128]{4,3,1,2,0:T(8,128)S(1)}, f32[2,4,2,128,128]{4,3,1,2,0:T(8,128)S(1)}, u32[]{:S(2)}, u32[]{:S(2)}) collective-permute-start(f32[2,4,2,128,128]{4,3,1,2,0:T(8,128)S(1)} %pad_maximum_fusion.14), channel_id=1, source_target_pairs={{0,1},{1,0},{2,3},{3,2},{4,5},{5,4},{6,7},{7,6},{8,9},{9,8},{10,11... | collective-permute-start | bytes 3145736 | tf_op jit(solution)/shard_map/while/body/eval_jaxpr/ppermute | solution.py:49
  222.3 6.4 %collective-permute-start.1 = (f32[4,3072]{1,0:T(4,128)S(1)}, f32[4,3072]{1,0:T(4,128)S(1)}, u32[]{:S(2)}, u32[]{:S(2)}) collective-permute-start(f32[4,3072]{1,0:T(4,128)S(1)} %select_add_fusion.2), channel_id=1, source_target_pairs={{0,6},{2,4},{4,2},{6,0},{1,7},{3,5},{5,3},{7,1},{8,14},{10,12},{12... | collective-permute-start | bytes 147464 | tf_op jit(solution)/shard_map/while/body/eval_jaxpr/ppermute | solution.py:33
  225.2 5.0 %collective-permute-start.2 = (f32[4,3072]{1,0:T(4,128)S(1)}, f32[4,3072]{1,0:T(4,128)S(1)}, u32[]{:S(2)}, u32[]{:S(2)}) collective-permute-start(f32[4,3072]{1,0:T(4,128)S(1)} %select_add_fusion.2), channel_id=1, source_target_pairs={{0,4},{2,6},{4,0},{6,2},{1,5},{3,7},{5,1},{7,3},{8,12},{10,14},{12... | collective-permute-start | bytes 147464 | tf_op jit(solution)/shard_map/while/body/eval_jaxpr/ppermute | solution.py:33
  225.2 5.1 %collective-permute-start.3 = (f32[4,3072]{1,0:T(4,128)S(1)}, f32[4,3072]{1,0:T(4,128)S(1)}, u32[]{:S(2)}, u32[]{:S(2)}) collective-permute-start(f32[4,3072]{1,0:T(4,128)S(1)} %select_add_fusion.2), channel_id=1, source_target_pairs={{0,2},{2,0},{4,6},{6,4},{1,3},{3,1},{5,7},{7,5},{8,10},{10,8},{12,... | collective-permute-start | bytes 147464 | tf_op jit(solution)/shard_map/while/body/eval_jaxpr/ppermute | solution.py:33
  230.5 5.2 %collective-permute-start.4 = (f32[4,3072]{1,0:T(4,128)S(1)}, f32[4,3072]{1,0:T(4,128)S(1)}, u32[]{:S(2)}, u32[]{:S(2)}) collective-permute-start(f32[4,3072]{1,0:T(4,128)S(1)} %fusion.52), channel_id=1, source_target_pairs={{0,24},{8,16},{16,8},{24,0},{1,25},{9,17},{17,9},{25,1},{2,26},{10... | collective-permute-start | bytes 147464 | tf_op jit(solution)/shard_map/while/body/eval_jaxpr/ppermute | solution.py:33
  233.4 4.1 %collective-permute-start.5 = (f32[4,3072]{1,0:T(4,128)S(1)}, f32[4,3072]{1,0:T(4,128)S(1)}, u32[]{:S(2)}, u32[]{:S(2)}) collective-permute-start(f32[4,3072]{1,0:T(4,128)S(1)} %fusion.52), channel_id=1, source_target_pairs={{0,16},{8,24},{16,0},{24,8},{1,17},{9,25},{17,1},{25,9},{2,18},{10... | collective-permute-start | bytes 147464 | tf_op jit(solution)/shard_map/while/body/eval_jaxpr/ppermute | solution.py:33
  233.4 4.1 %collective-permute-start.6 = (f32[4,3072]{1,0:T(4,128)S(1)}, f32[4,3072]{1,0:T(4,128)S(1)}, u32[]{:S(2)}, u32[]{:S(2)}) collective-permute-start(f32[4,3072]{1,0:T(4,128)S(1)} %fusion.52), channel_id=1, source_target_pairs={{0,8},{8,0},{16,24},{24,16},{1,9},{9,1},{17,25},{25,17},{2,10},{10... | collective-permute-start | bytes 147464 | tf_op jit(solution)/shard_map/while/body/eval_jaxpr/ppermute | solution.py:33
  238.2 1.4 collective-permute-start.7
  (2 other events, 6.8 us)

commit v14 on v12

--- a/solution.py
+++ b/solution.py
@@ -214,6 +214,7 @@
     other = lax.cond(is_diag, lambda: green_panel, lambda: received)
     mine_rows = green_panel.reshape(freq_count, 2 * span_j, local_pts)
     other_rows = other.reshape(freq_count, 2 * span_j, local_pts)
+    stacked_rows = jnp.concatenate([mine_rows, other_rows], axis=1)
     moved_table = jnp.array(moved, jnp.int32)[slot]
     first_block = arrived[moved_table[0]]
     second_block = arrived[moved_table[1]]
@@ -239,9 +240,15 @@
         both = swap_add(jnp.stack([corr_first, corr_second]), "pts")
         adj_first = (scale_first * (quad_weight * both[0] - obs_first)).astype(jnp.bfloat16)
         adj_second = (scale_second * (quad_weight * both[1] - obs_second)).astype(jnp.bfloat16)
-        term_first = point_terms(adj_first, other_rows, mine_rows, psd_field, quad_weight)
-        term_second = point_terms(adj_second, mine_rows, other_rows, psd_field, quad_weight)
-        point_part = jnp.where(keep_first, term_first, 0.0) + jnp.where(keep_second, term_second, 0.0)
+        block_first = jnp.where(keep_first, adjoint_block(adj_first), jnp.zeros((), jnp.bfloat16))
+        block_second = jnp.where(keep_second, adjoint_block(adj_second), jnp.zeros((), jnp.bfloat16))
+        empty = jnp.zeros_like(block_first)
+        crossed = jnp.concatenate(
+            [jnp.concatenate([empty, block_first], axis=2), jnp.concatenate([block_second, empty], axis=2)],
+            axis=1,
+        )
+        accumulated = jnp.einsum("fab,fbn->fan", crossed, stacked_rows, preferred_element_type=jnp.float32)
+        point_part = quad_weight * psd_field * jnp.sum(stacked_rows * accumulated, axis=1)
         gradient = butterfly_sum(point_part, axes)
         squares = swap_add(jnp.sum(gradient * gradient), "pts")
         return log_field - descent * gradient / jnp.sqrt(squares / entry_count + epsilon)

time: 242 us -> 263 us (1.087)
  matrix products: 18.5 us -> 29.8 us
  other arithmetic: 8.87 us -> 20 us
    dot_general x4 -> x2, matrix products: 18.5 us -> 29.8 us  [run_sweep(): jnp.einsum('fab,fbn->fan', crossed, stacked_rows, preferred_element_type=...]
    concatenate x0 -> x1, other arithmetic: none -> 10.5 us  [pair_body(): stacked_rows = jnp.concatenate([mine_rows, other_rows], axis=1)]
where the time goes in v14:
time: 263 us
  waiting for transfers between devices  134 us (51%)
  starting transfers between devices  44.6 us (17%)
  matrix products  29.8 us (11%)
  other arithmetic  20 us (8%)
  Pallas kernels  16.3 us (6%)
  local copies, waits for them, and re-layouts  9.32 us (4%)
  between operations  5.86 us (2%)
  loops' own time  2.91 us (1%)
    ppermute x18, waiting for transfers between devices, butterfly_sum(): got.append(lax.ppermute(value, axis, [(i, i ^ mask) for i in range(size)]))  126 us
    ppermute x18, starting transfers between devices, butterfly_sum(): got.append(lax.ppermute(value, axis, [(i, i ^ mask) for i in range(size)]))  35.2 us
    dot_general x2, matrix products, run_sweep(): jnp.einsum('fab,fbn->fan', crossed, stacked_rows, preferred_element_type=...  29.8 us
    pallas_call x2, Pallas kernels, pair_products(): pl.pallas_call(kernel, grid=(freq, points // tile), in_specs=[spec, spec,...  16.3 us
    concatenate x1, other arithmetic, pair_body(): stacked_rows = jnp.concatenate([mine_rows, other_rows], axis=1)  10.5 us
    ppermute x4, waiting for transfers between devices, swap_add(): return value + lax.ppermute(value, axis, [(0, 1), (1, 0)])  7.83 us
    ppermute x1, starting transfers between devices, pair_body(): received = lax.ppermute(green_panel, axes, panel_moves)  7.68 us
  transfers between devices with their start and end apart: 26, of which 15 were waited for; matrix products, arithmetic and copies ran while one was open for 2% of the time, Pallas kernels for 0%

profile of v14, /device:TPU:0, one launch (start us, length us, event | category | flops | bytes accessed | tf_op | source)
XLA Modules:
  0.0 262.5 jit_solution(13274748076656140594)
XLA Ops:
  0.0 7.7 %collective-permute-start.14 = (bf16[4,2,128,3072]{3,2,1,0:T(8,128)(2,1)}, bf16[4,2,128,3072]{3,2,1,0:T(8,128)(2,1)}, u32[]{:S(2)}, u32[]{:S(2)}) collective-permute-start(bf16[4,2,128,3072]{3,2,1,0:T(8,128)(2,1)} %param.10), channel_id=1, source_target_pairs={{0,2},{12,8},{16,22},{20,18},{10,14},{30,28},{1,3},{13,9},{17,23},... | collective-permute-start | bytes 18874376 | tf_op jit(solution)/shard_map/ppermute | solution.py:193
  8.6 3.6 %collective-permute-start.9 = (f32[4,3072]{1,0:T(4,128)S(1)}, f32[4,3072]{1,0:T(4,128)S(1)}, u32[]{:S(2)}, u32[]{:S(2)}) collective-permute-start(f32[4,3072]{1,0:T(4,128)S(1)} %dynamic_update_slice.3), channel_id=1, source_target_pairs={{0,16},{8,24},{16,0},{24,8},{1,17},{9,25},{17,1},{25,9},{2,18},{10... | collective-permute-start | bytes 147464 | tf_op jit(solution)/shard_map/ppermute | solution.py:33
  12.2 1.4 collective-permute-start.10
  25.8 1.4 collective-permute-start.11
  27.2 4.2 %collective-permute-start.12 = (f32[4,3072]{1,0:T(4,128)S(1)}, f32[4,3072]{1,0:T(4,128)S(1)}, u32[]{:S(2)}, u32[]{:S(2)}) collective-permute-start(f32[4,3072]{1,0:T(4,128)S(1)} %fusion.29), channel_id=1, source_target_pairs={{0,4},{2,6},{4,0},{6,2},{1,5},{3,7},{5,1},{7,3},{8,12},{10,14},{12... | collective-permute-start | bytes 147464 | tf_op jit(solution)/shard_map/ppermute | solution.py:33
  31.8 110.3 %collective-permute-done.11 = f32[4,3072]{1,0:T(4,128)S(1)} collective-permute-done((f32[4,3072]{1,0:T(4,128)S(1)}, f32[4,3072]{1,0:T(4,128)S(1)}, u32[]{:S(2)}, u32[]{:S(2)}) %collective-permute-start.11) | collective-permute-done | bytes 49184 | tf_op jit(solution)/shard_map/ppermute | solution.py:33
  145.0 2.6 conditional.1
  145.0 2.6 copy.11
  147.6 10.5 %pad_maximum_fusion.3 = bf16[4,512,3072]{2,1,0:T(8,128)(2,1)} fusion(bf16[4,256,3072]{2,1,0:T(8,128)(2,1)} %get-tuple-element.364, bf16[4,256,3072]{2,1,0:T(8,128)(2,1)} %bitcast.132), kind=kLoop, calls=%fused_computation.46 | loop fusion | flops 25165824 | bytes 25165824 | tf_op jit(solution)/shard_map/concatenate | solution.py:217
  158.1 103.7 %while.13 = (s32[]{:T(128)}, f32[4,3072]{1,0:T(4,128)S(1)}, bf16[4,512,3072]{2,1,0:T(8,128)(2,1)}, pred[]{:T(512)}, f32[1,128,128]{2,1,0:T(8,128)S(1)}, /*index=...) while((s32[]{:T(128)}, f32[4,3072]{1,0:T(4,128)S(1)}, ...), condition=%wide.region_5.6_spmd, body=%wide.region_2.5_spmd.sunk | while | flops 6477402112 | bytes 41911516 | solution.py:256
  158.8 8.1 %eval_jaxpr.5 = (f32[4,256,256]{2,1,0:T(8,128)}, f32[4,256,256]{2,1,0:T(8,128)}) custom-call(bf16[4,256,3072]{2,1,0:T(8,128)(2,1)} %get-tuple-element.403.mine_ref, bf16[4,256,3072]{2,1,0:T(8,128)(2,1)} %get-tuple-element.404.other_ref, f32[4,1,3072]{2,1,0:T(1,128)} %broadcast_in_dim.27.field_ref), custom_call_target="tpu_custom_call" | custom-call | tf_op jit(solution)/shard_map/while/body/eval_jaxpr/pallas_call | solution.py:79
  166.9 1.4 add_bitcast_fusion.6
  168.8 2.6 %collective-permute-done = f32[2,4,2,128,128]{4,3,1,2,0:T(8,128)S(1)} collective-permute-done((f32[2,4,2,128,128]{4,3,1,2,0:T(8,128)S(1)}, f32[2,4,2,128,128]{4,3,1,2,0:T(8,128)S(1)}, u32[]{:S(2)}, u32[]{:S(2)}) %collective-permute-start) | collective-permute-done | bytes 1048608 | tf_op jit(solution)/shard_map/while/body/eval_jaxpr/ppermute | solution.py:49
  172.1 14.9 %multiply_reduce_fusion.4 = f32[4,3072]{1,0:T(4,128)S(1)} fusion(bf16[4,512,3072]{2,1,0:T(8,128)(2,1)} %get-tuple-element.400, bf16[4,256,256]{2,1,0:T(8,128)(2,1)S(1)} %get-tuple-element.352, bf16[4,256,256]{2,1,0:T(8,128)(2,1)S(1)} %get-tuple-element.353), kind=kOutput, calls=%fused_computation.clone.1 | convolution fusion | flops 6469701632 | bytes 13680640 | tf_op jit(solution)/shard_map/while/body/eval_jaxpr/fab,fbn->fan/dot_general | solution.py:250
  187.0 2.8 %collective-permute-start.1 = (f32[4,3072]{1,0:T(4,128)S(1)}, f32[4,3072]{1,0:T(4,128)S(1)}, u32[]{:S(2)}, u32[]{:S(2)}) collective-permute-start(f32[4,3072]{1,0:T(4,128)S(1)} %multiply_multiply_fusion.2), channel_id=1, source_target_pairs={{0,24},{8,16},{16,8},{24,0},{1,25},{9,17},{17,9},{25,1},{2,26},{10... | collective-permute-start | bytes 147464 | tf_op jit(solution)/shard_map/while/body/eval_jaxpr/ppermute | solution.py:33
  189.9 7.0 %collective-permute-start.2 = (f32[4,3072]{1,0:T(4,128)S(1)}, f32[4,3072]{1,0:T(4,128)S(1)}, u32[]{:S(2)}, u32[]{:S(2)}) collective-permute-start(f32[4,3072]{1,0:T(4,128)S(1)} %multiply_multiply_fusion.2), channel_id=1, source_target_pairs={{0,16},{8,24},{16,0},{24,8},{1,17},{9,25},{17,1},{25,9},{2,18},{10... | collective-permute-start | bytes 147464 | tf_op jit(solution)/shard_map/while/body/eval_jaxpr/ppermute | solution.py:33
  196.8 2.1 collective-permute-done.2
  198.9 2.0 collective-permute-done.3
  201.1 5.9 %collective-permute-start.5 = (f32[4,3072]{1,0:T(4,128)S(1)}, f32[4,3072]{1,0:T(4,128)S(1)}, u32[]{:S(2)}, u32[]{:S(2)}) collective-permute-start(f32[4,3072]{1,0:T(4,128)S(1)} %fusion.43), channel_id=1, source_target_pairs={{0,4},{2,6},{4,0},{6,2},{1,5},{3,7},{5,1},{7,3},{8,12},{10,14},{12... | collective-permute-start | bytes 147464 | tf_op jit(solution)/shard_map/while/body/eval_jaxpr/ppermute | solution.py:33
  207.5 2.5 collective-permute-done.5
  211.8 1.3 collective-permute-done.7
  215.2 8.1 %eval_jaxpr.5 = (f32[4,256,256]{2,1,0:T(8,128)}, f32[4,256,256]{2,1,0:T(8,128)}) custom-call(bf16[4,256,3072]{2,1,0:T(8,128)(2,1)} %get-tuple-element.403.mine_ref, bf16[4,256,3072]{2,1,0:T(8,128)(2,1)} %get-tuple-element.404.other_ref, f32[4,1,3072]{2,1,0:T(1,128)} %broadcast_in_dim.27.field_ref), custom_call_target="tpu_custom_call" | custom-call | tf_op jit(solution)/shard_map/while/body/eval_jaxpr/pallas_call | solution.py:79
  223.3 1.4 add_bitcast_fusion.6
  225.4 2.5 collective-permute-done
  228.5 14.9 %multiply_reduce_fusion.4 = f32[4,3072]{1,0:T(4,128)S(1)} fusion(bf16[4,512,3072]{2,1,0:T(8,128)(2,1)} %get-tuple-element.400, bf16[4,256,256]{2,1,0:T(8,128)(2,1)S(1)} %get-tuple-element.352, bf16[4,256,256]{2,1,0:T(8,128)(2,1)S(1)} %get-tuple-element.353), kind=kOutput, calls=%fused_computation.clone.1 | convolution fusion | flops 6469701632 | bytes 13680640 | tf_op jit(solution)/shard_map/while/body/eval_jaxpr/fab,fbn->fan/dot_general | solution.py:250
  243.4 2.8 %collective-permute-start.1 = (f32[4,3072]{1,0:T(4,128)S(1)}, f32[4,3072]{1,0:T(4,128)S(1)}, u32[]{:S(2)}, u32[]{:S(2)}) collective-permute-start(f32[4,3072]{1,0:T(4,128)S(1)} %multiply_multiply_fusion.2), channel_id=1, source_target_pairs={{0,24},{8,16},{16,8},{24,0},{1,25},{9,17},{17,9},{25,1},{2,26},{10... | collective-permute-start | bytes 147464 | tf_op jit(solution)/shard_map/while/body/eval_jaxpr/ppermute | solution.py:33
  247.0 1.5 collective-permute-done.1
  248.5 1.9 collective-permute-done.2
  250.4 2.9 %collective-permute-start.4 = (f32[4,3072]{1,0:T(4,128)S(1)}, f32[4,3072]{1,0:T(4,128)S(1)}, u32[]{:S(2)}, u32[]{:S(2)}) collective-permute-start(f32[4,3072]{1,0:T(4,128)S(1)} %fusion.43), channel_id=1, source_target_pairs={{0,6},{2,4},{4,2},{6,0},{1,7},{3,5},{5,3},{7,1},{8,14},{10,12},{12... | collective-permute-start | bytes 147464 | tf_op jit(solution)/shard_map/while/body/eval_jaxpr/ppermute | solution.py:33
  253.4 1.5 collective-permute-start.6
  254.9 1.6 collective-permute-done.4
  256.5 1.9 collective-permute-done.5
  (104 shorter events, 20.4 us)
Async XLA Ops:
  0.0 20.7 %copy-start.1 = (s32[16]{0:T(128)S(1)}, s32[16]{0:T(128)}, u32[]{:S(2)}) copy-start(s32[16]{0:T(128)} %constant.207.clone) | copy-start | bytes 196
  0.0 143.6 %collective-permute-start.14 = (bf16[4,2,128,3072]{3,2,1,0:T(8,128)(2,1)}, bf16[4,2,128,3072]{3,2,1,0:T(8,128)(2,1)}, u32[]{:S(2)}, u32[]{:S(2)}) collective-permute-start(bf16[4,2,128,3072]{3,2,1,0:T(8,128)(2,1)} %param.10), channel_id=1, source_target_pairs={{0,2},{12,8},{16,22},{20,18},{10,14},{30,28},{1,3},{13,9},{17,23},... | collective-permute-start | bytes 18874376 | tf_op jit(solution)/shard_map/ppermute | solution.py:193
  8.5 16.4 %collective-permute-start.8 = (f32[4,3072]{1,0:T(4,128)S(1)}, f32[4,3072]{1,0:T(4,128)S(1)}, u32[]{:S(2)}, u32[]{:S(2)}) collective-permute-start(f32[4,3072]{1,0:T(4,128)S(1)} %dynamic_update_slice.3), channel_id=1, source_target_pairs={{0,8},{8,0},{16,24},{24,16},{1,9},{9,1},{17,25},{25,17},{2,10},{10... | collective-permute-start | bytes 147464 | tf_op jit(solution)/shard_map/ppermute | solution.py:33
  8.6 17.1 %collective-permute-start.9 = (f32[4,3072]{1,0:T(4,128)S(1)}, f32[4,3072]{1,0:T(4,128)S(1)}, u32[]{:S(2)}, u32[]{:S(2)}) collective-permute-start(f32[4,3072]{1,0:T(4,128)S(1)} %dynamic_update_slice.3), channel_id=1, source_target_pairs={{0,16},{8,24},{16,0},{24,8},{1,17},{9,25},{17,1},{25,9},{2,18},{10... | collective-permute-start | bytes 147464 | tf_op jit(solution)/shard_map/ppermute | solution.py:33
  12.2 13.5 %collective-permute-start.10 = (f32[4,3072]{1,0:T(4,128)S(1)}, f32[4,3072]{1,0:T(4,128)S(1)}, u32[]{:S(2)}, u32[]{:S(2)}) collective-permute-start(f32[4,3072]{1,0:T(4,128)S(1)} %dynamic_update_slice.3), channel_id=1, source_target_pairs={{0,24},{8,16},{16,8},{24,0},{1,25},{9,17},{17,9},{25,1},{2,26},{10... | collective-permute-start | bytes 147464 | tf_op jit(solution)/shard_map/ppermute | solution.py:33
  24.3 7.1 %collective-permute-start.15 = (f32[5,128,128]{2,1,0:T(8,128)S(1)}, f32[5,128,128]{2,1,0:T(8,128)S(1)}, u32[]{:S(2)}, u32[]{:S(2)}) collective-permute-start(f32[5,128,128]{2,1,0:T(8,128)S(1)} %fusion.25), channel_id=1, source_target_pairs={{8,2},{4,8},{24,22},{12,18},{26,14},{22,28},{9,3},{5,9},{25,23},{1... | collective-permute-start | bytes 983048 | tf_op jit(solution)/shard_map/ppermute | solution.py:205
  25.0 6.7 %collective-permute-start.16 = (f32[5,128,128]{2,1,0:T(8,128)S(1)}, f32[5,128,128]{2,1,0:T(8,128)S(1)}, u32[]{:S(2)}, u32[]{:S(2)}) collective-permute-start(f32[5,128,128]{2,1,0:T(8,128)S(1)} %fusion.25), channel_id=1, source_target_pairs={{16,8},{6,22},{17,9},{7,23}} | collective-permute-start | bytes 983048 | tf_op jit(solution)/shard_map/ppermute | solution.py:205
  25.8 116.4 %collective-permute-start.11 = (f32[4,3072]{1,0:T(4,128)S(1)}, f32[4,3072]{1,0:T(4,128)S(1)}, u32[]{:S(2)}, u32[]{:S(2)}) collective-permute-start(f32[4,3072]{1,0:T(4,128)S(1)} %fusion.29), channel_id=1, source_target_pairs={{0,2},{2,0},{4,6},{6,4},{1,3},{3,1},{5,7},{7,5},{8,10},{10,8},{12,... | collective-permute-start | bytes 147464 | tf_op jit(solution)/shard_map/ppermute | solution.py:33
  27.2 115.5 %collective-permute-start.12 = (f32[4,3072]{1,0:T(4,128)S(1)}, f32[4,3072]{1,0:T(4,128)S(1)}, u32[]{:S(2)}, u32[]{:S(2)}) collective-permute-start(f32[4,3072]{1,0:T(4,128)S(1)} %fusion.29), channel_id=1, source_target_pairs={{0,4},{2,6},{4,0},{6,2},{1,5},{3,7},{5,1},{7,3},{8,12},{10,14},{12... | collective-permute-start | bytes 147464 | tf_op jit(solution)/shard_map/ppermute | solution.py:33
  31.4 111.8 %collective-permute-start.13 = (f32[4,3072]{1,0:T(4,128)S(1)}, f32[4,3072]{1,0:T(4,128)S(1)}, u32[]{:S(2)}, u32[]{:S(2)}) collective-permute-start(f32[4,3072]{1,0:T(4,128)S(1)} %fusion.29), channel_id=1, source_target_pairs={{0,6},{2,4},{4,2},{6,0},{1,7},{3,5},{5,3},{7,1},{8,14},{10,12},{12... | collective-permute-start | bytes 147464 | tf_op jit(solution)/shard_map/ppermute | solution.py:33
  31.7 112.2 %slice-start = ((s8[6291456]{0:T(1024)(128)(4,1)}), s8[4194304]{0:T(1024)(128)(4,1)S(1)}, s32[]{:S(2)}) async-start(s8[6291456]{0:T(1024)(128)(4,1)} %bitcast.134), calls=%async_computation | async-start | bytes 8388608
  31.7 111.6 %collective-permute-start.17 = (f32[2,5,128,128]{3,2,1,0:T(8,128)S(1)}, f32[2,5,128,128]{3,2,1,0:T(8,128)S(1)}, u32[]{:S(2)}, u32[]{:S(2)}) collective-permute-start(f32[2,5,128,128]{3,2,1,0:T(8,128)S(1)} %pad_maximum_fusion.9), channel_id=1, source_target_pairs={{0,1},{1,0},{2,3},{3,2},{4,5},{5,4},{6,7},{7,6},{8,9},{9,8},{10,11... | collective-permute-start | bytes 1966088 | tf_op jit(solution)/shard_map/ppermute | solution.py:206
  143.4 1.6 slice-start.1
  166.9 1.6 copy-start
  168.7 2.7 %collective-permute-start = (f32[2,4,2,128,128]{4,3,1,2,0:T(8,128)S(1)}, f32[2,4,2,128,128]{4,3,1,2,0:T(8,128)S(1)}, u32[]{:S(2)}, u32[]{:S(2)}) collective-permute-start(f32[2,4,2,128,128]{4,3,1,2,0:T(8,128)S(1)} %pad_maximum_fusion.15), channel_id=1, source_target_pairs={{0,1},{1,0},{2,3},{3,2},{4,5},{5,4},{6,7},{7,6},{8,9},{9,8},{10,11... | collective-permute-start | bytes 3145736 | tf_op jit(solution)/shard_map/while/body/eval_jaxpr/ppermute | solution.py:49
  187.0 9.8 %collective-permute-start.1 = (f32[4,3072]{1,0:T(4,128)S(1)}, f32[4,3072]{1,0:T(4,128)S(1)}, u32[]{:S(2)}, u32[]{:S(2)}) collective-permute-start(f32[4,3072]{1,0:T(4,128)S(1)} %multiply_multiply_fusion.2), channel_id=1, source_target_pairs={{0,24},{8,16},{16,8},{24,0},{1,25},{9,17},{17,9},{25,1},{2,26},{10... | collective-permute-start | bytes 147464 | tf_op jit(solution)/shard_map/while/body/eval_jaxpr/ppermute | solution.py:33
  189.9 9.0 %collective-permute-start.2 = (f32[4,3072]{1,0:T(4,128)S(1)}, f32[4,3072]{1,0:T(4,128)S(1)}, u32[]{:S(2)}, u32[]{:S(2)}) collective-permute-start(f32[4,3072]{1,0:T(4,128)S(1)} %multiply_multiply_fusion.2), channel_id=1, source_target_pairs={{0,16},{8,24},{16,0},{24,8},{1,17},{9,25},{17,1},{25,9},{2,18},{10... | collective-permute-start | bytes 147464 | tf_op jit(solution)/shard_map/while/body/eval_jaxpr/ppermute | solution.py:33
  196.8 4.1 %collective-permute-start.3 = (f32[4,3072]{1,0:T(4,128)S(1)}, f32[4,3072]{1,0:T(4,128)S(1)}, u32[]{:S(2)}, u32[]{:S(2)}) collective-permute-start(f32[4,3072]{1,0:T(4,128)S(1)} %multiply_multiply_fusion.2), channel_id=1, source_target_pairs={{0,8},{8,0},{16,24},{24,16},{1,9},{9,1},{17,25},{25,17},{2,10},{10... | collective-permute-start | bytes 147464 | tf_op jit(solution)/shard_map/while/body/eval_jaxpr/ppermute | solution.py:33
  201.0 6.5 %collective-permute-start.4 = (f32[4,3072]{1,0:T(4,128)S(1)}, f32[4,3072]{1,0:T(4,128)S(1)}, u32[]{:S(2)}, u32[]{:S(2)}) collective-permute-start(f32[4,3072]{1,0:T(4,128)S(1)} %fusion.43), channel_id=1, source_target_pairs={{0,6},{2,4},{4,2},{6,0},{1,7},{3,5},{5,3},{7,1},{8,14},{10,12},{12... | collective-permute-start | bytes 147464 | tf_op jit(solution)/shard_map/while/body/eval_jaxpr/ppermute | solution.py:33
  201.1 8.9 %collective-permute-start.5 = (f32[4,3072]{1,0:T(4,128)S(1)}, f32[4,3072]{1,0:T(4,128)S(1)}, u32[]{:S(2)}, u32[]{:S(2)}) collective-permute-start(f32[4,3072]{1,0:T(4,128)S(1)} %fusion.43), channel_id=1, source_target_pairs={{0,4},{2,6},{4,0},{6,2},{1,5},{3,7},{5,1},{7,3},{8,12},{10,14},{12... | collective-permute-start | bytes 147464 | tf_op jit(solution)/shard_map/while/body/eval_jaxpr/ppermute | solution.py:33
  207.0 4.1 %collective-permute-start.6 = (f32[4,3072]{1,0:T(4,128)S(1)}, f32[4,3072]{1,0:T(4,128)S(1)}, u32[]{:S(2)}, u32[]{:S(2)}) collective-permute-start(f32[4,3072]{1,0:T(4,128)S(1)} %fusion.43), channel_id=1, source_target_pairs={{0,2},{2,0},{4,6},{6,4},{1,3},{3,1},{5,7},{7,5},{8,10},{10,8},{12,... | collective-permute-start | bytes 147464 | tf_op jit(solution)/shard_map/while/body/eval_jaxpr/ppermute | solution.py:33
  211.8 1.4 collective-permute-start.7
  223.3 1.6 copy-start
  225.1 2.7 %collective-permute-start = (f32[2,4,2,128,128]{4,3,1,2,0:T(8,128)S(1)}, f32[2,4,2,128,128]{4,3,1,2,0:T(8,128)S(1)}, u32[]{:S(2)}, u32[]{:S(2)}) collective-permute-start(f32[2,4,2,128,128]{4,3,1,2,0:T(8,128)S(1)} %pad_maximum_fusion.15), channel_id=1, source_target_pairs={{0,1},{1,0},{2,3},{3,2},{4,5},{5,4},{6,7},{7,6},{8,9},{9,8},{10,11... | collective-permute-start | bytes 3145736 | tf_op jit(solution)/shard_map/while/body/eval_jaxpr/ppermute | solution.py:49
  243.4 5.1 %collective-permute-start.1 = (f32[4,3072]{1,0:T(4,128)S(1)}, f32[4,3072]{1,0:T(4,128)S(1)}, u32[]{:S(2)}, u32[]{:S(2)}) collective-permute-start(f32[4,3072]{1,0:T(4,128)S(1)} %multiply_multiply_fusion.2), channel_id=1, source_target_pairs={{0,24},{8,16},{16,8},{24,0},{1,25},{9,17},{17,9},{25,1},{2,26},{10... | collective-permute-start | bytes 147464 | tf_op jit(solution)/shard_map/while/body/eval_jaxpr/ppermute | solution.py:33
  246.3 4.1 %collective-permute-start.2 = (f32[4,3072]{1,0:T(4,128)S(1)}, f32[4,3072]{1,0:T(4,128)S(1)}, u32[]{:S(2)}, u32[]{:S(2)}) collective-permute-start(f32[4,3072]{1,0:T(4,128)S(1)} %multiply_multiply_fusion.2), channel_id=1, source_target_pairs={{0,16},{8,24},{16,0},{24,8},{1,17},{9,25},{17,1},{25,9},{2,18},{10... | collective-permute-start | bytes 147464 | tf_op jit(solution)/shard_map/while/body/eval_jaxpr/ppermute | solution.py:33
  246.3 4.1 %collective-permute-start.3 = (f32[4,3072]{1,0:T(4,128)S(1)}, f32[4,3072]{1,0:T(4,128)S(1)}, u32[]{:S(2)}, u32[]{:S(2)}) collective-permute-start(f32[4,3072]{1,0:T(4,128)S(1)} %multiply_multiply_fusion.2), channel_id=1, source_target_pairs={{0,8},{8,0},{16,24},{24,16},{1,9},{9,1},{17,25},{25,17},{2,10},{10... | collective-permute-start | bytes 147464 | tf_op jit(solution)/shard_map/while/body/eval_jaxpr/ppermute | solution.py:33
  250.4 6.0 %collective-permute-start.4 = (f32[4,3072]{1,0:T(4,128)S(1)}, f32[4,3072]{1,0:T(4,128)S(1)}, u32[]{:S(2)}, u32[]{:S(2)}) collective-permute-start(f32[4,3072]{1,0:T(4,128)S(1)} %fusion.43), channel_id=1, source_target_pairs={{0,6},{2,4},{4,2},{6,0},{1,7},{3,5},{5,3},{7,1},{8,14},{10,12},{12... | collective-permute-start | bytes 147464 | tf_op jit(solution)/shard_map/while/body/eval_jaxpr/ppermute | solution.py:33
  253.4 5.0 %collective-permute-start.5 = (f32[4,3072]{1,0:T(4,128)S(1)}, f32[4,3072]{1,0:T(4,128)S(1)}, u32[]{:S(2)}, u32[]{:S(2)}) collective-permute-start(f32[4,3072]{1,0:T(4,128)S(1)} %fusion.43), channel_id=1, source_target_pairs={{0,4},{2,6},{4,0},{6,2},{1,5},{3,7},{5,1},{7,3},{8,12},{10,14},{12... | collective-permute-start | bytes 147464 | tf_op jit(solution)/shard_map/while/body/eval_jaxpr/ppermute | solution.py:33
  253.4 5.0 %collective-permute-start.6 = (f32[4,3072]{1,0:T(4,128)S(1)}, f32[4,3072]{1,0:T(4,128)S(1)}, u32[]{:S(2)}, u32[]{:S(2)}) collective-permute-start(f32[4,3072]{1,0:T(4,128)S(1)} %fusion.43), channel_id=1, source_target_pairs={{0,2},{2,0},{4,6},{6,4},{1,3},{3,1},{5,7},{7,5},{8,10},{10,8},{12,... | collective-permute-start | bytes 147464 | tf_op jit(solution)/shard_map/while/body/eval_jaxpr/ppermute | solution.py:33
  259.1 1.4 collective-permute-start.7

commit v15 on v12

--- a/solution.py
+++ b/solution.py
@@ -58,31 +58,30 @@
     return jnp.stack([corr_real, corr_imag], axis=1)
 
 
-def pair_products(mine, other, field, tile=3072):
+def pair_products(mine, other, field):
     freq, rows, points = mine.shape
+    half = rows // 2
+
     def kernel(mine_ref, other_ref, field_ref, first_ref, second_ref):
-        step = pl.program_id(1)
-        @pl.when(step == 0)
-        def _():
-            first_ref[...] = jnp.zeros_like(first_ref)
-            second_ref[...] = jnp.zeros_like(second_ref)
         spread = field_ref[0]
         mine_tile = mine_ref[0]
         other_tile = other_ref[0]
         weighted_other = (other_tile.astype(jnp.float32) * spread).astype(jnp.bfloat16)
         weighted_mine = (mine_tile.astype(jnp.float32) * spread).astype(jnp.bfloat16)
         dims = (((1,), (1,)), ((), ()))
-        first_ref[0] += jax.lax.dot_general(mine_tile, weighted_other, dims, preferred_element_type=jnp.float32)
-        second_ref[0] += jax.lax.dot_general(other_tile, weighted_mine, dims, preferred_element_type=jnp.float32)
-    spec = pl.BlockSpec((1, rows, tile), lambda f, t: (f, 0, t))
-    out_spec = pl.BlockSpec((1, rows, rows), lambda f, t: (f, 0, 0))
+        for out_ref, left, right in ((first_ref, mine_tile, weighted_other), (second_ref, other_tile, weighted_mine)):
+            products = jax.lax.dot_general(left, right, dims, preferred_element_type=jnp.float32)
+            out_ref[0, 0] = products[:half, :half] + products[half:, half:]
+            out_ref[0, 1] = products[half:, :half] - products[:half, half:]
+
+    spec = pl.BlockSpec((1, rows, points), lambda f: (f, 0, 0))
+    out_spec = pl.BlockSpec((1, 2, half, half), lambda f: (f, 0, 0, 0))
     return pl.pallas_call(
         kernel,
-        grid=(freq, points // tile),
-        in_specs=[spec, spec, pl.BlockSpec((1, 1, tile), lambda f, t: (f, 0, t))],
+        grid=(freq,),
+        in_specs=[spec, spec, pl.BlockSpec((1, 1, points), lambda f: (f, 0, 0))],
         out_specs=[out_spec, out_spec],
-        out_shape=[jax.ShapeDtypeStruct((freq, rows, rows), jnp.float32)] * 2,
-        compiler_params=pltpu.CompilerParams(dimension_semantics=("parallel", "arbitrary")),
+        out_shape=[jax.ShapeDtypeStruct((freq, 2, half, half), jnp.float32)] * 2,
     )(mine, other, field[:, None, :])
 
 
@@ -233,9 +232,7 @@
     def run_sweep(sweep_idx, log_field):
         psd_field = jnp.exp(log_field)
         spread = psd_field[:, None, None, :]
-        product_first, product_second = pair_products(mine_rows, other_rows, psd_field)
-        corr_first = combine(product_first, span_j, span_j)
-        corr_second = combine(product_second, span_j, span_j)
+        corr_first, corr_second = pair_products(mine_rows, other_rows, psd_field)
         both = swap_add(jnp.stack([corr_first, corr_second]), "pts")
         adj_first = (scale_first * (quad_weight * both[0] - obs_first)).astype(jnp.bfloat16)
         adj_second = (scale_second * (quad_weight * both[1] - obs_second)).astype(jnp.bfloat16)

time: 242 us -> 245 us (1.012)
  local copies, waits for them, and re-layouts: 9.12 us -> 15.4 us
    while x10 -> x12, local copies, waits for them, and re-layouts: 0.09 us -> 4.77 us  [the longest x2 0.07 us: pair_body(): log_field = lax.fori_loop(0, ITERS, run_sweep, log_field)]
    another operation x2 -> x0, other arithmetic: 3.61 us -> none  [combine(): return jnp.stack([corr_real, corr_imag], axis=1)]
  transfers between devices with their start and end apart: 26 -> 26, of which waited for: 15 -> 15; matrix products, arithmetic and copies ran while one was open for 2% -> 3% of each run, Pallas kernels for 0% -> 0%
where the time goes in v15:
time: 245 us; the launch traced here: 244 us
  waiting for transfers between devices  132 us (54%)
  starting transfers between devices  44.6 us (18%)
  matrix products  18.5 us (8%)
  Pallas kernels  15.8 us (6%)
  local copies, waits for them, and re-layouts  15.4 us (6%)
  other arithmetic  8.73 us (4%)
  between operations  5.7 us (2%)
  loops' own time  2.94 us (1%)
    ppermute x18, waiting for transfers between devices, butterfly_sum(): got.append(lax.ppermute(value, axis, [(i, i ^ mask) for i in range(size)]))  125 us
    ppermute x18, starting transfers between devices, butterfly_sum(): got.append(lax.ppermute(value, axis, [(i, i ^ mask) for i in range(size)]))  35.1 us
    dot_general x4, matrix products, point_terms(): jnp.einsum('fab,fbn->fan', adjoint_block(adjoint), right_rows, preferred_...  18.5 us
    pallas_call x2, Pallas kernels, pair_products(): pl.pallas_call(kernel, grid=(freq,), in_specs=[spec, spec, pl.BlockSpec((...  15.8 us
    ppermute x1, starting transfers between devices, pair_body(): received = lax.ppermute(green_panel, axes, panel_moves)  7.73 us
    ppermute x4, waiting for transfers between devices, swap_add(): return value + lax.ppermute(value, axis, [(0, 1), (1, 0)])  7.52 us
  transfers between devices with their start and end apart: 26, of which 15 were waited for; matrix products, arithmetic and copies ran while one was open for 3% of the time, Pallas kernels for 0%

profile of v15, /device:TPU:0, one launch (start us, length us, event | category | flops | bytes accessed | tf_op | source)
XLA Modules:
  0.0 244.0 jit_solution(876038786951303330)
XLA Ops:
  0.0 7.7 %collective-permute-start.14 = (bf16[4,2,128,3072]{3,2,1,0:T(8,128)(2,1)}, bf16[4,2,128,3072]{3,2,1,0:T(8,128)(2,1)}, u32[]{:S(2)}, u32[]{:S(2)}) collective-permute-start(bf16[4,2,128,3072]{3,2,1,0:T(8,128)(2,1)} %param.10), channel_id=1, source_target_pairs={{0,2},{12,8},{16,22},{20,18},{10,14},{30,28},{1,3},{13,9},{17,23},... | collective-permute-start | bytes 18874376 | tf_op jit(solution)/shard_map/ppermute | solution.py:192
  9.7 3.5 %collective-permute-start.9 = (f32[4,3072]{1,0:T(4,128)}, f32[4,3072]{1,0:T(4,128)}, u32[]{:S(2)}, u32[]{:S(2)}) collective-permute-start(f32[4,3072]{1,0:T(4,128)} %dynamic_update_slice.3), channel_id=1, source_target_pairs={{0,16},{8,24},{16,0},{24,8},{1,17},{9,25},{17,1},{25,9},{2,18},{10... | collective-permute-start | bytes 147464 | tf_op jit(solution)/shard_map/ppermute | solution.py:33
  13.3 1.5 collective-permute-start.10
  28.0 4.2 %collective-permute-start.12 = (f32[4,3072]{1,0:T(4,128)S(1)}, f32[4,3072]{1,0:T(4,128)S(1)}, u32[]{:S(2)}, u32[]{:S(2)}) collective-permute-start(f32[4,3072]{1,0:T(4,128)S(1)} %fusion.34), channel_id=1, source_target_pairs={{0,4},{2,6},{4,0},{6,2},{1,5},{3,7},{5,1},{7,3},{8,12},{10,14},{12... | collective-permute-start | bytes 147464 | tf_op jit(solution)/shard_map/ppermute | solution.py:33
  32.7 109.4 %collective-permute-done.11 = f32[4,3072]{1,0:T(4,128)S(1)} collective-permute-done((f32[4,3072]{1,0:T(4,128)S(1)}, f32[4,3072]{1,0:T(4,128)S(1)}, u32[]{:S(2)}, u32[]{:S(2)}) %collective-permute-start.11) | collective-permute-done | bytes 49184 | tf_op jit(solution)/shard_map/ppermute | solution.py:33
  143.8 1.7 slice-done.1
  145.5 2.6 %conditional.1 = (bf16[4,256,3072]{2,1,0:T(8,128)(2,1)}) conditional(s32[]{:T(128)} %bitcast.40, bf16[4,2,128,3072]{3,2,1,0:T(8,128)(2,1)} %collective-permute-done.14, bf16[4,2,128,3072]{3,2,1,0:T(8,128)(2,1)S(1)} %bitcast.123), branch_computations={%region_0.1_spmd, %region_1.2_spmd} | conditional | bytes 12582920 | solution.py:213
  145.5 2.6 %copy.13 = bf16[4,256,3072]{2,1,0:T(8,128)(2,1)} copy(bf16[4,256,3072]{2,1,0:T(8,128)(2,1)S(1)} %bitcast.124) | data formatting | bytes 12582912 | tf_op jit(solution)/shard_map/cond
  148.1 95.2 %while.13 = (s32[]{:T(128)}, f32[4,3072]{1,0:T(4,128)S(1)}, pred[]{:T(512)}, bf16[4,256,3072]{2,1,0:T(8,128)(2,1)}, f32[1,128,128]{2,1,0:T(8,128)S(1)}, /*index=...) while((s32[]{:T(128)}, f32[4,3072]{1,0:T(4,128)S(1)}, ...), condition=%wide.region_6.7_spmd, body=%wide.region_2.6_spmd.sunk | while | flops 3246776320 | bytes 72418608 | solution.py:246
  148.8 7.9 %eval_jaxpr.5 = (f32[4,2,128,128]{3,2,1,0:T(8,128)}, f32[4,2,128,128]{3,2,1,0:T(8,128)}) custom-call(bf16[4,256,3072]{2,1,0:T(8,128)(2,1)} %get-tuple-element.356.mine_ref, bf16[4,256,3072]{2,1,0:T(8,128)(2,1)} %get-tuple-element.358.other_ref, f32[4,1,3072]{2,1,0:T(1,128)} %broadcast_in_dim.36.field_ref), custom_call_target="tpu_custom_call" | custom-call | tf_op jit(solution)/shard_map/while/body/eval_jaxpr/pallas_call | solution.py:79
  158.2 2.6 %collective-permute-done = f32[2,4,2,128,128]{4,3,2,1,0:T(8,128)S(1)} collective-permute-done((f32[2,4,2,128,128]{4,3,2,1,0:T(8,128)S(1)}, f32[2,4,2,128,128]{4,3,2,1,0:T(8,128)S(1)}, u32[]{:S(2)}, u32[]{:S(2)}) %collective-permute-start) | collective-permute-done | bytes 1048608 | tf_op jit(solution)/shard_map/while/body/eval_jaxpr/ppermute | solution.py:49
  161.3 2.4 copy-done
  163.6 4.6 %multiply_reduce_fusion.7 = f32[4,3072]{1,0:T(4,128)S(1)} fusion(bf16[4,256,3072]{2,1,0:T(8,128)(2,1)S(1)} %copy-done, bf16[4,256,3072]{2,1,0:T(8,128)(2,1)} %get-tuple-element.358.other_ref, bf16[4,128,128]{2,1,0:T(8,128)(2,1)S(1)} %get-tuple-element.308, bf16[4,128,128]{2,1,0:T(8,128)(2,1)S(1)} %get-tuple-element.309, ...), kind=kOutput, calls=%fused_computation.1.clone.1 | convolution fusion | flops 1622134784 | bytes 13025280 | tf_op jit(solution)/shard_map/while/body/eval_jaxpr/fab,fbn->fan/dot_general | solution.py:103
  168.3 4.6 %multiply_reduce_fusion.6 = f32[4,3072]{1,0:T(4,128)S(1)} fusion(bf16[4,256,3072]{2,1,0:T(8,128)(2,1)} %get-tuple-element.358.other_ref, bf16[4,256,3072]{2,1,0:T(8,128)(2,1)S(1)} %copy-done, bf16[4,128,128]{2,1,0:T(8,128)(2,1)S(1)} %get-tuple-element.305, bf16[4,128,128]{2,1,0:T(8,128)(2,1)S(1)} %get-tuple-element.306, ...), kind=kOutput, calls=%fused_computation.clone.1 | convolution fusion | flops 1622134784 | bytes 13025280 | tf_op jit(solution)/shard_map/while/body/eval_jaxpr/fab,fbn->fan/dot_general | solution.py:103
  172.9 2.8 %collective-permute-start.1 = (f32[4,3072]{1,0:T(4,128)S(1)}, f32[4,3072]{1,0:T(4,128)S(1)}, u32[]{:S(2)}, u32[]{:S(2)}) collective-permute-start(f32[4,3072]{1,0:T(4,128)S(1)} %select_add_fusion.2), channel_id=1, source_target_pairs={{0,24},{8,16},{16,8},{24,0},{1,25},{9,17},{17,9},{25,1},{2,26},{10... | collective-permute-start | bytes 147464 | tf_op jit(solution)/shard_map/while/body/eval_jaxpr/ppermute | solution.py:33
  175.7 7.0 %collective-permute-start.2 = (f32[4,3072]{1,0:T(4,128)S(1)}, f32[4,3072]{1,0:T(4,128)S(1)}, u32[]{:S(2)}, u32[]{:S(2)}) collective-permute-start(f32[4,3072]{1,0:T(4,128)S(1)} %select_add_fusion.2), channel_id=1, source_target_pairs={{0,16},{8,24},{16,0},{24,8},{1,17},{9,25},{17,1},{25,9},{2,18},{10... | collective-permute-start | bytes 147464 | tf_op jit(solution)/shard_map/while/body/eval_jaxpr/ppermute | solution.py:33
  182.7 2.1 collective-permute-done.2
  184.8 2.0 collective-permute-done.3
  187.0 5.9 %collective-permute-start.5 = (f32[4,3072]{1,0:T(4,128)S(1)}, f32[4,3072]{1,0:T(4,128)S(1)}, u32[]{:S(2)}, u32[]{:S(2)}) collective-permute-start(f32[4,3072]{1,0:T(4,128)S(1)} %fusion.50), channel_id=1, source_target_pairs={{0,4},{2,6},{4,0},{6,2},{1,5},{3,7},{5,1},{7,3},{8,12},{10,14},{12... | collective-permute-start | bytes 147464 | tf_op jit(solution)/shard_map/while/body/eval_jaxpr/ppermute | solution.py:33
  193.4 2.5 %collective-permute-done.5 = f32[4,3072]{1,0:T(4,128)S(1)} collective-permute-done((f32[4,3072]{1,0:T(4,128)S(1)}, f32[4,3072]{1,0:T(4,128)S(1)}, u32[]{:S(2)}, u32[]{:S(2)}) %collective-permute-start.5) | collective-permute-done | bytes 49184 | tf_op jit(solution)/shard_map/while/body/eval_jaxpr/ppermute | solution.py:33
  201.0 7.9 %eval_jaxpr.5 = (f32[4,2,128,128]{3,2,1,0:T(8,128)}, f32[4,2,128,128]{3,2,1,0:T(8,128)}) custom-call(bf16[4,256,3072]{2,1,0:T(8,128)(2,1)} %get-tuple-element.356.mine_ref, bf16[4,256,3072]{2,1,0:T(8,128)(2,1)} %get-tuple-element.358.other_ref, f32[4,1,3072]{2,1,0:T(1,128)} %broadcast_in_dim.36.field_ref), custom_call_target="tpu_custom_call" | custom-call | tf_op jit(solution)/shard_map/while/body/eval_jaxpr/pallas_call | solution.py:79
  210.6 2.5 %collective-permute-done = f32[2,4,2,128,128]{4,3,2,1,0:T(8,128)S(1)} collective-permute-done((f32[2,4,2,128,128]{4,3,2,1,0:T(8,128)S(1)}, f32[2,4,2,128,128]{4,3,2,1,0:T(8,128)S(1)}, u32[]{:S(2)}, u32[]{:S(2)}) %collective-permute-start) | collective-permute-done | bytes 1048608 | tf_op jit(solution)/shard_map/while/body/eval_jaxpr/ppermute | solution.py:49
  213.5 2.4 copy-done
  215.8 4.6 %multiply_reduce_fusion.7 = f32[4,3072]{1,0:T(4,128)S(1)} fusion(bf16[4,256,3072]{2,1,0:T(8,128)(2,1)S(1)} %copy-done, bf16[4,256,3072]{2,1,0:T(8,128)(2,1)} %get-tuple-element.358.other_ref, bf16[4,128,128]{2,1,0:T(8,128)(2,1)S(1)} %get-tuple-element.308, bf16[4,128,128]{2,1,0:T(8,128)(2,1)S(1)} %get-tuple-element.309, ...), kind=kOutput, calls=%fused_computation.1.clone.1 | convolution fusion | flops 1622134784 | bytes 13025280 | tf_op jit(solution)/shard_map/while/body/eval_jaxpr/fab,fbn->fan/dot_general | solution.py:103
  220.5 4.6 %multiply_reduce_fusion.6 = f32[4,3072]{1,0:T(4,128)S(1)} fusion(bf16[4,256,3072]{2,1,0:T(8,128)(2,1)} %get-tuple-element.358.other_ref, bf16[4,256,3072]{2,1,0:T(8,128)(2,1)S(1)} %copy-done, bf16[4,128,128]{2,1,0:T(8,128)(2,1)S(1)} %get-tuple-element.305, bf16[4,128,128]{2,1,0:T(8,128)(2,1)S(1)} %get-tuple-element.306, ...), kind=kOutput, calls=%fused_computation.clone.1 | convolution fusion | flops 1622134784 | bytes 13025280 | tf_op jit(solution)/shard_map/while/body/eval_jaxpr/fab,fbn->fan/dot_general | solution.py:103
  225.1 2.8 %collective-permute-start.1 = (f32[4,3072]{1,0:T(4,128)S(1)}, f32[4,3072]{1,0:T(4,128)S(1)}, u32[]{:S(2)}, u32[]{:S(2)}) collective-permute-start(f32[4,3072]{1,0:T(4,128)S(1)} %select_add_fusion.2), channel_id=1, source_target_pairs={{0,24},{8,16},{16,8},{24,0},{1,25},{9,17},{17,9},{25,1},{2,26},{10... | collective-permute-start | bytes 147464 | tf_op jit(solution)/shard_map/while/body/eval_jaxpr/ppermute | solution.py:33
  228.7 1.5 collective-permute-done.1
  230.2 1.8 collective-permute-done.2
  232.1 2.9 %collective-permute-start.4 = (f32[4,3072]{1,0:T(4,128)S(1)}, f32[4,3072]{1,0:T(4,128)S(1)}, u32[]{:S(2)}, u32[]{:S(2)}) collective-permute-start(f32[4,3072]{1,0:T(4,128)S(1)} %fusion.50), channel_id=1, source_target_pairs={{0,6},{2,4},{4,2},{6,0},{1,7},{3,5},{5,3},{7,1},{8,14},{10,12},{12... | collective-permute-start | bytes 147464 | tf_op jit(solution)/shard_map/while/body/eval_jaxpr/ppermute | solution.py:33
  235.0 1.5 collective-permute-start.6
  236.6 1.6 collective-permute-done.4
  238.2 1.9 collective-permute-done.5
  (99 shorter events, 24.2 us)
Async XLA Ops:
  0.0 20.8 %copy-start.4 = (s32[16]{0:T(128)S(1)}, s32[16]{0:T(128)}, u32[]{:S(2)}) copy-start(s32[16]{0:T(128)} %constant.200.clone) | copy-start | bytes 196
  0.0 17.5 %copy-start.3 = (f32[4,2,128,128]{3,2,1,0:T(8,128)S(1)}, f32[4,2,128,128]{3,2,1,0:T(8,128)}, u32[]{:S(2)}) copy-start(f32[4,2,128,128]{3,2,1,0:T(8,128)} %param.12) | copy-start | bytes 1572868
  0.0 143.6 %collective-permute-start.14 = (bf16[4,2,128,3072]{3,2,1,0:T(8,128)(2,1)}, bf16[4,2,128,3072]{3,2,1,0:T(8,128)(2,1)}, u32[]{:S(2)}, u32[]{:S(2)}) collective-permute-start(bf16[4,2,128,3072]{3,2,1,0:T(8,128)(2,1)} %param.10), channel_id=1, source_target_pairs={{0,2},{12,8},{16,22},{20,18},{10,14},{30,28},{1,3},{13,9},{17,23},... | collective-permute-start | bytes 18874376 | tf_op jit(solution)/shard_map/ppermute | solution.py:192
  9.7 15.3 %collective-permute-start.8 = (f32[4,3072]{1,0:T(4,128)}, f32[4,3072]{1,0:T(4,128)}, u32[]{:S(2)}, u32[]{:S(2)}) collective-permute-start(f32[4,3072]{1,0:T(4,128)} %dynamic_update_slice.3), channel_id=1, source_target_pairs={{0,8},{8,0},{16,24},{24,16},{1,9},{9,1},{17,25},{25,17},{2,10},{10... | collective-permute-start | bytes 147464 | tf_op jit(solution)/shard_map/ppermute | solution.py:33
  9.7 16.0 %collective-permute-start.9 = (f32[4,3072]{1,0:T(4,128)}, f32[4,3072]{1,0:T(4,128)}, u32[]{:S(2)}, u32[]{:S(2)}) collective-permute-start(f32[4,3072]{1,0:T(4,128)} %dynamic_update_slice.3), channel_id=1, source_target_pairs={{0,16},{8,24},{16,0},{24,8},{1,17},{9,25},{17,1},{25,9},{2,18},{10... | collective-permute-start | bytes 147464 | tf_op jit(solution)/shard_map/ppermute | solution.py:33
  13.3 12.4 %collective-permute-start.10 = (f32[4,3072]{1,0:T(4,128)}, f32[4,3072]{1,0:T(4,128)}, u32[]{:S(2)}, u32[]{:S(2)}) collective-permute-start(f32[4,3072]{1,0:T(4,128)} %dynamic_update_slice.3), channel_id=1, source_target_pairs={{0,24},{8,16},{16,8},{24,0},{1,25},{9,17},{17,9},{25,1},{2,26},{10... | collective-permute-start | bytes 147464 | tf_op jit(solution)/shard_map/ppermute | solution.py:33
  17.5 126.3 %slice-start = ((s8[6291456]{0:T(1024)(128)(4,1)}), s8[2097152]{0:T(1024)(128)(4,1)S(1)}, s32[]{:S(2)}) async-start(s8[6291456]{0:T(1024)(128)(4,1)} %bitcast.122), calls=%async_computation | async-start | bytes 4194304
  24.3 7.9 %collective-permute-start.15 = (f32[5,128,128]{2,1,0:T(8,128)S(1)}, f32[5,128,128]{2,1,0:T(8,128)S(1)}, u32[]{:S(2)}, u32[]{:S(2)}) collective-permute-start(f32[5,128,128]{2,1,0:T(8,128)S(1)} %fusion.29), channel_id=1, source_target_pairs={{8,2},{4,8},{24,22},{12,18},{26,14},{22,28},{9,3},{5,9},{25,23},{1... | collective-permute-start | bytes 983048 | tf_op jit(solution)/shard_map/ppermute | solution.py:204
  25.0 7.6 %collective-permute-start.16 = (f32[5,128,128]{2,1,0:T(8,128)S(1)}, f32[5,128,128]{2,1,0:T(8,128)S(1)}, u32[]{:S(2)}, u32[]{:S(2)}) collective-permute-start(f32[5,128,128]{2,1,0:T(8,128)S(1)} %fusion.29), channel_id=1, source_target_pairs={{16,8},{6,22},{17,9},{7,23}} | collective-permute-start | bytes 983048 | tf_op jit(solution)/shard_map/ppermute | solution.py:204
  26.7 115.5 %collective-permute-start.11 = (f32[4,3072]{1,0:T(4,128)S(1)}, f32[4,3072]{1,0:T(4,128)S(1)}, u32[]{:S(2)}, u32[]{:S(2)}) collective-permute-start(f32[4,3072]{1,0:T(4,128)S(1)} %fusion.34), channel_id=1, source_target_pairs={{0,2},{2,0},{4,6},{6,4},{1,3},{3,1},{5,7},{7,5},{8,10},{10,8},{12,... | collective-permute-start | bytes 147464 | tf_op jit(solution)/shard_map/ppermute | solution.py:33
  28.0 114.6 %collective-permute-start.12 = (f32[4,3072]{1,0:T(4,128)S(1)}, f32[4,3072]{1,0:T(4,128)S(1)}, u32[]{:S(2)}, u32[]{:S(2)}) collective-permute-start(f32[4,3072]{1,0:T(4,128)S(1)} %fusion.34), channel_id=1, source_target_pairs={{0,4},{2,6},{4,0},{6,2},{1,5},{3,7},{5,1},{7,3},{8,12},{10,14},{12... | collective-permute-start | bytes 147464 | tf_op jit(solution)/shard_map/ppermute | solution.py:33
  32.3 111.0 %collective-permute-start.13 = (f32[4,3072]{1,0:T(4,128)S(1)}, f32[4,3072]{1,0:T(4,128)S(1)}, u32[]{:S(2)}, u32[]{:S(2)}) collective-permute-start(f32[4,3072]{1,0:T(4,128)S(1)} %fusion.34), channel_id=1, source_target_pairs={{0,6},{2,4},{4,2},{6,0},{1,7},{3,5},{5,3},{7,1},{8,14},{10,12},{12... | collective-permute-start | bytes 147464 | tf_op jit(solution)/shard_map/ppermute | solution.py:33
  32.6 110.7 %collective-permute-start.17 = (f32[2,5,128,128]{3,2,1,0:T(8,128)S(1)}, f32[2,5,128,128]{3,2,1,0:T(8,128)S(1)}, u32[]{:S(2)}, u32[]{:S(2)}) collective-permute-start(f32[2,5,128,128]{3,2,1,0:T(8,128)S(1)} %pad_maximum_fusion.8), channel_id=1, source_target_pairs={{0,1},{1,0},{2,3},{3,2},{4,5},{5,4},{6,7},{7,6},{8,9},{9,8},{10,11... | collective-permute-start | bytes 1966088 | tf_op jit(solution)/shard_map/ppermute | solution.py:205
  156.7 4.1 %copy-start.1 = (f32[4,2,128,128]{3,2,1,0:T(8,128)S(1)}, f32[4,2,128,128]{3,2,1,0:T(8,128)}, u32[]{:S(2)}) copy-start(f32[4,2,128,128]{3,2,1,0:T(8,128)} %get-tuple-element.302) | copy-start | bytes 1572868 | tf_op jit(solution)/shard_map/while
  156.7 4.1 %copy-start.2 = (f32[4,2,128,128]{3,2,1,0:T(8,128)S(1)}, f32[4,2,128,128]{3,2,1,0:T(8,128)}, u32[]{:S(2)}) copy-start(f32[4,2,128,128]{3,2,1,0:T(8,128)} %get-tuple-element.301) | copy-start | bytes 1572868 | tf_op jit(solution)/shard_map/while
  158.1 2.7 %collective-permute-start = (f32[2,4,2,128,128]{4,3,2,1,0:T(8,128)S(1)}, f32[2,4,2,128,128]{4,3,2,1,0:T(8,128)S(1)}, u32[]{:S(2)}, u32[]{:S(2)}) collective-permute-start(f32[2,4,2,128,128]{4,3,2,1,0:T(8,128)S(1)} %pad_maximum_fusion.14), channel_id=1, source_target_pairs={{0,1},{1,0},{2,3},{3,2},{4,5},{5,4},{6,7},{7,6},{8,9},{9,8},{10,11... | collective-permute-start | bytes 3145736 | tf_op jit(solution)/shard_map/while/body/eval_jaxpr/ppermute | solution.py:49
  172.9 9.8 %collective-permute-start.1 = (f32[4,3072]{1,0:T(4,128)S(1)}, f32[4,3072]{1,0:T(4,128)S(1)}, u32[]{:S(2)}, u32[]{:S(2)}) collective-permute-start(f32[4,3072]{1,0:T(4,128)S(1)} %select_add_fusion.2), channel_id=1, source_target_pairs={{0,24},{8,16},{16,8},{24,0},{1,25},{9,17},{17,9},{25,1},{2,26},{10... | collective-permute-start | bytes 147464 | tf_op jit(solution)/shard_map/while/body/eval_jaxpr/ppermute | solution.py:33
  175.7 9.0 %collective-permute-start.2 = (f32[4,3072]{1,0:T(4,128)S(1)}, f32[4,3072]{1,0:T(4,128)S(1)}, u32[]{:S(2)}, u32[]{:S(2)}) collective-permute-start(f32[4,3072]{1,0:T(4,128)S(1)} %select_add_fusion.2), channel_id=1, source_target_pairs={{0,16},{8,24},{16,0},{24,8},{1,17},{9,25},{17,1},{25,9},{2,18},{10... | collective-permute-start | bytes 147464 | tf_op jit(solution)/shard_map/while/body/eval_jaxpr/ppermute | solution.py:33
  182.7 4.1 %collective-permute-start.3 = (f32[4,3072]{1,0:T(4,128)S(1)}, f32[4,3072]{1,0:T(4,128)S(1)}, u32[]{:S(2)}, u32[]{:S(2)}) collective-permute-start(f32[4,3072]{1,0:T(4,128)S(1)} %select_add_fusion.2), channel_id=1, source_target_pairs={{0,8},{8,0},{16,24},{24,16},{1,9},{9,1},{17,25},{25,17},{2,10},{10... | collective-permute-start | bytes 147464 | tf_op jit(solution)/shard_map/while/body/eval_jaxpr/ppermute | solution.py:33
  186.9 6.5 %collective-permute-start.4 = (f32[4,3072]{1,0:T(4,128)S(1)}, f32[4,3072]{1,0:T(4,128)S(1)}, u32[]{:S(2)}, u32[]{:S(2)}) collective-permute-start(f32[4,3072]{1,0:T(4,128)S(1)} %fusion.50), channel_id=1, source_target_pairs={{0,6},{2,4},{4,2},{6,0},{1,7},{3,5},{5,3},{7,1},{8,14},{10,12},{12... | collective-permute-start | bytes 147464 | tf_op jit(solution)/shard_map/while/body/eval_jaxpr/ppermute | solution.py:33
  187.0 8.9 %collective-permute-start.5 = (f32[4,3072]{1,0:T(4,128)S(1)}, f32[4,3072]{1,0:T(4,128)S(1)}, u32[]{:S(2)}, u32[]{:S(2)}) collective-permute-start(f32[4,3072]{1,0:T(4,128)S(1)} %fusion.50), channel_id=1, source_target_pairs={{0,4},{2,6},{4,0},{6,2},{1,5},{3,7},{5,1},{7,3},{8,12},{10,14},{12... | collective-permute-start | bytes 147464 | tf_op jit(solution)/shard_map/while/body/eval_jaxpr/ppermute | solution.py:33
  192.9 4.1 %collective-permute-start.6 = (f32[4,3072]{1,0:T(4,128)S(1)}, f32[4,3072]{1,0:T(4,128)S(1)}, u32[]{:S(2)}, u32[]{:S(2)}) collective-permute-start(f32[4,3072]{1,0:T(4,128)S(1)} %fusion.50), channel_id=1, source_target_pairs={{0,2},{2,0},{4,6},{6,4},{1,3},{3,1},{5,7},{7,5},{8,10},{10,8},{12,... | collective-permute-start | bytes 147464 | tf_op jit(solution)/shard_map/while/body/eval_jaxpr/ppermute | solution.py:33
  197.7 1.2 collective-permute-start.7
  208.9 4.1 %copy-start.2 = (f32[4,2,128,128]{3,2,1,0:T(8,128)S(1)}, f32[4,2,128,128]{3,2,1,0:T(8,128)}, u32[]{:S(2)}) copy-start(f32[4,2,128,128]{3,2,1,0:T(8,128)} %get-tuple-element.301) | copy-start | bytes 1572868 | tf_op jit(solution)/shard_map/while
  210.3 2.7 %collective-permute-start = (f32[2,4,2,128,128]{4,3,2,1,0:T(8,128)S(1)}, f32[2,4,2,128,128]{4,3,2,1,0:T(8,128)S(1)}, u32[]{:S(2)}, u32[]{:S(2)}) collective-permute-start(f32[2,4,2,128,128]{4,3,2,1,0:T(8,128)S(1)} %pad_maximum_fusion.14), channel_id=1, source_target_pairs={{0,1},{1,0},{2,3},{3,2},{4,5},{5,4},{6,7},{7,6},{8,9},{9,8},{10,11... | collective-permute-start | bytes 3145736 | tf_op jit(solution)/shard_map/while/body/eval_jaxpr/ppermute | solution.py:49
  225.1 5.1 %collective-permute-start.1 = (f32[4,3072]{1,0:T(4,128)S(1)}, f32[4,3072]{1,0:T(4,128)S(1)}, u32[]{:S(2)}, u32[]{:S(2)}) collective-permute-start(f32[4,3072]{1,0:T(4,128)S(1)} %select_add_fusion.2), channel_id=1, source_target_pairs={{0,24},{8,16},{16,8},{24,0},{1,25},{9,17},{17,9},{25,1},{2,26},{10... | collective-permute-start | bytes 147464 | tf_op jit(solution)/shard_map/while/body/eval_jaxpr/ppermute | solution.py:33
  227.9 4.1 %collective-permute-start.2 = (f32[4,3072]{1,0:T(4,128)S(1)}, f32[4,3072]{1,0:T(4,128)S(1)}, u32[]{:S(2)}, u32[]{:S(2)}) collective-permute-start(f32[4,3072]{1,0:T(4,128)S(1)} %select_add_fusion.2), channel_id=1, source_target_pairs={{0,16},{8,24},{16,0},{24,8},{1,17},{9,25},{17,1},{25,9},{2,18},{10... | collective-permute-start | bytes 147464 | tf_op jit(solution)/shard_map/while/body/eval_jaxpr/ppermute | solution.py:33
  227.9 4.1 %collective-permute-start.3 = (f32[4,3072]{1,0:T(4,128)S(1)}, f32[4,3072]{1,0:T(4,128)S(1)}, u32[]{:S(2)}, u32[]{:S(2)}) collective-permute-start(f32[4,3072]{1,0:T(4,128)S(1)} %select_add_fusion.2), channel_id=1, source_target_pairs={{0,8},{8,0},{16,24},{24,16},{1,9},{9,1},{17,25},{25,17},{2,10},{10... | collective-permute-start | bytes 147464 | tf_op jit(solution)/shard_map/while/body/eval_jaxpr/ppermute | solution.py:33
  232.1 6.1 %collective-permute-start.4 = (f32[4,3072]{1,0:T(4,128)S(1)}, f32[4,3072]{1,0:T(4,128)S(1)}, u32[]{:S(2)}, u32[]{:S(2)}) collective-permute-start(f32[4,3072]{1,0:T(4,128)S(1)} %fusion.50), channel_id=1, source_target_pairs={{0,6},{2,4},{4,2},{6,0},{1,7},{3,5},{5,3},{7,1},{8,14},{10,12},{12... | collective-permute-start | bytes 147464 | tf_op jit(solution)/shard_map/while/body/eval_jaxpr/ppermute | solution.py:33
  235.0 5.0 %collective-permute-start.5 = (f32[4,3072]{1,0:T(4,128)S(1)}, f32[4,3072]{1,0:T(4,128)S(1)}, u32[]{:S(2)}, u32[]{:S(2)}) collective-permute-start(f32[4,3072]{1,0:T(4,128)S(1)} %fusion.50), channel_id=1, source_target_pairs={{0,4},{2,6},{4,0},{6,2},{1,5},{3,7},{5,1},{7,3},{8,12},{10,14},{12... | collective-permute-start | bytes 147464 | tf_op jit(solution)/shard_map/while/body/eval_jaxpr/ppermute | solution.py:33
  235.0 5.0 %collective-permute-start.6 = (f32[4,3072]{1,0:T(4,128)S(1)}, f32[4,3072]{1,0:T(4,128)S(1)}, u32[]{:S(2)}, u32[]{:S(2)}) collective-permute-start(f32[4,3072]{1,0:T(4,128)S(1)} %fusion.50), channel_id=1, source_target_pairs={{0,2},{2,0},{4,6},{6,4},{1,3},{3,1},{5,7},{7,5},{8,10},{10,8},{12,... | collective-permute-start | bytes 147464 | tf_op jit(solution)/shard_map/while/body/eval_jaxpr/ppermute | solution.py:33
  240.8 1.2 collective-permute-start.7
  (4 other events, 11.9 us)

commit v16 on v12

--- a/solution.py
+++ b/solution.py
@@ -236,7 +236,12 @@
         product_first, product_second = pair_products(mine_rows, other_rows, psd_field)
         corr_first = combine(product_first, span_j, span_j)
         corr_second = combine(product_second, span_j, span_j)
-        both = swap_add(jnp.stack([corr_first, corr_second]), "pts")
+        own_part = jnp.stack([corr_first, corr_second]).astype(jnp.bfloat16)
+        peer_part = lax.ppermute(own_part, "pts", [(0, 1), (1, 0)])
+        first_core = lax.axis_index("pts") == 0
+        low = jnp.where(first_core, own_part, peer_part).astype(jnp.float32)
+        high = jnp.where(first_core, peer_part, own_part).astype(jnp.float32)
+        both = low + high
         adj_first = (scale_first * (quad_weight * both[0] - obs_first)).astype(jnp.bfloat16)
         adj_second = (scale_second * (quad_weight * both[1] - obs_second)).astype(jnp.bfloat16)
         term_first = point_terms(adj_first, other_rows, mine_rows, psd_field, quad_weight)

time: 242 us -> 244 us (level)
  local copies, waits for them, and re-layouts: 9.12 us -> 13.7 us
    ppermute x4 -> x2, waiting for transfers between devices: 7.81 us -> 2.7 us  [swap_add(): return value + lax.ppermute(value, axis, [(0, 1), (1, 0)])]
    while x8 -> x4, local copies, waits for them, and re-layouts: 0.01 us -> 4.66 us
    ppermute x0 -> x2, waiting for transfers between devices: none -> 3.6 us  [run_sweep(): peer_part = lax.ppermute(own_part, 'pts', [(0, 1), (1, 0)])]
where the time goes in v16:
time: 244 us; the launch traced here: 243 us
  waiting for transfers between devices  133 us (55%)
  starting transfers between devices  44.7 us (18%)
  matrix products  18.5 us (8%)
  Pallas kernels  16.3 us (7%)
  local copies, waits for them, and re-layouts  13.7 us (6%)
  other arithmetic  8.54 us (3%)
  between operations  6.1 us (2%)
  loops' own time  2.9 us (1%)
    ppermute x18, waiting for transfers between devices, butterfly_sum(): got.append(lax.ppermute(value, axis, [(i, i ^ mask) for i in range(size)]))  126 us
    ppermute x18, starting transfers between devices, butterfly_sum(): got.append(lax.ppermute(value, axis, [(i, i ^ mask) for i in range(size)]))  35.2 us
    dot_general x4, matrix products, point_terms(): jnp.einsum('fab,fbn->fan', adjoint_block(adjoint), right_rows, preferred_...  18.5 us
    pallas_call x2, Pallas kernels, pair_products(): pl.pallas_call(kernel, grid=(freq, points // tile), in_specs=[spec, spec,...  16.3 us
    ppermute x1, starting transfers between devices, pair_body(): received = lax.ppermute(green_panel, axes, panel_moves)  7.74 us
  transfers between devices with their start and end apart: 26, of which 15 were waited for; matrix products, arithmetic and copies ran while one was open for 2% of the time, Pallas kernels for 0%

profile of v16, /device:TPU:0, one launch (start us, length us, event | category | flops | bytes accessed | tf_op | source)
XLA Modules:
  0.0 243.5 jit_solution(778499334880041913)
XLA Ops:
  0.0 7.7 %collective-permute-start.14 = (bf16[4,2,128,3072]{3,2,1,0:T(8,128)(2,1)}, bf16[4,2,128,3072]{3,2,1,0:T(8,128)(2,1)}, u32[]{:S(2)}, u32[]{:S(2)}) collective-permute-start(bf16[4,2,128,3072]{3,2,1,0:T(8,128)(2,1)} %param.10), channel_id=1, source_target_pairs={{0,2},{12,8},{16,22},{20,18},{10,14},{30,28},{1,3},{13,9},{17,23},... | collective-permute-start | bytes 18874376 | tf_op jit(solution)/shard_map/ppermute | solution.py:193
  8.7 3.6 %collective-permute-start.9 = (f32[4,3072]{1,0:T(4,128)S(1)}, f32[4,3072]{1,0:T(4,128)S(1)}, u32[]{:S(2)}, u32[]{:S(2)}) collective-permute-start(f32[4,3072]{1,0:T(4,128)S(1)} %dynamic_update_slice.3), channel_id=1, source_target_pairs={{0,16},{8,24},{16,0},{24,8},{1,17},{9,25},{17,1},{25,9},{2,18},{10... | collective-permute-start | bytes 147464 | tf_op jit(solution)/shard_map/ppermute | solution.py:33
  26.6 4.2 %collective-permute-start.12 = (f32[4,3072]{1,0:T(4,128)S(1)}, f32[4,3072]{1,0:T(4,128)S(1)}, u32[]{:S(2)}, u32[]{:S(2)}) collective-permute-start(f32[4,3072]{1,0:T(4,128)S(1)} %fusion.37), channel_id=1, source_target_pairs={{0,4},{2,6},{4,0},{6,2},{1,5},{3,7},{5,1},{7,3},{8,12},{10,14},{12... | collective-permute-start | bytes 147464 | tf_op jit(solution)/shard_map/ppermute | solution.py:33
  31.2 111.0 %collective-permute-done.11 = f32[4,3072]{1,0:T(4,128)S(1)} collective-permute-done((f32[4,3072]{1,0:T(4,128)S(1)}, f32[4,3072]{1,0:T(4,128)S(1)}, u32[]{:S(2)}, u32[]{:S(2)}) %collective-permute-start.11) | collective-permute-done | bytes 49184 | tf_op jit(solution)/shard_map/ppermute | solution.py:33
  145.0 2.6 %conditional.1 = (bf16[4,256,3072]{2,1,0:T(8,128)(2,1)}) conditional(s32[]{:T(128)} %bitcast.44, bf16[4,2,128,3072]{3,2,1,0:T(8,128)(2,1)} %collective-permute-done.14, bf16[4,2,128,3072]{3,2,1,0:T(8,128)(2,1)S(1)} %bitcast.135), branch_computations={%region_0.1_spmd, %region_1.2_spmd} | conditional | bytes 12582920 | solution.py:214
  145.0 2.6 %copy.11 = bf16[4,256,3072]{2,1,0:T(8,128)(2,1)} copy(bf16[4,256,3072]{2,1,0:T(8,128)(2,1)S(1)} %bitcast.136) | data formatting | bytes 12582912 | tf_op jit(solution)/shard_map/cond
  147.7 95.1 %while.13 = (s32[]{:T(128)}, f32[4,3072]{1,0:T(4,128)S(1)}, pred[]{:T(512)}, bf16[4,256,3072]{2,1,0:T(8,128)(2,1)}, f32[1,128,128]{2,1,0:T(8,128)S(1)}, /*index=...) while((s32[]{:T(128)}, f32[4,3072]{1,0:T(4,128)S(1)}, ...), condition=%wide.region_6.7_spmd, body=%wide.region_2.6_spmd.sunk | while | flops 3248611328 | bytes 67699984 | solution.py:254
  148.3 8.2 %eval_jaxpr.5 = (f32[4,256,256]{2,1,0:T(8,128)}, f32[4,256,256]{2,1,0:T(8,128)}) custom-call(bf16[4,256,3072]{2,1,0:T(8,128)(2,1)} %get-tuple-element.372.mine_ref, bf16[4,256,3072]{2,1,0:T(8,128)(2,1)} %get-tuple-element.374.other_ref, f32[4,1,3072]{2,1,0:T(1,128)} %broadcast_in_dim.36.field_ref), custom_call_target="tpu_custom_call" | custom-call | tf_op jit(solution)/shard_map/while/body/eval_jaxpr/pallas_call | solution.py:79
  156.5 1.7 fusion.51
  158.4 1.9 collective-permute-done
  160.7 2.3 copy-done
  163.1 4.6 %multiply_reduce_fusion.7 = f32[4,3072]{1,0:T(4,128)S(1)} fusion(bf16[4,256,3072]{2,1,0:T(8,128)(2,1)S(1)} %copy-done, bf16[4,256,3072]{2,1,0:T(8,128)(2,1)} %get-tuple-element.374.other_ref, bf16[4,128,128]{2,1,0:T(8,128)(2,1)S(1)} %get-tuple-element.325, bf16[4,128,128]{2,1,0:T(8,128)(2,1)S(1)} %get-tuple-element.326, ...), kind=kOutput, calls=%fused_computation.1.clone.1 | convolution fusion | flops 1622134784 | bytes 13025280 | tf_op jit(solution)/shard_map/while/body/eval_jaxpr/fab,fbn->fan/dot_general | solution.py:104
  167.7 4.6 %multiply_reduce_fusion.6 = f32[4,3072]{1,0:T(4,128)S(1)} fusion(bf16[4,256,3072]{2,1,0:T(8,128)(2,1)} %get-tuple-element.374.other_ref, bf16[4,256,3072]{2,1,0:T(8,128)(2,1)S(1)} %copy-done, bf16[4,128,128]{2,1,0:T(8,128)(2,1)S(1)} %get-tuple-element.322, bf16[4,128,128]{2,1,0:T(8,128)(2,1)S(1)} %get-tuple-element.323, ...), kind=kOutput, calls=%fused_computation.clone.1 | convolution fusion | flops 1622134784 | bytes 13025280 | tf_op jit(solution)/shard_map/while/body/eval_jaxpr/fab,fbn->fan/dot_general | solution.py:104
  172.4 2.8 %collective-permute-start.1 = (f32[4,3072]{1,0:T(4,128)S(1)}, f32[4,3072]{1,0:T(4,128)S(1)}, u32[]{:S(2)}, u32[]{:S(2)}) collective-permute-start(f32[4,3072]{1,0:T(4,128)S(1)} %select_add_fusion.2), channel_id=1, source_target_pairs={{0,24},{8,16},{16,8},{24,0},{1,25},{9,17},{17,9},{25,1},{2,26},{10... | collective-permute-start | bytes 147464 | tf_op jit(solution)/shard_map/while/body/eval_jaxpr/ppermute | solution.py:33
  175.2 7.0 %collective-permute-start.2 = (f32[4,3072]{1,0:T(4,128)S(1)}, f32[4,3072]{1,0:T(4,128)S(1)}, u32[]{:S(2)}, u32[]{:S(2)}) collective-permute-start(f32[4,3072]{1,0:T(4,128)S(1)} %select_add_fusion.2), channel_id=1, source_target_pairs={{0,16},{8,24},{16,0},{24,8},{1,17},{9,25},{17,1},{25,9},{2,18},{10... | collective-permute-start | bytes 147464 | tf_op jit(solution)/shard_map/while/body/eval_jaxpr/ppermute | solution.py:33
  182.2 2.1 collective-permute-done.2
  184.2 2.0 collective-permute-done.3
  186.4 5.9 %collective-permute-start.5 = (f32[4,3072]{1,0:T(4,128)S(1)}, f32[4,3072]{1,0:T(4,128)S(1)}, u32[]{:S(2)}, u32[]{:S(2)}) collective-permute-start(f32[4,3072]{1,0:T(4,128)S(1)} %fusion.55), channel_id=1, source_target_pairs={{0,4},{2,6},{4,0},{6,2},{1,5},{3,7},{5,1},{7,3},{8,12},{10,14},{12... | collective-permute-start | bytes 147464 | tf_op jit(solution)/shard_map/while/body/eval_jaxpr/ppermute | solution.py:33
  192.9 2.5 %collective-permute-done.5 = f32[4,3072]{1,0:T(4,128)S(1)} collective-permute-done((f32[4,3072]{1,0:T(4,128)S(1)}, f32[4,3072]{1,0:T(4,128)S(1)}, u32[]{:S(2)}, u32[]{:S(2)}) %collective-permute-start.5) | collective-permute-done | bytes 49184 | tf_op jit(solution)/shard_map/while/body/eval_jaxpr/ppermute | solution.py:33
  200.5 8.2 %eval_jaxpr.5 = (f32[4,256,256]{2,1,0:T(8,128)}, f32[4,256,256]{2,1,0:T(8,128)}) custom-call(bf16[4,256,3072]{2,1,0:T(8,128)(2,1)} %get-tuple-element.372.mine_ref, bf16[4,256,3072]{2,1,0:T(8,128)(2,1)} %get-tuple-element.374.other_ref, f32[4,1,3072]{2,1,0:T(1,128)} %broadcast_in_dim.36.field_ref), custom_call_target="tpu_custom_call" | custom-call | tf_op jit(solution)/shard_map/while/body/eval_jaxpr/pallas_call | solution.py:79
  208.7 1.7 fusion.51
  210.7 1.7 collective-permute-done
  212.9 2.3 copy-done
  215.2 4.6 %multiply_reduce_fusion.7 = f32[4,3072]{1,0:T(4,128)S(1)} fusion(bf16[4,256,3072]{2,1,0:T(8,128)(2,1)S(1)} %copy-done, bf16[4,256,3072]{2,1,0:T(8,128)(2,1)} %get-tuple-element.374.other_ref, bf16[4,128,128]{2,1,0:T(8,128)(2,1)S(1)} %get-tuple-element.325, bf16[4,128,128]{2,1,0:T(8,128)(2,1)S(1)} %get-tuple-element.326, ...), kind=kOutput, calls=%fused_computation.1.clone.1 | convolution fusion | flops 1622134784 | bytes 13025280 | tf_op jit(solution)/shard_map/while/body/eval_jaxpr/fab,fbn->fan/dot_general | solution.py:104
  219.9 4.6 %multiply_reduce_fusion.6 = f32[4,3072]{1,0:T(4,128)S(1)} fusion(bf16[4,256,3072]{2,1,0:T(8,128)(2,1)} %get-tuple-element.374.other_ref, bf16[4,256,3072]{2,1,0:T(8,128)(2,1)S(1)} %copy-done, bf16[4,128,128]{2,1,0:T(8,128)(2,1)S(1)} %get-tuple-element.322, bf16[4,128,128]{2,1,0:T(8,128)(2,1)S(1)} %get-tuple-element.323, ...), kind=kOutput, calls=%fused_computation.clone.1 | convolution fusion | flops 1622134784 | bytes 13025280 | tf_op jit(solution)/shard_map/while/body/eval_jaxpr/fab,fbn->fan/dot_general | solution.py:104
  224.5 2.8 %collective-permute-start.1 = (f32[4,3072]{1,0:T(4,128)S(1)}, f32[4,3072]{1,0:T(4,128)S(1)}, u32[]{:S(2)}, u32[]{:S(2)}) collective-permute-start(f32[4,3072]{1,0:T(4,128)S(1)} %select_add_fusion.2), channel_id=1, source_target_pairs={{0,24},{8,16},{16,8},{24,0},{1,25},{9,17},{17,9},{25,1},{2,26},{10... | collective-permute-start | bytes 147464 | tf_op jit(solution)/shard_map/while/body/eval_jaxpr/ppermute | solution.py:33
  228.1 1.5 collective-permute-done.1
  229.6 1.8 collective-permute-done.2
  231.5 2.9 %collective-permute-start.4 = (f32[4,3072]{1,0:T(4,128)S(1)}, f32[4,3072]{1,0:T(4,128)S(1)}, u32[]{:S(2)}, u32[]{:S(2)}) collective-permute-start(f32[4,3072]{1,0:T(4,128)S(1)} %fusion.55), channel_id=1, source_target_pairs={{0,6},{2,4},{4,2},{6,0},{1,7},{3,5},{5,3},{7,1},{8,14},{10,12},{12... | collective-permute-start | bytes 147464 | tf_op jit(solution)/shard_map/while/body/eval_jaxpr/ppermute | solution.py:33
  234.4 1.5 collective-permute-start.6
  236.0 1.6 collective-permute-done.4
  237.6 1.8 collective-permute-done.5
  (103 shorter events, 22.6 us)
Async XLA Ops:
  0.0 19.9 %copy-start.2 = (s32[16]{0:T(128)S(1)}, s32[16]{0:T(128)}, u32[]{:S(2)}) copy-start(s32[16]{0:T(128)} %constant.203.clone) | copy-start | bytes 196
  0.0 16.4 %copy-start.1 = (f32[4,2,128,128]{3,2,1,0:T(8,128)S(1)}, f32[4,2,128,128]{3,2,1,0:T(8,128)}, u32[]{:S(2)}) copy-start(f32[4,2,128,128]{3,2,1,0:T(8,128)} %param.12) | copy-start | bytes 1572868
  0.0 143.6 %collective-permute-start.14 = (bf16[4,2,128,3072]{3,2,1,0:T(8,128)(2,1)}, bf16[4,2,128,3072]{3,2,1,0:T(8,128)(2,1)}, u32[]{:S(2)}, u32[]{:S(2)}) collective-permute-start(bf16[4,2,128,3072]{3,2,1,0:T(8,128)(2,1)} %param.10), channel_id=1, source_target_pairs={{0,2},{12,8},{16,22},{20,18},{10,14},{30,28},{1,3},{13,9},{17,23},... | collective-permute-start | bytes 18874376 | tf_op jit(solution)/shard_map/ppermute | solution.py:193
  8.6 15.8 %collective-permute-start.8 = (f32[4,3072]{1,0:T(4,128)S(1)}, f32[4,3072]{1,0:T(4,128)S(1)}, u32[]{:S(2)}, u32[]{:S(2)}) collective-permute-start(f32[4,3072]{1,0:T(4,128)S(1)} %dynamic_update_slice.3), channel_id=1, source_target_pairs={{0,8},{8,0},{16,24},{24,16},{1,9},{9,1},{17,25},{25,17},{2,10},{10... | collective-permute-start | bytes 147464 | tf_op jit(solution)/shard_map/ppermute | solution.py:33
  8.7 16.4 %collective-permute-start.9 = (f32[4,3072]{1,0:T(4,128)S(1)}, f32[4,3072]{1,0:T(4,128)S(1)}, u32[]{:S(2)}, u32[]{:S(2)}) collective-permute-start(f32[4,3072]{1,0:T(4,128)S(1)} %dynamic_update_slice.3), channel_id=1, source_target_pairs={{0,16},{8,24},{16,0},{24,8},{1,17},{9,25},{17,1},{25,9},{2,18},{10... | collective-permute-start | bytes 147464 | tf_op jit(solution)/shard_map/ppermute | solution.py:33
  12.3 12.8 %collective-permute-start.10 = (f32[4,3072]{1,0:T(4,128)S(1)}, f32[4,3072]{1,0:T(4,128)S(1)}, u32[]{:S(2)}, u32[]{:S(2)}) collective-permute-start(f32[4,3072]{1,0:T(4,128)S(1)} %dynamic_update_slice.3), channel_id=1, source_target_pairs={{0,24},{8,16},{16,8},{24,0},{1,25},{9,17},{17,9},{25,1},{2,26},{10... | collective-permute-start | bytes 147464 | tf_op jit(solution)/shard_map/ppermute | solution.py:33
  23.7 7.1 %collective-permute-start.15 = (f32[5,128,128]{2,1,0:T(8,128)S(1)}, f32[5,128,128]{2,1,0:T(8,128)S(1)}, u32[]{:S(2)}, u32[]{:S(2)}) collective-permute-start(f32[5,128,128]{2,1,0:T(8,128)S(1)} %fusion.32), channel_id=1, source_target_pairs={{8,2},{4,8},{24,22},{12,18},{26,14},{22,28},{9,3},{5,9},{25,23},{1... | collective-permute-start | bytes 983048 | tf_op jit(solution)/shard_map/ppermute | solution.py:205
  24.4 6.7 %collective-permute-start.16 = (f32[5,128,128]{2,1,0:T(8,128)S(1)}, f32[5,128,128]{2,1,0:T(8,128)S(1)}, u32[]{:S(2)}, u32[]{:S(2)}) collective-permute-start(f32[5,128,128]{2,1,0:T(8,128)S(1)} %fusion.32), channel_id=1, source_target_pairs={{16,8},{6,22},{17,9},{7,23}} | collective-permute-start | bytes 983048 | tf_op jit(solution)/shard_map/ppermute | solution.py:205
  25.2 117.0 %collective-permute-start.11 = (f32[4,3072]{1,0:T(4,128)S(1)}, f32[4,3072]{1,0:T(4,128)S(1)}, u32[]{:S(2)}, u32[]{:S(2)}) collective-permute-start(f32[4,3072]{1,0:T(4,128)S(1)} %fusion.37), channel_id=1, source_target_pairs={{0,2},{2,0},{4,6},{6,4},{1,3},{3,1},{5,7},{7,5},{8,10},{10,8},{12,... | collective-permute-start | bytes 147464 | tf_op jit(solution)/shard_map/ppermute | solution.py:33
  26.6 116.1 %collective-permute-start.12 = (f32[4,3072]{1,0:T(4,128)S(1)}, f32[4,3072]{1,0:T(4,128)S(1)}, u32[]{:S(2)}, u32[]{:S(2)}) collective-permute-start(f32[4,3072]{1,0:T(4,128)S(1)} %fusion.37), channel_id=1, source_target_pairs={{0,4},{2,6},{4,0},{6,2},{1,5},{3,7},{5,1},{7,3},{8,12},{10,14},{12... | collective-permute-start | bytes 147464 | tf_op jit(solution)/shard_map/ppermute | solution.py:33
  30.8 112.4 %collective-permute-start.13 = (f32[4,3072]{1,0:T(4,128)S(1)}, f32[4,3072]{1,0:T(4,128)S(1)}, u32[]{:S(2)}, u32[]{:S(2)}) collective-permute-start(f32[4,3072]{1,0:T(4,128)S(1)} %fusion.37), channel_id=1, source_target_pairs={{0,6},{2,4},{4,2},{6,0},{1,7},{3,5},{5,3},{7,1},{8,14},{10,12},{12... | collective-permute-start | bytes 147464 | tf_op jit(solution)/shard_map/ppermute | solution.py:33
  31.1 112.7 %slice-start = ((s8[6291456]{0:T(1024)(128)(4,1)}), s8[4194304]{0:T(1024)(128)(4,1)S(1)}, s32[]{:S(2)}) async-start(s8[6291456]{0:T(1024)(128)(4,1)} %bitcast.134), calls=%async_computation | async-start | bytes 8388608
  31.1 112.2 %collective-permute-start.17 = (f32[2,5,128,128]{3,2,1,0:T(8,128)S(1)}, f32[2,5,128,128]{3,2,1,0:T(8,128)S(1)}, u32[]{:S(2)}, u32[]{:S(2)}) collective-permute-start(f32[2,5,128,128]{3,2,1,0:T(8,128)S(1)} %pad_maximum_fusion.8), channel_id=1, source_target_pairs={{0,1},{1,0},{2,3},{3,2},{4,5},{5,4},{6,7},{7,6},{8,9},{9,8},{10,11... | collective-permute-start | bytes 1966088 | tf_op jit(solution)/shard_map/ppermute | solution.py:206
  143.4 1.6 slice-start.1
  158.3 2.0 collective-permute-start
  160.3 2.8 %copy-start = (bf16[4,256,3072]{2,1,0:T(8,128)(2,1)S(1)}, bf16[4,256,3072]{2,1,0:T(8,128)(2,1)}, u32[]{:S(2)}) copy-start(bf16[4,256,3072]{2,1,0:T(8,128)(2,1)} %get-tuple-element.372.mine_ref) | copy-start | bytes 18874372 | tf_op jit(solution)/shard_map/while
  172.4 9.8 %collective-permute-start.1 = (f32[4,3072]{1,0:T(4,128)S(1)}, f32[4,3072]{1,0:T(4,128)S(1)}, u32[]{:S(2)}, u32[]{:S(2)}) collective-permute-start(f32[4,3072]{1,0:T(4,128)S(1)} %select_add_fusion.2), channel_id=1, source_target_pairs={{0,24},{8,16},{16,8},{24,0},{1,25},{9,17},{17,9},{25,1},{2,26},{10... | collective-permute-start | bytes 147464 | tf_op jit(solution)/shard_map/while/body/eval_jaxpr/ppermute | solution.py:33
  175.2 9.0 %collective-permute-start.2 = (f32[4,3072]{1,0:T(4,128)S(1)}, f32[4,3072]{1,0:T(4,128)S(1)}, u32[]{:S(2)}, u32[]{:S(2)}) collective-permute-start(f32[4,3072]{1,0:T(4,128)S(1)} %select_add_fusion.2), channel_id=1, source_target_pairs={{0,16},{8,24},{16,0},{24,8},{1,17},{9,25},{17,1},{25,9},{2,18},{10... | collective-permute-start | bytes 147464 | tf_op jit(solution)/shard_map/while/body/eval_jaxpr/ppermute | solution.py:33
  182.1 4.1 %collective-permute-start.3 = (f32[4,3072]{1,0:T(4,128)S(1)}, f32[4,3072]{1,0:T(4,128)S(1)}, u32[]{:S(2)}, u32[]{:S(2)}) collective-permute-start(f32[4,3072]{1,0:T(4,128)S(1)} %select_add_fusion.2), channel_id=1, source_target_pairs={{0,8},{8,0},{16,24},{24,16},{1,9},{9,1},{17,25},{25,17},{2,10},{10... | collective-permute-start | bytes 147464 | tf_op jit(solution)/shard_map/while/body/eval_jaxpr/ppermute | solution.py:33
  186.3 6.5 %collective-permute-start.4 = (f32[4,3072]{1,0:T(4,128)S(1)}, f32[4,3072]{1,0:T(4,128)S(1)}, u32[]{:S(2)}, u32[]{:S(2)}) collective-permute-start(f32[4,3072]{1,0:T(4,128)S(1)} %fusion.55), channel_id=1, source_target_pairs={{0,6},{2,4},{4,2},{6,0},{1,7},{3,5},{5,3},{7,1},{8,14},{10,12},{12... | collective-permute-start | bytes 147464 | tf_op jit(solution)/shard_map/while/body/eval_jaxpr/ppermute | solution.py:33
  186.4 9.0 %collective-permute-start.5 = (f32[4,3072]{1,0:T(4,128)S(1)}, f32[4,3072]{1,0:T(4,128)S(1)}, u32[]{:S(2)}, u32[]{:S(2)}) collective-permute-start(f32[4,3072]{1,0:T(4,128)S(1)} %fusion.55), channel_id=1, source_target_pairs={{0,4},{2,6},{4,0},{6,2},{1,5},{3,7},{5,1},{7,3},{8,12},{10,14},{12... | collective-permute-start | bytes 147464 | tf_op jit(solution)/shard_map/while/body/eval_jaxpr/ppermute | solution.py:33
  192.3 4.1 %collective-permute-start.6 = (f32[4,3072]{1,0:T(4,128)S(1)}, f32[4,3072]{1,0:T(4,128)S(1)}, u32[]{:S(2)}, u32[]{:S(2)}) collective-permute-start(f32[4,3072]{1,0:T(4,128)S(1)} %fusion.55), channel_id=1, source_target_pairs={{0,2},{2,0},{4,6},{6,4},{1,3},{3,1},{5,7},{7,5},{8,10},{10,8},{12,... | collective-permute-start | bytes 147464 | tf_op jit(solution)/shard_map/while/body/eval_jaxpr/ppermute | solution.py:33
  197.1 1.4 collective-permute-start.7
  210.5 2.0 collective-permute-start
  212.4 2.8 %copy-start = (bf16[4,256,3072]{2,1,0:T(8,128)(2,1)S(1)}, bf16[4,256,3072]{2,1,0:T(8,128)(2,1)}, u32[]{:S(2)}) copy-start(bf16[4,256,3072]{2,1,0:T(8,128)(2,1)} %get-tuple-element.372.mine_ref) | copy-start | bytes 18874372 | tf_op jit(solution)/shard_map/while
  224.5 5.1 %collective-permute-start.1 = (f32[4,3072]{1,0:T(4,128)S(1)}, f32[4,3072]{1,0:T(4,128)S(1)}, u32[]{:S(2)}, u32[]{:S(2)}) collective-permute-start(f32[4,3072]{1,0:T(4,128)S(1)} %select_add_fusion.2), channel_id=1, source_target_pairs={{0,24},{8,16},{16,8},{24,0},{1,25},{9,17},{17,9},{25,1},{2,26},{10... | collective-permute-start | bytes 147464 | tf_op jit(solution)/shard_map/while/body/eval_jaxpr/ppermute | solution.py:33
  227.3 4.1 %collective-permute-start.2 = (f32[4,3072]{1,0:T(4,128)S(1)}, f32[4,3072]{1,0:T(4,128)S(1)}, u32[]{:S(2)}, u32[]{:S(2)}) collective-permute-start(f32[4,3072]{1,0:T(4,128)S(1)} %select_add_fusion.2), channel_id=1, source_target_pairs={{0,16},{8,24},{16,0},{24,8},{1,17},{9,25},{17,1},{25,9},{2,18},{10... | collective-permute-start | bytes 147464 | tf_op jit(solution)/shard_map/while/body/eval_jaxpr/ppermute | solution.py:33
  227.3 4.1 %collective-permute-start.3 = (f32[4,3072]{1,0:T(4,128)S(1)}, f32[4,3072]{1,0:T(4,128)S(1)}, u32[]{:S(2)}, u32[]{:S(2)}) collective-permute-start(f32[4,3072]{1,0:T(4,128)S(1)} %select_add_fusion.2), channel_id=1, source_target_pairs={{0,8},{8,0},{16,24},{24,16},{1,9},{9,1},{17,25},{25,17},{2,10},{10... | collective-permute-start | bytes 147464 | tf_op jit(solution)/shard_map/while/body/eval_jaxpr/ppermute | solution.py:33
  231.5 6.1 %collective-permute-start.4 = (f32[4,3072]{1,0:T(4,128)S(1)}, f32[4,3072]{1,0:T(4,128)S(1)}, u32[]{:S(2)}, u32[]{:S(2)}) collective-permute-start(f32[4,3072]{1,0:T(4,128)S(1)} %fusion.55), channel_id=1, source_target_pairs={{0,6},{2,4},{4,2},{6,0},{1,7},{3,5},{5,3},{7,1},{8,14},{10,12},{12... | collective-permute-start | bytes 147464 | tf_op jit(solution)/shard_map/while/body/eval_jaxpr/ppermute | solution.py:33
  234.4 5.0 %collective-permute-start.5 = (f32[4,3072]{1,0:T(4,128)S(1)}, f32[4,3072]{1,0:T(4,128)S(1)}, u32[]{:S(2)}, u32[]{:S(2)}) collective-permute-start(f32[4,3072]{1,0:T(4,128)S(1)} %fusion.55), channel_id=1, source_target_pairs={{0,4},{2,6},{4,0},{6,2},{1,5},{3,7},{5,1},{7,3},{8,12},{10,14},{12... | collective-permute-start | bytes 147464 | tf_op jit(solution)/shard_map/while/body/eval_jaxpr/ppermute | solution.py:33
  234.4 5.0 %collective-permute-start.6 = (f32[4,3072]{1,0:T(4,128)S(1)}, f32[4,3072]{1,0:T(4,128)S(1)}, u32[]{:S(2)}, u32[]{:S(2)}) collective-permute-start(f32[4,3072]{1,0:T(4,128)S(1)} %fusion.55), channel_id=1, source_target_pairs={{0,2},{2,0},{4,6},{6,4},{1,3},{3,1},{5,7},{7,5},{8,10},{10,8},{12,... | collective-permute-start | bytes 147464 | tf_op jit(solution)/shard_map/while/body/eval_jaxpr/ppermute | solution.py:33
  240.1 1.4 collective-permute-start.7

commit v17 on v12

--- a/solution.py
+++ b/solution.py
@@ -66,20 +66,21 @@
         def _():
             first_ref[...] = jnp.zeros_like(first_ref)
             second_ref[...] = jnp.zeros_like(second_ref)
-        spread = field_ref[0]
-        mine_tile = mine_ref[0]
-        other_tile = other_ref[0]
-        weighted_other = (other_tile.astype(jnp.float32) * spread).astype(jnp.bfloat16)
-        weighted_mine = (mine_tile.astype(jnp.float32) * spread).astype(jnp.bfloat16)
-        dims = (((1,), (1,)), ((), ()))
-        first_ref[0] += jax.lax.dot_general(mine_tile, weighted_other, dims, preferred_element_type=jnp.float32)
-        second_ref[0] += jax.lax.dot_general(other_tile, weighted_mine, dims, preferred_element_type=jnp.float32)
-    spec = pl.BlockSpec((1, rows, tile), lambda f, t: (f, 0, t))
-    out_spec = pl.BlockSpec((1, rows, rows), lambda f, t: (f, 0, 0))
+        for k in range(2):
+            spread = field_ref[k]
+            mine_tile = mine_ref[k]
+            other_tile = other_ref[k]
+            weighted_other = (other_tile.astype(jnp.float32) * spread).astype(jnp.bfloat16)
+            weighted_mine = (mine_tile.astype(jnp.float32) * spread).astype(jnp.bfloat16)
+            dims = (((1,), (1,)), ((), ()))
+            first_ref[k] += jax.lax.dot_general(mine_tile, weighted_other, dims, preferred_element_type=jnp.float32)
+            second_ref[k] += jax.lax.dot_general(other_tile, weighted_mine, dims, preferred_element_type=jnp.float32)
+    spec = pl.BlockSpec((2, rows, tile), lambda f, t: (f, 0, t))
+    out_spec = pl.BlockSpec((2, rows, rows), lambda f, t: (f, 0, 0))
     return pl.pallas_call(
         kernel,
-        grid=(freq, points // tile),
-        in_specs=[spec, spec, pl.BlockSpec((1, 1, tile), lambda f, t: (f, 0, t))],
+        grid=(freq // 2, points // tile),
+        in_specs=[spec, spec, pl.BlockSpec((2, 1, tile), lambda f, t: (f, 0, t))],
         out_specs=[out_spec, out_spec],
         out_shape=[jax.ShapeDtypeStruct((freq, rows, rows), jnp.float32)] * 2,
         compiler_params=pltpu.CompilerParams(dimension_semantics=("parallel", "arbitrary")),

time: 242 us -> 241 us (level)
  no operation moved by 1% of the time
where the time goes in v17:
time: 241 us; the launch traced here: 240 us
  waiting for transfers between devices  134 us (56%)
  starting transfers between devices  44.7 us (19%)
  matrix products  18.5 us (8%)
  Pallas kernels  15.4 us (6%)
  local copies, waits for them, and re-layouts  9.12 us (4%)
  other arithmetic  8.87 us (4%)
  between operations  5.94 us (2%)
  loops' own time  3.07 us (1%)
    ppermute x18, waiting for transfers between devices, butterfly_sum(): got.append(lax.ppermute(value, axis, [(i, i ^ mask) for i in range(size)]))  127 us
    ppermute x18, starting transfers between devices, butterfly_sum(): got.append(lax.ppermute(value, axis, [(i, i ^ mask) for i in range(size)]))  35.2 us
    dot_general x4, matrix products, point_terms(): jnp.einsum('fab,fbn->fan', adjoint_block(adjoint), right_rows, preferred_...  18.5 us
    pallas_call x2, Pallas kernels, pair_products(): pl.pallas_call(kernel, grid=(freq // 2, points // tile), in_specs=[spec,...  15.4 us
    ppermute x4, waiting for transfers between devices, swap_add(): return value + lax.ppermute(value, axis, [(0, 1), (1, 0)])  7.82 us
    ppermute x1, starting transfers between devices, pair_body(): received = lax.ppermute(green_panel, axes, panel_moves)  7.72 us
  transfers between devices with their start and end apart: 26, of which 15 were waited for; matrix products, arithmetic and copies ran while one was open for 2% of the time, Pallas kernels for 0%

profile of v17, /device:TPU:0, one launch (start us, length us, event | category | flops | bytes accessed | tf_op | source)
XLA Modules:
  0.0 240.0 jit_solution(14197499603889173167)
XLA Ops:
  0.0 7.7 %collective-permute-start.14 = (bf16[4,2,128,3072]{3,2,1,0:T(8,128)(2,1)}, bf16[4,2,128,3072]{3,2,1,0:T(8,128)(2,1)}, u32[]{:S(2)}, u32[]{:S(2)}) collective-permute-start(bf16[4,2,128,3072]{3,2,1,0:T(8,128)(2,1)} %param.10), channel_id=1, source_target_pairs={{0,2},{12,8},{16,22},{20,18},{10,14},{30,28},{1,3},{13,9},{17,23},... | collective-permute-start | bytes 18874376 | tf_op jit(solution)/shard_map/ppermute | solution.py:194
  8.7 3.6 %collective-permute-start.9 = (f32[4,3072]{1,0:T(4,128)S(1)}, f32[4,3072]{1,0:T(4,128)S(1)}, u32[]{:S(2)}, u32[]{:S(2)}) collective-permute-start(f32[4,3072]{1,0:T(4,128)S(1)} %dynamic_update_slice.3), channel_id=1, source_target_pairs={{0,16},{8,24},{16,0},{24,8},{1,17},{9,25},{17,1},{25,9},{2,18},{10... | collective-permute-start | bytes 147464 | tf_op jit(solution)/shard_map/ppermute | solution.py:33
  12.3 1.4 collective-permute-start.10
  25.1 1.4 collective-permute-start.11
  26.5 4.2 %collective-permute-start.12 = (f32[4,3072]{1,0:T(4,128)S(1)}, f32[4,3072]{1,0:T(4,128)S(1)}, u32[]{:S(2)}, u32[]{:S(2)}) collective-permute-start(f32[4,3072]{1,0:T(4,128)S(1)} %fusion.34), channel_id=1, source_target_pairs={{0,4},{2,6},{4,0},{6,2},{1,5},{3,7},{5,1},{7,3},{8,12},{10,14},{12... | collective-permute-start | bytes 147464 | tf_op jit(solution)/shard_map/ppermute | solution.py:33
  31.1 111.1 %collective-permute-done.11 = f32[4,3072]{1,0:T(4,128)S(1)} collective-permute-done((f32[4,3072]{1,0:T(4,128)S(1)}, f32[4,3072]{1,0:T(4,128)S(1)}, u32[]{:S(2)}, u32[]{:S(2)}) %collective-permute-start.11) | collective-permute-done | bytes 49184 | tf_op jit(solution)/shard_map/ppermute | solution.py:33
  145.0 2.6 %conditional.1 = (bf16[4,256,3072]{2,1,0:T(8,128)(2,1)}) conditional(s32[]{:T(128)} %bitcast.44, bf16[4,2,128,3072]{3,2,1,0:T(8,128)(2,1)} %collective-permute-done.14, bf16[4,2,128,3072]{3,2,1,0:T(8,128)(2,1)S(1)} %bitcast.135), branch_computations={%region_0.1_spmd, %region_1.2_spmd} | conditional | bytes 12582920 | solution.py:215
  145.0 2.6 %copy.11 = bf16[4,256,3072]{2,1,0:T(8,128)(2,1)} copy(bf16[4,256,3072]{2,1,0:T(8,128)(2,1)S(1)} %bitcast.136) | data formatting | bytes 12582912 | tf_op jit(solution)/shard_map/cond
  147.7 91.6 %while.13 = (s32[]{:T(128)}, f32[4,3072]{1,0:T(4,128)S(1)}, pred[]{:T(512)}, bf16[4,256,3072]{2,1,0:T(8,128)(2,1)}, f32[1,128,128]{2,1,0:T(8,128)S(1)}, /*index=...) while((s32[]{:T(128)}, f32[4,3072]{1,0:T(4,128)S(1)}, ...), condition=%wide.region_6.7_spmd, body=%wide.region_2.6_spmd.sunk | while | flops 3247300608 | bytes 67175664 | solution.py:250
  148.3 7.7 %eval_jaxpr.5 = (f32[4,256,256]{2,1,0:T(8,128)}, f32[4,256,256]{2,1,0:T(8,128)}) custom-call(bf16[4,256,3072]{2,1,0:T(8,128)(2,1)} %get-tuple-element.372.mine_ref, bf16[4,256,3072]{2,1,0:T(8,128)(2,1)} %get-tuple-element.374.other_ref, f32[4,1,3072]{2,1,0:T(1,128)} %broadcast_in_dim.36.field_ref), custom_call_target="tpu_custom_call" | custom-call | tf_op jit(solution)/shard_map/while/body/eval_jaxpr/pallas_call | solution.py:80
  156.1 1.8 add_bitcast_fusion.4
  158.1 2.6 %collective-permute-done = f32[2,4,2,128,128]{4,3,1,2,0:T(8,128)S(1)} collective-permute-done((f32[2,4,2,128,128]{4,3,1,2,0:T(8,128)S(1)}, f32[2,4,2,128,128]{4,3,1,2,0:T(8,128)S(1)}, u32[]{:S(2)}, u32[]{:S(2)}) %collective-permute-start) | collective-permute-done | bytes 1048608 | tf_op jit(solution)/shard_map/while/body/eval_jaxpr/ppermute | solution.py:49
  161.2 4.6 %multiply_reduce_fusion.7 = f32[4,3072]{1,0:T(4,128)S(1)} fusion(bf16[4,256,3072]{2,1,0:T(8,128)(2,1)S(1)} %bitcast.138, bf16[4,256,3072]{2,1,0:T(8,128)(2,1)} %get-tuple-element.374.other_ref, bf16[4,128,128]{2,1,0:T(8,128)(2,1)S(1)} %get-tuple-element.325, bf16[4,128,128]{2,1,0:T(8,128)(2,1)S(1)} %get-tuple-element.326, ...), kind=kOutput, calls=%fused_computation.1.clone.1 | convolution fusion | flops 1622134784 | bytes 13025280 | tf_op jit(solution)/shard_map/while/body/eval_jaxpr/fab,fbn->fan/dot_general | solution.py:105
  165.9 4.6 %multiply_reduce_fusion.6 = f32[4,3072]{1,0:T(4,128)S(1)} fusion(bf16[4,256,3072]{2,1,0:T(8,128)(2,1)} %get-tuple-element.374.other_ref, bf16[4,256,3072]{2,1,0:T(8,128)(2,1)S(1)} %bitcast.138, bf16[4,128,128]{2,1,0:T(8,128)(2,1)S(1)} %get-tuple-element.322, bf16[4,128,128]{2,1,0:T(8,128)(2,1)S(1)} %get-tuple-element.323, ...), kind=kOutput, calls=%fused_computation.clone.1 | convolution fusion | flops 1622134784 | bytes 13025280 | tf_op jit(solution)/shard_map/while/body/eval_jaxpr/fab,fbn->fan/dot_general | solution.py:105
  170.5 2.8 %collective-permute-start.1 = (f32[4,3072]{1,0:T(4,128)S(1)}, f32[4,3072]{1,0:T(4,128)S(1)}, u32[]{:S(2)}, u32[]{:S(2)}) collective-permute-start(f32[4,3072]{1,0:T(4,128)S(1)} %select_add_fusion.2), channel_id=1, source_target_pairs={{0,24},{8,16},{16,8},{24,0},{1,25},{9,17},{17,9},{25,1},{2,26},{10... | collective-permute-start | bytes 147464 | tf_op jit(solution)/shard_map/while/body/eval_jaxpr/ppermute | solution.py:33
  173.3 7.0 %collective-permute-start.2 = (f32[4,3072]{1,0:T(4,128)S(1)}, f32[4,3072]{1,0:T(4,128)S(1)}, u32[]{:S(2)}, u32[]{:S(2)}) collective-permute-start(f32[4,3072]{1,0:T(4,128)S(1)} %select_add_fusion.2), channel_id=1, source_target_pairs={{0,16},{8,24},{16,0},{24,8},{1,17},{9,25},{17,1},{25,9},{2,18},{10... | collective-permute-start | bytes 147464 | tf_op jit(solution)/shard_map/while/body/eval_jaxpr/ppermute | solution.py:33
  180.3 2.1 collective-permute-done.2
  182.4 2.0 collective-permute-done.3
  184.6 5.9 %collective-permute-start.5 = (f32[4,3072]{1,0:T(4,128)S(1)}, f32[4,3072]{1,0:T(4,128)S(1)}, u32[]{:S(2)}, u32[]{:S(2)}) collective-permute-start(f32[4,3072]{1,0:T(4,128)S(1)} %fusion.52), channel_id=1, source_target_pairs={{0,4},{2,6},{4,0},{6,2},{1,5},{3,7},{5,1},{7,3},{8,12},{10,14},{12... | collective-permute-start | bytes 147464 | tf_op jit(solution)/shard_map/while/body/eval_jaxpr/ppermute | solution.py:33
  191.0 2.5 %collective-permute-done.5 = f32[4,3072]{1,0:T(4,128)S(1)} collective-permute-done((f32[4,3072]{1,0:T(4,128)S(1)}, f32[4,3072]{1,0:T(4,128)S(1)}, u32[]{:S(2)}, u32[]{:S(2)}) %collective-permute-start.5) | collective-permute-done | bytes 49184 | tf_op jit(solution)/shard_map/while/body/eval_jaxpr/ppermute | solution.py:33
  198.7 7.7 %eval_jaxpr.5 = (f32[4,256,256]{2,1,0:T(8,128)}, f32[4,256,256]{2,1,0:T(8,128)}) custom-call(bf16[4,256,3072]{2,1,0:T(8,128)(2,1)} %get-tuple-element.372.mine_ref, bf16[4,256,3072]{2,1,0:T(8,128)(2,1)} %get-tuple-element.374.other_ref, f32[4,1,3072]{2,1,0:T(1,128)} %broadcast_in_dim.36.field_ref), custom_call_target="tpu_custom_call" | custom-call | tf_op jit(solution)/shard_map/while/body/eval_jaxpr/pallas_call | solution.py:80
  206.4 1.8 add_bitcast_fusion.4
  208.7 2.5 %collective-permute-done = f32[2,4,2,128,128]{4,3,1,2,0:T(8,128)S(1)} collective-permute-done((f32[2,4,2,128,128]{4,3,1,2,0:T(8,128)S(1)}, f32[2,4,2,128,128]{4,3,1,2,0:T(8,128)S(1)}, u32[]{:S(2)}, u32[]{:S(2)}) %collective-permute-start) | collective-permute-done | bytes 1048608 | tf_op jit(solution)/shard_map/while/body/eval_jaxpr/ppermute | solution.py:49
  211.6 4.6 %multiply_reduce_fusion.7 = f32[4,3072]{1,0:T(4,128)S(1)} fusion(bf16[4,256,3072]{2,1,0:T(8,128)(2,1)S(1)} %bitcast.138, bf16[4,256,3072]{2,1,0:T(8,128)(2,1)} %get-tuple-element.374.other_ref, bf16[4,128,128]{2,1,0:T(8,128)(2,1)S(1)} %get-tuple-element.325, bf16[4,128,128]{2,1,0:T(8,128)(2,1)S(1)} %get-tuple-element.326, ...), kind=kOutput, calls=%fused_computation.1.clone.1 | convolution fusion | flops 1622134784 | bytes 13025280 | tf_op jit(solution)/shard_map/while/body/eval_jaxpr/fab,fbn->fan/dot_general | solution.py:105
  216.2 4.6 %multiply_reduce_fusion.6 = f32[4,3072]{1,0:T(4,128)S(1)} fusion(bf16[4,256,3072]{2,1,0:T(8,128)(2,1)} %get-tuple-element.374.other_ref, bf16[4,256,3072]{2,1,0:T(8,128)(2,1)S(1)} %bitcast.138, bf16[4,128,128]{2,1,0:T(8,128)(2,1)S(1)} %get-tuple-element.322, bf16[4,128,128]{2,1,0:T(8,128)(2,1)S(1)} %get-tuple-element.323, ...), kind=kOutput, calls=%fused_computation.clone.1 | convolution fusion | flops 1622134784 | bytes 13025280 | tf_op jit(solution)/shard_map/while/body/eval_jaxpr/fab,fbn->fan/dot_general | solution.py:105
  220.9 2.8 %collective-permute-start.1 = (f32[4,3072]{1,0:T(4,128)S(1)}, f32[4,3072]{1,0:T(4,128)S(1)}, u32[]{:S(2)}, u32[]{:S(2)}) collective-permute-start(f32[4,3072]{1,0:T(4,128)S(1)} %select_add_fusion.2), channel_id=1, source_target_pairs={{0,24},{8,16},{16,8},{24,0},{1,25},{9,17},{17,9},{25,1},{2,26},{10... | collective-permute-start | bytes 147464 | tf_op jit(solution)/shard_map/while/body/eval_jaxpr/ppermute | solution.py:33
  224.5 1.5 collective-permute-done.1
  226.0 1.8 collective-permute-done.2
  227.9 2.9 %collective-permute-start.4 = (f32[4,3072]{1,0:T(4,128)S(1)}, f32[4,3072]{1,0:T(4,128)S(1)}, u32[]{:S(2)}, u32[]{:S(2)}) collective-permute-start(f32[4,3072]{1,0:T(4,128)S(1)} %fusion.52), channel_id=1, source_target_pairs={{0,6},{2,4},{4,2},{6,0},{1,7},{3,5},{5,3},{7,1},{8,14},{10,12},{12... | collective-permute-start | bytes 147464 | tf_op jit(solution)/shard_map/while/body/eval_jaxpr/ppermute | solution.py:33
  230.8 1.5 collective-permute-start.6
  232.4 1.6 collective-permute-done.4
  234.0 1.9 collective-permute-done.5
  (109 shorter events, 20.0 us)
Async XLA Ops:
  0.0 19.8 %copy-start.1 = (s32[16]{0:T(128)S(1)}, s32[16]{0:T(128)}, u32[]{:S(2)}) copy-start(s32[16]{0:T(128)} %constant.200.clone) | copy-start | bytes 196
  0.0 16.4 %copy-start = (f32[4,2,128,128]{3,2,1,0:T(8,128)S(1)}, f32[4,2,128,128]{3,2,1,0:T(8,128)}, u32[]{:S(2)}) copy-start(f32[4,2,128,128]{3,2,1,0:T(8,128)} %param.12) | copy-start | bytes 1572868
  0.0 143.6 %collective-permute-start.14 = (bf16[4,2,128,3072]{3,2,1,0:T(8,128)(2,1)}, bf16[4,2,128,3072]{3,2,1,0:T(8,128)(2,1)}, u32[]{:S(2)}, u32[]{:S(2)}) collective-permute-start(bf16[4,2,128,3072]{3,2,1,0:T(8,128)(2,1)} %param.10), channel_id=1, source_target_pairs={{0,2},{12,8},{16,22},{20,18},{10,14},{30,28},{1,3},{13,9},{17,23},... | collective-permute-start | bytes 18874376 | tf_op jit(solution)/shard_map/ppermute | solution.py:194
  8.6 15.7 %collective-permute-start.8 = (f32[4,3072]{1,0:T(4,128)S(1)}, f32[4,3072]{1,0:T(4,128)S(1)}, u32[]{:S(2)}, u32[]{:S(2)}) collective-permute-start(f32[4,3072]{1,0:T(4,128)S(1)} %dynamic_update_slice.3), channel_id=1, source_target_pairs={{0,8},{8,0},{16,24},{24,16},{1,9},{9,1},{17,25},{25,17},{2,10},{10... | collective-permute-start | bytes 147464 | tf_op jit(solution)/shard_map/ppermute | solution.py:33
  8.7 16.3 %collective-permute-start.9 = (f32[4,3072]{1,0:T(4,128)S(1)}, f32[4,3072]{1,0:T(4,128)S(1)}, u32[]{:S(2)}, u32[]{:S(2)}) collective-permute-start(f32[4,3072]{1,0:T(4,128)S(1)} %dynamic_update_slice.3), channel_id=1, source_target_pairs={{0,16},{8,24},{16,0},{24,8},{1,17},{9,25},{17,1},{25,9},{2,18},{10... | collective-permute-start | bytes 147464 | tf_op jit(solution)/shard_map/ppermute | solution.py:33
  12.3 12.7 %collective-permute-start.10 = (f32[4,3072]{1,0:T(4,128)S(1)}, f32[4,3072]{1,0:T(4,128)S(1)}, u32[]{:S(2)}, u32[]{:S(2)}) collective-permute-start(f32[4,3072]{1,0:T(4,128)S(1)} %dynamic_update_slice.3), channel_id=1, source_target_pairs={{0,24},{8,16},{16,8},{24,0},{1,25},{9,17},{17,9},{25,1},{2,26},{10... | collective-permute-start | bytes 147464 | tf_op jit(solution)/shard_map/ppermute | solution.py:33
  23.6 7.1 %collective-permute-start.15 = (f32[5,128,128]{2,1,0:T(8,128)S(1)}, f32[5,128,128]{2,1,0:T(8,128)S(1)}, u32[]{:S(2)}, u32[]{:S(2)}) collective-permute-start(f32[5,128,128]{2,1,0:T(8,128)S(1)} %fusion.29), channel_id=1, source_target_pairs={{8,2},{4,8},{24,22},{12,18},{26,14},{22,28},{9,3},{5,9},{25,23},{1... | collective-permute-start | bytes 983048 | tf_op jit(solution)/shard_map/ppermute | solution.py:206
  24.3 6.7 %collective-permute-start.16 = (f32[5,128,128]{2,1,0:T(8,128)S(1)}, f32[5,128,128]{2,1,0:T(8,128)S(1)}, u32[]{:S(2)}, u32[]{:S(2)}) collective-permute-start(f32[5,128,128]{2,1,0:T(8,128)S(1)} %fusion.29), channel_id=1, source_target_pairs={{16,8},{6,22},{17,9},{7,23}} | collective-permute-start | bytes 983048 | tf_op jit(solution)/shard_map/ppermute | solution.py:206
  25.1 117.1 %collective-permute-start.11 = (f32[4,3072]{1,0:T(4,128)S(1)}, f32[4,3072]{1,0:T(4,128)S(1)}, u32[]{:S(2)}, u32[]{:S(2)}) collective-permute-start(f32[4,3072]{1,0:T(4,128)S(1)} %fusion.34), channel_id=1, source_target_pairs={{0,2},{2,0},{4,6},{6,4},{1,3},{3,1},{5,7},{7,5},{8,10},{10,8},{12,... | collective-permute-start | bytes 147464 | tf_op jit(solution)/shard_map/ppermute | solution.py:33
  26.5 116.2 %collective-permute-start.12 = (f32[4,3072]{1,0:T(4,128)S(1)}, f32[4,3072]{1,0:T(4,128)S(1)}, u32[]{:S(2)}, u32[]{:S(2)}) collective-permute-start(f32[4,3072]{1,0:T(4,128)S(1)} %fusion.34), channel_id=1, source_target_pairs={{0,4},{2,6},{4,0},{6,2},{1,5},{3,7},{5,1},{7,3},{8,12},{10,14},{12... | collective-permute-start | bytes 147464 | tf_op jit(solution)/shard_map/ppermute | solution.py:33
  30.7 112.5 %collective-permute-start.13 = (f32[4,3072]{1,0:T(4,128)S(1)}, f32[4,3072]{1,0:T(4,128)S(1)}, u32[]{:S(2)}, u32[]{:S(2)}) collective-permute-start(f32[4,3072]{1,0:T(4,128)S(1)} %fusion.34), channel_id=1, source_target_pairs={{0,6},{2,4},{4,2},{6,0},{1,7},{3,5},{5,3},{7,1},{8,14},{10,12},{12... | collective-permute-start | bytes 147464 | tf_op jit(solution)/shard_map/ppermute | solution.py:33
  31.0 112.8 %slice-start = ((s8[6291456]{0:T(1024)(128)(4,1)}), s8[4194304]{0:T(1024)(128)(4,1)S(1)}, s32[]{:S(2)}) async-start(s8[6291456]{0:T(1024)(128)(4,1)} %bitcast.134), calls=%async_computation | async-start | bytes 8388608
  31.0 112.3 %collective-permute-start.17 = (f32[2,5,128,128]{3,2,1,0:T(8,128)S(1)}, f32[2,5,128,128]{3,2,1,0:T(8,128)S(1)}, u32[]{:S(2)}, u32[]{:S(2)}) collective-permute-start(f32[2,5,128,128]{3,2,1,0:T(8,128)S(1)} %pad_maximum_fusion.8), channel_id=1, source_target_pairs={{0,1},{1,0},{2,3},{3,2},{4,5},{5,4},{6,7},{7,6},{8,9},{9,8},{10,11... | collective-permute-start | bytes 1966088 | tf_op jit(solution)/shard_map/ppermute | solution.py:207
  148.3 12.9 %slice-start.2 = ((s8[6291456]{0:T(1024)(128)(4,1)}), s8[2097152]{0:T(1024)(128)(4,1)S(1)}, s32[]{:S(2)}) async-start(s8[6291456]{0:T(1024)(128)(4,1)} %bitcast.137), calls=%async_computation.2 | async-start | bytes 4194304 | tf_op jit(solution)/shard_map/while
  156.0 5.2 %slice-start.3 = ((s8[6291456]{0:T(1024)(128)(4,1)}), s8[4194304]{0:T(1024)(128)(4,1)S(1)}, s32[]{:S(2)}) async-start(s8[6291456]{0:T(1024)(128)(4,1)} %bitcast.137), calls=%async_computation.3 | async-start | bytes 8388608 | tf_op jit(solution)/shard_map/while
  158.0 2.7 %collective-permute-start = (f32[2,4,2,128,128]{4,3,1,2,0:T(8,128)S(1)}, f32[2,4,2,128,128]{4,3,1,2,0:T(8,128)S(1)}, u32[]{:S(2)}, u32[]{:S(2)}) collective-permute-start(f32[2,4,2,128,128]{4,3,1,2,0:T(8,128)S(1)} %pad_maximum_fusion.14), channel_id=1, source_target_pairs={{0,1},{1,0},{2,3},{3,2},{4,5},{5,4},{6,7},{7,6},{8,9},{9,8},{10,11... | collective-permute-start | bytes 3145736 | tf_op jit(solution)/shard_map/while/body/eval_jaxpr/ppermute | solution.py:49
  170.5 9.8 %collective-permute-start.1 = (f32[4,3072]{1,0:T(4,128)S(1)}, f32[4,3072]{1,0:T(4,128)S(1)}, u32[]{:S(2)}, u32[]{:S(2)}) collective-permute-start(f32[4,3072]{1,0:T(4,128)S(1)} %select_add_fusion.2), channel_id=1, source_target_pairs={{0,24},{8,16},{16,8},{24,0},{1,25},{9,17},{17,9},{25,1},{2,26},{10... | collective-permute-start | bytes 147464 | tf_op jit(solution)/shard_map/while/body/eval_jaxpr/ppermute | solution.py:33
  173.3 9.0 %collective-permute-start.2 = (f32[4,3072]{1,0:T(4,128)S(1)}, f32[4,3072]{1,0:T(4,128)S(1)}, u32[]{:S(2)}, u32[]{:S(2)}) collective-permute-start(f32[4,3072]{1,0:T(4,128)S(1)} %select_add_fusion.2), channel_id=1, source_target_pairs={{0,16},{8,24},{16,0},{24,8},{1,17},{9,25},{17,1},{25,9},{2,18},{10... | collective-permute-start | bytes 147464 | tf_op jit(solution)/shard_map/while/body/eval_jaxpr/ppermute | solution.py:33
  180.3 4.1 %collective-permute-start.3 = (f32[4,3072]{1,0:T(4,128)S(1)}, f32[4,3072]{1,0:T(4,128)S(1)}, u32[]{:S(2)}, u32[]{:S(2)}) collective-permute-start(f32[4,3072]{1,0:T(4,128)S(1)} %select_add_fusion.2), channel_id=1, source_target_pairs={{0,8},{8,0},{16,24},{24,16},{1,9},{9,1},{17,25},{25,17},{2,10},{10... | collective-permute-start | bytes 147464 | tf_op jit(solution)/shard_map/while/body/eval_jaxpr/ppermute | solution.py:33
  184.5 6.5 %collective-permute-start.4 = (f32[4,3072]{1,0:T(4,128)S(1)}, f32[4,3072]{1,0:T(4,128)S(1)}, u32[]{:S(2)}, u32[]{:S(2)}) collective-permute-start(f32[4,3072]{1,0:T(4,128)S(1)} %fusion.52), channel_id=1, source_target_pairs={{0,6},{2,4},{4,2},{6,0},{1,7},{3,5},{5,3},{7,1},{8,14},{10,12},{12... | collective-permute-start | bytes 147464 | tf_op jit(solution)/shard_map/while/body/eval_jaxpr/ppermute | solution.py:33
  184.6 9.0 %collective-permute-start.5 = (f32[4,3072]{1,0:T(4,128)S(1)}, f32[4,3072]{1,0:T(4,128)S(1)}, u32[]{:S(2)}, u32[]{:S(2)}) collective-permute-start(f32[4,3072]{1,0:T(4,128)S(1)} %fusion.52), channel_id=1, source_target_pairs={{0,4},{2,6},{4,0},{6,2},{1,5},{3,7},{5,1},{7,3},{8,12},{10,14},{12... | collective-permute-start | bytes 147464 | tf_op jit(solution)/shard_map/while/body/eval_jaxpr/ppermute | solution.py:33
  190.5 4.1 %collective-permute-start.6 = (f32[4,3072]{1,0:T(4,128)S(1)}, f32[4,3072]{1,0:T(4,128)S(1)}, u32[]{:S(2)}, u32[]{:S(2)}) collective-permute-start(f32[4,3072]{1,0:T(4,128)S(1)} %fusion.52), channel_id=1, source_target_pairs={{0,2},{2,0},{4,6},{6,4},{1,3},{3,1},{5,7},{7,5},{8,10},{10,8},{12,... | collective-permute-start | bytes 147464 | tf_op jit(solution)/shard_map/while/body/eval_jaxpr/ppermute | solution.py:33
  195.3 1.4 collective-permute-start.7
  198.7 12.9 %slice-start.2 = ((s8[6291456]{0:T(1024)(128)(4,1)}), s8[2097152]{0:T(1024)(128)(4,1)S(1)}, s32[]{:S(2)}) async-start(s8[6291456]{0:T(1024)(128)(4,1)} %bitcast.137), calls=%async_computation.2 | async-start | bytes 4194304 | tf_op jit(solution)/shard_map/while
  208.4 2.7 %collective-permute-start = (f32[2,4,2,128,128]{4,3,1,2,0:T(8,128)S(1)}, f32[2,4,2,128,128]{4,3,1,2,0:T(8,128)S(1)}, u32[]{:S(2)}, u32[]{:S(2)}) collective-permute-start(f32[2,4,2,128,128]{4,3,1,2,0:T(8,128)S(1)} %pad_maximum_fusion.14), channel_id=1, source_target_pairs={{0,1},{1,0},{2,3},{3,2},{4,5},{5,4},{6,7},{7,6},{8,9},{9,8},{10,11... | collective-permute-start | bytes 3145736 | tf_op jit(solution)/shard_map/while/body/eval_jaxpr/ppermute | solution.py:49
  220.9 5.1 %collective-permute-start.1 = (f32[4,3072]{1,0:T(4,128)S(1)}, f32[4,3072]{1,0:T(4,128)S(1)}, u32[]{:S(2)}, u32[]{:S(2)}) collective-permute-start(f32[4,3072]{1,0:T(4,128)S(1)} %select_add_fusion.2), channel_id=1, source_target_pairs={{0,24},{8,16},{16,8},{24,0},{1,25},{9,17},{17,9},{25,1},{2,26},{10... | collective-permute-start | bytes 147464 | tf_op jit(solution)/shard_map/while/body/eval_jaxpr/ppermute | solution.py:33
  223.7 4.1 %collective-permute-start.2 = (f32[4,3072]{1,0:T(4,128)S(1)}, f32[4,3072]{1,0:T(4,128)S(1)}, u32[]{:S(2)}, u32[]{:S(2)}) collective-permute-start(f32[4,3072]{1,0:T(4,128)S(1)} %select_add_fusion.2), channel_id=1, source_target_pairs={{0,16},{8,24},{16,0},{24,8},{1,17},{9,25},{17,1},{25,9},{2,18},{10... | collective-permute-start | bytes 147464 | tf_op jit(solution)/shard_map/while/body/eval_jaxpr/ppermute | solution.py:33
  223.7 4.1 %collective-permute-start.3 = (f32[4,3072]{1,0:T(4,128)S(1)}, f32[4,3072]{1,0:T(4,128)S(1)}, u32[]{:S(2)}, u32[]{:S(2)}) collective-permute-start(f32[4,3072]{1,0:T(4,128)S(1)} %select_add_fusion.2), channel_id=1, source_target_pairs={{0,8},{8,0},{16,24},{24,16},{1,9},{9,1},{17,25},{25,17},{2,10},{10... | collective-permute-start | bytes 147464 | tf_op jit(solution)/shard_map/while/body/eval_jaxpr/ppermute | solution.py:33
  227.9 6.1 %collective-permute-start.4 = (f32[4,3072]{1,0:T(4,128)S(1)}, f32[4,3072]{1,0:T(4,128)S(1)}, u32[]{:S(2)}, u32[]{:S(2)}) collective-permute-start(f32[4,3072]{1,0:T(4,128)S(1)} %fusion.52), channel_id=1, source_target_pairs={{0,6},{2,4},{4,2},{6,0},{1,7},{3,5},{5,3},{7,1},{8,14},{10,12},{12... | collective-permute-start | bytes 147464 | tf_op jit(solution)/shard_map/while/body/eval_jaxpr/ppermute | solution.py:33
  230.8 5.0 %collective-permute-start.5 = (f32[4,3072]{1,0:T(4,128)S(1)}, f32[4,3072]{1,0:T(4,128)S(1)}, u32[]{:S(2)}, u32[]{:S(2)}) collective-permute-start(f32[4,3072]{1,0:T(4,128)S(1)} %fusion.52), channel_id=1, source_target_pairs={{0,4},{2,6},{4,0},{6,2},{1,5},{3,7},{5,1},{7,3},{8,12},{10,14},{12... | collective-permute-start | bytes 147464 | tf_op jit(solution)/shard_map/while/body/eval_jaxpr/ppermute | solution.py:33
  230.8 5.0 %collective-permute-start.6 = (f32[4,3072]{1,0:T(4,128)S(1)}, f32[4,3072]{1,0:T(4,128)S(1)}, u32[]{:S(2)}, u32[]{:S(2)}) collective-permute-start(f32[4,3072]{1,0:T(4,128)S(1)} %fusion.52), channel_id=1, source_target_pairs={{0,2},{2,0},{4,6},{6,4},{1,3},{3,1},{5,7},{7,5},{8,10},{10,8},{12,... | collective-permute-start | bytes 147464 | tf_op jit(solution)/shard_map/while/body/eval_jaxpr/ppermute | solution.py:33
  236.5 1.4 collective-permute-start.7
  (2 other events, 6.8 us)

commit v18 on v17

--- a/solution.py
+++ b/solution.py
@@ -66,7 +66,7 @@
         def _():
             first_ref[...] = jnp.zeros_like(first_ref)
             second_ref[...] = jnp.zeros_like(second_ref)
-        for k in range(2):
+        for k in range(4):
             spread = field_ref[k]
             mine_tile = mine_ref[k]
             other_tile = other_ref[k]
@@ -75,12 +75,12 @@
             dims = (((1,), (1,)), ((), ()))
             first_ref[k] += jax.lax.dot_general(mine_tile, weighted_other, dims, preferred_element_type=jnp.float32)
             second_ref[k] += jax.lax.dot_general(other_tile, weighted_mine, dims, preferred_element_type=jnp.float32)
-    spec = pl.BlockSpec((2, rows, tile), lambda f, t: (f, 0, t))
-    out_spec = pl.BlockSpec((2, rows, rows), lambda f, t: (f, 0, 0))
+    spec = pl.BlockSpec((4, rows, tile), lambda f, t: (f, 0, t))
+    out_spec = pl.BlockSpec((4, rows, rows), lambda f, t: (f, 0, 0))
     return pl.pallas_call(
         kernel,
-        grid=(freq // 2, points // tile),
-        in_specs=[spec, spec, pl.BlockSpec((2, 1, tile), lambda f, t: (f, 0, t))],
+        grid=(freq // 4, points // tile),
+        in_specs=[spec, spec, pl.BlockSpec((4, 1, tile), lambda f, t: (f, 0, t))],
         out_specs=[out_spec, out_spec],
         out_shape=[jax.ShapeDtypeStruct((freq, rows, rows), jnp.float32)] * 2,
         compiler_params=pltpu.CompilerParams(dimension_semantics=("parallel", "arbitrary")),

time: 241 us -> 244 us (1.012)
  Pallas kernels: 15.4 us -> 19.2 us
    pallas_call x2, Pallas kernels: 15.4 us -> 19.2 us  [pair_products(): pl.pallas_call(kernel, grid=(freq // 4, points // tile), in_specs=[spec,...]
where the time goes in v18:
time: 244 us
  waiting for transfers between devices  134 us (55%)
  starting transfers between devices  44.7 us (18%)
  Pallas kernels  19.2 us (8%)
  matrix products  18.5 us (8%)
  local copies, waits for them, and re-layouts  9.12 us (4%)
  other arithmetic  8.87 us (4%)
  between operations  5.94 us (2%)
  loops' own time  3.07 us (1%)
    ppermute x18, waiting for transfers between devices, butterfly_sum(): got.append(lax.ppermute(value, axis, [(i, i ^ mask) for i in range(size)]))  127 us
    ppermute x18, starting transfers between devices, butterfly_sum(): got.append(lax.ppermute(value, axis, [(i, i ^ mask) for i in range(size)]))  35.2 us
    pallas_call x2, Pallas kernels, pair_products(): pl.pallas_call(kernel, grid=(freq // 4, points // tile), in_specs=[spec,...  19.2 us
    dot_general x4, matrix products, point_terms(): jnp.einsum('fab,fbn->fan', adjoint_block(adjoint), right_rows, preferred_...  18.5 us
    ppermute x4, waiting for transfers between devices, swap_add(): return value + lax.ppermute(value, axis, [(0, 1), (1, 0)])  7.81 us
    ppermute x1, starting transfers between devices, pair_body(): received = lax.ppermute(green_panel, axes, panel_moves)  7.72 us
  transfers between devices with their start and end apart: 26, of which 15 were waited for; matrix products, arithmetic and copies ran while one was open for 2% of the time, Pallas kernels for 0%

profile of v18, /device:TPU:0, one launch (start us, length us, event | category | flops | bytes accessed | tf_op | source)
XLA Modules:
  0.0 243.7 jit_solution(1838205124439443260)
XLA Ops:
  0.0 7.7 %collective-permute-start.14 = (bf16[4,2,128,3072]{3,2,1,0:T(8,128)(2,1)}, bf16[4,2,128,3072]{3,2,1,0:T(8,128)(2,1)}, u32[]{:S(2)}, u32[]{:S(2)}) collective-permute-start(bf16[4,2,128,3072]{3,2,1,0:T(8,128)(2,1)} %param.10), channel_id=1, source_target_pairs={{0,2},{12,8},{16,22},{20,18},{10,14},{30,28},{1,3},{13,9},{17,23},... | collective-permute-start | bytes 18874376 | tf_op jit(solution)/shard_map/ppermute | solution.py:194
  8.7 3.6 %collective-permute-start.9 = (f32[4,3072]{1,0:T(4,128)S(1)}, f32[4,3072]{1,0:T(4,128)S(1)}, u32[]{:S(2)}, u32[]{:S(2)}) collective-permute-start(f32[4,3072]{1,0:T(4,128)S(1)} %dynamic_update_slice.3), channel_id=1, source_target_pairs={{0,16},{8,24},{16,0},{24,8},{1,17},{9,25},{17,1},{25,9},{2,18},{10... | collective-permute-start | bytes 147464 | tf_op jit(solution)/shard_map/ppermute | solution.py:33
  12.3 1.4 collective-permute-start.10
  25.1 1.4 collective-permute-start.11
  26.5 4.2 %collective-permute-start.12 = (f32[4,3072]{1,0:T(4,128)S(1)}, f32[4,3072]{1,0:T(4,128)S(1)}, u32[]{:S(2)}, u32[]{:S(2)}) collective-permute-start(f32[4,3072]{1,0:T(4,128)S(1)} %fusion.34), channel_id=1, source_target_pairs={{0,4},{2,6},{4,0},{6,2},{1,5},{3,7},{5,1},{7,3},{8,12},{10,14},{12... | collective-permute-start | bytes 147464 | tf_op jit(solution)/shard_map/ppermute | solution.py:33
  31.1 111.1 %collective-permute-done.11 = f32[4,3072]{1,0:T(4,128)S(1)} collective-permute-done((f32[4,3072]{1,0:T(4,128)S(1)}, f32[4,3072]{1,0:T(4,128)S(1)}, u32[]{:S(2)}, u32[]{:S(2)}) %collective-permute-start.11) | collective-permute-done | bytes 49184 | tf_op jit(solution)/shard_map/ppermute | solution.py:33
  145.0 2.6 %conditional.1 = (bf16[4,256,3072]{2,1,0:T(8,128)(2,1)}) conditional(s32[]{:T(128)} %bitcast.44, bf16[4,2,128,3072]{3,2,1,0:T(8,128)(2,1)} %collective-permute-done.14, bf16[4,2,128,3072]{3,2,1,0:T(8,128)(2,1)S(1)} %bitcast.135), branch_computations={%region_0.1_spmd, %region_1.2_spmd} | conditional | bytes 12582920 | solution.py:215
  145.0 2.6 %copy.11 = bf16[4,256,3072]{2,1,0:T(8,128)(2,1)} copy(bf16[4,256,3072]{2,1,0:T(8,128)(2,1)S(1)} %bitcast.136) | data formatting | bytes 12582912 | tf_op jit(solution)/shard_map/cond
  147.7 95.4 %while.13 = (s32[]{:T(128)}, f32[4,3072]{1,0:T(4,128)S(1)}, pred[]{:T(512)}, bf16[4,256,3072]{2,1,0:T(8,128)(2,1)}, f32[1,128,128]{2,1,0:T(8,128)S(1)}, /*index=...) while((s32[]{:T(128)}, f32[4,3072]{1,0:T(4,128)S(1)}, ...), condition=%wide.region_6.7_spmd, body=%wide.region_2.6_spmd.sunk | while | flops 3247300608 | bytes 67175664 | solution.py:250
  148.3 9.6 %eval_jaxpr.5 = (f32[4,256,256]{2,1,0:T(8,128)}, f32[4,256,256]{2,1,0:T(8,128)}) custom-call(bf16[4,256,3072]{2,1,0:T(8,128)(2,1)} %get-tuple-element.372.mine_ref, bf16[4,256,3072]{2,1,0:T(8,128)(2,1)} %get-tuple-element.374.other_ref, f32[4,1,3072]{2,1,0:T(1,128)} %broadcast_in_dim.36.field_ref), custom_call_target="tpu_custom_call" | custom-call | tf_op jit(solution)/shard_map/while/body/eval_jaxpr/pallas_call | solution.py:80
  157.9 1.8 add_bitcast_fusion.4
  160.0 2.6 %collective-permute-done = f32[2,4,2,128,128]{4,3,1,2,0:T(8,128)S(1)} collective-permute-done((f32[2,4,2,128,128]{4,3,1,2,0:T(8,128)S(1)}, f32[2,4,2,128,128]{4,3,1,2,0:T(8,128)S(1)}, u32[]{:S(2)}, u32[]{:S(2)}) %collective-permute-start) | collective-permute-done | bytes 1048608 | tf_op jit(solution)/shard_map/while/body/eval_jaxpr/ppermute | solution.py:49
  163.1 4.6 %multiply_reduce_fusion.7 = f32[4,3072]{1,0:T(4,128)S(1)} fusion(bf16[4,256,3072]{2,1,0:T(8,128)(2,1)S(1)} %bitcast.138, bf16[4,256,3072]{2,1,0:T(8,128)(2,1)} %get-tuple-element.374.other_ref, bf16[4,128,128]{2,1,0:T(8,128)(2,1)S(1)} %get-tuple-element.325, bf16[4,128,128]{2,1,0:T(8,128)(2,1)S(1)} %get-tuple-element.326, ...), kind=kOutput, calls=%fused_computation.1.clone.1 | convolution fusion | flops 1622134784 | bytes 13025280 | tf_op jit(solution)/shard_map/while/body/eval_jaxpr/fab,fbn->fan/dot_general | solution.py:105
  167.7 4.6 %multiply_reduce_fusion.6 = f32[4,3072]{1,0:T(4,128)S(1)} fusion(bf16[4,256,3072]{2,1,0:T(8,128)(2,1)} %get-tuple-element.374.other_ref, bf16[4,256,3072]{2,1,0:T(8,128)(2,1)S(1)} %bitcast.138, bf16[4,128,128]{2,1,0:T(8,128)(2,1)S(1)} %get-tuple-element.322, bf16[4,128,128]{2,1,0:T(8,128)(2,1)S(1)} %get-tuple-element.323, ...), kind=kOutput, calls=%fused_computation.clone.1 | convolution fusion | flops 1622134784 | bytes 13025280 | tf_op jit(solution)/shard_map/while/body/eval_jaxpr/fab,fbn->fan/dot_general | solution.py:105
  172.4 2.8 %collective-permute-start.1 = (f32[4,3072]{1,0:T(4,128)S(1)}, f32[4,3072]{1,0:T(4,128)S(1)}, u32[]{:S(2)}, u32[]{:S(2)}) collective-permute-start(f32[4,3072]{1,0:T(4,128)S(1)} %select_add_fusion.2), channel_id=1, source_target_pairs={{0,24},{8,16},{16,8},{24,0},{1,25},{9,17},{17,9},{25,1},{2,26},{10... | collective-permute-start | bytes 147464 | tf_op jit(solution)/shard_map/while/body/eval_jaxpr/ppermute | solution.py:33
  175.2 7.0 %collective-permute-start.2 = (f32[4,3072]{1,0:T(4,128)S(1)}, f32[4,3072]{1,0:T(4,128)S(1)}, u32[]{:S(2)}, u32[]{:S(2)}) collective-permute-start(f32[4,3072]{1,0:T(4,128)S(1)} %select_add_fusion.2), channel_id=1, source_target_pairs={{0,16},{8,24},{16,0},{24,8},{1,17},{9,25},{17,1},{25,9},{2,18},{10... | collective-permute-start | bytes 147464 | tf_op jit(solution)/shard_map/while/body/eval_jaxpr/ppermute | solution.py:33
  182.2 2.1 collective-permute-done.2
  184.3 2.0 collective-permute-done.3
  186.5 5.9 %collective-permute-start.5 = (f32[4,3072]{1,0:T(4,128)S(1)}, f32[4,3072]{1,0:T(4,128)S(1)}, u32[]{:S(2)}, u32[]{:S(2)}) collective-permute-start(f32[4,3072]{1,0:T(4,128)S(1)} %fusion.52), channel_id=1, source_target_pairs={{0,4},{2,6},{4,0},{6,2},{1,5},{3,7},{5,1},{7,3},{8,12},{10,14},{12... | collective-permute-start | bytes 147464 | tf_op jit(solution)/shard_map/while/body/eval_jaxpr/ppermute | solution.py:33
  192.9 2.5 %collective-permute-done.5 = f32[4,3072]{1,0:T(4,128)S(1)} collective-permute-done((f32[4,3072]{1,0:T(4,128)S(1)}, f32[4,3072]{1,0:T(4,128)S(1)}, u32[]{:S(2)}, u32[]{:S(2)}) %collective-permute-start.5) | collective-permute-done | bytes 49184 | tf_op jit(solution)/shard_map/while/body/eval_jaxpr/ppermute | solution.py:33
  200.6 9.6 %eval_jaxpr.5 = (f32[4,256,256]{2,1,0:T(8,128)}, f32[4,256,256]{2,1,0:T(8,128)}) custom-call(bf16[4,256,3072]{2,1,0:T(8,128)(2,1)} %get-tuple-element.372.mine_ref, bf16[4,256,3072]{2,1,0:T(8,128)(2,1)} %get-tuple-element.374.other_ref, f32[4,1,3072]{2,1,0:T(1,128)} %broadcast_in_dim.36.field_ref), custom_call_target="tpu_custom_call" | custom-call | tf_op jit(solution)/shard_map/while/body/eval_jaxpr/pallas_call | solution.py:80
  210.2 1.8 add_bitcast_fusion.4
  212.5 2.5 %collective-permute-done = f32[2,4,2,128,128]{4,3,1,2,0:T(8,128)S(1)} collective-permute-done((f32[2,4,2,128,128]{4,3,1,2,0:T(8,128)S(1)}, f32[2,4,2,128,128]{4,3,1,2,0:T(8,128)S(1)}, u32[]{:S(2)}, u32[]{:S(2)}) %collective-permute-start) | collective-permute-done | bytes 1048608 | tf_op jit(solution)/shard_map/while/body/eval_jaxpr/ppermute | solution.py:49
  215.4 4.6 %multiply_reduce_fusion.7 = f32[4,3072]{1,0:T(4,128)S(1)} fusion(bf16[4,256,3072]{2,1,0:T(8,128)(2,1)S(1)} %bitcast.138, bf16[4,256,3072]{2,1,0:T(8,128)(2,1)} %get-tuple-element.374.other_ref, bf16[4,128,128]{2,1,0:T(8,128)(2,1)S(1)} %get-tuple-element.325, bf16[4,128,128]{2,1,0:T(8,128)(2,1)S(1)} %get-tuple-element.326, ...), kind=kOutput, calls=%fused_computation.1.clone.1 | convolution fusion | flops 1622134784 | bytes 13025280 | tf_op jit(solution)/shard_map/while/body/eval_jaxpr/fab,fbn->fan/dot_general | solution.py:105
  220.0 4.6 %multiply_reduce_fusion.6 = f32[4,3072]{1,0:T(4,128)S(1)} fusion(bf16[4,256,3072]{2,1,0:T(8,128)(2,1)} %get-tuple-element.374.other_ref, bf16[4,256,3072]{2,1,0:T(8,128)(2,1)S(1)} %bitcast.138, bf16[4,128,128]{2,1,0:T(8,128)(2,1)S(1)} %get-tuple-element.322, bf16[4,128,128]{2,1,0:T(8,128)(2,1)S(1)} %get-tuple-element.323, ...), kind=kOutput, calls=%fused_computation.clone.1 | convolution fusion | flops 1622134784 | bytes 13025280 | tf_op jit(solution)/shard_map/while/body/eval_jaxpr/fab,fbn->fan/dot_general | solution.py:105
  224.7 2.8 %collective-permute-start.1 = (f32[4,3072]{1,0:T(4,128)S(1)}, f32[4,3072]{1,0:T(4,128)S(1)}, u32[]{:S(2)}, u32[]{:S(2)}) collective-permute-start(f32[4,3072]{1,0:T(4,128)S(1)} %select_add_fusion.2), channel_id=1, source_target_pairs={{0,24},{8,16},{16,8},{24,0},{1,25},{9,17},{17,9},{25,1},{2,26},{10... | collective-permute-start | bytes 147464 | tf_op jit(solution)/shard_map/while/body/eval_jaxpr/ppermute | solution.py:33
  228.2 1.5 collective-permute-done.1
  229.7 1.8 collective-permute-done.2
  231.7 2.9 %collective-permute-start.4 = (f32[4,3072]{1,0:T(4,128)S(1)}, f32[4,3072]{1,0:T(4,128)S(1)}, u32[]{:S(2)}, u32[]{:S(2)}) collective-permute-start(f32[4,3072]{1,0:T(4,128)S(1)} %fusion.52), channel_id=1, source_target_pairs={{0,6},{2,4},{4,2},{6,0},{1,7},{3,5},{5,3},{7,1},{8,14},{10,12},{12... | collective-permute-start | bytes 147464 | tf_op jit(solution)/shard_map/while/body/eval_jaxpr/ppermute | solution.py:33
  234.6 1.5 collective-permute-start.6
  236.2 1.6 collective-permute-done.4
  237.7 1.8 collective-permute-done.5
  (109 shorter events, 20.0 us)
Async XLA Ops:
  0.0 19.8 %copy-start.1 = (s32[16]{0:T(128)S(1)}, s32[16]{0:T(128)}, u32[]{:S(2)}) copy-start(s32[16]{0:T(128)} %constant.200.clone) | copy-start | bytes 196
  0.0 16.4 %copy-start = (f32[4,2,128,128]{3,2,1,0:T(8,128)S(1)}, f32[4,2,128,128]{3,2,1,0:T(8,128)}, u32[]{:S(2)}) copy-start(f32[4,2,128,128]{3,2,1,0:T(8,128)} %param.12) | copy-start | bytes 1572868
  0.0 143.6 %collective-permute-start.14 = (bf16[4,2,128,3072]{3,2,1,0:T(8,128)(2,1)}, bf16[4,2,128,3072]{3,2,1,0:T(8,128)(2,1)}, u32[]{:S(2)}, u32[]{:S(2)}) collective-permute-start(bf16[4,2,128,3072]{3,2,1,0:T(8,128)(2,1)} %param.10), channel_id=1, source_target_pairs={{0,2},{12,8},{16,22},{20,18},{10,14},{30,28},{1,3},{13,9},{17,23},... | collective-permute-start | bytes 18874376 | tf_op jit(solution)/shard_map/ppermute | solution.py:194
  8.6 15.7 %collective-permute-start.8 = (f32[4,3072]{1,0:T(4,128)S(1)}, f32[4,3072]{1,0:T(4,128)S(1)}, u32[]{:S(2)}, u32[]{:S(2)}) collective-permute-start(f32[4,3072]{1,0:T(4,128)S(1)} %dynamic_update_slice.3), channel_id=1, source_target_pairs={{0,8},{8,0},{16,24},{24,16},{1,9},{9,1},{17,25},{25,17},{2,10},{10... | collective-permute-start | bytes 147464 | tf_op jit(solution)/shard_map/ppermute | solution.py:33
  8.7 16.3 %collective-permute-start.9 = (f32[4,3072]{1,0:T(4,128)S(1)}, f32[4,3072]{1,0:T(4,128)S(1)}, u32[]{:S(2)}, u32[]{:S(2)}) collective-permute-start(f32[4,3072]{1,0:T(4,128)S(1)} %dynamic_update_slice.3), channel_id=1, source_target_pairs={{0,16},{8,24},{16,0},{24,8},{1,17},{9,25},{17,1},{25,9},{2,18},{10... | collective-permute-start | bytes 147464 | tf_op jit(solution)/shard_map/ppermute | solution.py:33
  12.3 12.7 %collective-permute-start.10 = (f32[4,3072]{1,0:T(4,128)S(1)}, f32[4,3072]{1,0:T(4,128)S(1)}, u32[]{:S(2)}, u32[]{:S(2)}) collective-permute-start(f32[4,3072]{1,0:T(4,128)S(1)} %dynamic_update_slice.3), channel_id=1, source_target_pairs={{0,24},{8,16},{16,8},{24,0},{1,25},{9,17},{17,9},{25,1},{2,26},{10... | collective-permute-start | bytes 147464 | tf_op jit(solution)/shard_map/ppermute | solution.py:33
  23.6 7.1 %collective-permute-start.15 = (f32[5,128,128]{2,1,0:T(8,128)S(1)}, f32[5,128,128]{2,1,0:T(8,128)S(1)}, u32[]{:S(2)}, u32[]{:S(2)}) collective-permute-start(f32[5,128,128]{2,1,0:T(8,128)S(1)} %fusion.29), channel_id=1, source_target_pairs={{8,2},{4,8},{24,22},{12,18},{26,14},{22,28},{9,3},{5,9},{25,23},{1... | collective-permute-start | bytes 983048 | tf_op jit(solution)/shard_map/ppermute | solution.py:206
  24.3 6.7 %collective-permute-start.16 = (f32[5,128,128]{2,1,0:T(8,128)S(1)}, f32[5,128,128]{2,1,0:T(8,128)S(1)}, u32[]{:S(2)}, u32[]{:S(2)}) collective-permute-start(f32[5,128,128]{2,1,0:T(8,128)S(1)} %fusion.29), channel_id=1, source_target_pairs={{16,8},{6,22},{17,9},{7,23}} | collective-permute-start | bytes 983048 | tf_op jit(solution)/shard_map/ppermute | solution.py:206
  25.1 117.1 %collective-permute-start.11 = (f32[4,3072]{1,0:T(4,128)S(1)}, f32[4,3072]{1,0:T(4,128)S(1)}, u32[]{:S(2)}, u32[]{:S(2)}) collective-permute-start(f32[4,3072]{1,0:T(4,128)S(1)} %fusion.34), channel_id=1, source_target_pairs={{0,2},{2,0},{4,6},{6,4},{1,3},{3,1},{5,7},{7,5},{8,10},{10,8},{12,... | collective-permute-start | bytes 147464 | tf_op jit(solution)/shard_map/ppermute | solution.py:33
  26.5 116.2 %collective-permute-start.12 = (f32[4,3072]{1,0:T(4,128)S(1)}, f32[4,3072]{1,0:T(4,128)S(1)}, u32[]{:S(2)}, u32[]{:S(2)}) collective-permute-start(f32[4,3072]{1,0:T(4,128)S(1)} %fusion.34), channel_id=1, source_target_pairs={{0,4},{2,6},{4,0},{6,2},{1,5},{3,7},{5,1},{7,3},{8,12},{10,14},{12... | collective-permute-start | bytes 147464 | tf_op jit(solution)/shard_map/ppermute | solution.py:33
  30.7 112.5 %collective-permute-start.13 = (f32[4,3072]{1,0:T(4,128)S(1)}, f32[4,3072]{1,0:T(4,128)S(1)}, u32[]{:S(2)}, u32[]{:S(2)}) collective-permute-start(f32[4,3072]{1,0:T(4,128)S(1)} %fusion.34), channel_id=1, source_target_pairs={{0,6},{2,4},{4,2},{6,0},{1,7},{3,5},{5,3},{7,1},{8,14},{10,12},{12... | collective-permute-start | bytes 147464 | tf_op jit(solution)/shard_map/ppermute | solution.py:33
  31.0 112.8 %slice-start = ((s8[6291456]{0:T(1024)(128)(4,1)}), s8[4194304]{0:T(1024)(128)(4,1)S(1)}, s32[]{:S(2)}) async-start(s8[6291456]{0:T(1024)(128)(4,1)} %bitcast.134), calls=%async_computation | async-start | bytes 8388608
  31.0 112.3 %collective-permute-start.17 = (f32[2,5,128,128]{3,2,1,0:T(8,128)S(1)}, f32[2,5,128,128]{3,2,1,0:T(8,128)S(1)}, u32[]{:S(2)}, u32[]{:S(2)}) collective-permute-start(f32[2,5,128,128]{3,2,1,0:T(8,128)S(1)} %pad_maximum_fusion.8), channel_id=1, source_target_pairs={{0,1},{1,0},{2,3},{3,2},{4,5},{5,4},{6,7},{7,6},{8,9},{9,8},{10,11... | collective-permute-start | bytes 1966088 | tf_op jit(solution)/shard_map/ppermute | solution.py:207
  148.3 14.7 %slice-start.2 = ((s8[6291456]{0:T(1024)(128)(4,1)}), s8[2097152]{0:T(1024)(128)(4,1)S(1)}, s32[]{:S(2)}) async-start(s8[6291456]{0:T(1024)(128)(4,1)} %bitcast.137), calls=%async_computation.2 | async-start | bytes 4194304 | tf_op jit(solution)/shard_map/while
  157.9 5.2 %slice-start.3 = ((s8[6291456]{0:T(1024)(128)(4,1)}), s8[4194304]{0:T(1024)(128)(4,1)S(1)}, s32[]{:S(2)}) async-start(s8[6291456]{0:T(1024)(128)(4,1)} %bitcast.137), calls=%async_computation.3 | async-start | bytes 8388608 | tf_op jit(solution)/shard_map/while
  159.9 2.7 %collective-permute-start = (f32[2,4,2,128,128]{4,3,1,2,0:T(8,128)S(1)}, f32[2,4,2,128,128]{4,3,1,2,0:T(8,128)S(1)}, u32[]{:S(2)}, u32[]{:S(2)}) collective-permute-start(f32[2,4,2,128,128]{4,3,1,2,0:T(8,128)S(1)} %pad_maximum_fusion.14), channel_id=1, source_target_pairs={{0,1},{1,0},{2,3},{3,2},{4,5},{5,4},{6,7},{7,6},{8,9},{9,8},{10,11... | collective-permute-start | bytes 3145736 | tf_op jit(solution)/shard_map/while/body/eval_jaxpr/ppermute | solution.py:49
  172.4 9.8 %collective-permute-start.1 = (f32[4,3072]{1,0:T(4,128)S(1)}, f32[4,3072]{1,0:T(4,128)S(1)}, u32[]{:S(2)}, u32[]{:S(2)}) collective-permute-start(f32[4,3072]{1,0:T(4,128)S(1)} %select_add_fusion.2), channel_id=1, source_target_pairs={{0,24},{8,16},{16,8},{24,0},{1,25},{9,17},{17,9},{25,1},{2,26},{10... | collective-permute-start | bytes 147464 | tf_op jit(solution)/shard_map/while/body/eval_jaxpr/ppermute | solution.py:33
  175.2 9.0 %collective-permute-start.2 = (f32[4,3072]{1,0:T(4,128)S(1)}, f32[4,3072]{1,0:T(4,128)S(1)}, u32[]{:S(2)}, u32[]{:S(2)}) collective-permute-start(f32[4,3072]{1,0:T(4,128)S(1)} %select_add_fusion.2), channel_id=1, source_target_pairs={{0,16},{8,24},{16,0},{24,8},{1,17},{9,25},{17,1},{25,9},{2,18},{10... | collective-permute-start | bytes 147464 | tf_op jit(solution)/shard_map/while/body/eval_jaxpr/ppermute | solution.py:33
  182.2 4.1 %collective-permute-start.3 = (f32[4,3072]{1,0:T(4,128)S(1)}, f32[4,3072]{1,0:T(4,128)S(1)}, u32[]{:S(2)}, u32[]{:S(2)}) collective-permute-start(f32[4,3072]{1,0:T(4,128)S(1)} %select_add_fusion.2), channel_id=1, source_target_pairs={{0,8},{8,0},{16,24},{24,16},{1,9},{9,1},{17,25},{25,17},{2,10},{10... | collective-permute-start | bytes 147464 | tf_op jit(solution)/shard_map/while/body/eval_jaxpr/ppermute | solution.py:33
  186.4 6.5 %collective-permute-start.4 = (f32[4,3072]{1,0:T(4,128)S(1)}, f32[4,3072]{1,0:T(4,128)S(1)}, u32[]{:S(2)}, u32[]{:S(2)}) collective-permute-start(f32[4,3072]{1,0:T(4,128)S(1)} %fusion.52), channel_id=1, source_target_pairs={{0,6},{2,4},{4,2},{6,0},{1,7},{3,5},{5,3},{7,1},{8,14},{10,12},{12... | collective-permute-start | bytes 147464 | tf_op jit(solution)/shard_map/while/body/eval_jaxpr/ppermute | solution.py:33
  186.5 9.0 %collective-permute-start.5 = (f32[4,3072]{1,0:T(4,128)S(1)}, f32[4,3072]{1,0:T(4,128)S(1)}, u32[]{:S(2)}, u32[]{:S(2)}) collective-permute-start(f32[4,3072]{1,0:T(4,128)S(1)} %fusion.52), channel_id=1, source_target_pairs={{0,4},{2,6},{4,0},{6,2},{1,5},{3,7},{5,1},{7,3},{8,12},{10,14},{12... | collective-permute-start | bytes 147464 | tf_op jit(solution)/shard_map/while/body/eval_jaxpr/ppermute | solution.py:33
  192.4 4.1 %collective-permute-start.6 = (f32[4,3072]{1,0:T(4,128)S(1)}, f32[4,3072]{1,0:T(4,128)S(1)}, u32[]{:S(2)}, u32[]{:S(2)}) collective-permute-start(f32[4,3072]{1,0:T(4,128)S(1)} %fusion.52), channel_id=1, source_target_pairs={{0,2},{2,0},{4,6},{6,4},{1,3},{3,1},{5,7},{7,5},{8,10},{10,8},{12,... | collective-permute-start | bytes 147464 | tf_op jit(solution)/shard_map/while/body/eval_jaxpr/ppermute | solution.py:33
  197.2 1.4 collective-permute-start.7
  200.6 14.7 %slice-start.2 = ((s8[6291456]{0:T(1024)(128)(4,1)}), s8[2097152]{0:T(1024)(128)(4,1)S(1)}, s32[]{:S(2)}) async-start(s8[6291456]{0:T(1024)(128)(4,1)} %bitcast.137), calls=%async_computation.2 | async-start | bytes 4194304 | tf_op jit(solution)/shard_map/while
  212.2 2.7 %collective-permute-start = (f32[2,4,2,128,128]{4,3,1,2,0:T(8,128)S(1)}, f32[2,4,2,128,128]{4,3,1,2,0:T(8,128)S(1)}, u32[]{:S(2)}, u32[]{:S(2)}) collective-permute-start(f32[2,4,2,128,128]{4,3,1,2,0:T(8,128)S(1)} %pad_maximum_fusion.14), channel_id=1, source_target_pairs={{0,1},{1,0},{2,3},{3,2},{4,5},{5,4},{6,7},{7,6},{8,9},{9,8},{10,11... | collective-permute-start | bytes 3145736 | tf_op jit(solution)/shard_map/while/body/eval_jaxpr/ppermute | solution.py:49
  224.7 5.1 %collective-permute-start.1 = (f32[4,3072]{1,0:T(4,128)S(1)}, f32[4,3072]{1,0:T(4,128)S(1)}, u32[]{:S(2)}, u32[]{:S(2)}) collective-permute-start(f32[4,3072]{1,0:T(4,128)S(1)} %select_add_fusion.2), channel_id=1, source_target_pairs={{0,24},{8,16},{16,8},{24,0},{1,25},{9,17},{17,9},{25,1},{2,26},{10... | collective-permute-start | bytes 147464 | tf_op jit(solution)/shard_map/while/body/eval_jaxpr/ppermute | solution.py:33
  227.5 4.1 %collective-permute-start.2 = (f32[4,3072]{1,0:T(4,128)S(1)}, f32[4,3072]{1,0:T(4,128)S(1)}, u32[]{:S(2)}, u32[]{:S(2)}) collective-permute-start(f32[4,3072]{1,0:T(4,128)S(1)} %select_add_fusion.2), channel_id=1, source_target_pairs={{0,16},{8,24},{16,0},{24,8},{1,17},{9,25},{17,1},{25,9},{2,18},{10... | collective-permute-start | bytes 147464 | tf_op jit(solution)/shard_map/while/body/eval_jaxpr/ppermute | solution.py:33
  227.5 4.1 %collective-permute-start.3 = (f32[4,3072]{1,0:T(4,128)S(1)}, f32[4,3072]{1,0:T(4,128)S(1)}, u32[]{:S(2)}, u32[]{:S(2)}) collective-permute-start(f32[4,3072]{1,0:T(4,128)S(1)} %select_add_fusion.2), channel_id=1, source_target_pairs={{0,8},{8,0},{16,24},{24,16},{1,9},{9,1},{17,25},{25,17},{2,10},{10... | collective-permute-start | bytes 147464 | tf_op jit(solution)/shard_map/while/body/eval_jaxpr/ppermute | solution.py:33
  231.7 6.1 %collective-permute-start.4 = (f32[4,3072]{1,0:T(4,128)S(1)}, f32[4,3072]{1,0:T(4,128)S(1)}, u32[]{:S(2)}, u32[]{:S(2)}) collective-permute-start(f32[4,3072]{1,0:T(4,128)S(1)} %fusion.52), channel_id=1, source_target_pairs={{0,6},{2,4},{4,2},{6,0},{1,7},{3,5},{5,3},{7,1},{8,14},{10,12},{12... | collective-permute-start | bytes 147464 | tf_op jit(solution)/shard_map/while/body/eval_jaxpr/ppermute | solution.py:33
  234.6 5.0 %collective-permute-start.5 = (f32[4,3072]{1,0:T(4,128)S(1)}, f32[4,3072]{1,0:T(4,128)S(1)}, u32[]{:S(2)}, u32[]{:S(2)}) collective-permute-start(f32[4,3072]{1,0:T(4,128)S(1)} %fusion.52), channel_id=1, source_target_pairs={{0,4},{2,6},{4,0},{6,2},{1,5},{3,7},{5,1},{7,3},{8,12},{10,14},{12... | collective-permute-start | bytes 147464 | tf_op jit(solution)/shard_map/while/body/eval_jaxpr/ppermute | solution.py:33
  234.6 5.0 %collective-permute-start.6 = (f32[4,3072]{1,0:T(4,128)S(1)}, f32[4,3072]{1,0:T(4,128)S(1)}, u32[]{:S(2)}, u32[]{:S(2)}) collective-permute-start(f32[4,3072]{1,0:T(4,128)S(1)} %fusion.52), channel_id=1, source_target_pairs={{0,2},{2,0},{4,6},{6,4},{1,3},{3,1},{5,7},{7,5},{8,10},{10,8},{12,... | collective-permute-start | bytes 147464 | tf_op jit(solution)/shard_map/while/body/eval_jaxpr/ppermute | solution.py:33
  240.3 1.4 collective-permute-start.7
  (2 other events, 6.8 us)
